TPU v7x, 256 devices: a whole 4x4x8 slice. The times are simulated.
256 devices in a mesh: shot: 16 (over y, x_lo, core), space: 16 (over z, x_hi).
Axes of the slice: x: 4 (x_hi: 2, x_lo: 2; x = x_hi * 2 + x_lo), y: 4, z: 8, core: 2. Of those that a mesh axis runs over, the one named last changes fastest.
Arguments:
- courant: float32 [128, 128, 128], P('space'), may hold values from 0.03 to 0.18
- checkpoint: float32 [16, 2, 2048, 8, 128], P('shot', None, 'space'), may hold values from -6 to 6
- block_target: int32 [16, 2048], P('shot'), may hold values from 0 to 2047, as said below
- adjoint_state: float32 [16, 2, 128, 128, 128], P('shot', None, 'space'), may hold values from -6 to 6
- wavelet: float32 [16, 4], P('shot'), may hold values from -8 to 8
- source_cell: int32 [16], P('shot'), may hold values from 0 to 2097151
- receiver_cell: int32 [16, 512], P('shot'), may hold values from 0 to 2097151
- residual: float32 [16, 4, 512], P('shot'), may hold values from -6 to 6
- check_rows: int32 [16, 128, 16], P('space'), may hold values from 0 to 1023
Outputs:
- gradient: float32 [128, 128, 128], P('space', 'shot')
- adjoint_carry: float32 [16, 2, 128, 128, 128], P('shot', None, 'space')
- checksums: float32 [16, 128, 128], P('space', 'shot')
Inputs may be any that keep to these rules, and one draw needn't show every extreme that they name: `block_target`: each shot's row is a permutation of the block positions. The stored blocks of one device (aligned blocks of 128 entries) name at most 32 positions of any one slab (128 consecutive positions); each device names exactly 32 of one slab, and each slab is named exactly 32 times by one device.
All inputs are finite; a program needn't handle non-finite values.
Results may differ from a plain program's by a relative error of at most 0.0003.
Values sent between devices are 32-bit elements; how exact they have to be, the bound alone decides.
No kernel may reach another device: no remote copies, remote signals or barrier semaphores. Data moves between devices by JAX's collectives and lax.ppermute only.
A program may use at most 128 MiB of HBM per device.

v0:
```python
import jax
import jax.numpy as jnp
from jax import lax
from jax.sharding import PartitionSpec as P

STENCIL = (-205.0 / 72.0, 8.0 / 5.0, -1.0 / 5.0, 8.0 / 315.0, -1.0 / 560.0)


def padded_2(array, sides, width):
    for axis, dim in sides:
        devices, length = (lax.axis_size(axis), array.shape[dim])
        up = [(i, (i + 1) % devices) for i in range(devices - 1)]
        down = [(j, i) for i, j in up]
        last = lax.slice_in_dim(array, length - width, length, axis=dim)
        initial = lax.slice_in_dim(array, 0, width, axis=dim)
        before = lax.ppermute(last, axis, up)
        after = lax.ppermute(initial, axis, down)
        array = jnp.concatenate([before, array, after], axis=dim)
    return array


def laplace(field):
    length = field.shape[0] - 8
    height = field.shape[1]
    breadth = field.shape[2]
    padded = jnp.pad(field, ((0, 0), (4, 4), (4, 4)))
    summed = 3.0 * STENCIL[0] * padded[4 : 4 + length, 4 : 4 + height, 4 : 4 + breadth]
    for offset in range(1, 5):
        summed = summed + STENCIL[offset] * (
            padded[4 + offset : 4 + offset + length, 4 : 4 + height, 4 : 4 + breadth]
            + padded[4 - offset : 4 - offset + length, 4 : 4 + height, 4 : 4 + breadth]
        )
    for offset in range(1, 5):
        summed = summed + STENCIL[offset] * (
            padded[4 : 4 + length, 4 + offset : 4 + offset + height, 4 : 4 + breadth]
            + padded[4 : 4 + length, 4 - offset : 4 - offset + height, 4 : 4 + breadth]
        )
    for offset in range(1, 5):
        summed = summed + STENCIL[offset] * (
            padded[4 : 4 + length, 4 : 4 + height, 4 + offset : 4 + offset + breadth]
            + padded[4 : 4 + length, 4 : 4 + height, 4 - offset : 4 - offset + breadth]
        )
    return summed


def inject(field, cell_index, values, first_row):
    plane_cells = field.shape[1] * field.shape[2]
    local_cell = cell_index - first_row * plane_cells
    inside = (local_cell >= 0) & (local_cell < field.shape[0] * plane_cells)
    target = jnp.where(inside, local_cell, field.shape[0] * plane_cells)
    flattened = field.reshape(-1).at[target].add(values, mode="drop")
    return flattened.reshape(field.shape)


def advance(before, current_ext, courant, wave_value, source, first_row):
    following = 2.0 * current_ext[4:-4] - before + courant * laplace(current_ext)
    return inject(following, source, wave_value, first_row)


def retreat(following, current, weighted_ext, values, cell_index, first_row):
    earlier = 2.0 * current - following + laplace(weighted_ext)
    return inject(earlier, cell_index, values, first_row)


def extend(field):
    return padded_2(field, (("space", 0),), 4)


def body(
    courant,
    checkpoint,
    block_target,
    adjoint_state,
    wavelet,
    source_cell,
    receiver_cell,
    residual,
    check_rows,
):
    devices = lax.axis_size("space")
    position = lax.axis_index("space")
    length, height, breadth = courant.shape
    first_row = position * length
    per_device = checkpoint.shape[2]
    block_rows = checkpoint.shape[3]
    capacity = per_device // 4
    targets = block_target[0]
    payload = checkpoint[0]
    peers = targets // per_device
    matches = (peers[:, None] == jnp.arange(devices, dtype=jnp.int32)[None, :]).astype(jnp.int32)
    grouped = matches.reshape(devices, per_device, devices)
    ranking = jnp.sum((jnp.cumsum(grouped, axis=1) - grouped) * grouped, axis=2)
    peer_grid = peers.reshape(devices, per_device)
    own_peers = lax.dynamic_index_in_dim(peer_grid, position, 0, keepdims=False)
    own_ranks = lax.dynamic_index_in_dim(ranking, position, 0, keepdims=False)
    slot_of = own_peers * capacity + own_ranks
    outgoing = (
        jnp.zeros((2, devices * capacity, block_rows, breadth), jnp.float32)
        .at[:, slot_of]
        .set(payload)
    )
    outgoing = outgoing.reshape(2, devices, capacity, block_rows, breadth)
    incoming = lax.all_to_all(outgoing, "space", split_axis=1, concat_axis=1, tiled=True)
    incoming = incoming.reshape(2, devices * capacity, block_rows, breadth)
    sender_grid = jnp.arange(devices, dtype=jnp.int32)[:, None] * capacity + ranking
    owned = peer_grid == position
    local_block = (targets % per_device).reshape(devices, per_device)
    where_from = (
        jnp.zeros((per_device,), jnp.int32)
        .at[jnp.where(owned, local_block, per_device).reshape(-1)]
        .set(sender_grid.reshape(-1), mode="drop")
    )
    placed = jnp.take(incoming, where_from, axis=1)
    levels = placed.reshape(2, length, height, breadth)
    wavelet_row = wavelet[0]
    receivers = receiver_cell[0]
    traces = residual[0]
    horizon = wavelet_row.shape[0]
    fields = [levels[0], levels[1]]
    adjoints = [None] * (horizon + 2)
    adjoints[horizon + 1] = adjoint_state[0, 0]
    adjoints[horizon] = adjoint_state[0, 1]
    for moment in range(1, horizon + 1):
        fields.append(
            advance(
                fields[-2],
                extend(fields[-1]),
                courant,
                wavelet_row[moment - 1 : moment],
                source_cell,
                first_row,
            )
        )
    for moment in range(horizon, 0, -1):
        weighted = extend(courant * adjoints[moment])
        adjoints[moment - 1] = retreat(
            adjoints[moment + 1],
            adjoints[moment],
            weighted,
            traces[moment - 1],
            receivers,
            first_row,
        )
    partial_value = jnp.zeros((length, height, breadth), jnp.float32)
    for moment in range(1, horizon + 1):
        partial_value = partial_value + adjoints[moment] * (
            fields[moment + 1] - 2.0 * fields[moment] + fields[moment - 1]
        )
    slab_rows = partial_value.reshape(length * height, breadth)
    check_part = jnp.sum(slab_rows[check_rows[0]], axis=1)
    grad_share = lax.psum_scatter(partial_value, "shot", scatter_dimension=1, tiled=True)
    check_share = lax.psum_scatter(check_part, "shot", scatter_dimension=0, tiled=True)
    adjoint_carry = jnp.stack([adjoints[1], adjoints[0]])[None]
    return (grad_share, adjoint_carry, check_share[None])


def solution(mesh):
    in_specs = (
        P("space", None, None),
        P("shot", None, "space", None, None),
        P("shot", None),
        P("shot", None, "space", None, None),
        P("shot", None),
        P("shot"),
        P("shot", None),
        P("shot", None, None),
        P("space", None, None),
    )
    out_specs = (
        P("space", "shot", None),
        P("shot", None, "space", None, None),
        P("space", "shot", None),
    )
    return jax.shard_map(body, mesh=mesh, in_specs=in_specs, out_specs=out_specs, check_vma=False)
```

profile of v0, /device:TPU:100, one launch (start us, length us, event | category | flops | bytes accessed | tf_op | source)
XLA Modules:
  0.0 527.3 jit_solution(15008843376083713308)
XLA Ops:
  14.6 13.6 %scatter_fusion.3 = f32[2,512,8,128]{3,2,1,0:T(8,128)} fusion(f32[2,512,8,128]{3,2,1,0:T(8,128)} %broadcast_in_dim.48, s32[128]{0:T(128)S(1)} %fusion.310, f32[128,2,8,128]{3,2,1,0:T(8,128)S(1)} %copy.34), kind=kCustom, calls=%fused_computation.6 | custom fusion | bytes 3146240 | tf_op jit(solution)/shard_map/scatter | solution.py:100
  28.2 4.7 copy.35
  32.8 10.2 %all-to-all-start = ((f32[2,16,32,8,128]{4,3,2,0,1:T(8,128)}), f32[2,16,32,8,128]{4,3,2,0,1:T(8,128)}, u32[]{:S(2)}, u32[]{:S(2)}) async-start(f32[2,16,32,8,128]{4,3,2,0,1:T(8,128)} %copy.35), calls=%async_computation | async-start | bytes 8388608 | tf_op jit(solution)/shard_map/all_to_all | solution.py:103
  45.8 7.0 %collective-permute-start.1 = (f32[4,128,128]{2,1,0:T(8,128)S(1)}, f32[4,128,128]{2,1,0:T(8,128)S(1)}, u32[]{:S(2)}, u32[]{:S(2)}) collective-permute-start(f32[4,128,128]{2,1,0:T(8,128)S(1)} %get-tuple-element.64), channel_id=1, source_target_pairs={{0,1},{1,2},{2,3},{3,4},{4,5},{5,6},{6,7},{7,8},{8,9},{9,10},{10,1... | collective-permute-start | bytes 786440 | tf_op jit(solution)/shard_map/ppermute | solution.py:16
  53.0 8.0 %scatter_custom_fusion.3 = s32[128]{0:T(128)S(1)} fusion(s32[2048]{0:T(1024)S(1)} %bitcast.210, s32[2048]{0:T(1024)S(1)} %add_bitcast_fusion, s32[]{:T(128)} %constant.152.clone.1), kind=kCustom, calls=%fused_computation.564 | custom fusion | bytes 516 | tf_op jit(solution)/shard_map/scatter | solution.py:111
  63.3 78.3 %collective-permute-done = f32[4,128,128]{2,1,0:T(8,128)S(1)} collective-permute-done((f32[4,128,128]{2,1,0:T(8,128)S(1)}, f32[4,128,128]{2,1,0:T(8,128)S(1)}, u32[]{:S(2)}, u32[]{:S(2)}) %collective-permute-start) | collective-permute-done | bytes 262176 | tf_op jit(solution)/shard_map/ppermute | solution.py:17
  147.6 3.7 scatter_fusion
  151.5 5.0 collective-permute-start.2
  156.5 4.9 collective-permute-start.3
  166.5 4.8 collective-permute-done.3
  173.1 4.7 copy.36
  177.8 4.0 gather_fusion
  185.2 7.8 %collective-permute-start.7 = (f32[4,128,128]{2,1,0:T(8,128)S(1)}, f32[4,128,128]{2,1,0:T(8,128)S(1)}, u32[]{:S(2)}, u32[]{:S(2)}) collective-permute-start(f32[4,128,128]{2,1,0:T(8,128)S(1)} %bitcast.199), channel_id=1, source_target_pairs={{0,1},{1,2},{2,3},{3,4},{4,5},{5,6},{6,7},{7,8},{8,9},{9,10},{10,1... | collective-permute-start | bytes 786440 | tf_op jit(solution)/shard_map/ppermute | solution.py:16
  197.1 5.5 %collective-permute-done.7 = f32[4,128,128]{2,1,0:T(8,128)S(1)} collective-permute-done((f32[4,128,128]{2,1,0:T(8,128)S(1)}, f32[4,128,128]{2,1,0:T(8,128)S(1)}, u32[]{:S(2)}, u32[]{:S(2)}) %collective-permute-start.7) | collective-permute-done | bytes 262176 | tf_op jit(solution)/shard_map/ppermute | solution.py:16
  204.6 11.8 %fusion.124 = f32[8,128,128]{2,1,0:T(8,128)S(1)} fusion(f32[8,128,128]{2,1,0:T(8,128)S(1)} %copy-done.3, f32[8,128,128]{2,1,0:T(8,128)S(1)} %bitcast.188, f32[4,128,128]{2,1,0:T(8,128)} %copy-done.31, f32[4,128,128]{2,1,0:T(8,128)} %copy-done.30, f32[16,136,136]{2,1,0:T(8,128)} %select_maximum_fusion.8, f32[8,128,128]{2,1,0:T(8,128)} %bitcast.194), kind=kLoop, calls=%fused_computation.252 | loop fusion | flops 6422528 | bytes 11010048 | tf_op jit(solution)/shard_map/add | solution.py:56
  221.3 7.5 %collective-permute-start.9 = (f32[4,128,128]{2,1,0:T(8,128)}, f32[4,128,128]{2,1,0:T(8,128)}, u32[]{:S(2)}, u32[]{:S(2)}) collective-permute-start(f32[4,128,128]{2,1,0:T(8,128)} %bitcast.33), channel_id=1, source_target_pairs={{0,1},{1,2},{2,3},{3,4},{4,5},{5,6},{6,7},{7,8},{8,9},{9,10},{10,1... | collective-permute-start | bytes 786440 | tf_op jit(solution)/shard_map/ppermute | solution.py:16
  232.3 3.8 scatter_fusion.1
  239.0 7.5 %collective-permute-start.5 = (f32[4,128,128]{2,1,0:T(8,128)}, f32[4,128,128]{2,1,0:T(8,128)}, u32[]{:S(2)}, u32[]{:S(2)}) collective-permute-start(f32[4,128,128]{2,1,0:T(8,128)} %get-tuple-element.60), channel_id=1, source_target_pairs={{0,1},{1,2},{2,3},{3,4},{4,5},{5,6},{6,7},{7,8},{8,9},{9,10},{10,1... | collective-permute-start | bytes 786440 | tf_op jit(solution)/shard_map/ppermute | solution.py:16
  248.3 3.5 fusion.98
  255.9 7.8 %collective-permute-start.11 = (f32[4,128,128]{2,1,0:T(8,128)S(1)}, f32[4,128,128]{2,1,0:T(8,128)S(1)}, u32[]{:S(2)}, u32[]{:S(2)}) collective-permute-start(f32[4,128,128]{2,1,0:T(8,128)S(1)} %bitcast.197), channel_id=1, source_target_pairs={{0,1},{1,2},{2,3},{3,4},{4,5},{5,6},{6,7},{7,8},{8,9},{9,10},{10,1... | collective-permute-start | bytes 786440 | tf_op jit(solution)/shard_map/ppermute | solution.py:16
  266.7 5.3 %collective-permute-done.11 = f32[4,128,128]{2,1,0:T(8,128)S(1)} collective-permute-done((f32[4,128,128]{2,1,0:T(8,128)S(1)}, f32[4,128,128]{2,1,0:T(8,128)S(1)}, u32[]{:S(2)}, u32[]{:S(2)}) %collective-permute-start.11) | collective-permute-done | bytes 262176 | tf_op jit(solution)/shard_map/ppermute | solution.py:16
  274.7 12.4 %fusion.72 = f32[8,128,128]{2,1,0:T(8,128)} fusion(f32[8,128,128]{2,1,0:T(8,128)S(1)} %copy-done.5, f32[8,128,128]{2,1,0:T(8,128)S(1)} %bitcast.177, f32[4,128,128]{2,1,0:T(8,128)} %copy-done.29, f32[4,128,128]{2,1,0:T(8,128)} %copy-done.28, f32[16,136,136]{2,1,0:T(8,128)} %select_maximum_fusion.4, f32[8,128,128]{2,1,0:T(8,128)S(1)} %bitcast.173), kind=kLoop, calls=%fused_computation.200 | loop fusion | flops 6422528 | bytes 11010048 | tf_op jit(solution)/shard_map/add | solution.py:56
  294.3 7.5 %collective-permute-start.13 = (f32[4,128,128]{2,1,0:T(8,128)}, f32[4,128,128]{2,1,0:T(8,128)}, u32[]{:S(2)}, u32[]{:S(2)}) collective-permute-start(f32[4,128,128]{2,1,0:T(8,128)} %bitcast.43), channel_id=1, source_target_pairs={{0,1},{1,2},{2,3},{3,4},{4,5},{5,6},{6,7},{7,8},{8,9},{9,10},{10,1... | collective-permute-start | bytes 786440 | tf_op jit(solution)/shard_map/ppermute | solution.py:16
  301.8 4.8 fusion.149
  306.6 5.0 scatter_fusion.2
  313.6 5.1 fusion.46
  329.0 7.5 %collective-permute-start.15 = (f32[4,128,128]{2,1,0:T(8,128)S(1)}, f32[4,128,128]{2,1,0:T(8,128)}, u32[]{:S(2)}, u32[]{:S(2)}) collective-permute-start(f32[4,128,128]{2,1,0:T(8,128)S(1)} %get-tuple-element.56), channel_id=1, source_target_pairs={{0,1},{1,2},{2,3},{3,4},{4,5},{5,6},{6,7},{7,8},{8,9},{9,10},{10,1... | collective-permute-start | bytes 786440 | tf_op jit(solution)/shard_map/ppermute | solution.py:16
  336.6 5.5 %gather_fusion.1 = f32[2048,128]{1,0:T(8,128)S(1)} fusion(f32[1024,128]{1,0:T(8,128)S(1)} %fusion.293, s32[2048]{0:T(1024)S(1)} %broadcast_clamp_fusion), kind=kCustom, calls=%fused_computation.1 | custom fusion | bytes 2105344 | tf_op jit(solution)/shard_map/gather | solution.py:150
  344.5 110.3 %all-reduce.11.cloned.1.call-done = f32[128,128]{1,0:T(8,128)} async-done(((f32[128,128]{1,0:T(8,128)}), f32[128,128]{1,0:T(8,128)}) %all-reduce.11.cloned.1.call-update) | async-done | bytes 65552
  457.8 4.9 fusion.20
  462.7 4.9 scatter_fusion.4
  469.6 50.8 %reduce-scatter.2.cloned.1.call-done = f32[8,8,128]{2,1,0:T(8,128)} async-done(((f32[8,128,128]{2,1,0:T(8,128)}), f32[8,8,128]{2,1,0:T(8,128)}) %reduce-scatter.2.cloned.1.call-update) | async-done | bytes 32784 | tf_op jit(solution)/shard_map/reduce_scatter | solution.py:151
  (159 shorter events, 82.5 us)
Async XLA Ops:
  32.8 140.3 %all-to-all-start = ((f32[2,16,32,8,128]{4,3,2,0,1:T(8,128)}), f32[2,16,32,8,128]{4,3,2,0,1:T(8,128)}, u32[]{:S(2)}, u32[]{:S(2)}) async-start(f32[2,16,32,8,128]{4,3,2,0,1:T(8,128)} %copy.35), calls=%async_computation | async-start | bytes 8388608 | tf_op jit(solution)/shard_map/all_to_all | solution.py:103
  43.1 19.0 %copy-start.36 = (s32[1,512]{1,0:T(1,128)S(1)}, s32[1,512]{1,0:T(1,128)}, u32[]{:S(2)}) copy-start(s32[1,512]{1,0:T(1,128)} %param.23) | copy-start | bytes 6148
  43.1 19.0 %copy-start.33 = (f32[1,4,512]{2,1,0:T(4,128)S(1)}, f32[1,4,512]{2,1,0:T(4,128)}, u32[]{:S(2)}) copy-start(f32[1,4,512]{2,1,0:T(4,128)} %param.24) | copy-start | bytes 24580
  43.1 19.6 %copy-start.35 = (f32[1,4]{1,0:T(1,128)S(1)}, f32[1,4]{1,0:T(1,128)}, u32[]{:S(2)}) copy-start(f32[1,4]{1,0:T(1,128)} %param.21) | copy-start | bytes 52
  43.1 20.2 %copy-start.34 = (s32[1,128,16]{1,2,0:T(8,128)S(1)}, s32[1,128,16]{1,2,0:T(8,128)}, u32[]{:S(2)}) copy-start(s32[1,128,16]{1,2,0:T(8,128)} %param.25) | copy-start | bytes 24580
  43.1 411.7 %all-reduce.11.cloned.1.call-start = ((), (), s32[]{:S(2)}) async-start(), calls=%async_computation.3 | async-start | bytes 131072
  43.2 98.4 %copy-start.22 = (f32[8,128,128]{2,1,0:T(8,128)}, f32[8,128,128]{2,1,0:T(8,128)S(1)}, u32[]{:S(2)}) copy-start(f32[8,128,128]{2,1,0:T(8,128)S(1)} %bitcast_multiply_fusion.5) | copy-start | bytes 1572868
  43.3 98.3 %collective-permute-start = (f32[4,128,128]{2,1,0:T(8,128)S(1)}, f32[4,128,128]{2,1,0:T(8,128)S(1)}, u32[]{:S(2)}, u32[]{:S(2)}) collective-permute-start(f32[4,128,128]{2,1,0:T(8,128)S(1)} %get-tuple-element.63), channel_id=1, source_target_pairs={{1,0},{2,1},{3,2},{4,3},{5,4},{6,5},{7,6},{8,7},{9,8},{10,9},{11,1... | collective-permute-start | bytes 786440 | tf_op jit(solution)/shard_map/ppermute | solution.py:17
  45.8 95.9 %collective-permute-start.1 = (f32[4,128,128]{2,1,0:T(8,128)S(1)}, f32[4,128,128]{2,1,0:T(8,128)S(1)}, u32[]{:S(2)}, u32[]{:S(2)}) collective-permute-start(f32[4,128,128]{2,1,0:T(8,128)S(1)} %get-tuple-element.64), channel_id=1, source_target_pairs={{0,1},{1,2},{2,3},{3,4},{4,5},{5,6},{6,7},{7,8},{8,9},{9,10},{10,1... | collective-permute-start | bytes 786440 | tf_op jit(solution)/shard_map/ppermute | solution.py:16
  151.4 15.1 %copy-start.19 = (f32[8,128,128]{2,1,0:T(8,128)}, f32[8,128,128]{2,1,0:T(8,128)S(1)}, u32[]{:S(2)}) copy-start(f32[8,128,128]{2,1,0:T(8,128)S(1)} %mul.453) | copy-start | bytes 1572868
  151.5 15.1 %collective-permute-start.2 = (f32[4,128,128]{2,1,0:T(8,128)S(1)}, f32[4,128,128]{2,1,0:T(8,128)S(1)}, u32[]{:S(2)}, u32[]{:S(2)}) collective-permute-start(f32[4,128,128]{2,1,0:T(8,128)S(1)} %get-tuple-element.61), channel_id=1, source_target_pairs={{1,0},{2,1},{3,2},{4,3},{5,4},{6,5},{7,6},{8,7},{9,8},{10,9},{11,1... | collective-permute-start | bytes 786440 | tf_op jit(solution)/shard_map/ppermute | solution.py:17
  156.5 14.9 %collective-permute-start.3 = (f32[4,128,128]{2,1,0:T(8,128)S(1)}, f32[4,128,128]{2,1,0:T(8,128)}, u32[]{:S(2)}, u32[]{:S(2)}) collective-permute-start(f32[4,128,128]{2,1,0:T(8,128)S(1)} %get-tuple-element.62), channel_id=1, source_target_pairs={{0,1},{1,2},{2,3},{3,4},{4,5},{5,6},{6,7},{7,8},{8,9},{9,10},{10,1... | collective-permute-start | bytes 786440 | tf_op jit(solution)/shard_map/ppermute | solution.py:16
  183.3 13.8 %collective-permute-start.6 = (f32[4,128,128]{2,1,0:T(8,128)S(1)}, f32[4,128,128]{2,1,0:T(8,128)S(1)}, u32[]{:S(2)}, u32[]{:S(2)}) collective-permute-start(f32[4,128,128]{2,1,0:T(8,128)S(1)} %bitcast.200), channel_id=1, source_target_pairs={{1,0},{2,1},{3,2},{4,3},{5,4},{6,5},{7,6},{8,7},{9,8},{10,9},{11,1... | collective-permute-start | bytes 786440 | tf_op jit(solution)/shard_map/ppermute | solution.py:17
  185.2 19.4 %copy-start.3 = (f32[8,128,128]{2,1,0:T(8,128)S(1)}, f32[8,128,128]{2,1,0:T(8,128)}, u32[]{:S(2)}) copy-start(f32[8,128,128]{2,1,0:T(8,128)} %param.17) | copy-start | bytes 1572868
  185.2 17.4 %collective-permute-start.7 = (f32[4,128,128]{2,1,0:T(8,128)S(1)}, f32[4,128,128]{2,1,0:T(8,128)S(1)}, u32[]{:S(2)}, u32[]{:S(2)}) collective-permute-start(f32[4,128,128]{2,1,0:T(8,128)S(1)} %bitcast.199), channel_id=1, source_target_pairs={{0,1},{1,2},{2,3},{3,4},{4,5},{5,6},{6,7},{7,8},{8,9},{9,10},{10,1... | collective-permute-start | bytes 786440 | tf_op jit(solution)/shard_map/ppermute | solution.py:16
  193.9 22.5 %copy-start.13 = (f32[1,128,8,128]{3,2,0,1:T(8,128)}, f32[1,128,8,128]{3,2,0,1:T(8,128)S(1)}, u32[]{:S(2)}) copy-start(f32[1,128,8,128]{3,2,0,1:T(8,128)S(1)} %get-tuple-element.52) | copy-start | bytes 1572868
  204.6 24.3 %copy-start.20 = (f32[8,128,128]{2,1,0:T(8,128)S(1)}, f32[8,128,128]{2,1,0:T(8,128)}, u32[]{:S(2)}) copy-start(f32[8,128,128]{2,1,0:T(8,128)} %copy-done.19) | copy-start | bytes 1572868
  218.5 13.8 %copy-start.7 = (f32[131072]{0:T(1024)}, f32[131072]{0:T(1024)S(1)}, u32[]{:S(2)}) copy-start(f32[131072]{0:T(1024)S(1)} %fusion.306) | copy-start | bytes 1572868
  219.4 27.2 %collective-permute-start.8 = (f32[4,128,128]{2,1,0:T(8,128)}, f32[4,128,128]{2,1,0:T(8,128)}, u32[]{:S(2)}, u32[]{:S(2)}) collective-permute-start(f32[4,128,128]{2,1,0:T(8,128)} %bitcast.32), channel_id=1, source_target_pairs={{1,0},{2,1},{3,2},{4,3},{5,4},{6,5},{7,6},{8,7},{9,8},{10,9},{11,1... | collective-permute-start | bytes 786440 | tf_op jit(solution)/shard_map/ppermute | solution.py:17
  221.3 25.2 %collective-permute-start.9 = (f32[4,128,128]{2,1,0:T(8,128)}, f32[4,128,128]{2,1,0:T(8,128)}, u32[]{:S(2)}, u32[]{:S(2)}) collective-permute-start(f32[4,128,128]{2,1,0:T(8,128)} %bitcast.33), channel_id=1, source_target_pairs={{0,1},{1,2},{2,3},{3,4},{4,5},{5,6},{6,7},{7,8},{8,9},{9,10},{10,1... | collective-permute-start | bytes 786440 | tf_op jit(solution)/shard_map/ppermute | solution.py:16
  237.1 26.6 %collective-permute-start.4 = (f32[4,128,128]{2,1,0:T(8,128)}, f32[4,128,128]{2,1,0:T(8,128)S(1)}, u32[]{:S(2)}, u32[]{:S(2)}) collective-permute-start(f32[4,128,128]{2,1,0:T(8,128)} %get-tuple-element.59), channel_id=1, source_target_pairs={{1,0},{2,1},{3,2},{4,3},{5,4},{6,5},{7,6},{8,7},{9,8},{10,9},{11,1... | collective-permute-start | bytes 786440 | tf_op jit(solution)/shard_map/ppermute | solution.py:17
  239.0 24.7 %collective-permute-start.5 = (f32[4,128,128]{2,1,0:T(8,128)}, f32[4,128,128]{2,1,0:T(8,128)}, u32[]{:S(2)}, u32[]{:S(2)}) collective-permute-start(f32[4,128,128]{2,1,0:T(8,128)} %get-tuple-element.60), channel_id=1, source_target_pairs={{0,1},{1,2},{2,3},{3,4},{4,5},{5,6},{6,7},{7,8},{8,9},{9,10},{10,1... | collective-permute-start | bytes 786440 | tf_op jit(solution)/shard_map/ppermute | solution.py:16
  253.9 20.8 %copy-start.10 = (f32[131072]{0:T(1024)}, f32[131072]{0:T(1024)S(1)}, u32[]{:S(2)}) copy-start(f32[131072]{0:T(1024)S(1)} %fusion.307) | copy-start | bytes 1572868
  254.0 12.7 %collective-permute-start.10 = (f32[4,128,128]{2,1,0:T(8,128)S(1)}, f32[4,128,128]{2,1,0:T(8,128)S(1)}, u32[]{:S(2)}, u32[]{:S(2)}) collective-permute-start(f32[4,128,128]{2,1,0:T(8,128)S(1)} %bitcast.198), channel_id=1, source_target_pairs={{1,0},{2,1},{3,2},{4,3},{5,4},{6,5},{7,6},{8,7},{9,8},{10,9},{11,1... | collective-permute-start | bytes 786440 | tf_op jit(solution)/shard_map/ppermute | solution.py:17
  255.9 16.1 %collective-permute-start.11 = (f32[4,128,128]{2,1,0:T(8,128)S(1)}, f32[4,128,128]{2,1,0:T(8,128)S(1)}, u32[]{:S(2)}, u32[]{:S(2)}) collective-permute-start(f32[4,128,128]{2,1,0:T(8,128)S(1)} %bitcast.197), channel_id=1, source_target_pairs={{0,1},{1,2},{2,3},{3,4},{4,5},{5,6},{6,7},{7,8},{8,9},{9,10},{10,1... | collective-permute-start | bytes 786440 | tf_op jit(solution)/shard_map/ppermute | solution.py:16
  292.4 19.3 %collective-permute-start.12 = (f32[4,128,128]{2,1,0:T(8,128)}, f32[4,128,128]{2,1,0:T(8,128)}, u32[]{:S(2)}, u32[]{:S(2)}) collective-permute-start(f32[4,128,128]{2,1,0:T(8,128)} %bitcast.42), channel_id=1, source_target_pairs={{1,0},{2,1},{3,2},{4,3},{5,4},{6,5},{7,6},{8,7},{9,8},{10,9},{11,1... | collective-permute-start | bytes 786440 | tf_op jit(solution)/shard_map/ppermute | solution.py:17
  294.3 17.4 %collective-permute-start.13 = (f32[4,128,128]{2,1,0:T(8,128)}, f32[4,128,128]{2,1,0:T(8,128)}, u32[]{:S(2)}, u32[]{:S(2)}) collective-permute-start(f32[4,128,128]{2,1,0:T(8,128)} %bitcast.43), channel_id=1, source_target_pairs={{0,1},{1,2},{2,3},{3,4},{4,5},{5,6},{6,7},{7,8},{8,9},{9,10},{10,1... | collective-permute-start | bytes 786440 | tf_op jit(solution)/shard_map/ppermute | solution.py:16
  327.1 129.0 %collective-permute-start.14 = (f32[4,128,128]{2,1,0:T(8,128)S(1)}, f32[4,128,128]{2,1,0:T(8,128)S(1)}, u32[]{:S(2)}, u32[]{:S(2)}) collective-permute-start(f32[4,128,128]{2,1,0:T(8,128)S(1)} %get-tuple-element.55), channel_id=1, source_target_pairs={{1,0},{2,1},{3,2},{4,3},{5,4},{6,5},{7,6},{8,7},{9,8},{10,9},{11,1... | collective-permute-start | bytes 786440 | tf_op jit(solution)/shard_map/ppermute | solution.py:17
  329.0 14.2 %copy-start.39 = (u32[256]{0:T(256)S(1)}, u32[256]{0:T(256)}, u32[]{:S(2)}) copy-start(u32[256]{0:T(256)} %constant.194) | copy-start | bytes 3076
  329.0 127.0 %collective-permute-start.15 = (f32[4,128,128]{2,1,0:T(8,128)S(1)}, f32[4,128,128]{2,1,0:T(8,128)}, u32[]{:S(2)}, u32[]{:S(2)}) collective-permute-start(f32[4,128,128]{2,1,0:T(8,128)S(1)} %get-tuple-element.56), channel_id=1, source_target_pairs={{0,1},{1,2},{2,3},{3,4},{4,5},{5,6},{6,7},{7,8},{8,9},{9,10},{10,1... | collective-permute-start | bytes 786440 | tf_op jit(solution)/shard_map/ppermute | solution.py:16
  342.8 115.0 %copy-start.1 = (f32[131072]{0:T(1024)S(1)}, f32[131072]{0:T(1024)}, u32[]{:S(2)}) copy-start(f32[131072]{0:T(1024)} %scatter_fusion.2) | copy-start | bytes 1572868
  342.9 177.6 %reduce-scatter.2.cloned.1.call-start = ((), (), s32[]{:S(2)}) async-start(), calls=%async_computation.2 | async-start | bytes 557056 | tf_op jit(solution)/shard_map/reduce_scatter | solution.py:151
  (27 other events, 159.5 us)
Sparse Core Ops, SparseCore 0:
  343.0 111.7 all-reduce.10
  457.9 62.5 reduce-scatter.1
where the time goes:
time: 530 us; the launch traced here: 527 us
  waiting for transfers between devices  262 us (49%)
  other arithmetic  105 us (20%)
  starting transfers between devices  87.1 us (16%)
  local copies, waits for them, and re-layouts  56.5 us (11%)
  between operations  16.6 us (3%)
    unnamed x3, waiting for transfers between devices  110 us
    ppermute x8, waiting for transfers between devices, padded_2(): after = lax.ppermute(initial, axis, down)  85 us
    ppermute x8, starting transfers between devices, padded_2(): before = lax.ppermute(last, axis, up)  57.6 us
    reduce_scatter x1, waiting for transfers between devices, body(): lax.psum_scatter(partial_value, 'shot', scatter_dimension=1, tiled=True)  50.8 us
    add x4, other arithmetic, advance(): 2.0 * current_ext[4:-4] - before + courant * laplace(current_ext)  32.8 us
    scatter-add x8, other arithmetic, inject(): flattened = field.reshape(-1).at[target].add(values, mode='drop')  28.2 us
    ppermute x8, starting transfers between devices, padded_2(): after = lax.ppermute(initial, axis, down)  18.9 us
    add x4, other arithmetic, retreat(): earlier = 2.0 * current - following + laplace(weighted_ext)  16.5 us
  transfers between devices with their start and end apart: 19, of which 9 were waited for; matrix products, arithmetic and copies ran while one was open for 14% of the time, Pallas kernels for 0%

commit v1 on v0

--- a/solution.py
+++ b/solution.py
@@ -52,9 +52,20 @@
     return flattened.reshape(field.shape)
 
 
+def inject_dense(field, cell_index, values, first_row):
+    plane_cells = field.shape[1] * field.shape[2]
+    local_cell = cell_index[0] - first_row * plane_cells
+    cells = (
+        lax.broadcasted_iota(jnp.int32, field.shape, 0) * plane_cells
+        + lax.broadcasted_iota(jnp.int32, field.shape, 1) * field.shape[2]
+        + lax.broadcasted_iota(jnp.int32, field.shape, 2)
+    )
+    return field + jnp.where(cells == local_cell, values[0], 0.0)
+
+
 def advance(before, current_ext, courant, wave_value, source, first_row):
     following = 2.0 * current_ext[4:-4] - before + courant * laplace(current_ext)
-    return inject(following, source, wave_value, first_row)
+    return inject_dense(following, source, wave_value, first_row)
 
 
 def retreat(following, current, weighted_ext, values, cell_index, first_row):
@@ -148,8 +159,10 @@
         )
     slab_rows = partial_value.reshape(length * height, breadth)
     check_part = jnp.sum(slab_rows[check_rows[0]], axis=1)
-    grad_share = lax.psum_scatter(partial_value, "shot", scatter_dimension=1, tiled=True)
-    check_share = lax.psum_scatter(check_part, "shot", scatter_dimension=0, tiled=True)
+    stacked = jnp.concatenate([partial_value, check_part[None]], axis=0)
+    shares = lax.psum_scatter(stacked, "shot", scatter_dimension=1, tiled=True)
+    grad_share = shares[:length]
+    check_share = shares[length]
     adjoint_carry = jnp.stack([adjoints[1], adjoints[0]])[None]
     return (grad_share, adjoint_carry, check_share[None])
 

time: 530 us -> 385 us (0.73)
  waiting for transfers between devices: 262 us -> 167 us
  other arithmetic: 105 us -> 65.1 us
  starting transfers between devices: 87.1 us -> 79 us
    unnamed x3 -> x1, waiting for transfers between devices: 110 us -> 0.02 us
    ppermute x8, waiting for transfers between devices: 15.7 us -> 86.4 us  [padded_2(): before = lax.ppermute(last, axis, up)]
    ppermute x8, waiting for transfers between devices: 85 us -> 23.8 us  [padded_2(): after = lax.ppermute(initial, axis, down)]
    add x4 -> x3, other arithmetic: 32.8 us -> 9.87 us  [inject_dense(): return field + jnp.where(cells == local_cell, values[0], 0.0)]
    scatter-add x8 -> x4, other arithmetic: 28.2 us -> 14.7 us  [inject(): flattened = field.reshape(-1).at[target].add(values, mode='drop')]
    reduce_scatter x1, waiting for transfers between devices: 50.8 us -> 56.3 us  [body(): shares = lax.psum_scatter(stacked, 'shot', scatter_dimension=1, tiled=True)]
    concatenate x8, other arithmetic: 14.6 us -> 9.27 us  [padded_2(): array = jnp.concatenate([before, array, after], axis=dim)]
  transfers between devices with their start and end apart: 19 -> 18, of which waited for: 9 -> 9; matrix products, arithmetic and copies ran while one was open for 14% -> 19% of each run, Pallas kernels for 0% -> 0%
where the time goes in v1:
time: 385 us; the launch traced here: 382 us
  waiting for transfers between devices  167 us (43%)
  starting transfers between devices  79 us (21%)
  other arithmetic  65.1 us (17%)
  local copies, waits for them, and re-layouts  55.8 us (14%)
  between operations  15.6 us (4%)
    ppermute x8, waiting for transfers between devices, padded_2(): before = lax.ppermute(last, axis, up)  86.4 us
    reduce_scatter x1, waiting for transfers between devices, body(): shares = lax.psum_scatter(stacked, 'shot', scatter_dimension=1, tiled=True)  56.3 us
    ppermute x8, starting transfers between devices, padded_2(): before = lax.ppermute(last, axis, up)  52.4 us
    ppermute x8, waiting for transfers between devices, padded_2(): after = lax.ppermute(initial, axis, down)  23.8 us
    ppermute x8, starting transfers between devices, padded_2(): after = lax.ppermute(initial, axis, down)  16.4 us
    add x4, other arithmetic, retreat(): earlier = 2.0 * current - following + laplace(weighted_ext)  15.9 us
    scatter-add x4, other arithmetic, inject(): flattened = field.reshape(-1).at[target].add(values, mode='drop')  14.7 us
    scatter x1, local copies, waits for them, and re-layouts, body(): outgoing = jnp.zeros((2, devices * capacity, block_rows, breadth), jnp.fl...  13.6 us
  transfers between devices with their start and end apart: 18, of which 9 were waited for; matrix products, arithmetic and copies ran while one was open for 19% of the time, Pallas kernels for 0%

profile of v1, /device:TPU:100, one launch (start us, length us, event | category | flops | bytes accessed | tf_op | source)
XLA Modules:
  0.0 382.1 jit_solution(9045375847774779806)
XLA Ops:
  14.5 13.6 %scatter_fusion.3 = f32[2,512,8,128]{3,2,1,0:T(8,128)} fusion(f32[2,512,8,128]{3,2,1,0:T(8,128)} %broadcast_in_dim.59, s32[128]{0:T(128)S(1)} %fusion.302, f32[128,2,8,128]{3,2,1,0:T(8,128)S(1)} %copy.34), kind=kCustom, calls=%fused_computation.6 | custom fusion | bytes 3146240 | tf_op jit(solution)/shard_map/scatter | solution.py:111
  28.1 4.7 %copy.35 = f32[2,16,32,8,128]{4,3,2,0,1:T(8,128)} copy(f32[2,16,32,8,128]{4,3,2,1,0:T(8,128)} %bitcast.90) | data formatting | bytes 8388608 | tf_op jit(solution)/shard_map/reshape | solution.py:113
  32.8 10.2 %all-to-all-start = ((f32[2,16,32,8,128]{4,3,2,0,1:T(8,128)}), f32[2,16,32,8,128]{4,3,2,0,1:T(8,128)}, u32[]{:S(2)}, u32[]{:S(2)}) async-start(f32[2,16,32,8,128]{4,3,2,0,1:T(8,128)} %copy.35), calls=%async_computation | async-start | bytes 8388608 | tf_op jit(solution)/shard_map/all_to_all | solution.py:114
  43.3 4.6 %collective-permute-start.1 = (f32[4,128,128]{2,1,0:T(8,128)S(1)}, f32[4,128,128]{2,1,0:T(8,128)S(1)}, u32[]{:S(2)}, u32[]{:S(2)}) collective-permute-start(f32[4,128,128]{2,1,0:T(8,128)S(1)} %get-tuple-element.14), channel_id=1, source_target_pairs={{0,1},{1,2},{2,3},{3,4},{4,5},{5,6},{6,7},{7,8},{8,9},{9,10},{10,1... | collective-permute-start | bytes 786440 | tf_op jit(solution)/shard_map/ppermute | solution.py:16
  50.9 8.0 %scatter_custom_fusion.3 = s32[128]{0:T(128)S(1)} fusion(s32[2048]{0:T(1024)S(1)} %bitcast.113, s32[2048]{0:T(1024)S(1)} %add_bitcast_fusion, s32[]{:T(128)} %constant.82.clone.1), kind=kCustom, calls=%fused_computation.543 | custom fusion | bytes 516 | tf_op jit(solution)/shard_map/scatter | solution.py:122
  61.9 79.0 %collective-permute-done.1 = f32[4,128,128]{2,1,0:T(8,128)S(1)} collective-permute-done((f32[4,128,128]{2,1,0:T(8,128)S(1)}, f32[4,128,128]{2,1,0:T(8,128)S(1)}, u32[]{:S(2)}, u32[]{:S(2)}) %collective-permute-start.1) | collective-permute-done | bytes 262176 | tf_op jit(solution)/shard_map/ppermute | solution.py:16
  142.8 3.3 fusion.207
  146.2 3.5 scatter_fusion
  151.7 7.8 %collective-permute-start.3 = (f32[4,128,128]{2,1,0:T(8,128)S(1)}, f32[4,128,128]{2,1,0:T(8,128)S(1)}, u32[]{:S(2)}, u32[]{:S(2)}) collective-permute-start(f32[4,128,128]{2,1,0:T(8,128)S(1)} %get-tuple-element.12), channel_id=1, source_target_pairs={{0,1},{1,2},{2,3},{3,4},{4,5},{5,6},{6,7},{7,8},{8,9},{9,10},{10,1... | collective-permute-start | bytes 786440 | tf_op jit(solution)/shard_map/ppermute | solution.py:16
  165.0 7.8 %collective-permute-done.2 = f32[4,128,128]{2,1,0:T(8,128)} collective-permute-done((f32[4,128,128]{2,1,0:T(8,128)S(1)}, f32[4,128,128]{2,1,0:T(8,128)}, u32[]{:S(2)}, u32[]{:S(2)}) %collective-permute-start.2) | collective-permute-done | bytes 262176 | tf_op jit(solution)/shard_map/ppermute | solution.py:17
  174.6 4.7 %copy.36 = f32[2,16,32,8,128]{4,3,2,1,0:T(8,128)} copy(f32[2,16,32,8,128]{4,3,2,0,1:T(8,128)} %all-to-all-done) | data formatting | bytes 8388608 | tf_op jit(solution)/shard_map/all_to_all | solution.py:114
  179.3 4.0 %gather_fusion = f32[128,2,8,128]{3,2,1,0:T(8,128)} fusion(f32[2,512,8,128]{3,2,1,0:T(8,128)} %bitcast.97, s32[1024]{0:T(1024)} %pad_clamp_fusion), kind=kCustom, calls=%fused_computation | custom fusion | bytes 2097664 | tf_op jit(solution)/shard_map/jit(_take)/gather | solution.py:124
  184.7 5.7 %collective-permute-start.7 = (f32[4,128,128]{2,1,0:T(8,128)S(1)}, f32[4,128,128]{2,1,0:T(8,128)S(1)}, u32[]{:S(2)}, u32[]{:S(2)}) collective-permute-start(f32[4,128,128]{2,1,0:T(8,128)S(1)} %bitcast.103), channel_id=1, source_target_pairs={{0,1},{1,2},{2,3},{3,4},{4,5},{5,6},{6,7},{7,8},{8,9},{9,10},{10,1... | collective-permute-start | bytes 786440 | tf_op jit(solution)/shard_map/ppermute | solution.py:16
  192.6 3.4 collective-permute-done.7
  196.0 7.7 %collective-permute-done.6 = f32[4,128,128]{2,1,0:T(8,128)S(1)} collective-permute-done((f32[4,128,128]{2,1,0:T(8,128)S(1)}, f32[4,128,128]{2,1,0:T(8,128)S(1)}, u32[]{:S(2)}, u32[]{:S(2)}) %collective-permute-start.6) | collective-permute-done | bytes 262176 | tf_op jit(solution)/shard_map/ppermute | solution.py:17
  204.4 2.9 fusion.132
  208.3 5.7 %collective-permute-start.9 = (f32[4,128,128]{2,1,0:T(8,128)}, f32[4,128,128]{2,1,0:T(8,128)}, u32[]{:S(2)}, u32[]{:S(2)}) collective-permute-start(f32[4,128,128]{2,1,0:T(8,128)} %get-tuple-element.20), channel_id=1, source_target_pairs={{0,1},{1,2},{2,3},{3,4},{4,5},{5,6},{6,7},{7,8},{8,9},{9,10},{10,1... | collective-permute-start | bytes 786440 | tf_op jit(solution)/shard_map/ppermute | solution.py:16
  215.9 4.4 %fusion.182 = f32[8,128,128]{2,1,0:T(8,128)S(1)} fusion(f32[8,128,128]{2,1,0:T(8,128)} %mul.443, f32[4,128,128]{2,1,0:T(8,128)S(1)} %collective-permute-done.3, f32[4,128,128]{2,1,0:T(8,128)} %collective-permute-done.2, f32[16,136,136]{2,1,0:T(8,128)S(1)} %select_maximum_fusion.12, f32[8,128,128]{2,1,0:T(8,128)S(1)} %bitcast.82, ...), kind=kLoop, calls=%fused_computation.311 | loop fusion | flops 6291456 | bytes 11010048 | tf_op jit(solution)/shard_map/add | solution.py:72
  220.3 3.8 %scatter_fusion.1 = f32[131072]{0:T(1024)S(1)} fusion(f32[131072]{0:T(1024)S(1)} %bitcast.85, s32[512]{0:T(512)S(1)} %bitcast.105, f32[512]{0:T(512)} %bitcast.111), kind=kCustom, calls=%fused_computation.3 | custom fusion | flops 512 | bytes 8192 | tf_op jit(solution)/shard_map/scatter-add | solution.py:51
  224.4 7.7 %collective-permute-start.5 = (f32[4,128,128]{2,1,0:T(8,128)S(1)}, f32[4,128,128]{2,1,0:T(8,128)S(1)}, u32[]{:S(2)}, u32[]{:S(2)}) collective-permute-start(f32[4,128,128]{2,1,0:T(8,128)S(1)} %get-tuple-element.10), channel_id=1, source_target_pairs={{0,1},{1,2},{2,3},{3,4},{4,5},{5,6},{6,7},{7,8},{8,9},{9,10},{10,1... | collective-permute-start | bytes 786440 | tf_op jit(solution)/shard_map/ppermute | solution.py:16
  235.7 4.1 %fusion.105 = f32[8,128,128]{2,1,0:T(8,128)S(1)} fusion(f32[8,128,128]{2,1,0:T(8,128)S(1)} %copy-done.1, f32[8,128,128]{2,1,0:T(8,128)S(1)} %copy-done.3, f32[4,128,128]{2,1,0:T(8,128)} %collective-permute-done.9, f32[4,128,128]{2,1,0:T(8,128)} %collective-permute-done.8, f32[16,136,136]{2,1,0:T(8,128)S(1)} %select_maximum_fusion.6, ...), kind=kLoop, calls=%fused_computation.234 | loop fusion | flops 7077888 | bytes 11010600 | tf_op jit(solution)/shard_map/add | solution.py:63
  239.8 7.5 %collective-permute-start.11 = (f32[4,128,128]{2,1,0:T(8,128)S(1)}, f32[4,128,128]{2,1,0:T(8,128)S(1)}, u32[]{:S(2)}, u32[]{:S(2)}) collective-permute-start(f32[4,128,128]{2,1,0:T(8,128)S(1)} %get-tuple-element.18), channel_id=1, source_target_pairs={{0,1},{1,2},{2,3},{3,4},{4,5},{5,6},{6,7},{7,8},{8,9},{9,10},{10,1... | collective-permute-start | bytes 786440 | tf_op jit(solution)/shard_map/ppermute | solution.py:16
  251.9 7.7 %collective-permute-done.10 = f32[4,128,128]{2,1,0:T(8,128)S(1)} collective-permute-done((f32[4,128,128]{2,1,0:T(8,128)S(1)}, f32[4,128,128]{2,1,0:T(8,128)S(1)}, u32[]{:S(2)}, u32[]{:S(2)}) %collective-permute-start.10) | collective-permute-done | bytes 262176 | tf_op jit(solution)/shard_map/ppermute | solution.py:17
  264.0 5.7 %collective-permute-start.13 = (f32[4,128,128]{2,1,0:T(8,128)}, f32[4,128,128]{2,1,0:T(8,128)S(1)}, u32[]{:S(2)}, u32[]{:S(2)}) collective-permute-start(f32[4,128,128]{2,1,0:T(8,128)} %get-tuple-element.16), channel_id=1, source_target_pairs={{0,1},{1,2},{2,3},{3,4},{4,5},{5,6},{6,7},{7,8},{8,9},{9,10},{10,1... | collective-permute-start | bytes 786440 | tf_op jit(solution)/shard_map/ppermute | solution.py:16
  271.7 4.6 %fusion.157 = f32[8,128,128]{2,1,0:T(8,128)S(1)} fusion(f32[8,128,128]{2,1,0:T(8,128)} %copy-done.11, f32[4,128,128]{2,1,0:T(8,128)} %copy-done.19, f32[4,128,128]{2,1,0:T(8,128)} %copy-done.20, f32[16,136,136]{2,1,0:T(8,128)S(1)} %select_maximum_fusion.10, f32[8,128,128]{2,1,0:T(8,128)S(1)} %bitcast.83, f32[8,128,128]{2,1,0:T(8,128)S(1)} %bitcast.87), kind=kLoop, calls=%fused_computation.286 | loop fusion | flops 6291456 | bytes 11010048 | tf_op jit(solution)/shard_map/add | solution.py:72
  276.3 3.8 scatter_fusion.2
  281.0 7.7 %collective-permute-start.15 = (f32[4,128,128]{2,1,0:T(8,128)}, f32[4,128,128]{2,1,0:T(8,128)}, u32[]{:S(2)}, u32[]{:S(2)}) collective-permute-start(f32[4,128,128]{2,1,0:T(8,128)} %get-tuple-element.8), channel_id=1, source_target_pairs={{0,1},{1,2},{2,3},{3,4},{4,5},{5,6},{6,7},{7,8},{8,9},{9,10},{10,1... | collective-permute-start | bytes 786440 | tf_op jit(solution)/shard_map/ppermute | solution.py:16
  292.3 4.1 %fusion.51 = f32[8,128,128]{2,1,0:T(8,128)S(1)} fusion(f32[8,128,128]{2,1,0:T(8,128)S(1)} %copy-done.5, f32[8,128,128]{2,1,0:T(8,128)S(1)} %copy-done.1, f32[8,128,128]{2,1,0:T(8,128)S(1)} %copy-done.10, f32[4,128,128]{2,1,0:T(8,128)S(1)} %collective-permute-done.13, f32[4,128,128]{2,1,0:T(8,128)} %collective-permute-done.12, ...), kind=kLoop, calls=%fused_computation.180 | loop fusion | flops 9437184 | bytes 14680616 | tf_op jit(solution)/shard_map/add | solution.py:157
  296.4 7.6 %gather_fusion.1 = f32[2048,128]{1,0:T(8,128)} fusion(f32[1024,128]{1,0:T(8,128)S(1)} %bitcast.74, s32[2048]{0:T(1024)S(1)} %broadcast_clamp_fusion), kind=kCustom, calls=%fused_computation.1 | custom fusion | bytes 2105344 | tf_op jit(solution)/shard_map/gather | solution.py:161
  308.1 3.6 fusion.20
  311.7 3.5 scatter_fusion.4
  316.3 56.3 %reduce-scatter.2.cloned.1.call-done = f32[9,8,128]{2,1,0:T(8,128)} async-done(((f32[9,128,128]{2,1,0:T(8,128)}), f32[9,8,128]{2,1,0:T(8,128)}) %reduce-scatter.2.cloned.1.call-update) | async-done | bytes 36880 | tf_op jit(solution)/shard_map/reduce_scatter | solution.py:163
  (139 shorter events, 57.8 us)
Async XLA Ops:
  32.8 141.8 %all-to-all-start = ((f32[2,16,32,8,128]{4,3,2,0,1:T(8,128)}), f32[2,16,32,8,128]{4,3,2,0,1:T(8,128)}, u32[]{:S(2)}, u32[]{:S(2)}) async-start(f32[2,16,32,8,128]{4,3,2,0,1:T(8,128)} %copy.35), calls=%async_computation | async-start | bytes 8388608 | tf_op jit(solution)/shard_map/all_to_all | solution.py:114
  43.0 16.5 %copy-start.31 = (f32[1,4]{1,0:T(1,128)S(1)}, f32[1,4]{1,0:T(1,128)}, u32[]{:S(2)}) copy-start(f32[1,4]{1,0:T(1,128)} %param.13) | copy-start | bytes 52
  43.0 17.7 %copy-start.32 = (s32[1,512]{1,0:T(1,128)S(1)}, s32[1,512]{1,0:T(1,128)}, u32[]{:S(2)}) copy-start(s32[1,512]{1,0:T(1,128)} %param.15) | copy-start | bytes 6148
  43.1 17.7 %copy-start.29 = (f32[1,4,512]{2,1,0:T(4,128)S(1)}, f32[1,4,512]{2,1,0:T(4,128)}, u32[]{:S(2)}) copy-start(f32[1,4,512]{2,1,0:T(4,128)} %param.16) | copy-start | bytes 24580
  43.1 18.8 %copy-start.30 = (s32[1,128,16]{1,2,0:T(8,128)S(1)}, s32[1,128,16]{1,2,0:T(8,128)}, u32[]{:S(2)}) copy-start(s32[1,128,16]{1,2,0:T(8,128)} %param.17) | copy-start | bytes 24580
  43.1 329.6 %reduce-scatter.2.cloned.1.call-start = ((), (), s32[]{:S(2)}) async-start(), calls=%async_computation.2 | async-start | bytes 626688 | tf_op jit(solution)/shard_map/reduce_scatter | solution.py:163
  43.3 97.6 %collective-permute-start.1 = (f32[4,128,128]{2,1,0:T(8,128)S(1)}, f32[4,128,128]{2,1,0:T(8,128)S(1)}, u32[]{:S(2)}, u32[]{:S(2)}) collective-permute-start(f32[4,128,128]{2,1,0:T(8,128)S(1)} %get-tuple-element.14), channel_id=1, source_target_pairs={{0,1},{1,2},{2,3},{3,4},{4,5},{5,6},{6,7},{7,8},{8,9},{9,10},{10,1... | collective-permute-start | bytes 786440 | tf_op jit(solution)/shard_map/ppermute | solution.py:16
  47.9 93.6 %collective-permute-start = (f32[4,128,128]{2,1,0:T(8,128)S(1)}, f32[4,128,128]{2,1,0:T(8,128)S(1)}, u32[]{:S(2)}, u32[]{:S(2)}) collective-permute-start(f32[4,128,128]{2,1,0:T(8,128)S(1)} %get-tuple-element.13), channel_id=1, source_target_pairs={{1,0},{2,1},{3,2},{4,3},{5,4},{6,5},{7,6},{8,7},{9,8},{10,9},{11,1... | collective-permute-start | bytes 786440 | tf_op jit(solution)/shard_map/ppermute | solution.py:17
  151.7 13.3 %collective-permute-start.3 = (f32[4,128,128]{2,1,0:T(8,128)S(1)}, f32[4,128,128]{2,1,0:T(8,128)S(1)}, u32[]{:S(2)}, u32[]{:S(2)}) collective-permute-start(f32[4,128,128]{2,1,0:T(8,128)S(1)} %get-tuple-element.12), channel_id=1, source_target_pairs={{0,1},{1,2},{2,3},{3,4},{4,5},{5,6},{6,7},{7,8},{8,9},{9,10},{10,1... | collective-permute-start | bytes 786440 | tf_op jit(solution)/shard_map/ppermute | solution.py:16
  159.5 13.3 %collective-permute-start.2 = (f32[4,128,128]{2,1,0:T(8,128)S(1)}, f32[4,128,128]{2,1,0:T(8,128)}, u32[]{:S(2)}, u32[]{:S(2)}) collective-permute-start(f32[4,128,128]{2,1,0:T(8,128)S(1)} %get-tuple-element.11), channel_id=1, source_target_pairs={{1,0},{2,1},{3,2},{4,3},{5,4},{6,5},{7,6},{8,7},{9,8},{10,9},{11,1... | collective-permute-start | bytes 786440 | tf_op jit(solution)/shard_map/ppermute | solution.py:17
  184.7 11.3 %collective-permute-start.7 = (f32[4,128,128]{2,1,0:T(8,128)S(1)}, f32[4,128,128]{2,1,0:T(8,128)S(1)}, u32[]{:S(2)}, u32[]{:S(2)}) collective-permute-start(f32[4,128,128]{2,1,0:T(8,128)S(1)} %bitcast.103), channel_id=1, source_target_pairs={{0,1},{1,2},{2,3},{3,4},{4,5},{5,6},{6,7},{7,8},{8,9},{9,10},{10,1... | collective-permute-start | bytes 786440 | tf_op jit(solution)/shard_map/ppermute | solution.py:16
  190.4 13.9 %copy-start.25 = (s32[128]{0:T(128)S(1)}, s32[128]{0:T(128)}, u32[]{:S(2)}) copy-start(s32[128]{0:T(128)} %iota_multiply_fusion) | copy-start | bytes 1540
  190.4 13.9 %copy-start.27 = (s32[8]{0:T(128)S(1)}, s32[8]{0:T(128)}, u32[]{:S(2)}) copy-start(s32[8]{0:T(128)} %iota_multiply_fusion.1) | copy-start | bytes 100
  190.4 13.3 %collective-permute-start.6 = (f32[4,128,128]{2,1,0:T(8,128)S(1)}, f32[4,128,128]{2,1,0:T(8,128)S(1)}, u32[]{:S(2)}, u32[]{:S(2)}) collective-permute-start(f32[4,128,128]{2,1,0:T(8,128)S(1)} %bitcast.102), channel_id=1, source_target_pairs={{1,0},{2,1},{3,2},{4,3},{5,4},{6,5},{7,6},{8,7},{9,8},{10,9},{11,1... | collective-permute-start | bytes 786440 | tf_op jit(solution)/shard_map/ppermute | solution.py:17
  192.6 14.7 %copy-start.6 = (f32[1,128,8,128]{3,2,0,1:T(8,128)}, f32[1,128,8,128]{3,2,0,1:T(8,128)S(1)}, u32[]{:S(2)}) copy-start(f32[1,128,8,128]{3,2,0,1:T(8,128)S(1)} %get-tuple-element.4) | copy-start | bytes 1572868
  192.6 14.7 %copy-start.17 = (f32[1,128,8,128]{3,2,0,1:T(8,128)}, f32[1,128,8,128]{3,2,0,1:T(8,128)S(1)}, u32[]{:S(2)}) copy-start(f32[1,128,8,128]{3,2,0,1:T(8,128)S(1)} %get-tuple-element.3) | copy-start | bytes 1572868
  208.3 25.7 %collective-permute-start.9 = (f32[4,128,128]{2,1,0:T(8,128)}, f32[4,128,128]{2,1,0:T(8,128)}, u32[]{:S(2)}, u32[]{:S(2)}) collective-permute-start(f32[4,128,128]{2,1,0:T(8,128)} %get-tuple-element.20), channel_id=1, source_target_pairs={{0,1},{1,2},{2,3},{3,4},{4,5},{5,6},{6,7},{7,8},{8,9},{9,10},{10,1... | collective-permute-start | bytes 786440 | tf_op jit(solution)/shard_map/ppermute | solution.py:16
  214.0 20.0 %collective-permute-start.8 = (f32[4,128,128]{2,1,0:T(8,128)}, f32[4,128,128]{2,1,0:T(8,128)}, u32[]{:S(2)}, u32[]{:S(2)}) collective-permute-start(f32[4,128,128]{2,1,0:T(8,128)} %get-tuple-element.19), channel_id=1, source_target_pairs={{1,0},{2,1},{3,2},{4,3},{5,4},{6,5},{7,6},{8,7},{9,8},{10,9},{11,1... | collective-permute-start | bytes 786440 | tf_op jit(solution)/shard_map/ppermute | solution.py:17
  224.3 25.1 %copy-start.11 = (f32[8,128,128]{2,1,0:T(8,128)}, f32[8,128,128]{2,1,0:T(8,128)S(1)}, u32[]{:S(2)}) copy-start(f32[8,128,128]{2,1,0:T(8,128)S(1)} %mul.458) | copy-start | bytes 1572868
  224.4 25.0 %collective-permute-start.5 = (f32[4,128,128]{2,1,0:T(8,128)S(1)}, f32[4,128,128]{2,1,0:T(8,128)S(1)}, u32[]{:S(2)}, u32[]{:S(2)}) collective-permute-start(f32[4,128,128]{2,1,0:T(8,128)S(1)} %get-tuple-element.10), channel_id=1, source_target_pairs={{0,1},{1,2},{2,3},{3,4},{4,5},{5,6},{6,7},{7,8},{8,9},{9,10},{10,1... | collective-permute-start | bytes 786440 | tf_op jit(solution)/shard_map/ppermute | solution.py:16
  232.0 17.3 %collective-permute-start.4 = (f32[4,128,128]{2,1,0:T(8,128)S(1)}, f32[4,128,128]{2,1,0:T(8,128)S(1)}, u32[]{:S(2)}, u32[]{:S(2)}) collective-permute-start(f32[4,128,128]{2,1,0:T(8,128)S(1)} %get-tuple-element.9), channel_id=1, source_target_pairs={{1,0},{2,1},{3,2},{4,3},{5,4},{6,5},{7,6},{8,7},{9,8},{10,9},{11,1... | collective-permute-start | bytes 786440 | tf_op jit(solution)/shard_map/ppermute | solution.py:17
  239.8 20.4 %copy-start.4 = (f32[8,128,128]{2,1,0:T(8,128)}, f32[8,128,128]{2,1,0:T(8,128)S(1)}, u32[]{:S(2)}) copy-start(f32[8,128,128]{2,1,0:T(8,128)S(1)} %fusion.105) | copy-start | bytes 1572868
  239.8 12.0 %collective-permute-start.11 = (f32[4,128,128]{2,1,0:T(8,128)S(1)}, f32[4,128,128]{2,1,0:T(8,128)S(1)}, u32[]{:S(2)}, u32[]{:S(2)}) collective-permute-start(f32[4,128,128]{2,1,0:T(8,128)S(1)} %get-tuple-element.18), channel_id=1, source_target_pairs={{0,1},{1,2},{2,3},{3,4},{4,5},{5,6},{6,7},{7,8},{8,9},{9,10},{10,1... | collective-permute-start | bytes 786440 | tf_op jit(solution)/shard_map/ppermute | solution.py:16
  247.4 12.2 %collective-permute-start.10 = (f32[4,128,128]{2,1,0:T(8,128)S(1)}, f32[4,128,128]{2,1,0:T(8,128)S(1)}, u32[]{:S(2)}, u32[]{:S(2)}) collective-permute-start(f32[4,128,128]{2,1,0:T(8,128)S(1)} %get-tuple-element.17), channel_id=1, source_target_pairs={{1,0},{2,1},{3,2},{4,3},{5,4},{6,5},{7,6},{8,7},{9,8},{10,9},{11,1... | collective-permute-start | bytes 786440 | tf_op jit(solution)/shard_map/ppermute | solution.py:17
  264.0 26.6 %collective-permute-start.13 = (f32[4,128,128]{2,1,0:T(8,128)}, f32[4,128,128]{2,1,0:T(8,128)S(1)}, u32[]{:S(2)}, u32[]{:S(2)}) collective-permute-start(f32[4,128,128]{2,1,0:T(8,128)} %get-tuple-element.16), channel_id=1, source_target_pairs={{0,1},{1,2},{2,3},{3,4},{4,5},{5,6},{6,7},{7,8},{8,9},{9,10},{10,1... | collective-permute-start | bytes 786440 | tf_op jit(solution)/shard_map/ppermute | solution.py:16
  269.7 20.9 %collective-permute-start.12 = (f32[4,128,128]{2,1,0:T(8,128)}, f32[4,128,128]{2,1,0:T(8,128)}, u32[]{:S(2)}, u32[]{:S(2)}) collective-permute-start(f32[4,128,128]{2,1,0:T(8,128)} %get-tuple-element.15), channel_id=1, source_target_pairs={{1,0},{2,1},{3,2},{4,3},{5,4},{6,5},{7,6},{8,7},{9,8},{10,9},{11,1... | collective-permute-start | bytes 786440 | tf_op jit(solution)/shard_map/ppermute | solution.py:17
  280.2 16.2 %copy-start.12 = (f32[8,128,128]{2,1,0:T(8,128)}, f32[8,128,128]{2,1,0:T(8,128)S(1)}, u32[]{:S(2)}) copy-start(f32[8,128,128]{2,1,0:T(8,128)S(1)} %mul.543) | copy-start | bytes 1572868
  280.2 12.1 %copy-start.5 = (f32[8,128,128]{2,1,0:T(8,128)S(1)}, f32[8,128,128]{2,1,0:T(8,128)}, u32[]{:S(2)}) copy-start(f32[8,128,128]{2,1,0:T(8,128)} %copy-done.4) | copy-start | bytes 1572868
  280.2 12.1 %copy-start.8 = (f32[1,128,8,128]{3,2,0,1:T(8,128)S(1)}, f32[1,128,8,128]{3,2,0,1:T(8,128)}, u32[]{:S(2)}) copy-start(f32[1,128,8,128]{3,2,0,1:T(8,128)} %copy-done.6) | copy-start | bytes 1572868
  280.2 12.1 %copy-start.16 = (f32[1,2,8,128,128]{4,3,2,1,0:T(8,128)S(1)}, f32[1,2,8,128,128]{4,3,2,1,0:T(8,128)}, u32[]{:S(2)}) copy-start(f32[1,2,8,128,128]{4,3,2,1,0:T(8,128)} %param.12) | copy-start | bytes 3145732
  281.0 25.3 %collective-permute-start.15 = (f32[4,128,128]{2,1,0:T(8,128)}, f32[4,128,128]{2,1,0:T(8,128)}, u32[]{:S(2)}, u32[]{:S(2)}) collective-permute-start(f32[4,128,128]{2,1,0:T(8,128)} %get-tuple-element.8), channel_id=1, source_target_pairs={{0,1},{1,2},{2,3},{3,4},{4,5},{5,6},{6,7},{7,8},{8,9},{9,10},{10,1... | collective-permute-start | bytes 786440 | tf_op jit(solution)/shard_map/ppermute | solution.py:16
  288.7 17.7 %collective-permute-start.14 = (f32[4,128,128]{2,1,0:T(8,128)}, f32[4,128,128]{2,1,0:T(8,128)}, u32[]{:S(2)}, u32[]{:S(2)}) collective-permute-start(f32[4,128,128]{2,1,0:T(8,128)} %get-tuple-element.7), channel_id=1, source_target_pairs={{1,0},{2,1},{3,2},{4,3},{5,4},{6,5},{7,6},{8,7},{9,8},{10,9},{11,1... | collective-permute-start | bytes 786440 | tf_op jit(solution)/shard_map/ppermute | solution.py:17
  (19 other events, 158.5 us)
Sparse Core Ops, SparseCore 0:
  306.5 66.0 reduce-scatter.1

commit v2 on v1

--- a/solution.py
+++ b/solution.py
@@ -98,22 +98,26 @@
     targets = block_target[0]
     payload = checkpoint[0]
     peers = targets // per_device
-    matches = (peers[:, None] == jnp.arange(devices, dtype=jnp.int32)[None, :]).astype(jnp.int32)
+    lanes = jnp.arange(devices, dtype=jnp.int32)
+    peer_grid = peers.reshape(devices, per_device)
+    own_peers = lax.dynamic_index_in_dim(peer_grid, position, 0, keepdims=False)
+    own_matches = (own_peers[:, None] == lanes[None, :]).astype(jnp.int32)
+    own_ranks = jnp.sum((jnp.cumsum(own_matches, axis=0) - own_matches) * own_matches, axis=1)
+    slot_of = own_peers * capacity + own_ranks
+    source_of = (
+        jnp.full((devices * capacity,), per_device, jnp.int32)
+        .at[slot_of]
+        .set(jnp.arange(per_device, dtype=jnp.int32))
+    )
+    by_block = jnp.transpose(payload, (1, 0, 2, 3))
+    outgoing = jnp.take(by_block, source_of, axis=0, mode="fill", fill_value=0.0)
+    outgoing = outgoing.reshape(devices, capacity, 2, block_rows, breadth)
+    incoming = lax.all_to_all(outgoing, "space", split_axis=0, concat_axis=0, tiled=True)
+    incoming = incoming.reshape(devices * capacity, 2, block_rows, breadth)
+    matches = (peers[:, None] == lanes[None, :]).astype(jnp.int32)
     grouped = matches.reshape(devices, per_device, devices)
     ranking = jnp.sum((jnp.cumsum(grouped, axis=1) - grouped) * grouped, axis=2)
-    peer_grid = peers.reshape(devices, per_device)
-    own_peers = lax.dynamic_index_in_dim(peer_grid, position, 0, keepdims=False)
-    own_ranks = lax.dynamic_index_in_dim(ranking, position, 0, keepdims=False)
-    slot_of = own_peers * capacity + own_ranks
-    outgoing = (
-        jnp.zeros((2, devices * capacity, block_rows, breadth), jnp.float32)
-        .at[:, slot_of]
-        .set(payload)
-    )
-    outgoing = outgoing.reshape(2, devices, capacity, block_rows, breadth)
-    incoming = lax.all_to_all(outgoing, "space", split_axis=1, concat_axis=1, tiled=True)
-    incoming = incoming.reshape(2, devices * capacity, block_rows, breadth)
-    sender_grid = jnp.arange(devices, dtype=jnp.int32)[:, None] * capacity + ranking
+    sender_grid = lanes[:, None] * capacity + ranking
     owned = peer_grid == position
     local_block = (targets % per_device).reshape(devices, per_device)
     where_from = (
@@ -121,7 +125,7 @@
         .at[jnp.where(owned, local_block, per_device).reshape(-1)]
         .set(sender_grid.reshape(-1), mode="drop")
     )
-    placed = jnp.take(incoming, where_from, axis=1)
+    placed = jnp.transpose(jnp.take(incoming, where_from, axis=0), (1, 0, 2, 3))
     levels = placed.reshape(2, length, height, breadth)
     wavelet_row = wavelet[0]
     receivers = receiver_cell[0]
@@ -160,7 +164,11 @@
     slab_rows = partial_value.reshape(length * height, breadth)
     check_part = jnp.sum(slab_rows[check_rows[0]], axis=1)
     stacked = jnp.concatenate([partial_value, check_part[None]], axis=0)
-    shares = lax.psum_scatter(stacked, "shot", scatter_dimension=1, tiled=True)
+    shot_devices = lax.axis_size("shot")
+    pieces = stacked.reshape(length + 1, shot_devices, height // shot_devices, breadth)
+    pieces = jnp.transpose(pieces, (1, 0, 2, 3))
+    gathered = lax.all_to_all(pieces, "shot", split_axis=0, concat_axis=0, tiled=True)
+    shares = jnp.sum(gathered, axis=0)
     grad_share = shares[:length]
     check_share = shares[length]
     adjoint_carry = jnp.stack([adjoints[1], adjoints[0]])[None]

time: 385 us -> 303 us (0.79)
  waiting for transfers between devices: 167 us -> 113 us
  local copies, waits for them, and re-layouts: 55.8 us -> 29.4 us
  between operations: 15.6 us -> 2.25 us
  other arithmetic: 65.1 us -> 71.6 us
  starting transfers between devices: 79 us -> 84.4 us
    reduce_scatter x1 -> x0, waiting for transfers between devices: 56.3 us -> none  [body(): shares = lax.psum_scatter(stacked, 'shot', scatter_dimension=1, tiled=True)]
    scatter x1, local copies, waits for them, and re-layouts: 13.6 us -> 0.98 us  [body(): source_of = jnp.full((devices * capacity,), per_device, jnp.int32).at[slo...]
    ppermute x8, waiting for transfers between devices: 23.8 us -> 31 us  [padded_2(): after = lax.ppermute(initial, axis, down)]
    all_to_all x1 -> x2, starting transfers between devices: 10.2 us -> 15.6 us  [the longest x1 10.2 us: body(): lax.all_to_all(outgoing, 'space', split_axis=0, concat_axis=0, tiled=True)]
    all_to_all x1 -> x0, local copies, waits for them, and re-layouts: 4.66 us -> none  [body(): lax.all_to_all(outgoing, 'space', split_axis=1, concat_axis=1, tiled=True)]
    reshape x1 -> x0, local copies, waits for them, and re-layouts: 4.66 us -> none  [body(): outgoing = outgoing.reshape(2, devices, capacity, block_rows, breadth)]
    ppermute x8, waiting for transfers between devices: 86.4 us -> 82.3 us  [padded_2(): before = lax.ppermute(last, axis, up)]
    select_n x3 -> x5, other arithmetic: 1.44 us -> 5.35 us  [the longest x2 3.9 us: body(): jnp.take(by_block, source_of, axis=0, mode='fill', fill_value=0.0)]
  transfers between devices with their start and end apart: 18 -> 18, of which waited for: 9 -> 9; matrix products, arithmetic and copies ran while one was open for 19% -> 24% of each run, Pallas kernels for 0% -> 0%
where the time goes in v2:
time: 303 us; the launch traced here: 301 us
  waiting for transfers between devices  113 us (37%)
  starting transfers between devices  84.4 us (28%)
  other arithmetic  71.6 us (24%)
  local copies, waits for them, and re-layouts  29.4 us (10%)
    ppermute x8, waiting for transfers between devices, padded_2(): before = lax.ppermute(last, axis, up)  82.3 us
    ppermute x8, starting transfers between devices, padded_2(): before = lax.ppermute(last, axis, up)  52.4 us
    ppermute x8, waiting for transfers between devices, padded_2(): after = lax.ppermute(initial, axis, down)  31 us
    add x4, other arithmetic, retreat(): earlier = 2.0 * current - following + laplace(weighted_ext)  17.1 us
    ppermute x8, starting transfers between devices, padded_2(): after = lax.ppermute(initial, axis, down)  16.4 us
    scatter-add x4, other arithmetic, inject(): flattened = field.reshape(-1).at[target].add(values, mode='drop')  15.7 us
    all_to_all x1, starting transfers between devices, body(): lax.all_to_all(outgoing, 'space', split_axis=0, concat_axis=0, tiled=True)  10.2 us
    add x3, other arithmetic, inject_dense(): return field + jnp.where(cells == local_cell, values[0], 0.0)  9.92 us
  transfers between devices with their start and end apart: 18, of which 9 were waited for; matrix products, arithmetic and copies ran while one was open for 24% of the time, Pallas kernels for 0%

profile of v2, /device:TPU:100, one launch (start us, length us, event | category | flops | bytes accessed | tf_op | source)
XLA Modules:
  0.0 301.0 jit_solution(2633108979269224454)
XLA Ops:
  3.0 3.5 %gather_fusion = f32[512,2,8,128]{3,2,1,0:T(8,128)} fusion(f32[128,2,8,128]{3,2,0,1:T(8,128)S(1)} %bitcast.83, s32[1024]{0:T(1024)S(1)} %pad_clamp_fusion.1), kind=kCustom, calls=%fused_computation | custom fusion | bytes 8390656 | tf_op jit(solution)/shard_map/jit(_take)/gather | solution.py:113
  6.6 3.9 %broadcast_select_fusion = f32[16,32,2,8,128]{4,3,2,1,0:T(8,128)} fusion(f32[16,32,2,8,128]{4,3,2,1,0:T(8,128)} %bitcast.103, pred[16,32]{1,0:T(8,128)(4,1)S(1)} %broadcast_in_dim.74), kind=kLoop, calls=%fused_computation.32 | loop fusion | flops 1048576 | bytes 8389120 | tf_op jit(solution)/shard_map/jit(_take)/select_n | solution.py:113
  10.5 10.2 %all-to-all-start = ((f32[16,32,2,8,128]{4,3,2,1,0:T(8,128)}), f32[16,32,2,8,128]{4,3,2,1,0:T(8,128)}, u32[]{:S(2)}, u32[]{:S(2)}) async-start(f32[16,32,2,8,128]{4,3,2,1,0:T(8,128)} %broadcast_select_fusion), calls=%async_computation | async-start | bytes 8388608 | tf_op jit(solution)/shard_map/all_to_all | solution.py:115
  21.9 4.6 %collective-permute-start.1 = (f32[4,128,128]{2,1,0:T(8,128)S(1)}, f32[4,128,128]{2,1,0:T(8,128)S(1)}, u32[]{:S(2)}, u32[]{:S(2)}) collective-permute-start(f32[4,128,128]{2,1,0:T(8,128)S(1)} %get-tuple-element.14), channel_id=1, source_target_pairs={{0,1},{1,2},{2,3},{3,4},{4,5},{5,6},{6,7},{7,8},{8,9},{9,10},{10,1... | collective-permute-start | bytes 786440 | tf_op jit(solution)/shard_map/ppermute | solution.py:16
  32.4 8.0 %scatter_custom_fusion.3 = s32[128]{0:T(128)S(1)} fusion(s32[2048]{0:T(1024)S(1)} %bitcast.122, s32[2048]{0:T(1024)S(1)} %add_bitcast_fusion, s32[]{:T(128)} %constant.96.clone.1), kind=kCustom, calls=%fused_computation.553 | custom fusion | bytes 516 | tf_op jit(solution)/shard_map/scatter | solution.py:126
  43.4 75.2 %collective-permute-done.1 = f32[4,128,128]{2,1,0:T(8,128)S(1)} collective-permute-done((f32[4,128,128]{2,1,0:T(8,128)S(1)}, f32[4,128,128]{2,1,0:T(8,128)S(1)}, u32[]{:S(2)}, u32[]{:S(2)}) %collective-permute-start.1) | collective-permute-done | bytes 262176 | tf_op jit(solution)/shard_map/ppermute | solution.py:16
  120.5 3.4 %fusion.207 = f32[8,128,128]{2,1,0:T(8,128)S(1)} fusion(f32[8,128,128]{2,1,0:T(8,128)S(1)} %bitcast_multiply_fusion, f32[4,128,128]{2,1,0:T(8,128)S(1)} %collective-permute-done.1, f32[4,128,128]{2,1,0:T(8,128)} %copy-done.22, f32[16,136,136]{2,1,0:T(8,128)S(1)} %select_maximum_fusion.14, f32[1,2,8,128,128]{4,3,2,1,0:T(8,128)} %param.12), kind=kLoop, calls=%fused_computation.338 | loop fusion | flops 6291456 | bytes 11010048 | tf_op jit(solution)/shard_map/add | solution.py:72
  124.0 3.5 %scatter_fusion = f32[131072]{0:T(1024)S(1)} fusion(f32[131072]{0:T(1024)S(1)} %bitcast.91, s32[512]{0:T(512)S(1)} %bitcast.113, f32[512]{0:T(512)S(1)} %bitcast.121), kind=kCustom, calls=%fused_computation.3 | custom fusion | flops 512 | bytes 8192 | tf_op jit(solution)/shard_map/scatter-add | solution.py:51
  127.7 7.9 %collective-permute-start.3 = (f32[4,128,128]{2,1,0:T(8,128)S(1)}, f32[4,128,128]{2,1,0:T(8,128)S(1)}, u32[]{:S(2)}, u32[]{:S(2)}) collective-permute-start(f32[4,128,128]{2,1,0:T(8,128)S(1)} %get-tuple-element.12), channel_id=1, source_target_pairs={{0,1},{1,2},{2,3},{3,4},{4,5},{5,6},{6,7},{7,8},{8,9},{9,10},{10,1... | collective-permute-start | bytes 786440 | tf_op jit(solution)/shard_map/ppermute | solution.py:16
  141.1 7.8 %collective-permute-done.2 = f32[4,128,128]{2,1,0:T(8,128)} collective-permute-done((f32[4,128,128]{2,1,0:T(8,128)S(1)}, f32[4,128,128]{2,1,0:T(8,128)}, u32[]{:S(2)}, u32[]{:S(2)}) %collective-permute-start.2) | collective-permute-done | bytes 262176 | tf_op jit(solution)/shard_map/ppermute | solution.py:17
  150.5 4.4 %fusion.182 = f32[8,128,128]{2,1,0:T(8,128)S(1)} fusion(f32[8,128,128]{2,1,0:T(8,128)} %copy-done.17, f32[4,128,128]{2,1,0:T(8,128)S(1)} %collective-permute-done.3, f32[4,128,128]{2,1,0:T(8,128)} %collective-permute-done.2, f32[16,136,136]{2,1,0:T(8,128)S(1)} %select_maximum_fusion.12, f32[8,128,128]{2,1,0:T(8,128)S(1)} %bitcast.93, ...), kind=kLoop, calls=%fused_computation.313 | loop fusion | flops 6291456 | bytes 11010048 | tf_op jit(solution)/shard_map/add | solution.py:72
  154.9 3.7 %scatter_fusion.1 = f32[131072]{0:T(1024)S(1)} fusion(f32[131072]{0:T(1024)S(1)} %bitcast.96, s32[512]{0:T(512)S(1)} %bitcast.114, f32[512]{0:T(512)S(1)} %bitcast.120), kind=kCustom, calls=%fused_computation.4 | custom fusion | flops 512 | bytes 8192 | tf_op jit(solution)/shard_map/scatter-add | solution.py:51
  159.7 5.7 %collective-permute-start.5 = (f32[4,128,128]{2,1,0:T(8,128)S(1)}, f32[4,128,128]{2,1,0:T(8,128)S(1)}, u32[]{:S(2)}, u32[]{:S(2)}) collective-permute-start(f32[4,128,128]{2,1,0:T(8,128)S(1)} %get-tuple-element.10), channel_id=1, source_target_pairs={{0,1},{1,2},{2,3},{3,4},{4,5},{5,6},{6,7},{7,8},{8,9},{9,10},{10,1... | collective-permute-start | bytes 786440 | tf_op jit(solution)/shard_map/ppermute | solution.py:16
  167.4 3.9 %gather_fusion.1 = f32[128,2,8,128]{3,2,1,0:T(8,128)} fusion(f32[512,2,8,128]{3,2,1,0:T(8,128)} %bitcast.24, s32[1024]{0:T(1024)} %pad_clamp_fusion), kind=kCustom, calls=%fused_computation.1 | custom fusion | bytes 2097664 | tf_op jit(solution)/shard_map/jit(_take)/gather | solution.py:128
  172.8 7.5 %collective-permute-start.7 = (f32[4,128,128]{2,1,0:T(8,128)S(1)}, f32[4,128,128]{2,1,0:T(8,128)S(1)}, u32[]{:S(2)}, u32[]{:S(2)}) collective-permute-start(f32[4,128,128]{2,1,0:T(8,128)S(1)} %bitcast.112), channel_id=1, source_target_pairs={{0,1},{1,2},{2,3},{3,4},{4,5},{5,6},{6,7},{7,8},{8,9},{9,10},{10,1... | collective-permute-start | bytes 786440 | tf_op jit(solution)/shard_map/ppermute | solution.py:16
  182.4 3.0 collective-permute-done.7
  185.4 7.7 %collective-permute-done.6 = f32[4,128,128]{2,1,0:T(8,128)S(1)} collective-permute-done((f32[4,128,128]{2,1,0:T(8,128)S(1)}, f32[4,128,128]{2,1,0:T(8,128)S(1)}, u32[]{:S(2)}, u32[]{:S(2)}) %collective-permute-start.6) | collective-permute-done | bytes 262176 | tf_op jit(solution)/shard_map/ppermute | solution.py:17
  193.7 2.9 fusion.132
  196.8 5.7 %collective-permute-start.9 = (f32[4,128,128]{2,1,0:T(8,128)S(1)}, f32[4,128,128]{2,1,0:T(8,128)S(1)}, u32[]{:S(2)}, u32[]{:S(2)}) collective-permute-start(f32[4,128,128]{2,1,0:T(8,128)S(1)} %get-tuple-element.20), channel_id=1, source_target_pairs={{0,1},{1,2},{2,3},{3,4},{4,5},{5,6},{6,7},{7,8},{8,9},{9,10},{10,1... | collective-permute-start | bytes 786440 | tf_op jit(solution)/shard_map/ppermute | solution.py:16
  208.1 7.7 %collective-permute-done.8 = f32[4,128,128]{2,1,0:T(8,128)S(1)} collective-permute-done((f32[4,128,128]{2,1,0:T(8,128)S(1)}, f32[4,128,128]{2,1,0:T(8,128)S(1)}, u32[]{:S(2)}, u32[]{:S(2)}) %collective-permute-start.8) | collective-permute-done | bytes 262176 | tf_op jit(solution)/shard_map/ppermute | solution.py:17
  220.2 5.7 %collective-permute-start.11 = (f32[4,128,128]{2,1,0:T(8,128)}, f32[4,128,128]{2,1,0:T(8,128)}, u32[]{:S(2)}, u32[]{:S(2)}) collective-permute-start(f32[4,128,128]{2,1,0:T(8,128)} %get-tuple-element.18), channel_id=1, source_target_pairs={{0,1},{1,2},{2,3},{3,4},{4,5},{5,6},{6,7},{7,8},{8,9},{9,10},{10,1... | collective-permute-start | bytes 786440 | tf_op jit(solution)/shard_map/ppermute | solution.py:16
  227.8 4.2 %fusion.157 = f32[8,128,128]{2,1,0:T(8,128)S(1)} fusion(f32[8,128,128]{2,1,0:T(8,128)} %copy-done.14, f32[4,128,128]{2,1,0:T(8,128)S(1)} %collective-permute-done.5, f32[4,128,128]{2,1,0:T(8,128)} %collective-permute-done.4, f32[16,136,136]{2,1,0:T(8,128)S(1)} %select_maximum_fusion.10, f32[8,128,128]{2,1,0:T(8,128)S(1)} %bitcast.94, ...), kind=kLoop, calls=%fused_computation.288 | loop fusion | flops 6291456 | bytes 11010048 | tf_op jit(solution)/shard_map/add | solution.py:72
  232.0 3.5 %scatter_fusion.2 = f32[131072]{0:T(1024)S(1)} fusion(f32[131072]{0:T(1024)S(1)} %bitcast.86, s32[512]{0:T(512)S(1)} %bitcast.115, f32[512]{0:T(512)S(1)} %bitcast.119), kind=kCustom, calls=%fused_computation.5 | custom fusion | flops 512 | bytes 8192 | tf_op jit(solution)/shard_map/scatter-add | solution.py:51
  235.8 7.7 %collective-permute-start.15 = (f32[4,128,128]{2,1,0:T(8,128)S(1)}, f32[4,128,128]{2,1,0:T(8,128)S(1)}, u32[]{:S(2)}, u32[]{:S(2)}) collective-permute-start(f32[4,128,128]{2,1,0:T(8,128)S(1)} %get-tuple-element.8), channel_id=1, source_target_pairs={{0,1},{1,2},{2,3},{3,4},{4,5},{5,6},{6,7},{7,8},{8,9},{9,10},{10,1... | collective-permute-start | bytes 786440 | tf_op jit(solution)/shard_map/ppermute | solution.py:16
  247.1 4.1 %fusion.78 = f32[8,128,128]{2,1,0:T(8,128)S(1)} fusion(f32[8,128,128]{2,1,0:T(8,128)S(1)} %copy-done.6, f32[8,128,128]{2,1,0:T(8,128)S(1)} %copy-done.11, f32[4,128,128]{2,1,0:T(8,128)} %collective-permute-done.11, f32[4,128,128]{2,1,0:T(8,128)} %collective-permute-done.10, f32[16,136,136]{2,1,0:T(8,128)S(1)} %select_maximum_fusion.4, ...), kind=kLoop, calls=%fused_computation.209 | loop fusion | flops 7077888 | bytes 11010600 | tf_op jit(solution)/shard_map/add | solution.py:63
  251.3 7.5 %collective-permute-start.13 = (f32[4,128,128]{2,1,0:T(8,128)S(1)}, f32[4,128,128]{2,1,0:T(8,128)S(1)}, u32[]{:S(2)}, u32[]{:S(2)}) collective-permute-start(f32[4,128,128]{2,1,0:T(8,128)S(1)} %get-tuple-element.16), channel_id=1, source_target_pairs={{0,1},{1,2},{2,3},{3,4},{4,5},{5,6},{6,7},{7,8},{8,9},{9,10},{10,1... | collective-permute-start | bytes 786440 | tf_op jit(solution)/shard_map/ppermute | solution.py:16
  263.8 7.2 %collective-permute-done.12 = f32[4,128,128]{2,1,0:T(8,128)S(1)} collective-permute-done((f32[4,128,128]{2,1,0:T(8,128)S(1)}, f32[4,128,128]{2,1,0:T(8,128)S(1)}, u32[]{:S(2)}, u32[]{:S(2)}) %collective-permute-start.12) | collective-permute-done | bytes 262176 | tf_op jit(solution)/shard_map/ppermute | solution.py:17
  271.7 2.9 fusion.51
  274.7 5.5 %gather_fusion.2 = f32[2048,128]{1,0:T(8,128)S(1)} fusion(f32[1024,128]{1,0:T(8,128)S(1)} %bitcast.84, s32[2048]{0:T(1024)S(1)} %broadcast_clamp_fusion), kind=kCustom, calls=%fused_computation.2 | custom fusion | bytes 2105344 | tf_op jit(solution)/shard_map/gather | solution.py:165
  281.3 5.4 %all-to-all-start.1 = ((f32[16,9,8,128]{3,2,1,0:T(8,128)}), f32[16,9,8,128]{3,2,1,0:T(8,128)}, u32[]{:S(2)}, u32[]{:S(2)}) async-start(f32[16,9,8,128]{3,2,1,0:T(8,128)} %copy.24), calls=%async_computation.1 | async-start | bytes 1179648 | tf_op jit(solution)/shard_map/all_to_all | solution.py:170
  286.7 5.0 %fusion.20 = f32[8,128,128]{2,1,0:T(8,128)} fusion(f32[8,128,128]{2,1,0:T(8,128)} %copy-done.16, f32[4,128,128]{2,1,0:T(8,128)S(1)} %collective-permute-done.15, f32[4,128,128]{2,1,0:T(8,128)} %copy-done.21, f32[16,136,136]{2,1,0:T(8,128)S(1)} %copy-done.1, f32[8,128,128]{2,1,0:T(8,128)} %bitcast.100, f32[8,128,128]{2,1,0:T(8,128)} %bitcast.89), kind=kLoop, calls=%fused_computation.151 | loop fusion | flops 6291456 | bytes 11010048 | tf_op jit(solution)/shard_map/add | solution.py:72
  291.7 4.9 %scatter_fusion.3 = f32[131072]{0:T(1024)} fusion(f32[131072]{0:T(1024)} %bitcast.101, s32[512]{0:T(512)S(1)} %bitcast.116, f32[512]{0:T(512)S(1)} %bitcast.118), kind=kCustom, calls=%fused_computation.8 | custom fusion | flops 512 | bytes 8192 | tf_op jit(solution)/shard_map/scatter-add | solution.py:51
  (148 shorter events, 54.6 us)
Async XLA Ops:
  10.5 156.9 %all-to-all-start = ((f32[16,32,2,8,128]{4,3,2,1,0:T(8,128)}), f32[16,32,2,8,128]{4,3,2,1,0:T(8,128)}, u32[]{:S(2)}, u32[]{:S(2)}) async-start(f32[16,32,2,8,128]{4,3,2,1,0:T(8,128)} %broadcast_select_fusion), calls=%async_computation | async-start | bytes 8388608 | tf_op jit(solution)/shard_map/all_to_all | solution.py:115
  20.7 20.4 %copy-start.31 = (f32[1,4]{1,0:T(1,128)S(1)}, f32[1,4]{1,0:T(1,128)}, u32[]{:S(2)}) copy-start(f32[1,4]{1,0:T(1,128)} %param.13) | copy-start | bytes 52
  20.7 21.5 %copy-start.32 = (s32[1,512]{1,0:T(1,128)S(1)}, s32[1,512]{1,0:T(1,128)}, u32[]{:S(2)}) copy-start(s32[1,512]{1,0:T(1,128)} %param.15) | copy-start | bytes 6148
  20.7 21.5 %copy-start.29 = (f32[1,4,512]{2,1,0:T(4,128)S(1)}, f32[1,4,512]{2,1,0:T(4,128)}, u32[]{:S(2)}) copy-start(f32[1,4,512]{2,1,0:T(4,128)} %param.16) | copy-start | bytes 24580
  20.7 22.6 %copy-start.30 = (s32[1,128,16]{1,2,0:T(8,128)S(1)}, s32[1,128,16]{1,2,0:T(8,128)}, u32[]{:S(2)}) copy-start(s32[1,128,16]{1,2,0:T(8,128)} %param.17) | copy-start | bytes 24580
  21.9 96.6 %collective-permute-start.1 = (f32[4,128,128]{2,1,0:T(8,128)S(1)}, f32[4,128,128]{2,1,0:T(8,128)S(1)}, u32[]{:S(2)}, u32[]{:S(2)}) collective-permute-start(f32[4,128,128]{2,1,0:T(8,128)S(1)} %get-tuple-element.14), channel_id=1, source_target_pairs={{0,1},{1,2},{2,3},{3,4},{4,5},{5,6},{6,7},{7,8},{8,9},{9,10},{10,1... | collective-permute-start | bytes 786440 | tf_op jit(solution)/shard_map/ppermute | solution.py:16
  26.5 92.7 %collective-permute-start = (f32[4,128,128]{2,1,0:T(8,128)S(1)}, f32[4,128,128]{2,1,0:T(8,128)S(1)}, u32[]{:S(2)}, u32[]{:S(2)}) collective-permute-start(f32[4,128,128]{2,1,0:T(8,128)S(1)} %get-tuple-element.13), channel_id=1, source_target_pairs={{1,0},{2,1},{3,2},{4,3},{5,4},{6,5},{7,6},{8,7},{9,8},{10,9},{11,1... | collective-permute-start | bytes 786440 | tf_op jit(solution)/shard_map/ppermute | solution.py:17
  127.6 21.3 %copy-start.17 = (f32[8,128,128]{2,1,0:T(8,128)}, f32[8,128,128]{2,1,0:T(8,128)S(1)}, u32[]{:S(2)}) copy-start(f32[8,128,128]{2,1,0:T(8,128)S(1)} %mul.448) | copy-start | bytes 1572868
  127.7 13.4 %collective-permute-start.3 = (f32[4,128,128]{2,1,0:T(8,128)S(1)}, f32[4,128,128]{2,1,0:T(8,128)S(1)}, u32[]{:S(2)}, u32[]{:S(2)}) collective-permute-start(f32[4,128,128]{2,1,0:T(8,128)S(1)} %get-tuple-element.12), channel_id=1, source_target_pairs={{0,1},{1,2},{2,3},{3,4},{4,5},{5,6},{6,7},{7,8},{8,9},{9,10},{10,1... | collective-permute-start | bytes 786440 | tf_op jit(solution)/shard_map/ppermute | solution.py:16
  135.6 13.3 %collective-permute-start.2 = (f32[4,128,128]{2,1,0:T(8,128)S(1)}, f32[4,128,128]{2,1,0:T(8,128)}, u32[]{:S(2)}, u32[]{:S(2)}) collective-permute-start(f32[4,128,128]{2,1,0:T(8,128)S(1)} %get-tuple-element.11), channel_id=1, source_target_pairs={{1,0},{2,1},{3,2},{4,3},{5,4},{6,5},{7,6},{8,7},{9,8},{10,9},{11,1... | collective-permute-start | bytes 786440 | tf_op jit(solution)/shard_map/ppermute | solution.py:17
  158.7 113.0 %copy-start.4 = (f32[131072]{0:T(1024)}, f32[131072]{0:T(1024)S(1)}, u32[]{:S(2)}) copy-start(f32[131072]{0:T(1024)S(1)} %scatter_fusion.1) | copy-start | bytes 1572868
  158.7 12.6 %copy-start.33 = (pred[128]{0:T(512)(128)(4,1)S(1)}, pred[128]{0:T(512)(128)(4,1)}, u32[]{:S(2)}) copy-start(pred[128]{0:T(512)(128)(4,1)} %compare_and_fusion.1) | copy-start | bytes 388
  159.7 44.7 %collective-permute-start.5 = (f32[4,128,128]{2,1,0:T(8,128)S(1)}, f32[4,128,128]{2,1,0:T(8,128)S(1)}, u32[]{:S(2)}, u32[]{:S(2)}) collective-permute-start(f32[4,128,128]{2,1,0:T(8,128)S(1)} %get-tuple-element.10), channel_id=1, source_target_pairs={{0,1},{1,2},{2,3},{3,4},{4,5},{5,6},{6,7},{7,8},{8,9},{9,10},{10,1... | collective-permute-start | bytes 786440 | tf_op jit(solution)/shard_map/ppermute | solution.py:16
  165.4 39.0 %collective-permute-start.4 = (f32[4,128,128]{2,1,0:T(8,128)S(1)}, f32[4,128,128]{2,1,0:T(8,128)}, u32[]{:S(2)}, u32[]{:S(2)}) collective-permute-start(f32[4,128,128]{2,1,0:T(8,128)S(1)} %get-tuple-element.9), channel_id=1, source_target_pairs={{1,0},{2,1},{3,2},{4,3},{5,4},{6,5},{7,6},{8,7},{9,8},{10,9},{11,1... | collective-permute-start | bytes 786440 | tf_op jit(solution)/shard_map/ppermute | solution.py:17
  172.8 12.6 %collective-permute-start.7 = (f32[4,128,128]{2,1,0:T(8,128)S(1)}, f32[4,128,128]{2,1,0:T(8,128)S(1)}, u32[]{:S(2)}, u32[]{:S(2)}) collective-permute-start(f32[4,128,128]{2,1,0:T(8,128)S(1)} %bitcast.112), channel_id=1, source_target_pairs={{0,1},{1,2},{2,3},{3,4},{4,5},{5,6},{6,7},{7,8},{8,9},{9,10},{10,1... | collective-permute-start | bytes 786440 | tf_op jit(solution)/shard_map/ppermute | solution.py:16
  180.3 13.4 %copy-start.25 = (s32[128]{0:T(128)S(1)}, s32[128]{0:T(128)}, u32[]{:S(2)}) copy-start(s32[128]{0:T(128)} %iota_multiply_fusion) | copy-start | bytes 1540
  180.3 13.4 %copy-start.27 = (s32[8]{0:T(128)S(1)}, s32[8]{0:T(128)}, u32[]{:S(2)}) copy-start(s32[8]{0:T(128)} %iota_multiply_fusion.1) | copy-start | bytes 100
  180.3 12.7 %collective-permute-start.6 = (f32[4,128,128]{2,1,0:T(8,128)S(1)}, f32[4,128,128]{2,1,0:T(8,128)S(1)}, u32[]{:S(2)}, u32[]{:S(2)}) collective-permute-start(f32[4,128,128]{2,1,0:T(8,128)S(1)} %bitcast.111), channel_id=1, source_target_pairs={{1,0},{2,1},{3,2},{4,3},{5,4},{6,5},{7,6},{8,7},{9,8},{10,9},{11,1... | collective-permute-start | bytes 786440 | tf_op jit(solution)/shard_map/ppermute | solution.py:17
  182.4 14.3 %copy-start.19 = (f32[1,128,8,128]{3,2,0,1:T(8,128)}, f32[1,128,8,128]{3,2,0,1:T(8,128)S(1)}, u32[]{:S(2)}) copy-start(f32[1,128,8,128]{3,2,0,1:T(8,128)S(1)} %get-tuple-element.3) | copy-start | bytes 1572868
  182.4 34.1 %copy-start.12 = (f32[1,128,8,128]{3,2,0,1:T(8,128)}, f32[1,128,8,128]{3,2,0,1:T(8,128)S(1)}, u32[]{:S(2)}) copy-start(f32[1,128,8,128]{3,2,0,1:T(8,128)S(1)} %get-tuple-element.4) | copy-start | bytes 1572868
  196.7 19.7 %copy-start.8 = (f32[8,128,128]{2,1,0:T(8,128)}, f32[8,128,128]{2,1,0:T(8,128)S(1)}, u32[]{:S(2)}) copy-start(f32[8,128,128]{2,1,0:T(8,128)S(1)} %fusion.132) | copy-start | bytes 1572868
  196.8 11.3 %collective-permute-start.9 = (f32[4,128,128]{2,1,0:T(8,128)S(1)}, f32[4,128,128]{2,1,0:T(8,128)S(1)}, u32[]{:S(2)}, u32[]{:S(2)}) collective-permute-start(f32[4,128,128]{2,1,0:T(8,128)S(1)} %get-tuple-element.20), channel_id=1, source_target_pairs={{0,1},{1,2},{2,3},{3,4},{4,5},{5,6},{6,7},{7,8},{8,9},{9,10},{10,1... | collective-permute-start | bytes 786440 | tf_op jit(solution)/shard_map/ppermute | solution.py:16
  202.5 13.3 %collective-permute-start.8 = (f32[4,128,128]{2,1,0:T(8,128)S(1)}, f32[4,128,128]{2,1,0:T(8,128)S(1)}, u32[]{:S(2)}, u32[]{:S(2)}) collective-permute-start(f32[4,128,128]{2,1,0:T(8,128)S(1)} %get-tuple-element.19), channel_id=1, source_target_pairs={{1,0},{2,1},{3,2},{4,3},{5,4},{6,5},{7,6},{8,7},{9,8},{10,9},{11,1... | collective-permute-start | bytes 786440 | tf_op jit(solution)/shard_map/ppermute | solution.py:17
  220.2 25.2 %collective-permute-start.11 = (f32[4,128,128]{2,1,0:T(8,128)}, f32[4,128,128]{2,1,0:T(8,128)}, u32[]{:S(2)}, u32[]{:S(2)}) collective-permute-start(f32[4,128,128]{2,1,0:T(8,128)} %get-tuple-element.18), channel_id=1, source_target_pairs={{0,1},{1,2},{2,3},{3,4},{4,5},{5,6},{6,7},{7,8},{8,9},{9,10},{10,1... | collective-permute-start | bytes 786440 | tf_op jit(solution)/shard_map/ppermute | solution.py:16
  225.9 19.5 %collective-permute-start.10 = (f32[4,128,128]{2,1,0:T(8,128)}, f32[4,128,128]{2,1,0:T(8,128)}, u32[]{:S(2)}, u32[]{:S(2)}) collective-permute-start(f32[4,128,128]{2,1,0:T(8,128)} %get-tuple-element.17), channel_id=1, source_target_pairs={{1,0},{2,1},{3,2},{4,3},{5,4},{6,5},{7,6},{8,7},{9,8},{10,9},{11,1... | collective-permute-start | bytes 786440 | tf_op jit(solution)/shard_map/ppermute | solution.py:17
  235.6 36.1 %copy-start.2 = (f32[131072]{0:T(1024)}, f32[131072]{0:T(1024)S(1)}, u32[]{:S(2)}) copy-start(f32[131072]{0:T(1024)S(1)} %scatter_fusion.2) | copy-start | bytes 1572868
  235.7 25.3 %copy-start.16 = (f32[8,128,128]{2,1,0:T(8,128)}, f32[8,128,128]{2,1,0:T(8,128)S(1)}, u32[]{:S(2)}) copy-start(f32[8,128,128]{2,1,0:T(8,128)S(1)} %mul.550) | copy-start | bytes 1572868
  235.8 25.2 %collective-permute-start.15 = (f32[4,128,128]{2,1,0:T(8,128)S(1)}, f32[4,128,128]{2,1,0:T(8,128)S(1)}, u32[]{:S(2)}, u32[]{:S(2)}) collective-permute-start(f32[4,128,128]{2,1,0:T(8,128)S(1)} %get-tuple-element.8), channel_id=1, source_target_pairs={{0,1},{1,2},{2,3},{3,4},{4,5},{5,6},{6,7},{7,8},{8,9},{9,10},{10,1... | collective-permute-start | bytes 786440 | tf_op jit(solution)/shard_map/ppermute | solution.py:16
  243.5 17.6 %collective-permute-start.14 = (f32[4,128,128]{2,1,0:T(8,128)S(1)}, f32[4,128,128]{2,1,0:T(8,128)S(1)}, u32[]{:S(2)}, u32[]{:S(2)}) collective-permute-start(f32[4,128,128]{2,1,0:T(8,128)S(1)} %get-tuple-element.7), channel_id=1, source_target_pairs={{1,0},{2,1},{3,2},{4,3},{5,4},{6,5},{7,6},{8,7},{9,8},{10,9},{11,1... | collective-permute-start | bytes 786440 | tf_op jit(solution)/shard_map/ppermute | solution.py:17
  251.3 12.5 %collective-permute-start.13 = (f32[4,128,128]{2,1,0:T(8,128)S(1)}, f32[4,128,128]{2,1,0:T(8,128)S(1)}, u32[]{:S(2)}, u32[]{:S(2)}) collective-permute-start(f32[4,128,128]{2,1,0:T(8,128)S(1)} %get-tuple-element.16), channel_id=1, source_target_pairs={{0,1},{1,2},{2,3},{3,4},{4,5},{5,6},{6,7},{7,8},{8,9},{9,10},{10,1... | collective-permute-start | bytes 786440 | tf_op jit(solution)/shard_map/ppermute | solution.py:16
  258.9 12.1 %collective-permute-start.12 = (f32[4,128,128]{2,1,0:T(8,128)S(1)}, f32[4,128,128]{2,1,0:T(8,128)S(1)}, u32[]{:S(2)}, u32[]{:S(2)}) collective-permute-start(f32[4,128,128]{2,1,0:T(8,128)S(1)} %get-tuple-element.15), channel_id=1, source_target_pairs={{1,0},{2,1},{3,2},{4,3},{5,4},{6,5},{7,6},{8,7},{9,8},{10,9},{11,1... | collective-permute-start | bytes 786440 | tf_op jit(solution)/shard_map/ppermute | solution.py:17
  281.3 17.4 %all-to-all-start.1 = ((f32[16,9,8,128]{3,2,1,0:T(8,128)}), f32[16,9,8,128]{3,2,1,0:T(8,128)}, u32[]{:S(2)}, u32[]{:S(2)}) async-start(f32[16,9,8,128]{3,2,1,0:T(8,128)} %copy.24), calls=%async_computation.1 | async-start | bytes 1179648 | tf_op jit(solution)/shard_map/all_to_all | solution.py:170
  (20 other events, 138.7 us)

commit v3 on v2

--- a/solution.py
+++ b/solution.py
@@ -75,6 +75,22 @@
 
 def extend(field):
     return padded_2(field, (("space", 0),), 4)
+
+
+def extend_many(fields, width=4):
+    devices = lax.axis_size("space")
+    up = [(i, (i + 1) % devices) for i in range(devices - 1)]
+    down = [(j, i) for i, j in up]
+    last = jnp.concatenate([f[f.shape[0] - width :] for f in fields], axis=0)
+    initial = jnp.concatenate([f[:width] for f in fields], axis=0)
+    before = lax.ppermute(last, "space", up)
+    after = lax.ppermute(initial, "space", down)
+    return [
+        jnp.concatenate(
+            [before[i * width : (i + 1) * width], f, after[i * width : (i + 1) * width]], axis=0
+        )
+        for i, f in enumerate(fields)
+    ]
 
 
 def body(
@@ -135,19 +151,19 @@
     adjoints = [None] * (horizon + 2)
     adjoints[horizon + 1] = adjoint_state[0, 0]
     adjoints[horizon] = adjoint_state[0, 1]
-    for moment in range(1, horizon + 1):
+    def forward_step(moment, current_ext):
         fields.append(
             advance(
                 fields[-2],
-                extend(fields[-1]),
+                current_ext,
                 courant,
                 wavelet_row[moment - 1 : moment],
                 source_cell,
                 first_row,
             )
         )
-    for moment in range(horizon, 0, -1):
-        weighted = extend(courant * adjoints[moment])
+
+    def adjoint_step(moment, weighted):
         adjoints[moment - 1] = retreat(
             adjoints[moment + 1],
             adjoints[moment],
@@ -156,13 +172,29 @@
             receivers,
             first_row,
         )
+
+    alone = horizon // 2
+    for moment in range(horizon, horizon - alone, -1):
+        adjoint_step(moment, extend(courant * adjoints[moment]))
+    for moment in range(1, horizon + 1):
+        back = horizon - alone + 1 - moment
+        if back >= 1:
+            current_ext, weighted = extend_many([fields[-1], courant * adjoints[back]])
+            forward_step(moment, current_ext)
+            adjoint_step(back, weighted)
+        else:
+            forward_step(moment, extend(fields[-1]))
     partial_value = jnp.zeros((length, height, breadth), jnp.float32)
     for moment in range(1, horizon + 1):
         partial_value = partial_value + adjoints[moment] * (
             fields[moment + 1] - 2.0 * fields[moment] + fields[moment - 1]
         )
     slab_rows = partial_value.reshape(length * height, breadth)
-    check_part = jnp.sum(slab_rows[check_rows[0]], axis=1)
+    row_ids = lax.broadcasted_iota(jnp.int32, (check_rows.shape[1], length * height), 1)
+    counts = jnp.zeros((check_rows.shape[1], length * height), jnp.float32)
+    for term in range(check_rows.shape[2]):
+        counts = counts + (check_rows[0, :, term : term + 1] == row_ids).astype(jnp.float32)
+    check_part = jnp.dot(counts, slab_rows, precision=lax.Precision.HIGHEST)
     stacked = jnp.concatenate([partial_value, check_part[None]], axis=0)
     shot_devices = lax.axis_size("shot")
     pieces = stacked.reshape(length + 1, shot_devices, height // shot_devices, breadth)

time: 303 us -> 332 us (1.096)
  waiting for transfers between devices: 113 us -> 135 us
  starting transfers between devices: 84.4 us -> 72.5 us
  other arithmetic: 71.6 us -> 81.1 us
  local copies, waits for them, and re-layouts: 29.4 us -> 37.4 us
    ppermute x0 -> x4, waiting for transfers between devices: none -> 33.9 us  [the longest x2 26.2 us: extend_many(): before = lax.ppermute(last, 'space', up)]
    ppermute x8 -> x4, starting transfers between devices: 52.4 us -> 30.9 us  [padded_2(): before = lax.ppermute(last, axis, up)]
    ppermute x0 -> x4, starting transfers between devices: none -> 17.4 us  [the longest x2 13.5 us: extend_many(): before = lax.ppermute(last, 'space', up)]
    ppermute x8 -> x4, waiting for transfers between devices: 31 us -> 16.4 us  [padded_2(): after = lax.ppermute(initial, axis, down)]
    eq x0 -> x16, local copies, waits for them, and re-layouts: none -> 10.9 us  [body(): check_rows[0, :, term:term + 1] == row_ids]
    add x4, other arithmetic: 17.1 us -> 26.2 us  [retreat(): earlier = 2.0 * current - following + laplace(weighted_ext)]
    concatenate x0 -> x7, other arithmetic: none -> 8.43 us  [the longest x3 6.68 us: extend_many(): jnp.concatenate([before[i * width:(i + 1) * width], f, after[i * width:(i...]
    ppermute x8 -> x4, starting transfers between devices: 16.4 us -> 8.75 us  [padded_2(): after = lax.ppermute(initial, axis, down)]
  transfers between devices with their start and end apart: 18 -> 14, of which waited for: 9 -> 10; matrix products, arithmetic and copies ran while one was open for 24% -> 17% of each run, Pallas kernels for 0% -> 0%
where the time goes in v3:
time: 332 us; the launch traced here: 330 us
  waiting for transfers between devices  135 us (41%)
  other arithmetic  81.1 us (24%)
  starting transfers between devices  72.5 us (22%)
  local copies, waits for them, and re-layouts  37.4 us (11%)
    ppermute x4, waiting for transfers between devices, padded_2(): before = lax.ppermute(last, axis, up)  84.3 us
    ppermute x4, starting transfers between devices, padded_2(): before = lax.ppermute(last, axis, up)  30.9 us
    add x4, other arithmetic, retreat(): earlier = 2.0 * current - following + laplace(weighted_ext)  26.2 us
    ppermute x2, waiting for transfers between devices, extend_many(): before = lax.ppermute(last, 'space', up)  26.2 us
    scatter-add x4, other arithmetic, inject(): flattened = field.reshape(-1).at[target].add(values, mode='drop')  17 us
    ppermute x4, waiting for transfers between devices, padded_2(): after = lax.ppermute(initial, axis, down)  16.4 us
    ppermute x2, starting transfers between devices, extend_many(): before = lax.ppermute(last, 'space', up)  13.5 us
    eq x16, local copies, waits for them, and re-layouts, body(): check_rows[0, :, term:term + 1] == row_ids  10.9 us
  transfers between devices with their start and end apart: 14, of which 10 were waited for; matrix products, arithmetic and copies ran while one was open for 17% of the time, Pallas kernels for 0%

profile of v3, /device:TPU:100, one launch (start us, length us, event | category | flops | bytes accessed | tf_op | source)
XLA Modules:
  0.0 330.3 jit_solution(14502568269189532397)
XLA Ops:
  3.0 3.5 %gather_fusion = f32[512,2,8,128]{3,2,1,0:T(8,128)} fusion(f32[128,2,8,128]{3,2,0,1:T(8,128)S(1)} %bitcast.84, s32[1024]{0:T(1024)S(1)} %pad_clamp_fusion.1), kind=kCustom, calls=%fused_computation | custom fusion | bytes 8390656 | tf_op jit(solution)/shard_map/jit(_take)/gather | solution.py:129
  6.5 3.9 %broadcast_select_fusion = f32[16,32,2,8,128]{4,3,2,1,0:T(8,128)} fusion(f32[16,32,2,8,128]{4,3,2,1,0:T(8,128)} %bitcast.102, pred[16,32]{1,0:T(8,128)(4,1)S(1)} %broadcast_in_dim.73), kind=kLoop, calls=%fused_computation.31 | loop fusion | flops 1048576 | bytes 8389120 | tf_op jit(solution)/shard_map/jit(_take)/select_n | solution.py:129
  10.4 10.2 %all-to-all-start = ((f32[16,32,2,8,128]{4,3,2,1,0:T(8,128)}), f32[16,32,2,8,128]{4,3,2,1,0:T(8,128)}, u32[]{:S(2)}, u32[]{:S(2)}) async-start(f32[16,32,2,8,128]{4,3,2,1,0:T(8,128)} %broadcast_select_fusion), calls=%async_computation | async-start | bytes 8388608 | tf_op jit(solution)/shard_map/all_to_all | solution.py:131
  20.8 4.6 %collective-permute-start.1 = (f32[4,128,128]{2,1,0:T(8,128)S(1)}, f32[4,128,128]{2,1,0:T(8,128)S(1)}, u32[]{:S(2)}, u32[]{:S(2)}) collective-permute-start(f32[4,128,128]{2,1,0:T(8,128)S(1)} %get-tuple-element.44), channel_id=1, source_target_pairs={{0,1},{1,2},{2,3},{3,4},{4,5},{5,6},{6,7},{7,8},{8,9},{9,10},{10,1... | collective-permute-start | bytes 786440 | tf_op jit(solution)/shard_map/ppermute | solution.py:16
  31.3 8.0 %scatter_custom_fusion.2 = s32[128]{0:T(128)S(1)} fusion(s32[2048]{0:T(1024)S(1)} %bitcast.122, s32[2048]{0:T(1024)S(1)} %add_bitcast_fusion, s32[]{:T(128)} %constant.94.clone.1), kind=kCustom, calls=%fused_computation.634 | custom fusion | bytes 516 | tf_op jit(solution)/shard_map/scatter | solution.py:142
  40.1 78.4 %collective-permute-done.1 = f32[4,128,128]{2,1,0:T(8,128)S(1)} collective-permute-done((f32[4,128,128]{2,1,0:T(8,128)S(1)}, f32[4,128,128]{2,1,0:T(8,128)S(1)}, u32[]{:S(2)}, u32[]{:S(2)}) %collective-permute-start.1) | collective-permute-done | bytes 262176 | tf_op jit(solution)/shard_map/ppermute | solution.py:16
  120.5 3.4 %fusion.207 = f32[8,128,128]{2,1,0:T(8,128)S(1)} fusion(f32[8,128,128]{2,1,0:T(8,128)S(1)} %bitcast_multiply_fusion, f32[4,128,128]{2,1,0:T(8,128)S(1)} %collective-permute-done.1, f32[4,128,128]{2,1,0:T(8,128)} %copy-done.34, f32[16,136,136]{2,1,0:T(8,128)S(1)} %select_maximum_fusion.14, f32[1,2,8,128,128]{4,3,2,1,0:T(8,128)} %param.12), kind=kLoop, calls=%fused_computation.337 | loop fusion | flops 6291456 | bytes 11010048 | tf_op jit(solution)/shard_map/add | solution.py:72
  123.9 3.5 %scatter_fusion = f32[131072]{0:T(1024)S(1)} fusion(f32[131072]{0:T(1024)S(1)} %bitcast.90, s32[512]{0:T(512)S(1)} %bitcast.113, f32[512]{0:T(512)S(1)} %bitcast.121), kind=kCustom, calls=%fused_computation.2 | custom fusion | flops 512 | bytes 8192 | tf_op jit(solution)/shard_map/scatter-add | solution.py:51
  127.6 7.9 %collective-permute-start.3 = (f32[4,128,128]{2,1,0:T(8,128)S(1)}, f32[4,128,128]{2,1,0:T(8,128)S(1)}, u32[]{:S(2)}, u32[]{:S(2)}) collective-permute-start(f32[4,128,128]{2,1,0:T(8,128)S(1)} %get-tuple-element.42), channel_id=1, source_target_pairs={{0,1},{1,2},{2,3},{3,4},{4,5},{5,6},{6,7},{7,8},{8,9},{9,10},{10,1... | collective-permute-start | bytes 786440 | tf_op jit(solution)/shard_map/ppermute | solution.py:16
  137.5 3.5 %collective-permute-done.3 = f32[4,128,128]{2,1,0:T(8,128)S(1)} collective-permute-done((f32[4,128,128]{2,1,0:T(8,128)S(1)}, f32[4,128,128]{2,1,0:T(8,128)S(1)}, u32[]{:S(2)}, u32[]{:S(2)}) %collective-permute-start.3) | collective-permute-done | bytes 262176 | tf_op jit(solution)/shard_map/ppermute | solution.py:16
  141.0 7.7 %collective-permute-done.2 = f32[4,128,128]{2,1,0:T(8,128)S(1)} collective-permute-done((f32[4,128,128]{2,1,0:T(8,128)S(1)}, f32[4,128,128]{2,1,0:T(8,128)S(1)}, u32[]{:S(2)}, u32[]{:S(2)}) %collective-permute-start.2) | collective-permute-done | bytes 262176 | tf_op jit(solution)/shard_map/ppermute | solution.py:17
  150.1 4.4 %fusion.182 = f32[8,128,128]{2,1,0:T(8,128)S(1)} fusion(f32[8,128,128]{2,1,0:T(8,128)} %copy-done.24, f32[4,128,128]{2,1,0:T(8,128)S(1)} %collective-permute-done.3, f32[4,128,128]{2,1,0:T(8,128)} %copy-done.35, f32[16,136,136]{2,1,0:T(8,128)S(1)} %select_maximum_fusion.12, f32[8,128,128]{2,1,0:T(8,128)S(1)} %bitcast.92, f32[1,2,8,128,128]{4,3,2,1,0:T(8,128)} %param.12), kind=kLoop, calls=%fused_computation.312 | loop fusion | flops 6291456 | bytes 11010048 | tf_op jit(solution)/shard_map/add | solution.py:72
  154.5 3.7 %scatter_fusion.1 = f32[131072]{0:T(1024)S(1)} fusion(f32[131072]{0:T(1024)S(1)} %bitcast.95, s32[512]{0:T(512)S(1)} %bitcast.114, f32[512]{0:T(512)S(1)} %bitcast.120), kind=kCustom, calls=%fused_computation.3 | custom fusion | flops 512 | bytes 8192 | tf_op jit(solution)/shard_map/scatter-add | solution.py:51
  159.3 3.8 %gather_fusion.1 = f32[128,2,8,128]{3,2,1,0:T(8,128)} fusion(f32[512,2,8,128]{3,2,1,0:T(8,128)} %bitcast.21, s32[1024]{0:T(1024)S(1)} %pad_clamp_fusion), kind=kCustom, calls=%fused_computation.1 | custom fusion | bytes 2097664 | tf_op jit(solution)/shard_map/jit(_take)/gather | solution.py:144
  165.4 5.7 %collective-permute-start.5 = (f32[8,128,128]{2,1,0:T(8,128)}, f32[8,128,128]{2,1,0:T(8,128)}, u32[]{:S(2)}, u32[]{:S(2)}) collective-permute-start(f32[8,128,128]{2,1,0:T(8,128)} %pad_maximum_fusion.17), channel_id=1, source_target_pairs={{0,1},{1,2},{2,3},{3,4},{4,5},{5,6},{6,7},{7,8},{8,9},{9,10},{10,1... | collective-permute-start | bytes 1572872 | tf_op jit(solution)/shard_map/ppermute | solution.py:86
  176.0 16.8 %collective-permute-done.5 = f32[8,128,128]{2,1,0:T(8,128)} collective-permute-done((f32[8,128,128]{2,1,0:T(8,128)}, f32[8,128,128]{2,1,0:T(8,128)}, u32[]{:S(2)}, u32[]{:S(2)}) %collective-permute-start.5) | collective-permute-done | bytes 524320 | tf_op jit(solution)/shard_map/ppermute | solution.py:86
  193.9 5.4 %select_maximum_fusion.8 = (f32[16,136,136]{2,1,0:T(8,128)S(1)}, f32[16,136,136]{2,1,0:T(8,128)}) fusion(f32[4,128,128]{2,1,0:T(8,128)S(1)} %get-tuple-element.36, f32[8,128,128]{2,1,0:T(8,128)S(1)} %bitcast.103, f32[4,128,128]{2,1,0:T(8,128)S(1)} %get-tuple-element.38, f32[4,128,128]{2,1,0:T(8,128)S(1)} %get-tuple-element.35, f32[8,128,128]{2,1,0:T(8,128)} %copy-done.23, ...), kind=kLoop, calls=%fused_computation.20 | loop fusion | flops 6806528 | bytes 4464640 | tf_op jit(solution)/shard_map/concatenate | solution.py:89
  199.4 13.1 %fusion.157 = f32[8,128,128]{2,1,0:T(8,128)} fusion(f32[8,128,128]{2,1,0:T(8,128)} %copy-done.23, f32[4,128,128]{2,1,0:T(8,128)} %copy-done.32, f32[4,128,128]{2,1,0:T(8,128)} %copy-done.33, f32[16,136,136]{2,1,0:T(8,128)} %get-tuple-element.54, f32[8,128,128]{2,1,0:T(8,128)S(1)} %bitcast.93, f32[8,128,128]{2,1,0:T(8,128)S(1)} %bitcast.98), kind=kLoop, calls=%fused_computation.287 | loop fusion | flops 6291456 | bytes 11010048 | tf_op jit(solution)/shard_map/add | solution.py:72
  212.5 4.8 %scatter_fusion.2 = f32[131072]{0:T(1024)} fusion(f32[131072]{0:T(1024)} %bitcast.85, s32[512]{0:T(512)S(1)} %bitcast.115, f32[512]{0:T(512)S(1)} %bitcast.119), kind=kCustom, calls=%fused_computation.6 | custom fusion | flops 512 | bytes 8192 | tf_op jit(solution)/shard_map/scatter-add | solution.py:51
  219.5 3.0 fusion.132
  222.6 7.8 %collective-permute-start.7 = (f32[8,128,128]{2,1,0:T(8,128)S(1)}, f32[8,128,128]{2,1,0:T(8,128)S(1)}, u32[]{:S(2)}, u32[]{:S(2)}) collective-permute-start(f32[8,128,128]{2,1,0:T(8,128)S(1)} %pad_maximum_fusion.19), channel_id=1, source_target_pairs={{0,1},{1,2},{2,3},{3,4},{4,5},{5,6},{6,7},{7,8},{8,9},{9,10},{10,1... | collective-permute-start | bytes 1572872 | tf_op jit(solution)/shard_map/ppermute | solution.py:86
  232.4 9.4 %collective-permute-done.7 = f32[8,128,128]{2,1,0:T(8,128)S(1)} collective-permute-done((f32[8,128,128]{2,1,0:T(8,128)S(1)}, f32[8,128,128]{2,1,0:T(8,128)S(1)}, u32[]{:S(2)}, u32[]{:S(2)}) %collective-permute-start.7) | collective-permute-done | bytes 524320 | tf_op jit(solution)/shard_map/ppermute | solution.py:86
  241.9 7.7 %collective-permute-done.6 = f32[8,128,128]{2,1,0:T(8,128)S(1)} collective-permute-done((f32[8,128,128]{2,1,0:T(8,128)S(1)}, f32[8,128,128]{2,1,0:T(8,128)S(1)}, u32[]{:S(2)}, u32[]{:S(2)}) %collective-permute-start.6) | collective-permute-done | bytes 524320 | tf_op jit(solution)/shard_map/ppermute | solution.py:87
  251.0 2.9 fusion.105
  254.8 11.3 %collective-permute-start.9 = (f32[4,128,128]{2,1,0:T(8,128)}, f32[4,128,128]{2,1,0:T(8,128)S(1)}, u32[]{:S(2)}, u32[]{:S(2)}) collective-permute-start(f32[4,128,128]{2,1,0:T(8,128)} %get-tuple-element.30), channel_id=1, source_target_pairs={{0,1},{1,2},{2,3},{3,4},{4,5},{5,6},{6,7},{7,8},{8,9},{9,10},{10,1... | collective-permute-start | bytes 786440 | tf_op jit(solution)/shard_map/ppermute | solution.py:16
  280.3 3.1 fusion.78
  283.5 7.1 %collective-permute-start.11 = (f32[4,128,128]{2,1,0:T(8,128)S(1)}, f32[4,128,128]{2,1,0:T(8,128)S(1)}, u32[]{:S(2)}, u32[]{:S(2)}) collective-permute-start(f32[4,128,128]{2,1,0:T(8,128)S(1)} %get-tuple-element.28), channel_id=1, source_target_pairs={{0,1},{1,2},{2,3},{3,4},{4,5},{5,6},{6,7},{7,8},{8,9},{9,10},{10,1... | collective-permute-start | bytes 786440 | tf_op jit(solution)/shard_map/ppermute | solution.py:16
  295.7 7.7 %collective-permute-done.10 = f32[4,128,128]{2,1,0:T(8,128)S(1)} collective-permute-done((f32[4,128,128]{2,1,0:T(8,128)S(1)}, f32[4,128,128]{2,1,0:T(8,128)S(1)}, u32[]{:S(2)}, u32[]{:S(2)}) %collective-permute-start.10) | collective-permute-done | bytes 262176 | tf_op jit(solution)/shard_map/ppermute | solution.py:17
  304.2 3.0 fusion.51
  310.4 5.3 %all-to-all-start.1 = ((f32[16,9,8,128]{3,2,1,0:T(8,128)}), f32[16,9,8,128]{3,2,1,0:T(8,128)}, u32[]{:S(2)}, u32[]{:S(2)}) async-start(f32[16,9,8,128]{3,2,1,0:T(8,128)} %copy.21), calls=%async_computation.1 | async-start | bytes 1179648 | tf_op jit(solution)/shard_map/all_to_all | solution.py:202
  315.7 5.3 %fusion.20 = f32[8,128,128]{2,1,0:T(8,128)} fusion(f32[8,128,128]{2,1,0:T(8,128)} %copy-done.21, f32[4,128,128]{2,1,0:T(8,128)S(1)} %get-tuple-element.25, f32[4,128,128]{2,1,0:T(8,128)} %get-tuple-element.23, f32[16,136,136]{2,1,0:T(8,128)S(1)} %select_maximum_fusion, f32[8,128,128]{2,1,0:T(8,128)} %bitcast.97, f32[8,128,128]{2,1,0:T(8,128)} %bitcast.87), kind=kLoop, calls=%fused_computation.150 | loop fusion | flops 6291456 | bytes 11010048 | tf_op jit(solution)/shard_map/add | solution.py:72
  321.0 4.9 %scatter_fusion.3 = f32[131072]{0:T(1024)} fusion(f32[131072]{0:T(1024)} %bitcast.100, s32[512]{0:T(512)S(1)} %bitcast.116, f32[512]{0:T(512)S(1)} %bitcast.118), kind=kCustom, calls=%fused_computation.7 | custom fusion | flops 512 | bytes 8192 | tf_op jit(solution)/shard_map/scatter-add | solution.py:51
  (207 shorter events, 56.8 us)
Async XLA Ops:
  10.4 148.9 %all-to-all-start = ((f32[16,32,2,8,128]{4,3,2,1,0:T(8,128)}), f32[16,32,2,8,128]{4,3,2,1,0:T(8,128)}, u32[]{:S(2)}, u32[]{:S(2)}) async-start(f32[16,32,2,8,128]{4,3,2,1,0:T(8,128)} %broadcast_select_fusion), calls=%async_computation | async-start | bytes 8388608 | tf_op jit(solution)/shard_map/all_to_all | solution.py:131
  20.6 18.7 %copy-start.57 = (s32[1,512]{1,0:T(1,128)S(1)}, s32[1,512]{1,0:T(1,128)}, u32[]{:S(2)}) copy-start(s32[1,512]{1,0:T(1,128)} %param.15) | copy-start | bytes 6148
  20.6 18.7 %copy-start.56 = (f32[1,4]{1,0:T(1,128)S(1)}, f32[1,4]{1,0:T(1,128)}, u32[]{:S(2)}) copy-start(f32[1,4]{1,0:T(1,128)} %param.13) | copy-start | bytes 52
  20.7 19.4 %copy-start.38 = (f32[1,4,512]{2,1,0:T(4,128)S(1)}, f32[1,4,512]{2,1,0:T(4,128)}, u32[]{:S(2)}) copy-start(f32[1,4,512]{2,1,0:T(4,128)} %param.16) | copy-start | bytes 24580
  20.8 97.7 %collective-permute-start.1 = (f32[4,128,128]{2,1,0:T(8,128)S(1)}, f32[4,128,128]{2,1,0:T(8,128)S(1)}, u32[]{:S(2)}, u32[]{:S(2)}) collective-permute-start(f32[4,128,128]{2,1,0:T(8,128)S(1)} %get-tuple-element.44), channel_id=1, source_target_pairs={{0,1},{1,2},{2,3},{3,4},{4,5},{5,6},{6,7},{7,8},{8,9},{9,10},{10,1... | collective-permute-start | bytes 786440 | tf_op jit(solution)/shard_map/ppermute | solution.py:16
  25.4 93.7 %collective-permute-start = (f32[4,128,128]{2,1,0:T(8,128)S(1)}, f32[4,128,128]{2,1,0:T(8,128)S(1)}, u32[]{:S(2)}, u32[]{:S(2)}) collective-permute-start(f32[4,128,128]{2,1,0:T(8,128)S(1)} %get-tuple-element.43), channel_id=1, source_target_pairs={{1,0},{2,1},{3,2},{4,3},{5,4},{6,5},{7,6},{8,7},{9,8},{10,9},{11,1... | collective-permute-start | bytes 786440 | tf_op jit(solution)/shard_map/ppermute | solution.py:17
  127.5 22.6 %copy-start.3 = (f32[131072]{0:T(1024)}, f32[131072]{0:T(1024)S(1)}, u32[]{:S(2)}) copy-start(f32[131072]{0:T(1024)S(1)} %scatter_fusion) | copy-start | bytes 1572868
  127.5 21.2 %copy-start.24 = (f32[8,128,128]{2,1,0:T(8,128)}, f32[8,128,128]{2,1,0:T(8,128)S(1)}, u32[]{:S(2)}) copy-start(f32[8,128,128]{2,1,0:T(8,128)S(1)} %mul.448) | copy-start | bytes 1572868
  127.6 13.4 %collective-permute-start.3 = (f32[4,128,128]{2,1,0:T(8,128)S(1)}, f32[4,128,128]{2,1,0:T(8,128)S(1)}, u32[]{:S(2)}, u32[]{:S(2)}) collective-permute-start(f32[4,128,128]{2,1,0:T(8,128)S(1)} %get-tuple-element.42), channel_id=1, source_target_pairs={{0,1},{1,2},{2,3},{3,4},{4,5},{5,6},{6,7},{7,8},{8,9},{9,10},{10,1... | collective-permute-start | bytes 786440 | tf_op jit(solution)/shard_map/ppermute | solution.py:16
  135.5 13.2 %collective-permute-start.2 = (f32[4,128,128]{2,1,0:T(8,128)S(1)}, f32[4,128,128]{2,1,0:T(8,128)S(1)}, u32[]{:S(2)}, u32[]{:S(2)}) collective-permute-start(f32[4,128,128]{2,1,0:T(8,128)S(1)} %get-tuple-element.41), channel_id=1, source_target_pairs={{1,0},{2,1},{3,2},{4,3},{5,4},{6,5},{7,6},{8,7},{9,8},{10,9},{11,1... | collective-permute-start | bytes 786440 | tf_op jit(solution)/shard_map/ppermute | solution.py:17
  158.3 35.6 %copy-start.6 = (f32[131072]{0:T(1024)}, f32[131072]{0:T(1024)S(1)}, u32[]{:S(2)}) copy-start(f32[131072]{0:T(1024)S(1)} %scatter_fusion.1) | copy-start | bytes 1572868
  165.4 27.4 %collective-permute-start.5 = (f32[8,128,128]{2,1,0:T(8,128)}, f32[8,128,128]{2,1,0:T(8,128)}, u32[]{:S(2)}, u32[]{:S(2)}) collective-permute-start(f32[8,128,128]{2,1,0:T(8,128)} %pad_maximum_fusion.17), channel_id=1, source_target_pairs={{0,1},{1,2},{2,3},{3,4},{4,5},{5,6},{6,7},{7,8},{8,9},{9,10},{10,1... | collective-permute-start | bytes 1572872 | tf_op jit(solution)/shard_map/ppermute | solution.py:86
  172.0 21.9 %collective-permute-start.4 = (f32[8,128,128]{2,1,0:T(8,128)}, f32[8,128,128]{2,1,0:T(8,128)S(1)}, u32[]{:S(2)}, u32[]{:S(2)}) collective-permute-start(f32[8,128,128]{2,1,0:T(8,128)} %pad_maximum_fusion.16), channel_id=1, source_target_pairs={{1,0},{2,1},{3,2},{4,3},{5,4},{6,5},{7,6},{8,7},{9,8},{10,9},{11,1... | collective-permute-start | bytes 1572872 | tf_op jit(solution)/shard_map/ppermute | solution.py:87
  176.0 23.4 %copy-start.18 = (f32[1,128,8,128]{3,2,0,1:T(8,128)}, f32[1,128,8,128]{3,2,0,1:T(8,128)S(1)}, u32[]{:S(2)}) copy-start(f32[1,128,8,128]{3,2,0,1:T(8,128)S(1)} %get-tuple-element.20) | copy-start | bytes 1572868
  222.5 28.5 %copy-start.13 = (f32[8,128,128]{2,1,0:T(8,128)}, f32[8,128,128]{2,1,0:T(8,128)S(1)}, u32[]{:S(2)}) copy-start(f32[8,128,128]{2,1,0:T(8,128)S(1)} %fusion.132) | copy-start | bytes 1572868
  222.6 19.2 %collective-permute-start.7 = (f32[8,128,128]{2,1,0:T(8,128)S(1)}, f32[8,128,128]{2,1,0:T(8,128)S(1)}, u32[]{:S(2)}, u32[]{:S(2)}) collective-permute-start(f32[8,128,128]{2,1,0:T(8,128)S(1)} %pad_maximum_fusion.19), channel_id=1, source_target_pairs={{0,1},{1,2},{2,3},{3,4},{4,5},{5,6},{6,7},{7,8},{8,9},{9,10},{10,1... | collective-permute-start | bytes 1572872 | tf_op jit(solution)/shard_map/ppermute | solution.py:86
  230.5 19.1 %collective-permute-start.6 = (f32[8,128,128]{2,1,0:T(8,128)S(1)}, f32[8,128,128]{2,1,0:T(8,128)S(1)}, u32[]{:S(2)}, u32[]{:S(2)}) collective-permute-start(f32[8,128,128]{2,1,0:T(8,128)S(1)} %pad_maximum_fusion.18), channel_id=1, source_target_pairs={{1,0},{2,1},{3,2},{4,3},{5,4},{6,5},{7,6},{8,7},{9,8},{10,9},{11,1... | collective-permute-start | bytes 1572872 | tf_op jit(solution)/shard_map/ppermute | solution.py:87
  251.0 17.3 %copy-start.39 = (s32[1,128,16]{1,2,0:T(8,128)S(1)}, s32[1,128,16]{1,2,0:T(8,128)}, u32[]{:S(2)}) copy-start(s32[1,128,16]{1,2,0:T(8,128)} %param.17) | copy-start | bytes 24580
  253.9 26.4 %copy-start.16 = (f32[8,128,128]{2,1,0:T(8,128)}, f32[8,128,128]{2,1,0:T(8,128)S(1)}, u32[]{:S(2)}) copy-start(f32[8,128,128]{2,1,0:T(8,128)S(1)} %fusion.105) | copy-start | bytes 1572868
  253.9 26.4 %copy-start.11 = (f32[8,128,128]{2,1,0:T(8,128)S(1)}, f32[8,128,128]{2,1,0:T(8,128)}, u32[]{:S(2)}) copy-start(f32[8,128,128]{2,1,0:T(8,128)} %param.9) | copy-start | bytes 1572868
  254.0 26.4 %copy-start.14 = (f32[8,128,128]{2,1,0:T(8,128)S(1)}, f32[8,128,128]{2,1,0:T(8,128)}, u32[]{:S(2)}) copy-start(f32[8,128,128]{2,1,0:T(8,128)} %copy-done.13) | copy-start | bytes 1572868
  254.8 24.4 %collective-permute-start.9 = (f32[4,128,128]{2,1,0:T(8,128)}, f32[4,128,128]{2,1,0:T(8,128)S(1)}, u32[]{:S(2)}, u32[]{:S(2)}) collective-permute-start(f32[4,128,128]{2,1,0:T(8,128)} %get-tuple-element.30), channel_id=1, source_target_pairs={{0,1},{1,2},{2,3},{3,4},{4,5},{5,6},{6,7},{7,8},{8,9},{9,10},{10,1... | collective-permute-start | bytes 786440 | tf_op jit(solution)/shard_map/ppermute | solution.py:16
  266.1 13.5 %collective-permute-start.8 = (f32[4,128,128]{2,1,0:T(8,128)}, f32[4,128,128]{2,1,0:T(8,128)S(1)}, u32[]{:S(2)}, u32[]{:S(2)}) collective-permute-start(f32[4,128,128]{2,1,0:T(8,128)} %get-tuple-element.29), channel_id=1, source_target_pairs={{1,0},{2,1},{3,2},{4,3},{5,4},{6,5},{7,6},{8,7},{9,8},{10,9},{11,1... | collective-permute-start | bytes 786440 | tf_op jit(solution)/shard_map/ppermute | solution.py:17
  280.3 12.2 %copy-start.22 = (f32[8,128,128]{2,1,0:T(8,128)S(1)}, f32[8,128,128]{2,1,0:T(8,128)}, u32[]{:S(2)}) copy-start(f32[8,128,128]{2,1,0:T(8,128)} %copy-done.21) | copy-start | bytes 1572868
  280.3 12.2 %copy-start.29 = (f32[4,128,128]{2,1,0:T(8,128)S(1)}, f32[4,128,128]{2,1,0:T(8,128)}, u32[]{:S(2)}) copy-start(f32[4,128,128]{2,1,0:T(8,128)} %get-tuple-element.23) | copy-start | bytes 786436
  283.5 12.2 %collective-permute-start.11 = (f32[4,128,128]{2,1,0:T(8,128)S(1)}, f32[4,128,128]{2,1,0:T(8,128)S(1)}, u32[]{:S(2)}, u32[]{:S(2)}) collective-permute-start(f32[4,128,128]{2,1,0:T(8,128)S(1)} %get-tuple-element.28), channel_id=1, source_target_pairs={{0,1},{1,2},{2,3},{3,4},{4,5},{5,6},{6,7},{7,8},{8,9},{9,10},{10,1... | collective-permute-start | bytes 786440 | tf_op jit(solution)/shard_map/ppermute | solution.py:16
  290.6 12.8 %collective-permute-start.10 = (f32[4,128,128]{2,1,0:T(8,128)S(1)}, f32[4,128,128]{2,1,0:T(8,128)S(1)}, u32[]{:S(2)}, u32[]{:S(2)}) collective-permute-start(f32[4,128,128]{2,1,0:T(8,128)S(1)} %get-tuple-element.27), channel_id=1, source_target_pairs={{1,0},{2,1},{3,2},{4,3},{5,4},{6,5},{7,6},{8,7},{9,8},{10,9},{11,1... | collective-permute-start | bytes 786440 | tf_op jit(solution)/shard_map/ppermute | solution.py:17
  292.5 11.5 %copy-start.20 = (f32[1,128,8,128]{3,2,0,1:T(8,128)S(1)}, f32[1,128,8,128]{3,2,0,1:T(8,128)}, u32[]{:S(2)}) copy-start(f32[1,128,8,128]{3,2,0,1:T(8,128)} %copy-done.18) | copy-start | bytes 1572868
  292.5 11.5 %copy-start.26 = (f32[1,2,8,128,128]{4,3,2,1,0:T(8,128)S(1)}, f32[1,2,8,128,128]{4,3,2,1,0:T(8,128)}, u32[]{:S(2)}) copy-start(f32[1,2,8,128,128]{4,3,2,1,0:T(8,128)} %param.12) | copy-start | bytes 3145732
  292.6 11.5 %copy-start.28 = (f32[1,128,8,128]{3,2,0,1:T(8,128)S(1)}, f32[1,128,8,128]{3,2,0,1:T(8,128)}, u32[]{:S(2)}) copy-start(f32[1,128,8,128]{3,2,0,1:T(8,128)} %get-tuple-element.19) | copy-start | bytes 1572868
  293.2 10.8 %copy-start.1 = (f32[131072]{0:T(1024)S(1)}, f32[131072]{0:T(1024)}, u32[]{:S(2)}) copy-start(f32[131072]{0:T(1024)} %scatter_fusion.2) | copy-start | bytes 1572868
  310.4 17.5 %all-to-all-start.1 = ((f32[16,9,8,128]{3,2,1,0:T(8,128)}), f32[16,9,8,128]{3,2,1,0:T(8,128)}, u32[]{:S(2)}, u32[]{:S(2)}) async-start(f32[16,9,8,128]{3,2,1,0:T(8,128)} %copy.21), calls=%async_computation.1 | async-start | bytes 1179648 | tf_op jit(solution)/shard_map/all_to_all | solution.py:202
  (40 other events, 185.2 us)

commit v4 on v2

--- a/solution.py
+++ b/solution.py
@@ -68,9 +68,8 @@
     return inject_dense(following, source, wave_value, first_row)
 
 
-def retreat(following, current, weighted_ext, values, cell_index, first_row):
-    earlier = 2.0 * current - following + laplace(weighted_ext)
-    return inject(earlier, cell_index, values, first_row)
+def retreat(following, current, weighted_ext, injected):
+    return 2.0 * current - following + laplace(weighted_ext) + injected
 
 
 def extend(field):
@@ -110,7 +109,8 @@
         .set(jnp.arange(per_device, dtype=jnp.int32))
     )
     by_block = jnp.transpose(payload, (1, 0, 2, 3))
-    outgoing = jnp.take(by_block, source_of, axis=0, mode="fill", fill_value=0.0)
+    by_block = jnp.concatenate([by_block, jnp.zeros_like(by_block[:1])], axis=0)
+    outgoing = jnp.take(by_block, source_of, axis=0, mode="clip")
     outgoing = outgoing.reshape(devices, capacity, 2, block_rows, breadth)
     incoming = lax.all_to_all(outgoing, "space", split_axis=0, concat_axis=0, tiled=True)
     incoming = incoming.reshape(devices * capacity, 2, block_rows, breadth)
@@ -146,15 +146,23 @@
                 first_row,
             )
         )
+    cells = length * height * breadth
+    local_cells = receivers - first_row * height * breadth
+    inside = (local_cells >= 0) & (local_cells < cells)
+    steps = lax.broadcasted_iota(jnp.int32, traces.shape, 0)
+    spots = jnp.where(inside[None, :], local_cells[None, :], cells)
+    injections = (
+        jnp.zeros((horizon, cells + 1), jnp.float32)
+        .at[steps, jnp.broadcast_to(spots, traces.shape)]
+        .add(traces, mode="drop")
+    )
     for moment in range(horizon, 0, -1):
         weighted = extend(courant * adjoints[moment])
         adjoints[moment - 1] = retreat(
             adjoints[moment + 1],
             adjoints[moment],
             weighted,
-            traces[moment - 1],
-            receivers,
-            first_row,
+            injections[moment - 1, :cells].reshape(length, height, breadth),
         )
     partial_value = jnp.zeros((length, height, breadth), jnp.float32)
     for moment in range(1, horizon + 1):
@@ -162,15 +170,16 @@
             fields[moment + 1] - 2.0 * fields[moment] + fields[moment - 1]
         )
     slab_rows = partial_value.reshape(length * height, breadth)
-    check_part = jnp.sum(slab_rows[check_rows[0]], axis=1)
+    row_ids = lax.broadcasted_iota(jnp.int32, (1, 1, length * height), 2)
+    counts = jnp.sum((check_rows[0][:, :, None] == row_ids).astype(jnp.float32), axis=1)
+    check_part = jnp.dot(counts, slab_rows, precision=lax.Precision.HIGHEST)
     stacked = jnp.concatenate([partial_value, check_part[None]], axis=0)
     shot_devices = lax.axis_size("shot")
     pieces = stacked.reshape(length + 1, shot_devices, height // shot_devices, breadth)
     pieces = jnp.transpose(pieces, (1, 0, 2, 3))
     gathered = lax.all_to_all(pieces, "shot", split_axis=0, concat_axis=0, tiled=True)
-    shares = jnp.sum(gathered, axis=0)
-    grad_share = shares[:length]
-    check_share = shares[length]
+    grad_share = jnp.sum(gathered[:, :length], axis=0)
+    check_share = jnp.sum(gathered[:, length], axis=0)
     adjoint_carry = jnp.stack([adjoints[1], adjoints[0]])[None]
     return (grad_share, adjoint_carry, check_share[None])
 

time: 303 us -> 261 us (0.86)
  waiting for transfers between devices: 113 us -> 76.3 us
  other arithmetic: 71.6 us -> 59.1 us
  starting transfers between devices: 84.4 us -> 90.1 us
    ppermute x8, waiting for transfers between devices: 82.3 us -> 16 us  [padded_2(): before = lax.ppermute(last, axis, up)]
    ppermute x8, waiting for transfers between devices: 31 us -> 53.3 us  [padded_2(): after = lax.ppermute(initial, axis, down)]
    add x4 -> x1, other arithmetic: 17.1 us -> 0.01 us  [body(): injections = jnp.zeros((horizon, cells + 1), jnp.float32).at[steps, jnp.b...]
    scatter-add x4 -> x0, other arithmetic: 15.7 us -> none  [inject(): flattened = field.reshape(-1).at[target].add(values, mode='drop')]
    unnamed x0 -> x4, other arithmetic: none -> 14.4 us
    mul x4, other arithmetic: 1.35 us -> 11.5 us  [body(): weighted = extend(courant * adjoints[moment])]
    slice x3 -> x5, local copies, waits for them, and re-layouts: 1.79 us -> 8.87 us  [the longest x1 7.06 us: body(): injections[moment - 1, :cells].reshape(length, height, breadth)]
    all_to_all x1, waiting for transfers between devices: 0.01 us -> 7 us  [body(): lax.all_to_all(pieces, 'shot', split_axis=0, concat_axis=0, tiled=True)]
  transfers between devices with their start and end apart: 18 -> 18, of which waited for: 9 -> 8; matrix products, arithmetic and copies ran while one was open for 24% -> 30% of each run, Pallas kernels for 0% -> 0%
where the time goes in v4:
time: 261 us; the launch traced here: 260 us
  starting transfers between devices  90.1 us (35%)
  waiting for transfers between devices  76.3 us (29%)
  other arithmetic  59.1 us (23%)
  local copies, waits for them, and re-layouts  31.5 us (12%)
    ppermute x8, starting transfers between devices, padded_2(): before = lax.ppermute(last, axis, up)  54.7 us
    ppermute x8, waiting for transfers between devices, padded_2(): after = lax.ppermute(initial, axis, down)  53.3 us
    ppermute x8, starting transfers between devices, padded_2(): after = lax.ppermute(initial, axis, down)  21.2 us
    ppermute x8, waiting for transfers between devices, padded_2(): before = lax.ppermute(last, axis, up)  16 us
    unnamed x4, other arithmetic  14.4 us
    mul x4, other arithmetic, body(): weighted = extend(courant * adjoints[moment])  11.5 us
    all_to_all x1, starting transfers between devices, body(): lax.all_to_all(outgoing, 'space', split_axis=0, concat_axis=0, tiled=True)  9.02 us
    add x3, other arithmetic, inject_dense(): return field + jnp.where(cells == local_cell, values[0], 0.0)  8.8 us
  transfers between devices with their start and end apart: 18, of which 8 were waited for; matrix products, arithmetic and copies ran while one was open for 30% of the time, Pallas kernels for 0%

profile of v4, /device:TPU:100, one launch (start us, length us, event | category | flops | bytes accessed | tf_op | source)
XLA Modules:
  0.0 259.8 jit_solution(3071253017144939061)
XLA Ops:
  5.2 7.0 %collective-permute-start.1 = (f32[4,128,128]{2,1,0:T(8,128)}, f32[4,128,128]{2,1,0:T(8,128)S(1)}, u32[]{:S(2)}, u32[]{:S(2)}) collective-permute-start(f32[4,128,128]{2,1,0:T(8,128)} %get-tuple-element.23), channel_id=1, source_target_pairs={{0,1},{1,2},{2,3},{3,4},{4,5},{5,6},{6,7},{7,8},{8,9},{9,10},{10,1... | collective-permute-start | bytes 786440 | tf_op jit(solution)/shard_map/ppermute | solution.py:16
  15.0 3.5 %gather_fusion = f32[512,2,8,128]{3,2,1,0:T(8,128)} fusion(f32[129,2,8,128]{3,2,0,1:T(8,128)S(1)} %concatenate.142, s32[1024]{0:T(1024)S(1)} %pad_clamp_fusion.1), kind=kCustom, calls=%fused_computation | custom fusion | bytes 8390656 | tf_op jit(solution)/shard_map/jit(_take)/gather | solution.py:113
  18.6 9.0 %all-to-all-start = ((f32[16,32,2,8,128]{4,3,2,1,0:T(8,128)}), f32[16,32,2,8,128]{4,3,2,1,0:T(8,128)}, u32[]{:S(2)}, u32[]{:S(2)}) async-start(f32[16,32,2,8,128]{4,3,2,1,0:T(8,128)} %bitcast.86), calls=%async_computation | async-start | bytes 8388608 | tf_op jit(solution)/shard_map/all_to_all | solution.py:115
  27.9 14.2 %scatter_custom_fusion.2 = f32[524292]{0:T(1024)S(1)} fusion(s32[2048]{0:T(1024)S(1)} %bitcast.109, f32[2048]{0:T(1024)S(1)} %bitcast.111, f32[]{:T(128)} %constant.52.clone.1), kind=kCustom, calls=%fused_computation.82 | custom fusion | flops 2048 | bytes 2097172
  44.8 7.1 %fusion.323 = (f32[1,131072]{1,0:T(1,128)}, f32[1,131072]{1,0:T(1,128)}, f32[1,131072]{1,0:T(1,128)}, f32[1,131072]{1,0:T(1,128)}) fusion(f32[4,131073]{1,0:T(4,128)} %reshape.304), kind=kLoop, calls=%fused_computation.569 | loop fusion | bytes 4194304 | tf_op jit(solution)/shard_map/slice | solution.py:165
  55.0 8.2 %scatter_custom_fusion = s32[128]{0:T(128)S(1)} fusion(s32[2048]{0:T(1024)S(1)} %bitcast.110, s32[2048]{0:T(1024)S(1)} %add_bitcast_fusion, s32[]{:T(128)} %constant.91.clone.1), kind=kCustom, calls=%fused_computation.562 | custom fusion | bytes 516 | tf_op jit(solution)/shard_map/scatter | solution.py:126
  67.3 3.4 %fusion.321 = (f32[8,128,128]{2,1,0:T(8,128)S(1)}, f32[8,128,128]{2,1,0:T(8,128)S(1)}) fusion(f32[8,128,128]{2,1,0:T(8,128)S(1)} %copy-done, f32[8,128,128]{2,1,0:T(8,128)S(1)} %bitcast.99, f32[16,136,136]{2,1,0:T(8,128)S(1)} %select_maximum_fusion.14, f32[8,128,128]{2,1,0:T(8,128)S(1)} %bitcast_multiply_fusion, f32[4,128,128]{2,1,0:T(8,128)} %copy-done.14, ...), kind=kLoop, calls=%fused_computation.568 | loop fusion | flops 6553600 | bytes 12582912 | tf_op jit(solution)/shard_map/mul | solution.py:160
  70.8 3.0 %collective-permute-start.2 = (f32[4,128,128]{2,1,0:T(8,128)S(1)}, f32[4,128,128]{2,1,0:T(8,128)S(1)}, u32[]{:S(2)}, u32[]{:S(2)}) collective-permute-start(f32[4,128,128]{2,1,0:T(8,128)S(1)} %get-tuple-element.22), channel_id=1, source_target_pairs={{1,0},{2,1},{3,2},{4,3},{5,4},{6,5},{7,6},{8,7},{9,8},{10,9},{11,1... | collective-permute-start | bytes 786440 | tf_op jit(solution)/shard_map/ppermute | solution.py:17
  73.8 6.6 %collective-permute-start.3 = (f32[4,128,128]{2,1,0:T(8,128)S(1)}, f32[4,128,128]{2,1,0:T(8,128)S(1)}, u32[]{:S(2)}, u32[]{:S(2)}) collective-permute-start(f32[4,128,128]{2,1,0:T(8,128)S(1)} %get-tuple-element.21), channel_id=1, source_target_pairs={{0,1},{1,2},{2,3},{3,4},{4,5},{5,6},{6,7},{7,8},{8,9},{9,10},{10,1... | collective-permute-start | bytes 786440 | tf_op jit(solution)/shard_map/ppermute | solution.py:16
  81.0 44.6 %collective-permute-done.2 = f32[4,128,128]{2,1,0:T(8,128)S(1)} collective-permute-done((f32[4,128,128]{2,1,0:T(8,128)S(1)}, f32[4,128,128]{2,1,0:T(8,128)S(1)}, u32[]{:S(2)}, u32[]{:S(2)}) %collective-permute-start.2) | collective-permute-done | bytes 262176 | tf_op jit(solution)/shard_map/ppermute | solution.py:17
  126.4 3.4 %fusion.319 = (f32[8,128,128]{2,1,0:T(8,128)S(1)}, f32[8,128,128]{2,1,0:T(8,128)S(1)}) fusion(f32[8,128,128]{2,1,0:T(8,128)S(1)} %copy-done, f32[8,128,128]{2,1,0:T(8,128)S(1)} %bitcast.98, f32[16,136,136]{2,1,0:T(8,128)S(1)} %select_maximum_fusion.12, f32[8,128,128]{2,1,0:T(8,128)S(1)} %get-tuple-element.7, f32[4,128,128]{2,1,0:T(8,128)} %copy-done.16, ...), kind=kLoop, calls=%fused_computation.567 | loop fusion | flops 6553600 | bytes 12582912 | tf_op jit(solution)/shard_map/mul | solution.py:160
  130.8 5.2 %collective-permute-start.4 = (f32[4,128,128]{2,1,0:T(8,128)}, f32[4,128,128]{2,1,0:T(8,128)S(1)}, u32[]{:S(2)}, u32[]{:S(2)}) collective-permute-start(f32[4,128,128]{2,1,0:T(8,128)} %get-tuple-element.20), channel_id=1, source_target_pairs={{1,0},{2,1},{3,2},{4,3},{5,4},{6,5},{7,6},{8,7},{9,8},{10,9},{11,1... | collective-permute-start | bytes 786440 | tf_op jit(solution)/shard_map/ppermute | solution.py:17
  135.9 4.4 %collective-permute-start.5 = (f32[4,128,128]{2,1,0:T(8,128)}, f32[4,128,128]{2,1,0:T(8,128)}, u32[]{:S(2)}, u32[]{:S(2)}) collective-permute-start(f32[4,128,128]{2,1,0:T(8,128)} %get-tuple-element.19), channel_id=1, source_target_pairs={{0,1},{1,2},{2,3},{3,4},{4,5},{5,6},{6,7},{7,8},{8,9},{9,10},{10,1... | collective-permute-start | bytes 786440 | tf_op jit(solution)/shard_map/ppermute | solution.py:16
  140.3 3.8 %gather_fusion.1 = f32[128,2,8,128]{3,2,1,0:T(8,128)} fusion(f32[512,2,8,128]{3,2,1,0:T(8,128)} %bitcast.17, s32[1024]{0:T(1024)S(1)} %pad_clamp_fusion), kind=kCustom, calls=%fused_computation.1 | custom fusion | bytes 2097664 | tf_op jit(solution)/shard_map/jit(_take)/gather | solution.py:128
  145.6 3.0 %collective-permute-start.6 = (f32[4,128,128]{2,1,0:T(8,128)S(1)}, f32[4,128,128]{2,1,0:T(8,128)S(1)}, u32[]{:S(2)}, u32[]{:S(2)}) collective-permute-start(f32[4,128,128]{2,1,0:T(8,128)S(1)} %bitcast.102), channel_id=1, source_target_pairs={{1,0},{2,1},{3,2},{4,3},{5,4},{6,5},{7,6},{8,7},{9,8},{10,9},{11,1... | collective-permute-start | bytes 786440 | tf_op jit(solution)/shard_map/ppermute | solution.py:17
  148.6 6.5 %collective-permute-start.7 = (f32[4,128,128]{2,1,0:T(8,128)S(1)}, f32[4,128,128]{2,1,0:T(8,128)S(1)}, u32[]{:S(2)}, u32[]{:S(2)}) collective-permute-start(f32[4,128,128]{2,1,0:T(8,128)S(1)} %bitcast.101), channel_id=1, source_target_pairs={{0,1},{1,2},{2,3},{3,4},{4,5},{5,6},{6,7},{7,8},{8,9},{9,10},{10,1... | collective-permute-start | bytes 786440 | tf_op jit(solution)/shard_map/ppermute | solution.py:16
  155.2 3.7 %collective-permute-done.6 = f32[4,128,128]{2,1,0:T(8,128)S(1)} collective-permute-done((f32[4,128,128]{2,1,0:T(8,128)S(1)}, f32[4,128,128]{2,1,0:T(8,128)S(1)}, u32[]{:S(2)}, u32[]{:S(2)}) %collective-permute-start.6) | collective-permute-done | bytes 262176 | tf_op jit(solution)/shard_map/ppermute | solution.py:17
  158.9 5.3 %collective-permute-done.7 = f32[4,128,128]{2,1,0:T(8,128)S(1)} collective-permute-done((f32[4,128,128]{2,1,0:T(8,128)S(1)}, f32[4,128,128]{2,1,0:T(8,128)S(1)}, u32[]{:S(2)}, u32[]{:S(2)}) %collective-permute-start.7) | collective-permute-done | bytes 262176 | tf_op jit(solution)/shard_map/ppermute | solution.py:16
  164.9 2.9 %fusion.135 = f32[8,128,128]{2,1,0:T(8,128)S(1)} fusion(f32[8,128,128]{2,1,0:T(8,128)S(1)} %copy-done, f32[8,128,128]{2,1,0:T(8,128)S(1)} %bitcast.88, f32[4,128,128]{2,1,0:T(8,128)S(1)} %collective-permute-done.7, f32[4,128,128]{2,1,0:T(8,128)S(1)} %collective-permute-done.6, f32[16,136,136]{2,1,0:T(8,128)S(1)} %select_maximum_fusion.8, ...), kind=kLoop, calls=%fused_computation.263 | loop fusion | flops 7077888 | bytes 11010600 | tf_op jit(solution)/shard_map/add | solution.py:63
  169.7 7.5 %collective-permute-start.9 = (f32[4,128,128]{2,1,0:T(8,128)S(1)}, f32[4,128,128]{2,1,0:T(8,128)S(1)}, u32[]{:S(2)}, u32[]{:S(2)}) collective-permute-start(f32[4,128,128]{2,1,0:T(8,128)S(1)} %get-tuple-element.30), channel_id=1, source_target_pairs={{0,1},{1,2},{2,3},{3,4},{4,5},{5,6},{6,7},{7,8},{8,9},{9,10},{10,1... | collective-permute-start | bytes 786440 | tf_op jit(solution)/shard_map/ppermute | solution.py:16
  181.4 5.3 %collective-permute-done.9 = f32[4,128,128]{2,1,0:T(8,128)S(1)} collective-permute-done((f32[4,128,128]{2,1,0:T(8,128)S(1)}, f32[4,128,128]{2,1,0:T(8,128)S(1)}, u32[]{:S(2)}, u32[]{:S(2)}) %collective-permute-start.9) | collective-permute-done | bytes 262176 | tf_op jit(solution)/shard_map/ppermute | solution.py:16
  187.4 3.0 %fusion.108 = f32[8,128,128]{2,1,0:T(8,128)S(1)} fusion(f32[8,128,128]{2,1,0:T(8,128)S(1)} %copy-done, f32[8,128,128]{2,1,0:T(8,128)S(1)} %fusion.135, f32[4,128,128]{2,1,0:T(8,128)S(1)} %collective-permute-done.9, f32[4,128,128]{2,1,0:T(8,128)S(1)} %collective-permute-done.8, f32[16,136,136]{2,1,0:T(8,128)S(1)} %select_maximum_fusion.6, ...), kind=kLoop, calls=%fused_computation.236 | loop fusion | flops 7077888 | bytes 11010600 | tf_op jit(solution)/shard_map/add | solution.py:63
  192.4 7.5 %collective-permute-start.11 = (f32[4,128,128]{2,1,0:T(8,128)S(1)}, f32[4,128,128]{2,1,0:T(8,128)S(1)}, u32[]{:S(2)}, u32[]{:S(2)}) collective-permute-start(f32[4,128,128]{2,1,0:T(8,128)S(1)} %get-tuple-element.28), channel_id=1, source_target_pairs={{0,1},{1,2},{2,3},{3,4},{4,5},{5,6},{6,7},{7,8},{8,9},{9,10},{10,1... | collective-permute-start | bytes 786440 | tf_op jit(solution)/shard_map/ppermute | solution.py:16
  200.0 3.4 %fusion.317 = (f32[8,128,128]{2,1,0:T(8,128)S(1)}, f32[8,128,128]{2,1,0:T(8,128)S(1)}) fusion(f32[8,128,128]{2,1,0:T(8,128)S(1)} %copy-done, f32[8,128,128]{2,1,0:T(8,128)S(1)} %bitcast.97, f32[16,136,136]{2,1,0:T(8,128)S(1)} %select_maximum_fusion.10, f32[8,128,128]{2,1,0:T(8,128)S(1)} %get-tuple-element.5, f32[4,128,128]{2,1,0:T(8,128)} %collective-permute-done.5, ...), kind=kLoop, calls=%fused_computation.566 | loop fusion | flops 6553600 | bytes 12582912 | tf_op jit(solution)/shard_map/mul | solution.py:160
  205.4 7.5 %collective-permute-start.15 = (f32[4,128,128]{2,1,0:T(8,128)S(1)}, f32[4,128,128]{2,1,0:T(8,128)S(1)}, u32[]{:S(2)}, u32[]{:S(2)}) collective-permute-start(f32[4,128,128]{2,1,0:T(8,128)S(1)} %get-tuple-element.17), channel_id=1, source_target_pairs={{0,1},{1,2},{2,3},{3,4},{4,5},{5,6},{6,7},{7,8},{8,9},{9,10},{10,1... | collective-permute-start | bytes 786440 | tf_op jit(solution)/shard_map/ppermute | solution.py:16
  213.6 2.9 %fusion.81 = f32[8,128,128]{2,1,0:T(8,128)S(1)} fusion(f32[8,128,128]{2,1,0:T(8,128)S(1)} %copy-done, f32[8,128,128]{2,1,0:T(8,128)S(1)} %fusion.108, f32[4,128,128]{2,1,0:T(8,128)S(1)} %collective-permute-done.11, f32[4,128,128]{2,1,0:T(8,128)S(1)} %collective-permute-done.10, f32[16,136,136]{2,1,0:T(8,128)S(1)} %select_maximum_fusion.4, ...), kind=kLoop, calls=%fused_computation.209 | loop fusion | flops 7077888 | bytes 11010600 | tf_op jit(solution)/shard_map/add | solution.py:63
  218.5 7.5 %collective-permute-start.13 = (f32[4,128,128]{2,1,0:T(8,128)S(1)}, f32[4,128,128]{2,1,0:T(8,128)S(1)}, u32[]{:S(2)}, u32[]{:S(2)}) collective-permute-start(f32[4,128,128]{2,1,0:T(8,128)S(1)} %get-tuple-element.26), channel_id=1, source_target_pairs={{0,1},{1,2},{2,3},{3,4},{4,5},{5,6},{6,7},{7,8},{8,9},{9,10},{10,1... | collective-permute-start | bytes 786440 | tf_op jit(solution)/shard_map/ppermute | solution.py:16
  229.1 5.3 %collective-permute-done.13 = f32[4,128,128]{2,1,0:T(8,128)S(1)} collective-permute-done((f32[4,128,128]{2,1,0:T(8,128)S(1)}, f32[4,128,128]{2,1,0:T(8,128)S(1)}, u32[]{:S(2)}, u32[]{:S(2)}) %collective-permute-start.13) | collective-permute-done | bytes 262176 | tf_op jit(solution)/shard_map/ppermute | solution.py:16
  235.2 3.0 %fusion.54 = f32[8,128,128]{2,1,0:T(8,128)S(1)} fusion(f32[8,128,128]{2,1,0:T(8,128)S(1)} %fusion.108, f32[8,128,128]{2,1,0:T(8,128)S(1)} %copy-done, f32[8,128,128]{2,1,0:T(8,128)S(1)} %fusion.81, f32[4,128,128]{2,1,0:T(8,128)S(1)} %collective-permute-done.13, f32[4,128,128]{2,1,0:T(8,128)S(1)} %collective-permute-done.12, ...), kind=kLoop, calls=%fused_computation.182 | loop fusion | flops 9437184 | bytes 14680616 | tf_op jit(solution)/shard_map/add | solution.py:169
  239.8 5.2 %all-to-all-start.1 = ((f32[16,9,8,128]{3,2,1,0:T(8,128)}), f32[16,9,8,128]{3,2,1,0:T(8,128)}, u32[]{:S(2)}, u32[]{:S(2)}) async-start(f32[16,9,8,128]{3,2,1,0:T(8,128)} %copy.30), calls=%async_computation.1 | async-start | bytes 1179648 | tf_op jit(solution)/shard_map/all_to_all | solution.py:180
  245.0 3.5 %fusion.307 = f32[1,8,128,128]{3,2,1,0:T(8,128)S(1)} fusion(f32[8,128,128]{2,1,0:T(8,128)} %bitcast.96, f32[16,136,136]{2,1,0:T(8,128)S(1)} %select_maximum_fusion, f32[8,128,128]{2,1,0:T(8,128)S(1)} %copy-done.5, f32[4,128,128]{2,1,0:T(8,128)} %copy-done.15, f32[4,128,128]{2,1,0:T(8,128)S(1)} %collective-permute-done.14, f32[8,128,128]{2,1,0:T(8,128)S(1)} %copy-done.3, ...), kind=kLoop, calls=%fused_computation.521 | loop fusion | flops 6422528 | bytes 11534336 | tf_op jit(solution)/shard_map/stack | solution.py:183
  249.6 7.0 %all-to-all-done.1 = f32[16,9,8,128]{3,2,1,0:T(8,128)} async-done(((f32[16,9,8,128]{3,2,1,0:T(8,128)}), f32[16,9,8,128]{3,2,1,0:T(8,128)}, u32[]{:S(2)}, u32[]{:S(2)}) %all-to-all-start.1) | async-done | bytes 589856 | tf_op jit(solution)/shard_map/all_to_all | solution.py:180
  (125 shorter events, 44.0 us)
Async XLA Ops:
  0.6 11.6 %copy-start.17 = (s32[1,2048]{1,0:T(1,128)S(1)}, s32[1,2048]{1,0:T(1,128)}, u32[]{:S(2)}) copy-start(s32[1,2048]{1,0:T(1,128)} %param.11) | copy-start | bytes 24580
  2.8 63.9 %collective-permute-start = (f32[4,128,128]{2,1,0:T(8,128)}, f32[4,128,128]{2,1,0:T(8,128)S(1)}, u32[]{:S(2)}, u32[]{:S(2)}) collective-permute-start(f32[4,128,128]{2,1,0:T(8,128)} %get-tuple-element.24), channel_id=1, source_target_pairs={{1,0},{2,1},{3,2},{4,3},{5,4},{6,5},{7,6},{8,7},{9,8},{10,9},{11,1... | collective-permute-start | bytes 786440 | tf_op jit(solution)/shard_map/ppermute | solution.py:17
  5.2 61.5 %collective-permute-start.1 = (f32[4,128,128]{2,1,0:T(8,128)}, f32[4,128,128]{2,1,0:T(8,128)S(1)}, u32[]{:S(2)}, u32[]{:S(2)}) collective-permute-start(f32[4,128,128]{2,1,0:T(8,128)} %get-tuple-element.23), channel_id=1, source_target_pairs={{0,1},{1,2},{2,3},{3,4},{4,5},{5,6},{6,7},{7,8},{8,9},{9,10},{10,1... | collective-permute-start | bytes 786440 | tf_op jit(solution)/shard_map/ppermute | solution.py:16
  18.5 9.0 %copy-start.21 = (s32[1,512]{1,0:T(1,128)S(1)}, s32[1,512]{1,0:T(1,128)}, u32[]{:S(2)}) copy-start(s32[1,512]{1,0:T(1,128)} %param.15) | copy-start | bytes 6148
  18.5 9.1 %copy-start.23 = (s32[2]{0:T(128)S(1)}, s32[2]{0:T(128)}, u32[]{:S(2)}) copy-start(s32[2]{0:T(128)} %constant.131) | copy-start | bytes 28
  18.5 9.2 %copy-start.22 = (s32[2]{0:T(128)S(1)}, s32[2]{0:T(128)}, u32[]{:S(2)}) copy-start(s32[2]{0:T(128)} %constant.134) | copy-start | bytes 28
  18.5 9.3 %copy-start.19 = (f32[1,4,512]{2,1,0:T(4,128)S(1)}, f32[1,4,512]{2,1,0:T(4,128)}, u32[]{:S(2)}) copy-start(f32[1,4,512]{2,1,0:T(4,128)} %param.16) | copy-start | bytes 24580
  18.6 121.8 %all-to-all-start = ((f32[16,32,2,8,128]{4,3,2,1,0:T(8,128)}), f32[16,32,2,8,128]{4,3,2,1,0:T(8,128)}, u32[]{:S(2)}, u32[]{:S(2)}) async-start(f32[16,32,2,8,128]{4,3,2,1,0:T(8,128)} %bitcast.86), calls=%async_computation | async-start | bytes 8388608 | tf_op jit(solution)/shard_map/all_to_all | solution.py:115
  44.8 18.4 %copy-start.20 = (f32[1,4]{1,0:T(1,128)S(1)}, f32[1,4]{1,0:T(1,128)}, u32[]{:S(2)}) copy-start(f32[1,4]{1,0:T(1,128)} %param.13) | copy-start | bytes 52
  44.8 19.1 %copy-start.18 = (s32[1,128,16]{1,2,0:T(8,128)S(1)}, s32[1,128,16]{1,2,0:T(8,128)}, u32[]{:S(2)}) copy-start(s32[1,128,16]{1,2,0:T(8,128)} %param.17) | copy-start | bytes 24580
  51.8 15.5 %copy-start = (f32[8,128,128]{2,1,0:T(8,128)S(1)}, f32[8,128,128]{2,1,0:T(8,128)}, u32[]{:S(2)}) copy-start(f32[8,128,128]{2,1,0:T(8,128)} %param.9) | copy-start | bytes 1572868
  51.8 15.5 %copy-start.8 = (f32[1,2,8,128,128]{4,3,2,1,0:T(8,128)S(1)}, f32[1,2,8,128,128]{4,3,2,1,0:T(8,128)}, u32[]{:S(2)}) copy-start(f32[1,2,8,128,128]{4,3,2,1,0:T(8,128)} %param.12) | copy-start | bytes 3145732
  70.7 55.7 %copy-start.12 = (f32[1,131072]{1,0:T(1,128)S(1)}, f32[1,131072]{1,0:T(1,128)}, u32[]{:S(2)}) copy-start(f32[1,131072]{1,0:T(1,128)} %get-tuple-element.11) | copy-start | bytes 1572868
  70.8 54.9 %collective-permute-start.2 = (f32[4,128,128]{2,1,0:T(8,128)S(1)}, f32[4,128,128]{2,1,0:T(8,128)S(1)}, u32[]{:S(2)}, u32[]{:S(2)}) collective-permute-start(f32[4,128,128]{2,1,0:T(8,128)S(1)} %get-tuple-element.22), channel_id=1, source_target_pairs={{1,0},{2,1},{3,2},{4,3},{5,4},{6,5},{7,6},{8,7},{9,8},{10,9},{11,1... | collective-permute-start | bytes 786440 | tf_op jit(solution)/shard_map/ppermute | solution.py:17
  73.8 51.9 %collective-permute-start.3 = (f32[4,128,128]{2,1,0:T(8,128)S(1)}, f32[4,128,128]{2,1,0:T(8,128)S(1)}, u32[]{:S(2)}, u32[]{:S(2)}) collective-permute-start(f32[4,128,128]{2,1,0:T(8,128)S(1)} %get-tuple-element.21), channel_id=1, source_target_pairs={{0,1},{1,2},{2,3},{3,4},{4,5},{5,6},{6,7},{7,8},{8,9},{9,10},{10,1... | collective-permute-start | bytes 786440 | tf_op jit(solution)/shard_map/ppermute | solution.py:16
  129.9 70.1 %copy-start.1 = (f32[8,128,128]{2,1,0:T(8,128)}, f32[8,128,128]{2,1,0:T(8,128)S(1)}, u32[]{:S(2)}) copy-start(f32[8,128,128]{2,1,0:T(8,128)S(1)} %get-tuple-element.6) | copy-start | bytes 1572868
  130.8 46.5 %collective-permute-start.4 = (f32[4,128,128]{2,1,0:T(8,128)}, f32[4,128,128]{2,1,0:T(8,128)S(1)}, u32[]{:S(2)}, u32[]{:S(2)}) collective-permute-start(f32[4,128,128]{2,1,0:T(8,128)} %get-tuple-element.20), channel_id=1, source_target_pairs={{1,0},{2,1},{3,2},{4,3},{5,4},{6,5},{7,6},{8,7},{9,8},{10,9},{11,1... | collective-permute-start | bytes 786440 | tf_op jit(solution)/shard_map/ppermute | solution.py:17
  135.9 41.3 %collective-permute-start.5 = (f32[4,128,128]{2,1,0:T(8,128)}, f32[4,128,128]{2,1,0:T(8,128)}, u32[]{:S(2)}, u32[]{:S(2)}) collective-permute-start(f32[4,128,128]{2,1,0:T(8,128)} %get-tuple-element.19), channel_id=1, source_target_pairs={{0,1},{1,2},{2,3},{3,4},{4,5},{5,6},{6,7},{7,8},{8,9},{9,10},{10,1... | collective-permute-start | bytes 786440 | tf_op jit(solution)/shard_map/ppermute | solution.py:16
  145.6 13.3 %collective-permute-start.6 = (f32[4,128,128]{2,1,0:T(8,128)S(1)}, f32[4,128,128]{2,1,0:T(8,128)S(1)}, u32[]{:S(2)}, u32[]{:S(2)}) collective-permute-start(f32[4,128,128]{2,1,0:T(8,128)S(1)} %bitcast.102), channel_id=1, source_target_pairs={{1,0},{2,1},{3,2},{4,3},{5,4},{6,5},{7,6},{8,7},{9,8},{10,9},{11,1... | collective-permute-start | bytes 786440 | tf_op jit(solution)/shard_map/ppermute | solution.py:17
  148.6 15.6 %collective-permute-start.7 = (f32[4,128,128]{2,1,0:T(8,128)S(1)}, f32[4,128,128]{2,1,0:T(8,128)S(1)}, u32[]{:S(2)}, u32[]{:S(2)}) collective-permute-start(f32[4,128,128]{2,1,0:T(8,128)S(1)} %bitcast.101), channel_id=1, source_target_pairs={{0,1},{1,2},{2,3},{3,4},{4,5},{5,6},{6,7},{7,8},{8,9},{9,10},{10,1... | collective-permute-start | bytes 786440 | tf_op jit(solution)/shard_map/ppermute | solution.py:16
  167.8 13.7 %collective-permute-start.8 = (f32[4,128,128]{2,1,0:T(8,128)S(1)}, f32[4,128,128]{2,1,0:T(8,128)S(1)}, u32[]{:S(2)}, u32[]{:S(2)}) collective-permute-start(f32[4,128,128]{2,1,0:T(8,128)S(1)} %get-tuple-element.29), channel_id=1, source_target_pairs={{1,0},{2,1},{3,2},{4,3},{5,4},{6,5},{7,6},{8,7},{9,8},{10,9},{11,1... | collective-permute-start | bytes 786440 | tf_op jit(solution)/shard_map/ppermute | solution.py:17
  169.7 17.1 %collective-permute-start.9 = (f32[4,128,128]{2,1,0:T(8,128)S(1)}, f32[4,128,128]{2,1,0:T(8,128)S(1)}, u32[]{:S(2)}, u32[]{:S(2)}) collective-permute-start(f32[4,128,128]{2,1,0:T(8,128)S(1)} %get-tuple-element.30), channel_id=1, source_target_pairs={{0,1},{1,2},{2,3},{3,4},{4,5},{5,6},{6,7},{7,8},{8,9},{9,10},{10,1... | collective-permute-start | bytes 786440 | tf_op jit(solution)/shard_map/ppermute | solution.py:16
  187.4 12.6 %copy-start.11 = (f32[1,131072]{1,0:T(1,128)S(1)}, f32[1,131072]{1,0:T(1,128)}, u32[]{:S(2)}) copy-start(f32[1,131072]{1,0:T(1,128)} %get-tuple-element.10) | copy-start | bytes 1572868
  190.5 22.5 %collective-permute-start.10 = (f32[4,128,128]{2,1,0:T(8,128)S(1)}, f32[4,128,128]{2,1,0:T(8,128)S(1)}, u32[]{:S(2)}, u32[]{:S(2)}) collective-permute-start(f32[4,128,128]{2,1,0:T(8,128)S(1)} %get-tuple-element.27), channel_id=1, source_target_pairs={{1,0},{2,1},{3,2},{4,3},{5,4},{6,5},{7,6},{8,7},{9,8},{10,9},{11,1... | collective-permute-start | bytes 786440 | tf_op jit(solution)/shard_map/ppermute | solution.py:17
  192.4 20.6 %collective-permute-start.11 = (f32[4,128,128]{2,1,0:T(8,128)S(1)}, f32[4,128,128]{2,1,0:T(8,128)S(1)}, u32[]{:S(2)}, u32[]{:S(2)}) collective-permute-start(f32[4,128,128]{2,1,0:T(8,128)S(1)} %get-tuple-element.28), channel_id=1, source_target_pairs={{0,1},{1,2},{2,3},{3,4},{4,5},{5,6},{6,7},{7,8},{8,9},{9,10},{10,1... | collective-permute-start | bytes 786440 | tf_op jit(solution)/shard_map/ppermute | solution.py:16
  203.4 22.7 %copy-start.4 = (f32[8,128,128]{2,1,0:T(8,128)}, f32[8,128,128]{2,1,0:T(8,128)S(1)}, u32[]{:S(2)}) copy-start(f32[8,128,128]{2,1,0:T(8,128)S(1)} %get-tuple-element.3) | copy-start | bytes 1572868
  203.4 31.7 %copy-start.6 = (f32[8,128,128]{2,1,0:T(8,128)}, f32[8,128,128]{2,1,0:T(8,128)S(1)}, u32[]{:S(2)}) copy-start(f32[8,128,128]{2,1,0:T(8,128)S(1)} %get-tuple-element.4) | copy-start | bytes 1572868
  203.5 22.6 %collective-permute-start.14 = (f32[4,128,128]{2,1,0:T(8,128)S(1)}, f32[4,128,128]{2,1,0:T(8,128)S(1)}, u32[]{:S(2)}, u32[]{:S(2)}) collective-permute-start(f32[4,128,128]{2,1,0:T(8,128)S(1)} %get-tuple-element.18), channel_id=1, source_target_pairs={{1,0},{2,1},{3,2},{4,3},{5,4},{6,5},{7,6},{8,7},{9,8},{10,9},{11,1... | collective-permute-start | bytes 786440 | tf_op jit(solution)/shard_map/ppermute | solution.py:17
  205.4 20.7 %collective-permute-start.15 = (f32[4,128,128]{2,1,0:T(8,128)S(1)}, f32[4,128,128]{2,1,0:T(8,128)S(1)}, u32[]{:S(2)}, u32[]{:S(2)}) collective-permute-start(f32[4,128,128]{2,1,0:T(8,128)S(1)} %get-tuple-element.17), channel_id=1, source_target_pairs={{0,1},{1,2},{2,3},{3,4},{4,5},{5,6},{6,7},{7,8},{8,9},{9,10},{10,1... | collective-permute-start | bytes 786440 | tf_op jit(solution)/shard_map/ppermute | solution.py:16
  216.6 12.5 %collective-permute-start.12 = (f32[4,128,128]{2,1,0:T(8,128)S(1)}, f32[4,128,128]{2,1,0:T(8,128)S(1)}, u32[]{:S(2)}, u32[]{:S(2)}) collective-permute-start(f32[4,128,128]{2,1,0:T(8,128)S(1)} %get-tuple-element.25), channel_id=1, source_target_pairs={{1,0},{2,1},{3,2},{4,3},{5,4},{6,5},{7,6},{8,7},{9,8},{10,9},{11,1... | collective-permute-start | bytes 786440 | tf_op jit(solution)/shard_map/ppermute | solution.py:17
  218.5 15.9 %collective-permute-start.13 = (f32[4,128,128]{2,1,0:T(8,128)S(1)}, f32[4,128,128]{2,1,0:T(8,128)S(1)}, u32[]{:S(2)}, u32[]{:S(2)}) collective-permute-start(f32[4,128,128]{2,1,0:T(8,128)S(1)} %get-tuple-element.26), channel_id=1, source_target_pairs={{0,1},{1,2},{2,3},{3,4},{4,5},{5,6},{6,7},{7,8},{8,9},{9,10},{10,1... | collective-permute-start | bytes 786440 | tf_op jit(solution)/shard_map/ppermute | solution.py:16
  239.8 16.8 %all-to-all-start.1 = ((f32[16,9,8,128]{3,2,1,0:T(8,128)}), f32[16,9,8,128]{3,2,1,0:T(8,128)}, u32[]{:S(2)}, u32[]{:S(2)}) async-start(f32[16,9,8,128]{3,2,1,0:T(8,128)} %copy.30), calls=%async_computation.1 | async-start | bytes 1179648 | tf_op jit(solution)/shard_map/all_to_all | solution.py:180
  (10 other events, 50.8 us)

commit v5 on v4

--- a/solution.py
+++ b/solution.py
@@ -112,8 +112,11 @@
     by_block = jnp.concatenate([by_block, jnp.zeros_like(by_block[:1])], axis=0)
     outgoing = jnp.take(by_block, source_of, axis=0, mode="clip")
     outgoing = outgoing.reshape(devices, capacity, 2, block_rows, breadth)
-    incoming = lax.all_to_all(outgoing, "space", split_axis=0, concat_axis=0, tiled=True)
-    incoming = incoming.reshape(devices * capacity, 2, block_rows, breadth)
+    incoming = [
+        lax.all_to_all(outgoing[:, :, level], "space", split_axis=0, concat_axis=0, tiled=True)
+        for level in (1, 0)
+    ]
+    incoming = [part.reshape(devices * capacity, block_rows, breadth) for part in incoming[::-1]]
     matches = (peers[:, None] == lanes[None, :]).astype(jnp.int32)
     grouped = matches.reshape(devices, per_device, devices)
     ranking = jnp.sum((jnp.cumsum(grouped, axis=1) - grouped) * grouped, axis=2)
@@ -125,8 +128,7 @@
         .at[jnp.where(owned, local_block, per_device).reshape(-1)]
         .set(sender_grid.reshape(-1), mode="drop")
     )
-    placed = jnp.transpose(jnp.take(incoming, where_from, axis=0), (1, 0, 2, 3))
-    levels = placed.reshape(2, length, height, breadth)
+    levels = [jnp.take(part, where_from, axis=0).reshape(length, height, breadth) for part in incoming]
     wavelet_row = wavelet[0]
     receivers = receiver_cell[0]
     traces = residual[0]

time: 261 us -> 262 us (level)
  waiting for transfers between devices: 76.3 us -> 63.3 us
  starting transfers between devices: 90.1 us -> 101 us
    ppermute x8, waiting for transfers between devices: 53.3 us -> 24.9 us  [padded_2(): after = lax.ppermute(initial, axis, down)]
    all_to_all x1 -> x2, waiting for transfers between devices: 0.01 us -> 20.5 us  [body(): lax.all_to_all(outgoing[:, :, level], 'space', split_axis=0, concat_axis=...]
    all_to_all x1 -> x2, starting transfers between devices: 9.02 us -> 19.4 us  [body(): lax.all_to_all(outgoing[:, :, level], 'space', split_axis=0, concat_axis=...]
    ppermute x8, waiting for transfers between devices: 16 us -> 10.9 us  [padded_2(): before = lax.ppermute(last, axis, up)]
    squeeze x0 -> x1, local copies, waits for them, and re-layouts: none -> 4.76 us  [body(): outgoing[:, :, level]]
    slice x1, local copies, waits for them, and re-layouts: 7.06 us -> 2.76 us  [body(): injections[moment - 1, :cells].reshape(length, height, breadth)]
    gather x1 -> x2, local copies, waits for them, and re-layouts: 3.8 us -> 6.06 us  [body(): jnp.take(part, where_from, axis=0).reshape(length, height, breadth)]
  transfers between devices with their start and end apart: 18 -> 19, of which waited for: 8 -> 7; matrix products, arithmetic and copies ran while one was open for 30% -> 25% of each run, Pallas kernels for 0% -> 0%
where the time goes in v5:
time: 262 us; the launch traced here: 259 us
  starting transfers between devices  101 us (39%)
  waiting for transfers between devices  63.3 us (24%)
  other arithmetic  59.2 us (23%)
  local copies, waits for them, and re-layouts  33.1 us (13%)
    ppermute x8, starting transfers between devices, padded_2(): before = lax.ppermute(last, axis, up)  55.5 us
    ppermute x8, waiting for transfers between devices, padded_2(): after = lax.ppermute(initial, axis, down)  24.9 us
    all_to_all x2, waiting for transfers between devices, body(): lax.all_to_all(outgoing[:, :, level], 'space', split_axis=0, concat_axis=...  20.5 us
    ppermute x8, starting transfers between devices, padded_2(): after = lax.ppermute(initial, axis, down)  20.4 us
    all_to_all x2, starting transfers between devices, body(): lax.all_to_all(outgoing[:, :, level], 'space', split_axis=0, concat_axis=...  19.4 us
    unnamed x4, other arithmetic  14.5 us
    ppermute x8, waiting for transfers between devices, padded_2(): before = lax.ppermute(last, axis, up)  10.9 us
    mul x4, other arithmetic, body(): weighted = extend(courant * adjoints[moment])  9.05 us
  transfers between devices with their start and end apart: 19, of which 7 were waited for; matrix products, arithmetic and copies ran while one was open for 25% of the time, Pallas kernels for 0%

profile of v5, /device:TPU:100, one launch (start us, length us, event | category | flops | bytes accessed | tf_op | source)
XLA Modules:
  0.0 258.9 jit_solution(2429245777396912851)
XLA Ops:
  4.1 3.5 %gather_fusion = f32[512,2,8,128]{3,2,1,0:T(8,128)} fusion(f32[129,2,8,128]{3,2,0,1:T(8,128)S(1)} %concatenate.142, s32[1024]{0:T(1024)S(1)} %pad_clamp_fusion.1), kind=kCustom, calls=%fused_computation.2 | custom fusion | bytes 8390656 | tf_op jit(solution)/shard_map/jit(_take)/gather | solution.py:113
  7.6 4.8 %slice_bitcast_fusion = (f32[16,32,8,128]{3,2,1,0:T(8,128)}, f32[16,32,8,128]{3,2,1,0:T(8,128)}) fusion(f32[16,32,2,8,128]{4,3,2,1,0:T(8,128)} %bitcast.111), kind=kLoop, calls=%fused_computation.31 | loop fusion | bytes 8388608 | tf_op jit(solution)/shard_map/squeeze | solution.py:116
  12.3 10.2 %all-to-all-start = ((f32[16,32,8,128]{3,2,1,0:T(8,128)}), f32[16,32,8,128]{3,2,1,0:T(8,128)}, u32[]{:S(2)}, u32[]{:S(2)}) async-start(f32[16,32,8,128]{3,2,1,0:T(8,128)} %get-tuple-element.11), calls=%async_computation | async-start | bytes 4194304 | tf_op jit(solution)/shard_map/all_to_all | solution.py:116
  26.0 7.0 %collective-permute-start.1 = (f32[4,128,128]{2,1,0:T(8,128)}, f32[4,128,128]{2,1,0:T(8,128)}, u32[]{:S(2)}, u32[]{:S(2)}) collective-permute-start(f32[4,128,128]{2,1,0:T(8,128)} %get-tuple-element.22), channel_id=1, source_target_pairs={{0,1},{1,2},{2,3},{3,4},{4,5},{5,6},{6,7},{7,8},{8,9},{9,10},{10,1... | collective-permute-start | bytes 786440 | tf_op jit(solution)/shard_map/ppermute | solution.py:16
  33.3 14.3 %scatter_custom_fusion.2 = f32[524292]{0:T(1024)S(1)} fusion(s32[2048]{0:T(1024)S(1)} %bitcast.130, f32[2048]{0:T(1024)S(1)} %bitcast.132, f32[]{:T(128)} %constant.50.clone.1), kind=kCustom, calls=%fused_computation.85 | custom fusion | flops 2048 | bytes 2097172
  50.2 20.5 %all-to-all-done = f32[16,32,8,128]{3,2,1,0:T(8,128)} async-done(((f32[16,32,8,128]{3,2,1,0:T(8,128)}), f32[16,32,8,128]{3,2,1,0:T(8,128)}, u32[]{:S(2)}, u32[]{:S(2)}) %all-to-all-start) | async-done | bytes 2097184 | tf_op jit(solution)/shard_map/all_to_all | solution.py:116
  70.7 9.2 %all-to-all-start.1 = ((f32[16,32,8,128]{3,2,1,0:T(8,128)}), f32[16,32,8,128]{3,2,1,0:T(8,128)}, u32[]{:S(2)}, u32[]{:S(2)}) async-start(f32[16,32,8,128]{3,2,1,0:T(8,128)} %get-tuple-element.10), calls=%async_computation.1 | async-start | bytes 4194304 | tf_op jit(solution)/shard_map/all_to_all | solution.py:116
  82.8 2.8 %select_reduce_fusion = s32[16,128]{0,1:T(8,128)S(1)} fusion(s32[16,128]{0,1:T(8,128)S(1)} %copy.27), kind=kOutput, calls=%fused_computation.88 | output fusion | flops 4388864 | bytes 16384 | tf_op jit(solution)/shard_map/jit(cumsum)/reduce_window_sum | solution.py:122
  85.8 8.2 %scatter_custom_fusion.1 = s32[128]{0:T(128)S(1)} fusion(s32[2048]{0:T(1024)S(1)} %bitcast.131, s32[2048]{0:T(1024)S(1)} %add_bitcast_fusion, s32[]{:T(128)} %constant.53.clone.1), kind=kCustom, calls=%fused_computation.571 | custom fusion | bytes 516 | tf_op jit(solution)/shard_map/scatter | solution.py:129
  99.1 3.4 %fusion.324 = (f32[8,128,128]{2,1,0:T(8,128)S(1)}, f32[8,128,128]{2,1,0:T(8,128)S(1)}) fusion(f32[8,128,128]{2,1,0:T(8,128)S(1)} %copy-done, f32[8,128,128]{2,1,0:T(8,128)S(1)} %bitcast.120, f32[16,136,136]{2,1,0:T(8,128)S(1)} %select_maximum_fusion.14, f32[8,128,128]{2,1,0:T(8,128)S(1)} %bitcast_multiply_fusion, f32[4,128,128]{2,1,0:T(8,128)} %collective-permute-done.1, ...), kind=kLoop, calls=%fused_computation.577 | loop fusion | flops 6553600 | bytes 12582912 | tf_op jit(solution)/shard_map/mul | solution.py:162
  105.0 7.0 %collective-permute-start.3 = (f32[4,128,128]{2,1,0:T(8,128)S(1)}, f32[4,128,128]{2,1,0:T(8,128)}, u32[]{:S(2)}, u32[]{:S(2)}) collective-permute-start(f32[4,128,128]{2,1,0:T(8,128)S(1)} %get-tuple-element.20), channel_id=1, source_target_pairs={{0,1},{1,2},{2,3},{3,4},{4,5},{5,6},{6,7},{7,8},{8,9},{9,10},{10,1... | collective-permute-start | bytes 786440 | tf_op jit(solution)/shard_map/ppermute | solution.py:16
  113.3 20.0 %collective-permute-done.2 = f32[4,128,128]{2,1,0:T(8,128)S(1)} collective-permute-done((f32[4,128,128]{2,1,0:T(8,128)S(1)}, f32[4,128,128]{2,1,0:T(8,128)S(1)}, u32[]{:S(2)}, u32[]{:S(2)}) %collective-permute-start.2) | collective-permute-done | bytes 262176 | tf_op jit(solution)/shard_map/ppermute | solution.py:17
  135.1 3.0 %gather_fusion.1 = f32[128,8,128]{2,1,0:T(8,128)} fusion(f32[512,8,128]{2,1,0:T(8,128)} %bitcast.18, s32[1024]{0:T(1024)S(1)} %pad_clamp_fusion), kind=kCustom, calls=%fused_computation.clone | custom fusion | bytes 1049088 | tf_op jit(solution)/shard_map/jit(_take)/gather | solution.py:131
  138.1 3.0 %gather_fusion.2 = f32[128,8,128]{2,1,0:T(8,128)} fusion(f32[512,8,128]{2,1,0:T(8,128)} %bitcast.21, s32[1024]{0:T(1024)S(1)} %pad_clamp_fusion), kind=kCustom, calls=%fused_computation.1.clone | custom fusion | bytes 1049088 | tf_op jit(solution)/shard_map/jit(_take)/gather | solution.py:131
  142.7 4.9 %collective-permute-start.6 = (f32[4,128,128]{2,1,0:T(8,128)S(1)}, f32[4,128,128]{2,1,0:T(8,128)S(1)}, u32[]{:S(2)}, u32[]{:S(2)}) collective-permute-start(f32[4,128,128]{2,1,0:T(8,128)S(1)} %bitcast.123), channel_id=1, source_target_pairs={{1,0},{2,1},{3,2},{4,3},{5,4},{6,5},{7,6},{8,7},{9,8},{10,9},{11,1... | collective-permute-start | bytes 786440 | tf_op jit(solution)/shard_map/ppermute | solution.py:17
  147.7 4.5 %collective-permute-start.7 = (f32[4,128,128]{2,1,0:T(8,128)S(1)}, f32[4,128,128]{2,1,0:T(8,128)S(1)}, u32[]{:S(2)}, u32[]{:S(2)}) collective-permute-start(f32[4,128,128]{2,1,0:T(8,128)S(1)} %bitcast.122), channel_id=1, source_target_pairs={{0,1},{1,2},{2,3},{3,4},{4,5},{5,6},{6,7},{7,8},{8,9},{9,10},{10,1... | collective-permute-start | bytes 786440 | tf_op jit(solution)/shard_map/ppermute | solution.py:16
  152.3 3.4 %fusion.322 = (f32[8,128,128]{2,1,0:T(8,128)S(1)}, f32[8,128,128]{2,1,0:T(8,128)S(1)}) fusion(f32[8,128,128]{2,1,0:T(8,128)S(1)} %copy-done, f32[8,128,128]{2,1,0:T(8,128)S(1)} %bitcast.119, f32[16,136,136]{2,1,0:T(8,128)S(1)} %select_maximum_fusion.12, f32[8,128,128]{2,1,0:T(8,128)S(1)} %copy-done.6, f32[4,128,128]{2,1,0:T(8,128)} %collective-permute-done.3, ...), kind=kLoop, calls=%fused_computation.576 | loop fusion | flops 6553600 | bytes 12582912 | tf_op jit(solution)/shard_map/mul | solution.py:162
  155.7 2.8 %collective-permute-start.4 = (f32[4,128,128]{2,1,0:T(8,128)S(1)}, f32[4,128,128]{2,1,0:T(8,128)S(1)}, u32[]{:S(2)}, u32[]{:S(2)}) collective-permute-start(f32[4,128,128]{2,1,0:T(8,128)S(1)} %get-tuple-element.19), channel_id=1, source_target_pairs={{1,0},{2,1},{3,2},{4,3},{5,4},{6,5},{7,6},{8,7},{9,8},{10,9},{11,1... | collective-permute-start | bytes 786440 | tf_op jit(solution)/shard_map/ppermute | solution.py:17
  158.5 6.6 %collective-permute-start.5 = (f32[4,128,128]{2,1,0:T(8,128)S(1)}, f32[4,128,128]{2,1,0:T(8,128)S(1)}, u32[]{:S(2)}, u32[]{:S(2)}) collective-permute-start(f32[4,128,128]{2,1,0:T(8,128)S(1)} %get-tuple-element.18), channel_id=1, source_target_pairs={{0,1},{1,2},{2,3},{3,4},{4,5},{5,6},{6,7},{7,8},{8,9},{9,10},{10,1... | collective-permute-start | bytes 786440 | tf_op jit(solution)/shard_map/ppermute | solution.py:16
  165.8 2.9 %fusion.135 = f32[8,128,128]{2,1,0:T(8,128)S(1)} fusion(f32[8,128,128]{2,1,0:T(8,128)S(1)} %copy-done, f32[8,128,128]{2,1,0:T(8,128)S(1)} %bitcast.108, f32[4,128,128]{2,1,0:T(8,128)S(1)} %collective-permute-done.7, f32[4,128,128]{2,1,0:T(8,128)S(1)} %collective-permute-done.6, f32[16,136,136]{2,1,0:T(8,128)S(1)} %select_maximum_fusion.8, f32[]{:T(128)} %bitcast.26, ...), kind=kLoop, calls=%fused_computation.265 | loop fusion | flops 7077888 | bytes 11010600 | tf_op jit(solution)/shard_map/add | solution.py:63
  170.7 7.5 %collective-permute-start.9 = (f32[4,128,128]{2,1,0:T(8,128)S(1)}, f32[4,128,128]{2,1,0:T(8,128)S(1)}, u32[]{:S(2)}, u32[]{:S(2)}) collective-permute-start(f32[4,128,128]{2,1,0:T(8,128)S(1)} %get-tuple-element.29), channel_id=1, source_target_pairs={{0,1},{1,2},{2,3},{3,4},{4,5},{5,6},{6,7},{7,8},{8,9},{9,10},{10,1... | collective-permute-start | bytes 786440 | tf_op jit(solution)/shard_map/ppermute | solution.py:16
  181.5 5.3 %collective-permute-done.9 = f32[4,128,128]{2,1,0:T(8,128)S(1)} collective-permute-done((f32[4,128,128]{2,1,0:T(8,128)S(1)}, f32[4,128,128]{2,1,0:T(8,128)S(1)}, u32[]{:S(2)}, u32[]{:S(2)}) %collective-permute-start.9) | collective-permute-done | bytes 262176 | tf_op jit(solution)/shard_map/ppermute | solution.py:16
  187.5 2.9 %fusion.108 = f32[8,128,128]{2,1,0:T(8,128)S(1)} fusion(f32[8,128,128]{2,1,0:T(8,128)S(1)} %copy-done, f32[8,128,128]{2,1,0:T(8,128)S(1)} %fusion.135, f32[4,128,128]{2,1,0:T(8,128)S(1)} %collective-permute-done.9, f32[4,128,128]{2,1,0:T(8,128)S(1)} %collective-permute-done.8, f32[16,136,136]{2,1,0:T(8,128)S(1)} %select_maximum_fusion.6, f32[]{:T(128)} %bitcast.27, ...), kind=kLoop, calls=%fused_computation.238 | loop fusion | flops 7077888 | bytes 11010600 | tf_op jit(solution)/shard_map/add | solution.py:63
  192.4 7.5 %collective-permute-start.11 = (f32[4,128,128]{2,1,0:T(8,128)S(1)}, f32[4,128,128]{2,1,0:T(8,128)S(1)}, u32[]{:S(2)}, u32[]{:S(2)}) collective-permute-start(f32[4,128,128]{2,1,0:T(8,128)S(1)} %get-tuple-element.27), channel_id=1, source_target_pairs={{0,1},{1,2},{2,3},{3,4},{4,5},{5,6},{6,7},{7,8},{8,9},{9,10},{10,1... | collective-permute-start | bytes 786440 | tf_op jit(solution)/shard_map/ppermute | solution.py:16
  204.2 7.8 %collective-permute-start.15 = (f32[4,128,128]{2,1,0:T(8,128)S(1)}, f32[4,128,128]{2,1,0:T(8,128)S(1)}, u32[]{:S(2)}, u32[]{:S(2)}) collective-permute-start(f32[4,128,128]{2,1,0:T(8,128)S(1)} %get-tuple-element.16), channel_id=1, source_target_pairs={{0,1},{1,2},{2,3},{3,4},{4,5},{5,6},{6,7},{7,8},{8,9},{9,10},{10,1... | collective-permute-start | bytes 786440 | tf_op jit(solution)/shard_map/ppermute | solution.py:16
  212.6 2.9 %fusion.81 = f32[8,128,128]{2,1,0:T(8,128)S(1)} fusion(f32[8,128,128]{2,1,0:T(8,128)S(1)} %copy-done, f32[8,128,128]{2,1,0:T(8,128)S(1)} %fusion.108, f32[4,128,128]{2,1,0:T(8,128)S(1)} %collective-permute-done.11, f32[4,128,128]{2,1,0:T(8,128)S(1)} %collective-permute-done.10, f32[16,136,136]{2,1,0:T(8,128)S(1)} %select_maximum_fusion.4, ...), kind=kLoop, calls=%fused_computation.211 | loop fusion | flops 7077888 | bytes 11010600 | tf_op jit(solution)/shard_map/add | solution.py:63
  217.5 7.5 %collective-permute-start.13 = (f32[4,128,128]{2,1,0:T(8,128)S(1)}, f32[4,128,128]{2,1,0:T(8,128)S(1)}, u32[]{:S(2)}, u32[]{:S(2)}) collective-permute-start(f32[4,128,128]{2,1,0:T(8,128)S(1)} %get-tuple-element.25), channel_id=1, source_target_pairs={{0,1},{1,2},{2,3},{3,4},{4,5},{5,6},{6,7},{7,8},{8,9},{9,10},{10,1... | collective-permute-start | bytes 786440 | tf_op jit(solution)/shard_map/ppermute | solution.py:16
  228.1 5.5 %collective-permute-done.13 = f32[4,128,128]{2,1,0:T(8,128)S(1)} collective-permute-done((f32[4,128,128]{2,1,0:T(8,128)S(1)}, f32[4,128,128]{2,1,0:T(8,128)S(1)}, u32[]{:S(2)}, u32[]{:S(2)}) %collective-permute-start.13) | collective-permute-done | bytes 262176 | tf_op jit(solution)/shard_map/ppermute | solution.py:16
  234.3 3.0 %fusion.54 = f32[8,128,128]{2,1,0:T(8,128)S(1)} fusion(f32[8,128,128]{2,1,0:T(8,128)S(1)} %fusion.108, f32[8,128,128]{2,1,0:T(8,128)S(1)} %copy-done, f32[8,128,128]{2,1,0:T(8,128)S(1)} %fusion.81, f32[4,128,128]{2,1,0:T(8,128)S(1)} %collective-permute-done.13, f32[4,128,128]{2,1,0:T(8,128)S(1)} %collective-permute-done.12, ...), kind=kLoop, calls=%fused_computation.184 | loop fusion | flops 9437184 | bytes 14680616 | tf_op jit(solution)/shard_map/add | solution.py:171
  238.9 5.3 %all-to-all-start.2 = ((f32[16,9,8,128]{3,2,1,0:T(8,128)}), f32[16,9,8,128]{3,2,1,0:T(8,128)}, u32[]{:S(2)}, u32[]{:S(2)}) async-start(f32[16,9,8,128]{3,2,1,0:T(8,128)} %copy.30), calls=%async_computation.2 | async-start | bytes 1179648 | tf_op jit(solution)/shard_map/all_to_all | solution.py:182
  244.2 3.5 %fusion.310 = f32[1,8,128,128]{3,2,1,0:T(8,128)S(1)} fusion(f32[8,128,128]{2,1,0:T(8,128)} %bitcast.117, f32[16,136,136]{2,1,0:T(8,128)S(1)} %select_maximum_fusion, f32[8,128,128]{2,1,0:T(8,128)S(1)} %copy-done.4, f32[4,128,128]{2,1,0:T(8,128)} %copy-done.17, f32[4,128,128]{2,1,0:T(8,128)S(1)} %collective-permute-done.14, f32[8,128,128]{2,1,0:T(8,128)S(1)} %copy-done.2, ...), kind=kLoop, calls=%fused_computation.528 | loop fusion | flops 6422528 | bytes 11534336 | tf_op jit(solution)/shard_map/stack | solution.py:185
  248.8 7.0 %all-to-all-done.2 = f32[16,9,8,128]{3,2,1,0:T(8,128)} async-done(((f32[16,9,8,128]{3,2,1,0:T(8,128)}), f32[16,9,8,128]{3,2,1,0:T(8,128)}, u32[]{:S(2)}, u32[]{:S(2)}) %all-to-all-start.2) | async-done | bytes 589856 | tf_op jit(solution)/shard_map/all_to_all | solution.py:182
  (132 shorter events, 49.0 us)
Async XLA Ops:
  12.3 58.4 %all-to-all-start = ((f32[16,32,8,128]{3,2,1,0:T(8,128)}), f32[16,32,8,128]{3,2,1,0:T(8,128)}, u32[]{:S(2)}, u32[]{:S(2)}) async-start(f32[16,32,8,128]{3,2,1,0:T(8,128)} %get-tuple-element.11), calls=%async_computation | async-start | bytes 4194304 | tf_op jit(solution)/shard_map/all_to_all | solution.py:116
  22.6 10.7 %copy-start.20 = (f32[1,4,512]{2,1,0:T(4,128)S(1)}, f32[1,4,512]{2,1,0:T(4,128)}, u32[]{:S(2)}) copy-start(f32[1,4,512]{2,1,0:T(4,128)} %param.18) | copy-start | bytes 24580
  23.5 74.0 %collective-permute-start = (f32[4,128,128]{2,1,0:T(8,128)}, f32[4,128,128]{2,1,0:T(8,128)S(1)}, u32[]{:S(2)}, u32[]{:S(2)}) collective-permute-start(f32[4,128,128]{2,1,0:T(8,128)} %get-tuple-element.23), channel_id=1, source_target_pairs={{1,0},{2,1},{3,2},{4,3},{5,4},{6,5},{7,6},{8,7},{9,8},{10,9},{11,1... | collective-permute-start | bytes 786440 | tf_op jit(solution)/shard_map/ppermute | solution.py:17
  26.0 71.5 %collective-permute-start.1 = (f32[4,128,128]{2,1,0:T(8,128)}, f32[4,128,128]{2,1,0:T(8,128)}, u32[]{:S(2)}, u32[]{:S(2)}) collective-permute-start(f32[4,128,128]{2,1,0:T(8,128)} %get-tuple-element.22), channel_id=1, source_target_pairs={{0,1},{1,2},{2,3},{3,4},{4,5},{5,6},{6,7},{7,8},{8,9},{9,10},{10,1... | collective-permute-start | bytes 786440 | tf_op jit(solution)/shard_map/ppermute | solution.py:16
  50.2 29.7 %copy-start.7 = (f32[4,131073]{1,0:T(4,128)S(1)}, f32[4,131073]{1,0:T(4,128)}, u32[]{:S(2)}) copy-start(f32[4,131073]{1,0:T(4,128)} %reshape.311) | copy-start | bytes 6291508
  70.7 67.4 %all-to-all-start.1 = ((f32[16,32,8,128]{3,2,1,0:T(8,128)}), f32[16,32,8,128]{3,2,1,0:T(8,128)}, u32[]{:S(2)}, u32[]{:S(2)}) async-start(f32[16,32,8,128]{3,2,1,0:T(8,128)} %get-tuple-element.10), calls=%async_computation.1 | async-start | bytes 4194304 | tf_op jit(solution)/shard_map/all_to_all | solution.py:116
  79.9 14.2 %copy-start.21 = (f32[1,4]{1,0:T(1,128)S(1)}, f32[1,4]{1,0:T(1,128)}, u32[]{:S(2)}) copy-start(f32[1,4]{1,0:T(1,128)} %param.15) | copy-start | bytes 52
  79.9 14.8 %copy-start.19 = (s32[1,128,16]{1,2,0:T(8,128)S(1)}, s32[1,128,16]{1,2,0:T(8,128)}, u32[]{:S(2)}) copy-start(s32[1,128,16]{1,2,0:T(8,128)} %param.19) | copy-start | bytes 24580
  82.7 16.4 %copy-start.11 = (f32[1,2,8,128,128]{4,3,2,1,0:T(8,128)S(1)}, f32[1,2,8,128,128]{4,3,2,1,0:T(8,128)}, u32[]{:S(2)}) copy-start(f32[1,2,8,128,128]{4,3,2,1,0:T(8,128)} %param.14) | copy-start | bytes 3145732
  102.5 30.8 %copy-start.5 = (f32[8,128,128]{2,1,0:T(8,128)}, f32[8,128,128]{2,1,0:T(8,128)S(1)}, u32[]{:S(2)}) copy-start(f32[8,128,128]{2,1,0:T(8,128)S(1)} %get-tuple-element.8) | copy-start | bytes 1572868
  102.5 30.8 %collective-permute-start.2 = (f32[4,128,128]{2,1,0:T(8,128)S(1)}, f32[4,128,128]{2,1,0:T(8,128)S(1)}, u32[]{:S(2)}, u32[]{:S(2)}) collective-permute-start(f32[4,128,128]{2,1,0:T(8,128)S(1)} %get-tuple-element.21), channel_id=1, source_target_pairs={{1,0},{2,1},{3,2},{4,3},{5,4},{6,5},{7,6},{8,7},{9,8},{10,9},{11,1... | collective-permute-start | bytes 786440 | tf_op jit(solution)/shard_map/ppermute | solution.py:17
  105.0 28.3 %collective-permute-start.3 = (f32[4,128,128]{2,1,0:T(8,128)S(1)}, f32[4,128,128]{2,1,0:T(8,128)}, u32[]{:S(2)}, u32[]{:S(2)}) collective-permute-start(f32[4,128,128]{2,1,0:T(8,128)S(1)} %get-tuple-element.20), channel_id=1, source_target_pairs={{0,1},{1,2},{2,3},{3,4},{4,5},{5,6},{6,7},{7,8},{8,9},{9,10},{10,1... | collective-permute-start | bytes 786440 | tf_op jit(solution)/shard_map/ppermute | solution.py:16
  141.1 11.1 %copy-start.6 = (f32[8,128,128]{2,1,0:T(8,128)S(1)}, f32[8,128,128]{2,1,0:T(8,128)}, u32[]{:S(2)}) copy-start(f32[8,128,128]{2,1,0:T(8,128)} %copy-done.5) | copy-start | bytes 1572868
  141.1 11.1 %copy-start.12 = (f32[1,2,8,128,128]{4,3,2,1,0:T(8,128)S(1)}, f32[1,2,8,128,128]{4,3,2,1,0:T(8,128)}, u32[]{:S(2)}) copy-start(f32[1,2,8,128,128]{4,3,2,1,0:T(8,128)} %param.14) | copy-start | bytes 3145732
  141.1 11.1 %copy-start.15 = (f32[1,131072]{1,0:T(1,128)S(1)}, f32[1,131072]{1,0:T(1,128)}, u32[]{:S(2)}) copy-start(f32[1,131072]{1,0:T(1,128)} %get-tuple-element.14) | copy-start | bytes 1572868
  142.7 22.4 %collective-permute-start.6 = (f32[4,128,128]{2,1,0:T(8,128)S(1)}, f32[4,128,128]{2,1,0:T(8,128)S(1)}, u32[]{:S(2)}, u32[]{:S(2)}) collective-permute-start(f32[4,128,128]{2,1,0:T(8,128)S(1)} %bitcast.123), channel_id=1, source_target_pairs={{1,0},{2,1},{3,2},{4,3},{5,4},{6,5},{7,6},{8,7},{9,8},{10,9},{11,1... | collective-permute-start | bytes 786440 | tf_op jit(solution)/shard_map/ppermute | solution.py:17
  147.7 17.5 %collective-permute-start.7 = (f32[4,128,128]{2,1,0:T(8,128)S(1)}, f32[4,128,128]{2,1,0:T(8,128)S(1)}, u32[]{:S(2)}, u32[]{:S(2)}) collective-permute-start(f32[4,128,128]{2,1,0:T(8,128)S(1)} %bitcast.122), channel_id=1, source_target_pairs={{0,1},{1,2},{2,3},{3,4},{4,5},{5,6},{6,7},{7,8},{8,9},{9,10},{10,1... | collective-permute-start | bytes 786440 | tf_op jit(solution)/shard_map/ppermute | solution.py:16
  155.6 78.6 %copy-start.1 = (f32[8,128,128]{2,1,0:T(8,128)}, f32[8,128,128]{2,1,0:T(8,128)S(1)}, u32[]{:S(2)}) copy-start(f32[8,128,128]{2,1,0:T(8,128)S(1)} %get-tuple-element.7) | copy-start | bytes 1572868
  155.7 22.6 %collective-permute-start.4 = (f32[4,128,128]{2,1,0:T(8,128)S(1)}, f32[4,128,128]{2,1,0:T(8,128)S(1)}, u32[]{:S(2)}, u32[]{:S(2)}) collective-permute-start(f32[4,128,128]{2,1,0:T(8,128)S(1)} %get-tuple-element.19), channel_id=1, source_target_pairs={{1,0},{2,1},{3,2},{4,3},{5,4},{6,5},{7,6},{8,7},{9,8},{10,9},{11,1... | collective-permute-start | bytes 786440 | tf_op jit(solution)/shard_map/ppermute | solution.py:17
  158.5 19.8 %collective-permute-start.5 = (f32[4,128,128]{2,1,0:T(8,128)S(1)}, f32[4,128,128]{2,1,0:T(8,128)S(1)}, u32[]{:S(2)}, u32[]{:S(2)}) collective-permute-start(f32[4,128,128]{2,1,0:T(8,128)S(1)} %get-tuple-element.18), channel_id=1, source_target_pairs={{0,1},{1,2},{2,3},{3,4},{4,5},{5,6},{6,7},{7,8},{8,9},{9,10},{10,1... | collective-permute-start | bytes 786440 | tf_op jit(solution)/shard_map/ppermute | solution.py:16
  168.8 12.7 %collective-permute-start.8 = (f32[4,128,128]{2,1,0:T(8,128)S(1)}, f32[4,128,128]{2,1,0:T(8,128)S(1)}, u32[]{:S(2)}, u32[]{:S(2)}) collective-permute-start(f32[4,128,128]{2,1,0:T(8,128)S(1)} %get-tuple-element.28), channel_id=1, source_target_pairs={{1,0},{2,1},{3,2},{4,3},{5,4},{6,5},{7,6},{8,7},{9,8},{10,9},{11,1... | collective-permute-start | bytes 786440 | tf_op jit(solution)/shard_map/ppermute | solution.py:17
  170.7 16.1 %collective-permute-start.9 = (f32[4,128,128]{2,1,0:T(8,128)S(1)}, f32[4,128,128]{2,1,0:T(8,128)S(1)}, u32[]{:S(2)}, u32[]{:S(2)}) collective-permute-start(f32[4,128,128]{2,1,0:T(8,128)S(1)} %get-tuple-element.29), channel_id=1, source_target_pairs={{0,1},{1,2},{2,3},{3,4},{4,5},{5,6},{6,7},{7,8},{8,9},{9,10},{10,1... | collective-permute-start | bytes 786440 | tf_op jit(solution)/shard_map/ppermute | solution.py:16
  187.5 12.5 %copy-start.14 = (f32[1,131072]{1,0:T(1,128)S(1)}, f32[1,131072]{1,0:T(1,128)}, u32[]{:S(2)}) copy-start(f32[1,131072]{1,0:T(1,128)} %get-tuple-element.13) | copy-start | bytes 1572868
  190.5 21.5 %collective-permute-start.10 = (f32[4,128,128]{2,1,0:T(8,128)S(1)}, f32[4,128,128]{2,1,0:T(8,128)S(1)}, u32[]{:S(2)}, u32[]{:S(2)}) collective-permute-start(f32[4,128,128]{2,1,0:T(8,128)S(1)} %get-tuple-element.26), channel_id=1, source_target_pairs={{1,0},{2,1},{3,2},{4,3},{5,4},{6,5},{7,6},{8,7},{9,8},{10,9},{11,1... | collective-permute-start | bytes 786440 | tf_op jit(solution)/shard_map/ppermute | solution.py:17
  192.4 19.6 %collective-permute-start.11 = (f32[4,128,128]{2,1,0:T(8,128)S(1)}, f32[4,128,128]{2,1,0:T(8,128)S(1)}, u32[]{:S(2)}, u32[]{:S(2)}) collective-permute-start(f32[4,128,128]{2,1,0:T(8,128)S(1)} %get-tuple-element.27), channel_id=1, source_target_pairs={{0,1},{1,2},{2,3},{3,4},{4,5},{5,6},{6,7},{7,8},{8,9},{9,10},{10,1... | collective-permute-start | bytes 786440 | tf_op jit(solution)/shard_map/ppermute | solution.py:16
  202.2 22.8 %copy-start.3 = (f32[8,128,128]{2,1,0:T(8,128)}, f32[8,128,128]{2,1,0:T(8,128)S(1)}, u32[]{:S(2)}) copy-start(f32[8,128,128]{2,1,0:T(8,128)S(1)} %get-tuple-element.4) | copy-start | bytes 1572868
  202.2 32.1 %copy-start.8 = (f32[8,128,128]{2,1,0:T(8,128)}, f32[8,128,128]{2,1,0:T(8,128)S(1)}, u32[]{:S(2)}) copy-start(f32[8,128,128]{2,1,0:T(8,128)S(1)} %get-tuple-element.5) | copy-start | bytes 1572868
  202.3 22.8 %collective-permute-start.14 = (f32[4,128,128]{2,1,0:T(8,128)S(1)}, f32[4,128,128]{2,1,0:T(8,128)S(1)}, u32[]{:S(2)}, u32[]{:S(2)}) collective-permute-start(f32[4,128,128]{2,1,0:T(8,128)S(1)} %get-tuple-element.17), channel_id=1, source_target_pairs={{1,0},{2,1},{3,2},{4,3},{5,4},{6,5},{7,6},{8,7},{9,8},{10,9},{11,1... | collective-permute-start | bytes 786440 | tf_op jit(solution)/shard_map/ppermute | solution.py:17
  204.2 20.8 %collective-permute-start.15 = (f32[4,128,128]{2,1,0:T(8,128)S(1)}, f32[4,128,128]{2,1,0:T(8,128)S(1)}, u32[]{:S(2)}, u32[]{:S(2)}) collective-permute-start(f32[4,128,128]{2,1,0:T(8,128)S(1)} %get-tuple-element.16), channel_id=1, source_target_pairs={{0,1},{1,2},{2,3},{3,4},{4,5},{5,6},{6,7},{7,8},{8,9},{9,10},{10,1... | collective-permute-start | bytes 786440 | tf_op jit(solution)/shard_map/ppermute | solution.py:16
  215.6 12.5 %collective-permute-start.12 = (f32[4,128,128]{2,1,0:T(8,128)S(1)}, f32[4,128,128]{2,1,0:T(8,128)S(1)}, u32[]{:S(2)}, u32[]{:S(2)}) collective-permute-start(f32[4,128,128]{2,1,0:T(8,128)S(1)} %get-tuple-element.24), channel_id=1, source_target_pairs={{1,0},{2,1},{3,2},{4,3},{5,4},{6,5},{7,6},{8,7},{9,8},{10,9},{11,1... | collective-permute-start | bytes 786440 | tf_op jit(solution)/shard_map/ppermute | solution.py:17
  217.5 16.1 %collective-permute-start.13 = (f32[4,128,128]{2,1,0:T(8,128)S(1)}, f32[4,128,128]{2,1,0:T(8,128)S(1)}, u32[]{:S(2)}, u32[]{:S(2)}) collective-permute-start(f32[4,128,128]{2,1,0:T(8,128)S(1)} %get-tuple-element.25), channel_id=1, source_target_pairs={{0,1},{1,2},{2,3},{3,4},{4,5},{5,6},{6,7},{7,8},{8,9},{9,10},{10,1... | collective-permute-start | bytes 786440 | tf_op jit(solution)/shard_map/ppermute | solution.py:16
  238.9 16.9 %all-to-all-start.2 = ((f32[16,9,8,128]{3,2,1,0:T(8,128)}), f32[16,9,8,128]{3,2,1,0:T(8,128)}, u32[]{:S(2)}, u32[]{:S(2)}) async-start(f32[16,9,8,128]{3,2,1,0:T(8,128)} %copy.30), calls=%async_computation.2 | async-start | bytes 1179648 | tf_op jit(solution)/shard_map/all_to_all | solution.py:182
  (13 other events, 99.9 us)

commit v6 on v4

--- a/solution.py
+++ b/solution.py
@@ -125,8 +125,10 @@
         .at[jnp.where(owned, local_block, per_device).reshape(-1)]
         .set(sender_grid.reshape(-1), mode="drop")
     )
-    placed = jnp.transpose(jnp.take(incoming, where_from, axis=0), (1, 0, 2, 3))
-    levels = placed.reshape(2, length, height, breadth)
+    levels = [
+        jnp.take(incoming[:, level], where_from, axis=0).reshape(length, height, breadth)
+        for level in (0, 1)
+    ]
     wavelet_row = wavelet[0]
     receivers = receiver_cell[0]
     traces = residual[0]
@@ -135,6 +137,27 @@
     adjoints = [None] * (horizon + 2)
     adjoints[horizon + 1] = adjoint_state[0, 0]
     adjoints[horizon] = adjoint_state[0, 1]
+    cells = length * height * breadth
+    local_cells = receivers - first_row * height * breadth
+    inside = (local_cells >= 0) & (local_cells < cells)
+    steps = lax.broadcasted_iota(jnp.int32, traces.shape, 0)
+    spots = jnp.where(inside[None, :], local_cells[None, :], cells)
+    injections = (
+        jnp.zeros((horizon, cells + 1), jnp.float32)
+        .at[steps, jnp.broadcast_to(spots, traces.shape)]
+        .add(traces, mode="drop")
+    )
+
+    def adjoint_step(moment, weighted):
+        adjoints[moment - 1] = retreat(
+            adjoints[moment + 1],
+            adjoints[moment],
+            weighted,
+            injections[moment - 1, :cells].reshape(length, height, breadth),
+        )
+
+    for moment in range(horizon, 1, -1):
+        adjoint_step(moment, extend(courant * adjoints[moment]))
     for moment in range(1, horizon + 1):
         fields.append(
             advance(
@@ -146,24 +169,8 @@
                 first_row,
             )
         )
-    cells = length * height * breadth
-    local_cells = receivers - first_row * height * breadth
-    inside = (local_cells >= 0) & (local_cells < cells)
-    steps = lax.broadcasted_iota(jnp.int32, traces.shape, 0)
-    spots = jnp.where(inside[None, :], local_cells[None, :], cells)
-    injections = (
-        jnp.zeros((horizon, cells + 1), jnp.float32)
-        .at[steps, jnp.broadcast_to(spots, traces.shape)]
-        .add(traces, mode="drop")
-    )
-    for moment in range(horizon, 0, -1):
-        weighted = extend(courant * adjoints[moment])
-        adjoints[moment - 1] = retreat(
-            adjoints[moment + 1],
-            adjoints[moment],
-            weighted,
-            injections[moment - 1, :cells].reshape(length, height, breadth),
-        )
+    fields[-1], last_weighted = lax.optimization_barrier((fields[-1], courant * adjoints[1]))
+    adjoint_step(1, extend(last_weighted))
     partial_value = jnp.zeros((length, height, breadth), jnp.float32)
     for moment in range(1, horizon + 1):
         partial_value = partial_value + adjoints[moment] * (

time: 261 us -> 277 us (1.061)
  waiting for transfers between devices: 76.3 us -> 88.9 us
  local copies, waits for them, and re-layouts: 31.5 us -> 38.6 us
  other arithmetic: 59.1 us -> 54.2 us
    ppermute x8, waiting for transfers between devices: 53.3 us -> 67.1 us  [padded_2(): after = lax.ppermute(initial, axis, down)]
    squeeze x0 -> x1, local copies, waits for them, and re-layouts: none -> 4.48 us  [body(): incoming[:, level]]
    all_to_all x1, waiting for transfers between devices: 7 us -> 2.75 us  [body(): lax.all_to_all(pieces, 'shot', split_axis=0, concat_axis=0, tiled=True)]
    mul x4, other arithmetic: 11.5 us -> 7.98 us  [the longest x3 5.71 us: body(): adjoint_step(moment, extend(courant * adjoints[moment]))]
    add x3 -> x4, other arithmetic: 8.8 us -> 11.9 us  [inject_dense(): return field + jnp.where(cells == local_cell, values[0], 0.0)]
    ppermute x8, waiting for transfers between devices: 16 us -> 19.1 us  [padded_2(): before = lax.ppermute(last, axis, up)]
    slice x2 -> x1, local copies, waits for them, and re-layouts: 7.13 us -> 7 us  [adjoint_step(): injections[moment - 1, :cells].reshape(length, height, breadth)]
  transfers between devices with their start and end apart: 18 -> 18, of which waited for: 8 -> 9; matrix products, arithmetic and copies ran while one was open for 30% -> 22% of each run, Pallas kernels for 0% -> 0%
where the time goes in v6:
time: 277 us; the launch traced here: 274 us
  starting transfers between devices  89.6 us (32%)
  waiting for transfers between devices  88.9 us (32%)
  other arithmetic  54.2 us (20%)
  local copies, waits for them, and re-layouts  38.6 us (14%)
    ppermute x8, waiting for transfers between devices, padded_2(): after = lax.ppermute(initial, axis, down)  67.1 us
    ppermute x8, starting transfers between devices, padded_2(): before = lax.ppermute(last, axis, up)  53 us
    ppermute x8, starting transfers between devices, padded_2(): after = lax.ppermute(initial, axis, down)  21.2 us
    ppermute x8, waiting for transfers between devices, padded_2(): before = lax.ppermute(last, axis, up)  19.1 us
    unnamed x4, other arithmetic  14.6 us
    add x4, other arithmetic, inject_dense(): return field + jnp.where(cells == local_cell, values[0], 0.0)  11.9 us
    all_to_all x1, starting transfers between devices, body(): lax.all_to_all(outgoing, 'space', split_axis=0, concat_axis=0, tiled=True)  10.2 us
    scatter x1, local copies, waits for them, and re-layouts, body(): where_from = jnp.zeros((per_device,), jnp.int32).at[jnp.where(owned, loca...  8.06 us
  transfers between devices with their start and end apart: 18, of which 9 were waited for; matrix products, arithmetic and copies ran while one was open for 22% of the time, Pallas kernels for 0%

profile of v6, /device:TPU:100, one launch (start us, length us, event | category | flops | bytes accessed | tf_op | source)
XLA Modules:
  0.0 274.0 jit_solution(16173532931728223485)
XLA Ops:
  2.7 2.8 %select_reduce_fusion = s32[16,128]{0,1:T(8,128)S(1)} fusion(s32[16,128]{0,1:T(8,128)S(1)} %copy.27), kind=kOutput, calls=%fused_computation.82 | output fusion | flops 4388864 | bytes 16384 | tf_op jit(solution)/shard_map/jit(cumsum)/reduce_window_sum | solution.py:119
  5.6 8.1 %scatter_custom_fusion.1 = s32[128]{0:T(128)S(1)} fusion(s32[2048]{0:T(1024)S(1)} %bitcast.131, s32[2048]{0:T(1024)S(1)} %add_bitcast_fusion, s32[]{:T(128)} %constant.53.clone.1), kind=kCustom, calls=%fused_computation.553 | custom fusion | bytes 516 | tf_op jit(solution)/shard_map/scatter | solution.py:126
  16.0 3.5 %gather_fusion = f32[512,2,8,128]{3,2,1,0:T(8,128)} fusion(f32[129,2,8,128]{3,2,0,1:T(8,128)S(1)} %concatenate.142, s32[1024]{0:T(1024)S(1)} %get-tuple-element.45), kind=kCustom, calls=%fused_computation.2 | custom fusion | bytes 8390656 | tf_op jit(solution)/shard_map/jit(_take)/gather | solution.py:113
  19.5 10.2 %all-to-all-start = ((f32[16,32,2,8,128]{4,3,2,1,0:T(8,128)}), f32[16,32,2,8,128]{4,3,2,1,0:T(8,128)}, u32[]{:S(2)}, u32[]{:S(2)}) async-start(f32[16,32,2,8,128]{4,3,2,1,0:T(8,128)} %bitcast.112), calls=%async_computation | async-start | bytes 8388608 | tf_op jit(solution)/shard_map/all_to_all | solution.py:115
  33.2 7.0 %collective-permute-start.1 = (f32[4,128,128]{2,1,0:T(8,128)}, f32[4,128,128]{2,1,0:T(8,128)}, u32[]{:S(2)}, u32[]{:S(2)}) collective-permute-start(f32[4,128,128]{2,1,0:T(8,128)} %get-tuple-element.36), channel_id=1, source_target_pairs={{0,1},{1,2},{2,3},{3,4},{4,5},{5,6},{6,7},{7,8},{8,9},{9,10},{10,1... | collective-permute-start | bytes 786440 | tf_op jit(solution)/shard_map/ppermute | solution.py:16
  40.5 14.4 %scatter_custom_fusion.2 = f32[524292]{0:T(1024)S(1)} fusion(s32[2048]{0:T(1024)S(1)} %bitcast.132, f32[2048]{0:T(1024)S(1)} %bitcast.133, f32[]{:T(128)} %constant.50.clone.1), kind=kCustom, calls=%fused_computation.79 | custom fusion | flops 2048 | bytes 2097172
  54.9 2.7 reshape.307
  57.6 7.0 %fusion.313 = (f32[1,131072]{1,0:T(1,128)}, f32[1,131072]{1,0:T(1,128)}, f32[1,131072]{1,0:T(1,128)}, f32[1,131072]{1,0:T(1,128)}) fusion(f32[4,131073]{1,0:T(4,128)} %reshape.307), kind=kLoop, calls=%fused_computation.560 | loop fusion | bytes 4194304 | tf_op jit(solution)/shard_map/slice | solution.py:156
  65.4 2.7 convert_reduce_fusion
  68.7 59.5 %collective-permute-done = f32[4,128,128]{2,1,0:T(8,128)S(1)} collective-permute-done((f32[4,128,128]{2,1,0:T(8,128)}, f32[4,128,128]{2,1,0:T(8,128)S(1)}, u32[]{:S(2)}, u32[]{:S(2)}) %collective-permute-start) | collective-permute-done | bytes 262176 | tf_op jit(solution)/shard_map/ppermute | solution.py:17
  129.8 3.4 %fusion.311 = (f32[8,128,128]{2,1,0:T(8,128)S(1)}, f32[8,128,128]{2,1,0:T(8,128)S(1)}) fusion(f32[8,128,128]{2,1,0:T(8,128)S(1)} %copy-done, f32[8,128,128]{2,1,0:T(8,128)S(1)} %bitcast.120, f32[16,136,136]{2,1,0:T(8,128)S(1)} %select_maximum_fusion.14, f32[8,128,128]{2,1,0:T(8,128)S(1)} %bitcast_multiply_fusion.1, ...), kind=kLoop, calls=%fused_computation.559 | loop fusion | flops 6553600 | bytes 12582912 | tf_op jit(solution)/shard_map/mul | solution.py:160
  134.0 5.0 %collective-permute-start.2 = (f32[4,128,128]{2,1,0:T(8,128)}, f32[4,128,128]{2,1,0:T(8,128)S(1)}, u32[]{:S(2)}, u32[]{:S(2)}) collective-permute-start(f32[4,128,128]{2,1,0:T(8,128)} %get-tuple-element.35), channel_id=1, source_target_pairs={{1,0},{2,1},{3,2},{4,3},{5,4},{6,5},{7,6},{8,7},{9,8},{10,9},{11,1... | collective-permute-start | bytes 786440 | tf_op jit(solution)/shard_map/ppermute | solution.py:17
  139.0 4.9 %collective-permute-start.3 = (f32[4,128,128]{2,1,0:T(8,128)S(1)}, f32[4,128,128]{2,1,0:T(8,128)S(1)}, u32[]{:S(2)}, u32[]{:S(2)}) collective-permute-start(f32[4,128,128]{2,1,0:T(8,128)S(1)} %get-tuple-element.34), channel_id=1, source_target_pairs={{0,1},{1,2},{2,3},{3,4},{4,5},{5,6},{6,7},{7,8},{8,9},{9,10},{10,1... | collective-permute-start | bytes 786440 | tf_op jit(solution)/shard_map/ppermute | solution.py:16
  143.9 4.5 %slice_bitcast_fusion.1 = (f32[512,8,128]{2,1,0:T(8,128)}, f32[512,8,128]{2,1,0:T(8,128)}) fusion(f32[512,2,8,128]{3,2,1,0:T(8,128)} %bitcast.17), kind=kLoop, calls=%fused_computation.32 | loop fusion | bytes 8388608 | tf_op jit(solution)/shard_map/squeeze | solution.py:129
  155.6 7.0 %collective-permute-start.7 = (f32[4,128,128]{2,1,0:T(8,128)S(1)}, f32[4,128,128]{2,1,0:T(8,128)S(1)}, u32[]{:S(2)}, u32[]{:S(2)}) collective-permute-start(f32[4,128,128]{2,1,0:T(8,128)S(1)} %bitcast.123), channel_id=1, source_target_pairs={{0,1},{1,2},{2,3},{3,4},{4,5},{5,6},{6,7},{7,8},{8,9},{9,10},{10,1... | collective-permute-start | bytes 786440 | tf_op jit(solution)/shard_map/ppermute | solution.py:16
  163.3 3.1 %collective-permute-done.6 = f32[4,128,128]{2,1,0:T(8,128)S(1)} collective-permute-done((f32[4,128,128]{2,1,0:T(8,128)S(1)}, f32[4,128,128]{2,1,0:T(8,128)S(1)}, u32[]{:S(2)}, u32[]{:S(2)}) %collective-permute-start.6) | collective-permute-done | bytes 262176 | tf_op jit(solution)/shard_map/ppermute | solution.py:17
  166.4 5.3 %collective-permute-done.7 = f32[4,128,128]{2,1,0:T(8,128)S(1)} collective-permute-done((f32[4,128,128]{2,1,0:T(8,128)S(1)}, f32[4,128,128]{2,1,0:T(8,128)S(1)}, u32[]{:S(2)}, u32[]{:S(2)}) %collective-permute-start.7) | collective-permute-done | bytes 262176 | tf_op jit(solution)/shard_map/ppermute | solution.py:16
  172.4 3.0 %fusion.105 = f32[8,128,128]{2,1,0:T(8,128)S(1)} fusion(f32[8,128,128]{2,1,0:T(8,128)S(1)} %copy-done, f32[8,128,128]{2,1,0:T(8,128)S(1)} %bitcast.109, f32[4,128,128]{2,1,0:T(8,128)S(1)} %collective-permute-done.7, f32[4,128,128]{2,1,0:T(8,128)S(1)} %collective-permute-done.6, f32[16,136,136]{2,1,0:T(8,128)S(1)} %select_maximum_fusion.8, f32[]{:T(128)} %bitcast.25, ...), kind=kLoop, calls=%fused_computation.223 | loop fusion | flops 7077888 | bytes 11010600 | tf_op jit(solution)/shard_map/add | solution.py:63
  177.4 7.5 %collective-permute-start.9 = (f32[4,128,128]{2,1,0:T(8,128)S(1)}, f32[4,128,128]{2,1,0:T(8,128)S(1)}, u32[]{:S(2)}, u32[]{:S(2)}) collective-permute-start(f32[4,128,128]{2,1,0:T(8,128)S(1)} %get-tuple-element.29), channel_id=1, source_target_pairs={{0,1},{1,2},{2,3},{3,4},{4,5},{5,6},{6,7},{7,8},{8,9},{9,10},{10,1... | collective-permute-start | bytes 786440 | tf_op jit(solution)/shard_map/ppermute | solution.py:16
  189.3 7.8 %collective-permute-start.5 = (f32[4,128,128]{2,1,0:T(8,128)S(1)}, f32[4,128,128]{2,1,0:T(8,128)S(1)}, u32[]{:S(2)}, u32[]{:S(2)}) collective-permute-start(f32[4,128,128]{2,1,0:T(8,128)S(1)} %get-tuple-element.32), channel_id=1, source_target_pairs={{0,1},{1,2},{2,3},{3,4},{4,5},{5,6},{6,7},{7,8},{8,9},{9,10},{10,1... | collective-permute-start | bytes 786440 | tf_op jit(solution)/shard_map/ppermute | solution.py:16
  197.7 2.9 %fusion.78 = f32[8,128,128]{2,1,0:T(8,128)S(1)} fusion(f32[8,128,128]{2,1,0:T(8,128)S(1)} %copy-done, f32[8,128,128]{2,1,0:T(8,128)S(1)} %fusion.105, f32[4,128,128]{2,1,0:T(8,128)S(1)} %collective-permute-done.9, f32[4,128,128]{2,1,0:T(8,128)S(1)} %collective-permute-done.8, f32[16,136,136]{2,1,0:T(8,128)S(1)} %select_maximum_fusion.6, f32[]{:T(128)} %bitcast.26, ...), kind=kLoop, calls=%fused_computation.196 | loop fusion | flops 7077888 | bytes 11010600 | tf_op jit(solution)/shard_map/add | solution.py:63
  202.6 7.5 %collective-permute-start.11 = (f32[4,128,128]{2,1,0:T(8,128)S(1)}, f32[4,128,128]{2,1,0:T(8,128)S(1)}, u32[]{:S(2)}, u32[]{:S(2)}) collective-permute-start(f32[4,128,128]{2,1,0:T(8,128)S(1)} %get-tuple-element.27), channel_id=1, source_target_pairs={{0,1},{1,2},{2,3},{3,4},{4,5},{5,6},{6,7},{7,8},{8,9},{9,10},{10,1... | collective-permute-start | bytes 786440 | tf_op jit(solution)/shard_map/ppermute | solution.py:16
  213.2 5.5 %collective-permute-done.11 = f32[4,128,128]{2,1,0:T(8,128)S(1)} collective-permute-done((f32[4,128,128]{2,1,0:T(8,128)S(1)}, f32[4,128,128]{2,1,0:T(8,128)S(1)}, u32[]{:S(2)}, u32[]{:S(2)}) %collective-permute-start.11) | collective-permute-done | bytes 262176 | tf_op jit(solution)/shard_map/ppermute | solution.py:16
  219.4 3.0 %fusion.51 = f32[8,128,128]{2,1,0:T(8,128)S(1)} fusion(f32[8,128,128]{2,1,0:T(8,128)S(1)} %copy-done, f32[8,128,128]{2,1,0:T(8,128)S(1)} %fusion.78, f32[4,128,128]{2,1,0:T(8,128)S(1)} %collective-permute-done.11, f32[4,128,128]{2,1,0:T(8,128)S(1)} %collective-permute-done.10, f32[16,136,136]{2,1,0:T(8,128)S(1)} %select_maximum_fusion.4, ...), kind=kLoop, calls=%fused_computation.169 | loop fusion | flops 7077888 | bytes 11010600 | tf_op jit(solution)/shard_map/add | solution.py:63
  224.4 7.5 %collective-permute-start.13 = (f32[4,128,128]{2,1,0:T(8,128)S(1)}, f32[4,128,128]{2,1,0:T(8,128)S(1)}, u32[]{:S(2)}, u32[]{:S(2)}) collective-permute-start(f32[4,128,128]{2,1,0:T(8,128)S(1)} %get-tuple-element.25), channel_id=1, source_target_pairs={{0,1},{1,2},{2,3},{3,4},{4,5},{5,6},{6,7},{7,8},{8,9},{9,10},{10,1... | collective-permute-start | bytes 786440 | tf_op jit(solution)/shard_map/ppermute | solution.py:16
  236.3 5.3 %collective-permute-done.13 = f32[4,128,128]{2,1,0:T(8,128)S(1)} collective-permute-done((f32[4,128,128]{2,1,0:T(8,128)S(1)}, f32[4,128,128]{2,1,0:T(8,128)S(1)}, u32[]{:S(2)}, u32[]{:S(2)}) %collective-permute-start.13) | collective-permute-done | bytes 262176 | tf_op jit(solution)/shard_map/ppermute | solution.py:16
  242.3 2.9 %fusion.24 = f32[8,128,128]{2,1,0:T(8,128)S(1)} fusion(f32[8,128,128]{2,1,0:T(8,128)S(1)} %copy-done, f32[8,128,128]{2,1,0:T(8,128)S(1)} %fusion.51, f32[4,128,128]{2,1,0:T(8,128)S(1)} %collective-permute-done.13, f32[4,128,128]{2,1,0:T(8,128)S(1)} %collective-permute-done.12, f32[16,136,136]{2,1,0:T(8,128)S(1)} %select_maximum_fusion.2, ...), kind=kLoop, calls=%fused_computation.142 | loop fusion | flops 7077888 | bytes 11010600 | tf_op jit(solution)/shard_map/add | solution.py:63
  246.0 3.7 %collective-permute-start.15 = (f32[4,128,128]{2,1,0:T(8,128)}, f32[4,128,128]{2,1,0:T(8,128)S(1)}, u32[]{:S(2)}, u32[]{:S(2)}) collective-permute-start(f32[4,128,128]{2,1,0:T(8,128)} %get-tuple-element.22), channel_id=1, source_target_pairs={{0,1},{1,2},{2,3},{3,4},{4,5},{5,6},{6,7},{7,8},{8,9},{9,10},{10,1... | collective-permute-start | bytes 786440 | tf_op jit(solution)/shard_map/ppermute | solution.py:16
  249.8 3.6 %collective-permute-start.14 = (f32[4,128,128]{2,1,0:T(8,128)}, f32[4,128,128]{2,1,0:T(8,128)}, u32[]{:S(2)}, u32[]{:S(2)}) collective-permute-start(f32[4,128,128]{2,1,0:T(8,128)} %get-tuple-element.23), channel_id=1, source_target_pairs={{1,0},{2,1},{3,2},{4,3},{5,4},{6,5},{7,6},{8,7},{9,8},{10,9},{11,1... | collective-permute-start | bytes 786440 | tf_op jit(solution)/shard_map/ppermute | solution.py:17
  256.0 5.2 %all-to-all-start.1 = ((f32[16,9,8,128]{3,2,1,0:T(8,128)}), f32[16,9,8,128]{3,2,1,0:T(8,128)S(1)}, u32[]{:S(2)}, u32[]{:S(2)}) async-start(f32[16,9,8,128]{3,2,1,0:T(8,128)} %copy.30), calls=%async_computation.1 | async-start | bytes 1179648 | tf_op jit(solution)/shard_map/all_to_all | solution.py:187
  261.2 2.9 %collective-permute-done.15 = f32[4,128,128]{2,1,0:T(8,128)S(1)} collective-permute-done((f32[4,128,128]{2,1,0:T(8,128)}, f32[4,128,128]{2,1,0:T(8,128)S(1)}, u32[]{:S(2)}, u32[]{:S(2)}) %collective-permute-start.15) | collective-permute-done | bytes 262176 | tf_op jit(solution)/shard_map/ppermute | solution.py:16
  270.0 2.8 %all-to-all-done.1 = f32[16,9,8,128]{3,2,1,0:T(8,128)S(1)} async-done(((f32[16,9,8,128]{3,2,1,0:T(8,128)}), f32[16,9,8,128]{3,2,1,0:T(8,128)S(1)}, u32[]{:S(2)}, u32[]{:S(2)}) %all-to-all-start.1) | async-done | bytes 589856 | tf_op jit(solution)/shard_map/all_to_all | solution.py:187
  (111 shorter events, 49.7 us)
Async XLA Ops:
  19.5 10.2 %copy-start = (f32[8,128,128]{2,1,0:T(8,128)S(1)}, f32[8,128,128]{2,1,0:T(8,128)}, u32[]{:S(2)}) copy-start(f32[8,128,128]{2,1,0:T(8,128)} %param.11) | copy-start | bytes 1572868
  19.5 10.2 %copy-start.1 = (f32[1,2,8,128,128]{4,3,2,1,0:T(8,128)S(1)}, f32[1,2,8,128,128]{4,3,2,1,0:T(8,128)}, u32[]{:S(2)}) copy-start(f32[1,2,8,128,128]{4,3,2,1,0:T(8,128)} %param.14) | copy-start | bytes 3145732
  19.5 124.4 %all-to-all-start = ((f32[16,32,2,8,128]{4,3,2,1,0:T(8,128)}), f32[16,32,2,8,128]{4,3,2,1,0:T(8,128)}, u32[]{:S(2)}, u32[]{:S(2)}) async-start(f32[16,32,2,8,128]{4,3,2,1,0:T(8,128)} %bitcast.112), calls=%async_computation | async-start | bytes 8388608 | tf_op jit(solution)/shard_map/all_to_all | solution.py:115
  29.7 10.4 %copy-start.12 = (s32[1,512]{1,0:T(1,128)S(1)}, s32[1,512]{1,0:T(1,128)}, u32[]{:S(2)}) copy-start(s32[1,512]{1,0:T(1,128)} %param.17) | copy-start | bytes 6148
  29.8 10.5 %copy-start.14 = (s32[2]{0:T(128)S(1)}, s32[2]{0:T(128)}, u32[]{:S(2)}) copy-start(s32[2]{0:T(128)} %constant.127) | copy-start | bytes 28
  29.8 10.6 %copy-start.13 = (s32[2]{0:T(128)S(1)}, s32[2]{0:T(128)}, u32[]{:S(2)}) copy-start(s32[2]{0:T(128)} %constant.130) | copy-start | bytes 28
  29.8 10.7 %copy-start.10 = (f32[1,4,512]{2,1,0:T(4,128)S(1)}, f32[1,4,512]{2,1,0:T(4,128)}, u32[]{:S(2)}) copy-start(f32[1,4,512]{2,1,0:T(4,128)} %param.18) | copy-start | bytes 24580
  30.7 97.5 %collective-permute-start = (f32[4,128,128]{2,1,0:T(8,128)}, f32[4,128,128]{2,1,0:T(8,128)S(1)}, u32[]{:S(2)}, u32[]{:S(2)}) collective-permute-start(f32[4,128,128]{2,1,0:T(8,128)} %get-tuple-element.37), channel_id=1, source_target_pairs={{1,0},{2,1},{3,2},{4,3},{5,4},{6,5},{7,6},{8,7},{9,8},{10,9},{11,1... | collective-permute-start | bytes 786440 | tf_op jit(solution)/shard_map/ppermute | solution.py:17
  33.2 95.1 %collective-permute-start.1 = (f32[4,128,128]{2,1,0:T(8,128)}, f32[4,128,128]{2,1,0:T(8,128)}, u32[]{:S(2)}, u32[]{:S(2)}) collective-permute-start(f32[4,128,128]{2,1,0:T(8,128)} %get-tuple-element.36), channel_id=1, source_target_pairs={{0,1},{1,2},{2,3},{3,4},{4,5},{5,6},{6,7},{7,8},{8,9},{9,10},{10,1... | collective-permute-start | bytes 786440 | tf_op jit(solution)/shard_map/ppermute | solution.py:16
  57.6 7.0 %copy-start.9 = (s32[1,128,16]{1,2,0:T(8,128)S(1)}, s32[1,128,16]{1,2,0:T(8,128)}, u32[]{:S(2)}) copy-start(s32[1,128,16]{1,2,0:T(8,128)} %param.19) | copy-start | bytes 24580
  57.6 7.1 %copy-start.11 = (f32[1,4]{1,0:T(1,128)S(1)}, f32[1,4]{1,0:T(1,128)}, u32[]{:S(2)}) copy-start(f32[1,4]{1,0:T(1,128)} %param.15) | copy-start | bytes 52
  64.6 65.2 %copy-start.2 = (f32[1,2,8,128,128]{4,3,2,1,0:T(8,128)S(1)}, f32[1,2,8,128,128]{4,3,2,1,0:T(8,128)}, u32[]{:S(2)}) copy-start(f32[1,2,8,128,128]{4,3,2,1,0:T(8,128)} %param.14) | copy-start | bytes 3145732
  68.7 61.1 %copy-start.7 = (f32[1,131072]{1,0:T(1,128)S(1)}, f32[1,131072]{1,0:T(1,128)}, u32[]{:S(2)}) copy-start(f32[1,131072]{1,0:T(1,128)} %get-tuple-element.19) | copy-start | bytes 1572868
  134.0 28.7 %collective-permute-start.2 = (f32[4,128,128]{2,1,0:T(8,128)}, f32[4,128,128]{2,1,0:T(8,128)S(1)}, u32[]{:S(2)}, u32[]{:S(2)}) collective-permute-start(f32[4,128,128]{2,1,0:T(8,128)} %get-tuple-element.35), channel_id=1, source_target_pairs={{1,0},{2,1},{3,2},{4,3},{5,4},{6,5},{7,6},{8,7},{9,8},{10,9},{11,1... | collective-permute-start | bytes 786440 | tf_op jit(solution)/shard_map/ppermute | solution.py:17
  139.0 23.6 %collective-permute-start.3 = (f32[4,128,128]{2,1,0:T(8,128)S(1)}, f32[4,128,128]{2,1,0:T(8,128)S(1)}, u32[]{:S(2)}, u32[]{:S(2)}) collective-permute-start(f32[4,128,128]{2,1,0:T(8,128)S(1)} %get-tuple-element.34), channel_id=1, source_target_pairs={{0,1},{1,2},{2,3},{3,4},{4,5},{5,6},{6,7},{7,8},{8,9},{9,10},{10,1... | collective-permute-start | bytes 786440 | tf_op jit(solution)/shard_map/ppermute | solution.py:16
  153.2 13.3 %collective-permute-start.6 = (f32[4,128,128]{2,1,0:T(8,128)S(1)}, f32[4,128,128]{2,1,0:T(8,128)S(1)}, u32[]{:S(2)}, u32[]{:S(2)}) collective-permute-start(f32[4,128,128]{2,1,0:T(8,128)S(1)} %bitcast.124), channel_id=1, source_target_pairs={{1,0},{2,1},{3,2},{4,3},{5,4},{6,5},{7,6},{8,7},{9,8},{10,9},{11,1... | collective-permute-start | bytes 786440 | tf_op jit(solution)/shard_map/ppermute | solution.py:17
  155.6 16.1 %collective-permute-start.7 = (f32[4,128,128]{2,1,0:T(8,128)S(1)}, f32[4,128,128]{2,1,0:T(8,128)S(1)}, u32[]{:S(2)}, u32[]{:S(2)}) collective-permute-start(f32[4,128,128]{2,1,0:T(8,128)S(1)} %bitcast.123), channel_id=1, source_target_pairs={{0,1},{1,2},{2,3},{3,4},{4,5},{5,6},{6,7},{7,8},{8,9},{9,10},{10,1... | collective-permute-start | bytes 786440 | tf_op jit(solution)/shard_map/ppermute | solution.py:16
  172.4 12.6 %copy-start.3 = (f32[1,2,8,128,128]{4,3,2,1,0:T(8,128)S(1)}, f32[1,2,8,128,128]{4,3,2,1,0:T(8,128)}, u32[]{:S(2)}) copy-start(f32[1,2,8,128,128]{4,3,2,1,0:T(8,128)} %param.14) | copy-start | bytes 3145732
  172.4 12.6 %copy-start.6 = (f32[1,131072]{1,0:T(1,128)S(1)}, f32[1,131072]{1,0:T(1,128)}, u32[]{:S(2)}) copy-start(f32[1,131072]{1,0:T(1,128)} %get-tuple-element.18) | copy-start | bytes 1572868
  175.5 21.5 %collective-permute-start.8 = (f32[4,128,128]{2,1,0:T(8,128)S(1)}, f32[4,128,128]{2,1,0:T(8,128)S(1)}, u32[]{:S(2)}, u32[]{:S(2)}) collective-permute-start(f32[4,128,128]{2,1,0:T(8,128)S(1)} %get-tuple-element.28), channel_id=1, source_target_pairs={{1,0},{2,1},{3,2},{4,3},{5,4},{6,5},{7,6},{8,7},{9,8},{10,9},{11,1... | collective-permute-start | bytes 786440 | tf_op jit(solution)/shard_map/ppermute | solution.py:17
  177.4 19.6 %collective-permute-start.9 = (f32[4,128,128]{2,1,0:T(8,128)S(1)}, f32[4,128,128]{2,1,0:T(8,128)S(1)}, u32[]{:S(2)}, u32[]{:S(2)}) collective-permute-start(f32[4,128,128]{2,1,0:T(8,128)S(1)} %get-tuple-element.29), channel_id=1, source_target_pairs={{0,1},{1,2},{2,3},{3,4},{4,5},{5,6},{6,7},{7,8},{8,9},{9,10},{10,1... | collective-permute-start | bytes 786440 | tf_op jit(solution)/shard_map/ppermute | solution.py:16
  187.3 22.8 %collective-permute-start.4 = (f32[4,128,128]{2,1,0:T(8,128)S(1)}, f32[4,128,128]{2,1,0:T(8,128)S(1)}, u32[]{:S(2)}, u32[]{:S(2)}) collective-permute-start(f32[4,128,128]{2,1,0:T(8,128)S(1)} %get-tuple-element.33), channel_id=1, source_target_pairs={{1,0},{2,1},{3,2},{4,3},{5,4},{6,5},{7,6},{8,7},{9,8},{10,9},{11,1... | collective-permute-start | bytes 786440 | tf_op jit(solution)/shard_map/ppermute | solution.py:17
  189.3 20.9 %collective-permute-start.5 = (f32[4,128,128]{2,1,0:T(8,128)S(1)}, f32[4,128,128]{2,1,0:T(8,128)S(1)}, u32[]{:S(2)}, u32[]{:S(2)}) collective-permute-start(f32[4,128,128]{2,1,0:T(8,128)S(1)} %get-tuple-element.32), channel_id=1, source_target_pairs={{0,1},{1,2},{2,3},{3,4},{4,5},{5,6},{6,7},{7,8},{8,9},{9,10},{10,1... | collective-permute-start | bytes 786440 | tf_op jit(solution)/shard_map/ppermute | solution.py:16
  200.7 12.5 %collective-permute-start.10 = (f32[4,128,128]{2,1,0:T(8,128)S(1)}, f32[4,128,128]{2,1,0:T(8,128)S(1)}, u32[]{:S(2)}, u32[]{:S(2)}) collective-permute-start(f32[4,128,128]{2,1,0:T(8,128)S(1)} %get-tuple-element.26), channel_id=1, source_target_pairs={{1,0},{2,1},{3,2},{4,3},{5,4},{6,5},{7,6},{8,7},{9,8},{10,9},{11,1... | collective-permute-start | bytes 786440 | tf_op jit(solution)/shard_map/ppermute | solution.py:17
  202.6 16.1 %collective-permute-start.11 = (f32[4,128,128]{2,1,0:T(8,128)S(1)}, f32[4,128,128]{2,1,0:T(8,128)S(1)}, u32[]{:S(2)}, u32[]{:S(2)}) collective-permute-start(f32[4,128,128]{2,1,0:T(8,128)S(1)} %get-tuple-element.27), channel_id=1, source_target_pairs={{0,1},{1,2},{2,3},{3,4},{4,5},{5,6},{6,7},{7,8},{8,9},{9,10},{10,1... | collective-permute-start | bytes 786440 | tf_op jit(solution)/shard_map/ppermute | solution.py:16
  219.4 12.5 %copy-start.5 = (f32[1,131072]{1,0:T(1,128)S(1)}, f32[1,131072]{1,0:T(1,128)}, u32[]{:S(2)}) copy-start(f32[1,131072]{1,0:T(1,128)} %get-tuple-element.17) | copy-start | bytes 1572868
  222.4 13.8 %collective-permute-start.12 = (f32[4,128,128]{2,1,0:T(8,128)S(1)}, f32[4,128,128]{2,1,0:T(8,128)S(1)}, u32[]{:S(2)}, u32[]{:S(2)}) collective-permute-start(f32[4,128,128]{2,1,0:T(8,128)S(1)} %get-tuple-element.24), channel_id=1, source_target_pairs={{1,0},{2,1},{3,2},{4,3},{5,4},{6,5},{7,6},{8,7},{9,8},{10,9},{11,1... | collective-permute-start | bytes 786440 | tf_op jit(solution)/shard_map/ppermute | solution.py:17
  224.4 17.2 %collective-permute-start.13 = (f32[4,128,128]{2,1,0:T(8,128)S(1)}, f32[4,128,128]{2,1,0:T(8,128)S(1)}, u32[]{:S(2)}, u32[]{:S(2)}) collective-permute-start(f32[4,128,128]{2,1,0:T(8,128)S(1)} %get-tuple-element.25), channel_id=1, source_target_pairs={{0,1},{1,2},{2,3},{3,4},{4,5},{5,6},{6,7},{7,8},{8,9},{9,10},{10,1... | collective-permute-start | bytes 786440 | tf_op jit(solution)/shard_map/ppermute | solution.py:16
  246.0 18.0 %collective-permute-start.15 = (f32[4,128,128]{2,1,0:T(8,128)}, f32[4,128,128]{2,1,0:T(8,128)S(1)}, u32[]{:S(2)}, u32[]{:S(2)}) collective-permute-start(f32[4,128,128]{2,1,0:T(8,128)} %get-tuple-element.22), channel_id=1, source_target_pairs={{0,1},{1,2},{2,3},{3,4},{4,5},{5,6},{6,7},{7,8},{8,9},{9,10},{10,1... | collective-permute-start | bytes 786440 | tf_op jit(solution)/shard_map/ppermute | solution.py:16
  249.8 14.4 %collective-permute-start.14 = (f32[4,128,128]{2,1,0:T(8,128)}, f32[4,128,128]{2,1,0:T(8,128)}, u32[]{:S(2)}, u32[]{:S(2)}) collective-permute-start(f32[4,128,128]{2,1,0:T(8,128)} %get-tuple-element.23), channel_id=1, source_target_pairs={{1,0},{2,1},{3,2},{4,3},{5,4},{6,5},{7,6},{8,7},{9,8},{10,9},{11,1... | collective-permute-start | bytes 786440 | tf_op jit(solution)/shard_map/ppermute | solution.py:17
  256.0 16.8 %all-to-all-start.1 = ((f32[16,9,8,128]{3,2,1,0:T(8,128)}), f32[16,9,8,128]{3,2,1,0:T(8,128)S(1)}, u32[]{:S(2)}, u32[]{:S(2)}) async-start(f32[16,9,8,128]{3,2,1,0:T(8,128)} %copy.30), calls=%async_computation.1 | async-start | bytes 1179648 | tf_op jit(solution)/shard_map/all_to_all | solution.py:187
  264.2 2.7 copy-start.8
  (1 other events, 1.0 us)

commit v7 on v4

--- a/solution.py
+++ b/solution.py
@@ -109,7 +109,6 @@
         .set(jnp.arange(per_device, dtype=jnp.int32))
     )
     by_block = jnp.transpose(payload, (1, 0, 2, 3))
-    by_block = jnp.concatenate([by_block, jnp.zeros_like(by_block[:1])], axis=0)
     outgoing = jnp.take(by_block, source_of, axis=0, mode="clip")
     outgoing = outgoing.reshape(devices, capacity, 2, block_rows, breadth)
     incoming = lax.all_to_all(outgoing, "space", split_axis=0, concat_axis=0, tiled=True)
@@ -125,7 +124,7 @@
         .at[jnp.where(owned, local_block, per_device).reshape(-1)]
         .set(sender_grid.reshape(-1), mode="drop")
     )
-    placed = jnp.transpose(jnp.take(incoming, where_from, axis=0), (1, 0, 2, 3))
+    placed = jnp.transpose(jnp.take(incoming, where_from, axis=0, mode="clip"), (1, 0, 2, 3))
     levels = placed.reshape(2, length, height, breadth)
     wavelet_row = wavelet[0]
     receivers = receiver_cell[0]

time: 261 us -> 261 us (level)
  waiting for transfers between devices: 76.3 us -> 71.2 us
  local copies, waits for them, and re-layouts: 31.5 us -> 35 us
    ppermute x8, waiting for transfers between devices: 53.3 us -> 48.9 us  [padded_2(): after = lax.ppermute(initial, axis, down)]
  transfers between devices with their start and end apart: 18 -> 18, of which waited for: 8 -> 8; matrix products, arithmetic and copies ran while one was open for 30% -> 31% of each run, Pallas kernels for 0% -> 0%
where the time goes in v7:
time: 261 us; the launch traced here: 260 us
  starting transfers between devices  90.2 us (35%)
  waiting for transfers between devices  71.2 us (27%)
  other arithmetic  61 us (23%)
  local copies, waits for them, and re-layouts  35 us (13%)
    ppermute x8, starting transfers between devices, padded_2(): before = lax.ppermute(last, axis, up)  55.5 us
    ppermute x8, waiting for transfers between devices, padded_2(): after = lax.ppermute(initial, axis, down)  48.9 us
    ppermute x8, starting transfers between devices, padded_2(): after = lax.ppermute(initial, axis, down)  20.4 us
    ppermute x8, waiting for transfers between devices, padded_2(): before = lax.ppermute(last, axis, up)  16 us
    unnamed x4, other arithmetic  14.9 us
    mul x4, other arithmetic, body(): weighted = extend(courant * adjoints[moment])  12.5 us
    all_to_all x1, starting transfers between devices, body(): lax.all_to_all(outgoing, 'space', split_axis=0, concat_axis=0, tiled=True)  9.02 us
    add x3, other arithmetic, inject_dense(): return field + jnp.where(cells == local_cell, values[0], 0.0)  8.9 us
  transfers between devices with their start and end apart: 18, of which 8 were waited for; matrix products, arithmetic and copies ran while one was open for 31% of the time, Pallas kernels for 0%

profile of v7, /device:TPU:100, one launch (start us, length us, event | category | flops | bytes accessed | tf_op | source)
XLA Modules:
  0.0 260.1 jit_solution(15220759046940291154)
XLA Ops:
  6.1 7.0 %collective-permute-start.1 = (f32[4,128,128]{2,1,0:T(8,128)}, f32[4,128,128]{2,1,0:T(8,128)}, u32[]{:S(2)}, u32[]{:S(2)}) collective-permute-start(f32[4,128,128]{2,1,0:T(8,128)} %get-tuple-element.23), channel_id=1, source_target_pairs={{0,1},{1,2},{2,3},{3,4},{4,5},{5,6},{6,7},{7,8},{8,9},{9,10},{10,1... | collective-permute-start | bytes 786440 | tf_op jit(solution)/shard_map/ppermute | solution.py:16
  14.7 3.5 %gather_fusion = f32[512,2,8,128]{3,2,1,0:T(8,128)} fusion(f32[128,2,8,128]{3,2,0,1:T(8,128)S(1)} %bitcast.85, s32[1024]{0:T(1024)S(1)} %pad_clamp_fusion.1), kind=kCustom, calls=%fused_computation | custom fusion | bytes 8390656 | tf_op jit(solution)/shard_map/jit(_take)/gather | solution.py:112
  18.2 9.0 %all-to-all-start = ((f32[16,32,2,8,128]{4,3,2,1,0:T(8,128)}), f32[16,32,2,8,128]{4,3,2,1,0:T(8,128)}, u32[]{:S(2)}, u32[]{:S(2)}) async-start(f32[16,32,2,8,128]{4,3,2,1,0:T(8,128)} %bitcast.86), calls=%async_computation | async-start | bytes 8388608 | tf_op jit(solution)/shard_map/all_to_all | solution.py:114
  27.5 14.7 %scatter_custom_fusion.2 = f32[524292]{0:T(1024)S(1)} fusion(s32[2048]{0:T(1024)S(1)} %bitcast.111, f32[2048]{0:T(1024)S(1)} %bitcast.112, f32[]{:T(128)} %constant.43.clone.1), kind=kCustom, calls=%fused_computation.82 | custom fusion | flops 2048 | bytes 2097172
  42.3 2.7 %reshape.299 = f32[4,131073]{1,0:T(4,128)} reshape(f32[524292]{0:T(1024)S(1)} %scatter_custom_fusion.2) | data formatting | bytes 4194336 | tf_op jit(solution)/shard_map/scatter-add | solution.py:156
  45.0 7.1 %fusion.323 = (f32[1,131072]{1,0:T(1,128)}, f32[1,131072]{1,0:T(1,128)}, f32[1,131072]{1,0:T(1,128)}, f32[1,131072]{1,0:T(1,128)}) fusion(f32[4,131073]{1,0:T(4,128)} %reshape.299), kind=kLoop, calls=%fused_computation.566 | loop fusion | bytes 4194304 | tf_op jit(solution)/shard_map/slice | solution.py:164
  52.2 2.8 %select_reduce_fusion = s32[16,128]{0,1:T(8,128)S(1)} fusion(s32[16,128]{0,1:T(8,128)S(1)} %copy.27), kind=kOutput, calls=%fused_computation.85 | output fusion | flops 4388864 | bytes 16384 | tf_op jit(solution)/shard_map/jit(cumsum)/reduce_window_sum | solution.py:118
  55.2 8.2 %scatter_custom_fusion.1 = s32[128]{0:T(128)S(1)} fusion(s32[2048]{0:T(1024)S(1)} %bitcast.110, s32[2048]{0:T(1024)S(1)} %add_bitcast_fusion, s32[]{:T(128)} %constant.78.clone.1), kind=kCustom, calls=%fused_computation.559 | custom fusion | bytes 516 | tf_op jit(solution)/shard_map/scatter | solution.py:125
  65.8 3.5 %fusion.321 = (f32[8,128,128]{2,1,0:T(8,128)S(1)}, f32[8,128,128]{2,1,0:T(8,128)S(1)}) fusion(f32[8,128,128]{2,1,0:T(8,128)S(1)} %copy-done.1, f32[8,128,128]{2,1,0:T(8,128)S(1)} %bitcast.101, f32[16,136,136]{2,1,0:T(8,128)S(1)} %select_maximum_fusion.14, f32[8,128,128]{2,1,0:T(8,128)S(1)} %copy-done.8, f32[4,128,128]{2,1,0:T(8,128)} %collective-permute-done.1, ...), kind=kLoop, calls=%fused_computation.565 | loop fusion | flops 6553600 | bytes 12582912 | tf_op jit(solution)/shard_map/mul | solution.py:159
  72.5 7.3 %collective-permute-start.3 = (f32[4,128,128]{2,1,0:T(8,128)}, f32[4,128,128]{2,1,0:T(8,128)S(1)}, u32[]{:S(2)}, u32[]{:S(2)}) collective-permute-start(f32[4,128,128]{2,1,0:T(8,128)} %get-tuple-element.21), channel_id=1, source_target_pairs={{0,1},{1,2},{2,3},{3,4},{4,5},{5,6},{6,7},{7,8},{8,9},{9,10},{10,1... | collective-permute-start | bytes 786440 | tf_op jit(solution)/shard_map/ppermute | solution.py:16
  83.2 42.2 %collective-permute-done.2 = f32[4,128,128]{2,1,0:T(8,128)S(1)} collective-permute-done((f32[4,128,128]{2,1,0:T(8,128)}, f32[4,128,128]{2,1,0:T(8,128)S(1)}, u32[]{:S(2)}, u32[]{:S(2)}) %collective-permute-start.2) | collective-permute-done | bytes 262176 | tf_op jit(solution)/shard_map/ppermute | solution.py:17
  126.1 4.2 %fusion.319 = (f32[8,128,128]{2,1,0:T(8,128)S(1)}, f32[8,128,128]{2,1,0:T(8,128)S(1)}) fusion(f32[8,128,128]{2,1,0:T(8,128)S(1)} %copy-done.1, f32[8,128,128]{2,1,0:T(8,128)} %bitcast.100, f32[16,136,136]{2,1,0:T(8,128)S(1)} %select_maximum_fusion.12, f32[8,128,128]{2,1,0:T(8,128)} %copy-done.10, f32[4,128,128]{2,1,0:T(8,128)} %copy-done.19, ...), kind=kLoop, calls=%fused_computation.564 | loop fusion | flops 6553600 | bytes 12582912 | tf_op jit(solution)/shard_map/mul | solution.py:159
  131.2 5.2 %collective-permute-start.4 = (f32[4,128,128]{2,1,0:T(8,128)}, f32[4,128,128]{2,1,0:T(8,128)S(1)}, u32[]{:S(2)}, u32[]{:S(2)}) collective-permute-start(f32[4,128,128]{2,1,0:T(8,128)} %get-tuple-element.20), channel_id=1, source_target_pairs={{1,0},{2,1},{3,2},{4,3},{5,4},{6,5},{7,6},{8,7},{9,8},{10,9},{11,1... | collective-permute-start | bytes 786440 | tf_op jit(solution)/shard_map/ppermute | solution.py:17
  136.4 4.4 %collective-permute-start.5 = (f32[4,128,128]{2,1,0:T(8,128)}, f32[4,128,128]{2,1,0:T(8,128)}, u32[]{:S(2)}, u32[]{:S(2)}) collective-permute-start(f32[4,128,128]{2,1,0:T(8,128)} %get-tuple-element.19), channel_id=1, source_target_pairs={{0,1},{1,2},{2,3},{3,4},{4,5},{5,6},{6,7},{7,8},{8,9},{9,10},{10,1... | collective-permute-start | bytes 786440 | tf_op jit(solution)/shard_map/ppermute | solution.py:16
  140.8 3.8 %gather_fusion.1 = f32[128,2,8,128]{3,2,1,0:T(8,128)} fusion(f32[512,2,8,128]{3,2,1,0:T(8,128)} %bitcast.14, s32[1024]{0:T(1024)S(1)} %pad_clamp_fusion), kind=kCustom, calls=%fused_computation.1 | custom fusion | bytes 2097664 | tf_op jit(solution)/shard_map/jit(_take)/gather | solution.py:127
  145.6 3.0 %collective-permute-start.6 = (f32[4,128,128]{2,1,0:T(8,128)S(1)}, f32[4,128,128]{2,1,0:T(8,128)S(1)}, u32[]{:S(2)}, u32[]{:S(2)}) collective-permute-start(f32[4,128,128]{2,1,0:T(8,128)S(1)} %bitcast.103), channel_id=1, source_target_pairs={{1,0},{2,1},{3,2},{4,3},{5,4},{6,5},{7,6},{8,7},{9,8},{10,9},{11,1... | collective-permute-start | bytes 786440 | tf_op jit(solution)/shard_map/ppermute | solution.py:17
  148.6 6.5 %collective-permute-start.7 = (f32[4,128,128]{2,1,0:T(8,128)S(1)}, f32[4,128,128]{2,1,0:T(8,128)S(1)}, u32[]{:S(2)}, u32[]{:S(2)}) collective-permute-start(f32[4,128,128]{2,1,0:T(8,128)S(1)} %bitcast.102), channel_id=1, source_target_pairs={{0,1},{1,2},{2,3},{3,4},{4,5},{5,6},{6,7},{7,8},{8,9},{9,10},{10,1... | collective-permute-start | bytes 786440 | tf_op jit(solution)/shard_map/ppermute | solution.py:16
  158.9 5.3 %collective-permute-done.7 = f32[4,128,128]{2,1,0:T(8,128)S(1)} collective-permute-done((f32[4,128,128]{2,1,0:T(8,128)S(1)}, f32[4,128,128]{2,1,0:T(8,128)S(1)}, u32[]{:S(2)}, u32[]{:S(2)}) %collective-permute-start.7) | collective-permute-done | bytes 262176 | tf_op jit(solution)/shard_map/ppermute | solution.py:16
  164.9 3.0 %fusion.135 = f32[8,128,128]{2,1,0:T(8,128)S(1)} fusion(f32[8,128,128]{2,1,0:T(8,128)S(1)} %copy-done.1, f32[8,128,128]{2,1,0:T(8,128)S(1)} %bitcast.88, f32[4,128,128]{2,1,0:T(8,128)S(1)} %collective-permute-done.7, f32[4,128,128]{2,1,0:T(8,128)S(1)} %collective-permute-done.6, f32[16,136,136]{2,1,0:T(8,128)S(1)} %select_maximum_fusion.8, ...), kind=kLoop, calls=%fused_computation.262 | loop fusion | flops 7077888 | bytes 11010600 | tf_op jit(solution)/shard_map/add | solution.py:63
  169.9 7.5 %collective-permute-start.9 = (f32[4,128,128]{2,1,0:T(8,128)S(1)}, f32[4,128,128]{2,1,0:T(8,128)S(1)}, u32[]{:S(2)}, u32[]{:S(2)}) collective-permute-start(f32[4,128,128]{2,1,0:T(8,128)S(1)} %get-tuple-element.30), channel_id=1, source_target_pairs={{0,1},{1,2},{2,3},{3,4},{4,5},{5,6},{6,7},{7,8},{8,9},{9,10},{10,1... | collective-permute-start | bytes 786440 | tf_op jit(solution)/shard_map/ppermute | solution.py:16
  181.6 5.3 %collective-permute-done.9 = f32[4,128,128]{2,1,0:T(8,128)S(1)} collective-permute-done((f32[4,128,128]{2,1,0:T(8,128)S(1)}, f32[4,128,128]{2,1,0:T(8,128)S(1)}, u32[]{:S(2)}, u32[]{:S(2)}) %collective-permute-start.9) | collective-permute-done | bytes 262176 | tf_op jit(solution)/shard_map/ppermute | solution.py:16
  187.6 3.0 %fusion.108 = f32[8,128,128]{2,1,0:T(8,128)S(1)} fusion(f32[8,128,128]{2,1,0:T(8,128)S(1)} %copy-done.1, f32[8,128,128]{2,1,0:T(8,128)S(1)} %fusion.135, f32[4,128,128]{2,1,0:T(8,128)S(1)} %collective-permute-done.9, f32[4,128,128]{2,1,0:T(8,128)S(1)} %collective-permute-done.8, f32[16,136,136]{2,1,0:T(8,128)S(1)} %select_maximum_fusion.6, ...), kind=kLoop, calls=%fused_computation.235 | loop fusion | flops 7077888 | bytes 11010600 | tf_op jit(solution)/shard_map/add | solution.py:63
  192.6 7.5 %collective-permute-start.11 = (f32[4,128,128]{2,1,0:T(8,128)S(1)}, f32[4,128,128]{2,1,0:T(8,128)S(1)}, u32[]{:S(2)}, u32[]{:S(2)}) collective-permute-start(f32[4,128,128]{2,1,0:T(8,128)S(1)} %get-tuple-element.28), channel_id=1, source_target_pairs={{0,1},{1,2},{2,3},{3,4},{4,5},{5,6},{6,7},{7,8},{8,9},{9,10},{10,1... | collective-permute-start | bytes 786440 | tf_op jit(solution)/shard_map/ppermute | solution.py:16
  200.2 3.3 %fusion.317 = (f32[8,128,128]{2,1,0:T(8,128)S(1)}, f32[8,128,128]{2,1,0:T(8,128)S(1)}) fusion(f32[8,128,128]{2,1,0:T(8,128)S(1)} %copy-done.1, f32[8,128,128]{2,1,0:T(8,128)S(1)} %bitcast.99, f32[16,136,136]{2,1,0:T(8,128)S(1)} %select_maximum_fusion.10, f32[8,128,128]{2,1,0:T(8,128)S(1)} %get-tuple-element.5, f32[4,128,128]{2,1,0:T(8,128)} %collective-permute-done.5, ...), kind=kLoop, calls=%fused_computation.563 | loop fusion | flops 6553600 | bytes 12582912 | tf_op jit(solution)/shard_map/mul | solution.py:159
  205.5 7.8 %collective-permute-start.15 = (f32[4,128,128]{2,1,0:T(8,128)S(1)}, f32[4,128,128]{2,1,0:T(8,128)S(1)}, u32[]{:S(2)}, u32[]{:S(2)}) collective-permute-start(f32[4,128,128]{2,1,0:T(8,128)S(1)} %get-tuple-element.17), channel_id=1, source_target_pairs={{0,1},{1,2},{2,3},{3,4},{4,5},{5,6},{6,7},{7,8},{8,9},{9,10},{10,1... | collective-permute-start | bytes 786440 | tf_op jit(solution)/shard_map/ppermute | solution.py:16
  213.9 2.9 %fusion.81 = f32[8,128,128]{2,1,0:T(8,128)S(1)} fusion(f32[8,128,128]{2,1,0:T(8,128)S(1)} %copy-done.1, f32[8,128,128]{2,1,0:T(8,128)S(1)} %fusion.108, f32[4,128,128]{2,1,0:T(8,128)S(1)} %collective-permute-done.11, f32[4,128,128]{2,1,0:T(8,128)S(1)} %collective-permute-done.10, f32[16,136,136]{2,1,0:T(8,128)S(1)} %select_maximum_fusion.4, ...), kind=kLoop, calls=%fused_computation.208 | loop fusion | flops 7077888 | bytes 11010600 | tf_op jit(solution)/shard_map/add | solution.py:63
  218.8 7.5 %collective-permute-start.13 = (f32[4,128,128]{2,1,0:T(8,128)S(1)}, f32[4,128,128]{2,1,0:T(8,128)S(1)}, u32[]{:S(2)}, u32[]{:S(2)}) collective-permute-start(f32[4,128,128]{2,1,0:T(8,128)S(1)} %get-tuple-element.26), channel_id=1, source_target_pairs={{0,1},{1,2},{2,3},{3,4},{4,5},{5,6},{6,7},{7,8},{8,9},{9,10},{10,1... | collective-permute-start | bytes 786440 | tf_op jit(solution)/shard_map/ppermute | solution.py:16
  229.4 5.3 %collective-permute-done.13 = f32[4,128,128]{2,1,0:T(8,128)S(1)} collective-permute-done((f32[4,128,128]{2,1,0:T(8,128)S(1)}, f32[4,128,128]{2,1,0:T(8,128)S(1)}, u32[]{:S(2)}, u32[]{:S(2)}) %collective-permute-start.13) | collective-permute-done | bytes 262176 | tf_op jit(solution)/shard_map/ppermute | solution.py:16
  235.5 3.0 %fusion.54 = f32[8,128,128]{2,1,0:T(8,128)S(1)} fusion(f32[8,128,128]{2,1,0:T(8,128)S(1)} %fusion.108, f32[8,128,128]{2,1,0:T(8,128)S(1)} %copy-done.2, f32[8,128,128]{2,1,0:T(8,128)S(1)} %fusion.81, f32[4,128,128]{2,1,0:T(8,128)S(1)} %collective-permute-done.13, f32[4,128,128]{2,1,0:T(8,128)S(1)} %collective-permute-done.12, ...), kind=kLoop, calls=%fused_computation.181 | loop fusion | flops 9437184 | bytes 14680616 | tf_op jit(solution)/shard_map/add | solution.py:168
  240.0 5.3 %all-to-all-start.1 = ((f32[16,9,8,128]{3,2,1,0:T(8,128)}), f32[16,9,8,128]{3,2,1,0:T(8,128)}, u32[]{:S(2)}, u32[]{:S(2)}) async-start(f32[16,9,8,128]{3,2,1,0:T(8,128)} %copy.30), calls=%async_computation.1 | async-start | bytes 1179648 | tf_op jit(solution)/shard_map/all_to_all | solution.py:179
  245.3 4.3 %fusion.307 = f32[1,8,128,128]{3,2,1,0:T(8,128)S(1)} fusion(f32[8,128,128]{2,1,0:T(8,128)} %bitcast.98, f32[16,136,136]{2,1,0:T(8,128)S(1)} %select_maximum_fusion, f32[8,128,128]{2,1,0:T(8,128)} %copy-done.9, f32[4,128,128]{2,1,0:T(8,128)} %copy-done.18, f32[4,128,128]{2,1,0:T(8,128)S(1)} %collective-permute-done.14, f32[8,128,128]{2,1,0:T(8,128)} %copy-done.5, ...), kind=kLoop, calls=%fused_computation.520 | loop fusion | flops 6422528 | bytes 11534336 | tf_op jit(solution)/shard_map/stack | solution.py:182
  250.7 6.2 %all-to-all-done.1 = f32[16,9,8,128]{3,2,1,0:T(8,128)} async-done(((f32[16,9,8,128]{3,2,1,0:T(8,128)}), f32[16,9,8,128]{3,2,1,0:T(8,128)}, u32[]{:S(2)}, u32[]{:S(2)}) %all-to-all-start.1) | async-done | bytes 589856 | tf_op jit(solution)/shard_map/all_to_all | solution.py:179
  (127 shorter events, 45.3 us)
Async XLA Ops:
  0.6 14.0 %copy-start = (f32[1,2,128,8,128]{4,3,2,1,0:T(8,128)S(1)}, f32[1,2,128,8,128]{4,3,2,1,0:T(8,128)}, u32[]{:S(2)}) copy-start(f32[1,2,128,8,128]{4,3,2,1,0:T(8,128)} %param.10) | copy-start | bytes 3145732
  0.6 12.5 %copy-start.20 = (s32[1,2048]{1,0:T(1,128)S(1)}, s32[1,2048]{1,0:T(1,128)}, u32[]{:S(2)}) copy-start(s32[1,2048]{1,0:T(1,128)} %param.11) | copy-start | bytes 24580
  3.7 60.5 %collective-permute-start = (f32[4,128,128]{2,1,0:T(8,128)}, f32[4,128,128]{2,1,0:T(8,128)S(1)}, u32[]{:S(2)}, u32[]{:S(2)}) collective-permute-start(f32[4,128,128]{2,1,0:T(8,128)} %get-tuple-element.24), channel_id=1, source_target_pairs={{1,0},{2,1},{3,2},{4,3},{5,4},{6,5},{7,6},{8,7},{9,8},{10,9},{11,1... | collective-permute-start | bytes 786440 | tf_op jit(solution)/shard_map/ppermute | solution.py:17
  6.1 58.1 %collective-permute-start.1 = (f32[4,128,128]{2,1,0:T(8,128)}, f32[4,128,128]{2,1,0:T(8,128)}, u32[]{:S(2)}, u32[]{:S(2)}) collective-permute-start(f32[4,128,128]{2,1,0:T(8,128)} %get-tuple-element.23), channel_id=1, source_target_pairs={{0,1},{1,2},{2,3},{3,4},{4,5},{5,6},{6,7},{7,8},{8,9},{9,10},{10,1... | collective-permute-start | bytes 786440 | tf_op jit(solution)/shard_map/ppermute | solution.py:16
  18.2 9.3 %copy-start.22 = (f32[1,4,512]{2,1,0:T(4,128)S(1)}, f32[1,4,512]{2,1,0:T(4,128)}, u32[]{:S(2)}) copy-start(f32[1,4,512]{2,1,0:T(4,128)} %param.16) | copy-start | bytes 24580
  18.2 122.6 %all-to-all-start = ((f32[16,32,2,8,128]{4,3,2,1,0:T(8,128)}), f32[16,32,2,8,128]{4,3,2,1,0:T(8,128)}, u32[]{:S(2)}, u32[]{:S(2)}) async-start(f32[16,32,2,8,128]{4,3,2,1,0:T(8,128)} %bitcast.86), calls=%async_computation | async-start | bytes 8388608 | tf_op jit(solution)/shard_map/all_to_all | solution.py:114
  45.0 18.5 %copy-start.23 = (f32[1,4]{1,0:T(1,128)S(1)}, f32[1,4]{1,0:T(1,128)}, u32[]{:S(2)}) copy-start(f32[1,4]{1,0:T(1,128)} %param.13) | copy-start | bytes 52
  45.0 19.2 %copy-start.8 = (f32[8,128,128]{2,1,0:T(8,128)S(1)}, f32[8,128,128]{2,1,0:T(8,128)}, u32[]{:S(2)}) copy-start(f32[8,128,128]{2,1,0:T(8,128)} %copy-done.7) | copy-start | bytes 1572868
  52.1 13.7 %copy-start.1 = (f32[8,128,128]{2,1,0:T(8,128)S(1)}, f32[8,128,128]{2,1,0:T(8,128)}, u32[]{:S(2)}) copy-start(f32[8,128,128]{2,1,0:T(8,128)} %param.9) | copy-start | bytes 1572868
  65.8 14.6 %copy-start.21 = (s32[1,128,16]{1,2,0:T(8,128)S(1)}, s32[1,128,16]{1,2,0:T(8,128)}, u32[]{:S(2)}) copy-start(s32[1,128,16]{1,2,0:T(8,128)} %param.17) | copy-start | bytes 24580
  69.3 56.7 %copy-start.10 = (f32[8,128,128]{2,1,0:T(8,128)}, f32[8,128,128]{2,1,0:T(8,128)S(1)}, u32[]{:S(2)}) copy-start(f32[8,128,128]{2,1,0:T(8,128)S(1)} %get-tuple-element.7) | copy-start | bytes 1572868
  69.3 130.8 %copy-start.3 = (f32[8,128,128]{2,1,0:T(8,128)}, f32[8,128,128]{2,1,0:T(8,128)S(1)}, u32[]{:S(2)}) copy-start(f32[8,128,128]{2,1,0:T(8,128)S(1)} %get-tuple-element.8) | copy-start | bytes 1572868
  70.3 55.1 %collective-permute-start.2 = (f32[4,128,128]{2,1,0:T(8,128)}, f32[4,128,128]{2,1,0:T(8,128)S(1)}, u32[]{:S(2)}, u32[]{:S(2)}) collective-permute-start(f32[4,128,128]{2,1,0:T(8,128)} %get-tuple-element.22), channel_id=1, source_target_pairs={{1,0},{2,1},{3,2},{4,3},{5,4},{6,5},{7,6},{8,7},{9,8},{10,9},{11,1... | collective-permute-start | bytes 786440 | tf_op jit(solution)/shard_map/ppermute | solution.py:17
  72.5 52.9 %collective-permute-start.3 = (f32[4,128,128]{2,1,0:T(8,128)}, f32[4,128,128]{2,1,0:T(8,128)S(1)}, u32[]{:S(2)}, u32[]{:S(2)}) collective-permute-start(f32[4,128,128]{2,1,0:T(8,128)} %get-tuple-element.21), channel_id=1, source_target_pairs={{0,1},{1,2},{2,3},{3,4},{4,5},{5,6},{6,7},{7,8},{8,9},{9,10},{10,1... | collective-permute-start | bytes 786440 | tf_op jit(solution)/shard_map/ppermute | solution.py:16
  80.5 45.5 %copy-start.13 = (f32[1,2,8,128,128]{4,3,2,1,0:T(8,128)S(1)}, f32[1,2,8,128,128]{4,3,2,1,0:T(8,128)}, u32[]{:S(2)}) copy-start(f32[1,2,8,128,128]{4,3,2,1,0:T(8,128)} %param.12) | copy-start | bytes 3145732
  130.3 69.8 %copy-start.5 = (f32[8,128,128]{2,1,0:T(8,128)}, f32[8,128,128]{2,1,0:T(8,128)S(1)}, u32[]{:S(2)}) copy-start(f32[8,128,128]{2,1,0:T(8,128)S(1)} %get-tuple-element.6) | copy-start | bytes 1572868
  131.2 46.2 %collective-permute-start.4 = (f32[4,128,128]{2,1,0:T(8,128)}, f32[4,128,128]{2,1,0:T(8,128)S(1)}, u32[]{:S(2)}, u32[]{:S(2)}) collective-permute-start(f32[4,128,128]{2,1,0:T(8,128)} %get-tuple-element.20), channel_id=1, source_target_pairs={{1,0},{2,1},{3,2},{4,3},{5,4},{6,5},{7,6},{8,7},{9,8},{10,9},{11,1... | collective-permute-start | bytes 786440 | tf_op jit(solution)/shard_map/ppermute | solution.py:17
  136.4 41.0 %collective-permute-start.5 = (f32[4,128,128]{2,1,0:T(8,128)}, f32[4,128,128]{2,1,0:T(8,128)}, u32[]{:S(2)}, u32[]{:S(2)}) collective-permute-start(f32[4,128,128]{2,1,0:T(8,128)} %get-tuple-element.19), channel_id=1, source_target_pairs={{0,1},{1,2},{2,3},{3,4},{4,5},{5,6},{6,7},{7,8},{8,9},{9,10},{10,1... | collective-permute-start | bytes 786440 | tf_op jit(solution)/shard_map/ppermute | solution.py:16
  145.6 13.3 %collective-permute-start.6 = (f32[4,128,128]{2,1,0:T(8,128)S(1)}, f32[4,128,128]{2,1,0:T(8,128)S(1)}, u32[]{:S(2)}, u32[]{:S(2)}) collective-permute-start(f32[4,128,128]{2,1,0:T(8,128)S(1)} %bitcast.103), channel_id=1, source_target_pairs={{1,0},{2,1},{3,2},{4,3},{5,4},{6,5},{7,6},{8,7},{9,8},{10,9},{11,1... | collective-permute-start | bytes 786440 | tf_op jit(solution)/shard_map/ppermute | solution.py:17
  148.6 15.6 %collective-permute-start.7 = (f32[4,128,128]{2,1,0:T(8,128)S(1)}, f32[4,128,128]{2,1,0:T(8,128)S(1)}, u32[]{:S(2)}, u32[]{:S(2)}) collective-permute-start(f32[4,128,128]{2,1,0:T(8,128)S(1)} %bitcast.102), channel_id=1, source_target_pairs={{0,1},{1,2},{2,3},{3,4},{4,5},{5,6},{6,7},{7,8},{8,9},{9,10},{10,1... | collective-permute-start | bytes 786440 | tf_op jit(solution)/shard_map/ppermute | solution.py:16
  167.9 13.7 %collective-permute-start.8 = (f32[4,128,128]{2,1,0:T(8,128)S(1)}, f32[4,128,128]{2,1,0:T(8,128)S(1)}, u32[]{:S(2)}, u32[]{:S(2)}) collective-permute-start(f32[4,128,128]{2,1,0:T(8,128)S(1)} %get-tuple-element.29), channel_id=1, source_target_pairs={{1,0},{2,1},{3,2},{4,3},{5,4},{6,5},{7,6},{8,7},{9,8},{10,9},{11,1... | collective-permute-start | bytes 786440 | tf_op jit(solution)/shard_map/ppermute | solution.py:17
  169.9 17.1 %collective-permute-start.9 = (f32[4,128,128]{2,1,0:T(8,128)S(1)}, f32[4,128,128]{2,1,0:T(8,128)S(1)}, u32[]{:S(2)}, u32[]{:S(2)}) collective-permute-start(f32[4,128,128]{2,1,0:T(8,128)S(1)} %get-tuple-element.30), channel_id=1, source_target_pairs={{0,1},{1,2},{2,3},{3,4},{4,5},{5,6},{6,7},{7,8},{8,9},{9,10},{10,1... | collective-permute-start | bytes 786440 | tf_op jit(solution)/shard_map/ppermute | solution.py:16
  187.6 12.6 %copy-start.16 = (f32[1,131072]{1,0:T(1,128)S(1)}, f32[1,131072]{1,0:T(1,128)}, u32[]{:S(2)}) copy-start(f32[1,131072]{1,0:T(1,128)} %get-tuple-element.10) | copy-start | bytes 1572868
  190.7 22.6 %collective-permute-start.10 = (f32[4,128,128]{2,1,0:T(8,128)S(1)}, f32[4,128,128]{2,1,0:T(8,128)S(1)}, u32[]{:S(2)}, u32[]{:S(2)}) collective-permute-start(f32[4,128,128]{2,1,0:T(8,128)S(1)} %get-tuple-element.27), channel_id=1, source_target_pairs={{1,0},{2,1},{3,2},{4,3},{5,4},{6,5},{7,6},{8,7},{9,8},{10,9},{11,1... | collective-permute-start | bytes 786440 | tf_op jit(solution)/shard_map/ppermute | solution.py:17
  192.6 20.7 %collective-permute-start.11 = (f32[4,128,128]{2,1,0:T(8,128)S(1)}, f32[4,128,128]{2,1,0:T(8,128)S(1)}, u32[]{:S(2)}, u32[]{:S(2)}) collective-permute-start(f32[4,128,128]{2,1,0:T(8,128)S(1)} %get-tuple-element.28), channel_id=1, source_target_pairs={{0,1},{1,2},{2,3},{3,4},{4,5},{5,6},{6,7},{7,8},{8,9},{9,10},{10,1... | collective-permute-start | bytes 786440 | tf_op jit(solution)/shard_map/ppermute | solution.py:16
  203.5 22.9 %copy-start.9 = (f32[8,128,128]{2,1,0:T(8,128)}, f32[8,128,128]{2,1,0:T(8,128)S(1)}, u32[]{:S(2)}) copy-start(f32[8,128,128]{2,1,0:T(8,128)S(1)} %get-tuple-element.3) | copy-start | bytes 1572868
  203.5 31.9 %copy-start.11 = (f32[8,128,128]{2,1,0:T(8,128)}, f32[8,128,128]{2,1,0:T(8,128)S(1)}, u32[]{:S(2)}) copy-start(f32[8,128,128]{2,1,0:T(8,128)S(1)} %get-tuple-element.4) | copy-start | bytes 1572868
  203.6 22.8 %collective-permute-start.14 = (f32[4,128,128]{2,1,0:T(8,128)S(1)}, f32[4,128,128]{2,1,0:T(8,128)S(1)}, u32[]{:S(2)}, u32[]{:S(2)}) collective-permute-start(f32[4,128,128]{2,1,0:T(8,128)S(1)} %get-tuple-element.18), channel_id=1, source_target_pairs={{1,0},{2,1},{3,2},{4,3},{5,4},{6,5},{7,6},{8,7},{9,8},{10,9},{11,1... | collective-permute-start | bytes 786440 | tf_op jit(solution)/shard_map/ppermute | solution.py:17
  205.5 20.9 %collective-permute-start.15 = (f32[4,128,128]{2,1,0:T(8,128)S(1)}, f32[4,128,128]{2,1,0:T(8,128)S(1)}, u32[]{:S(2)}, u32[]{:S(2)}) collective-permute-start(f32[4,128,128]{2,1,0:T(8,128)S(1)} %get-tuple-element.17), channel_id=1, source_target_pairs={{0,1},{1,2},{2,3},{3,4},{4,5},{5,6},{6,7},{7,8},{8,9},{9,10},{10,1... | collective-permute-start | bytes 786440 | tf_op jit(solution)/shard_map/ppermute | solution.py:16
  216.9 12.5 %collective-permute-start.12 = (f32[4,128,128]{2,1,0:T(8,128)S(1)}, f32[4,128,128]{2,1,0:T(8,128)S(1)}, u32[]{:S(2)}, u32[]{:S(2)}) collective-permute-start(f32[4,128,128]{2,1,0:T(8,128)S(1)} %get-tuple-element.25), channel_id=1, source_target_pairs={{1,0},{2,1},{3,2},{4,3},{5,4},{6,5},{7,6},{8,7},{9,8},{10,9},{11,1... | collective-permute-start | bytes 786440 | tf_op jit(solution)/shard_map/ppermute | solution.py:17
  218.8 15.9 %collective-permute-start.13 = (f32[4,128,128]{2,1,0:T(8,128)S(1)}, f32[4,128,128]{2,1,0:T(8,128)S(1)}, u32[]{:S(2)}, u32[]{:S(2)}) collective-permute-start(f32[4,128,128]{2,1,0:T(8,128)S(1)} %get-tuple-element.26), channel_id=1, source_target_pairs={{0,1},{1,2},{2,3},{3,4},{4,5},{5,6},{6,7},{7,8},{8,9},{9,10},{10,1... | collective-permute-start | bytes 786440 | tf_op jit(solution)/shard_map/ppermute | solution.py:16
  240.0 16.9 %all-to-all-start.1 = ((f32[16,9,8,128]{3,2,1,0:T(8,128)}), f32[16,9,8,128]{3,2,1,0:T(8,128)}, u32[]{:S(2)}, u32[]{:S(2)}) async-start(f32[16,9,8,128]{3,2,1,0:T(8,128)} %copy.30), calls=%async_computation.1 | async-start | bytes 1179648 | tf_op jit(solution)/shard_map/all_to_all | solution.py:179
  (13 other events, 69.9 us)

commit v8 on v4

--- a/solution.py
+++ b/solution.py
@@ -19,27 +19,31 @@
     return array
 
 
+def shifted(field, offset, axis):
+    length = field.shape[axis]
+    pad = [(0, 0)] * field.ndim
+    if offset > 0:
+        part = lax.slice_in_dim(field, offset, length, axis=axis)
+        pad[axis] = (0, offset)
+    else:
+        part = lax.slice_in_dim(field, 0, length + offset, axis=axis)
+        pad[axis] = (-offset, 0)
+    return jnp.pad(part, pad)
+
+
 def laplace(field):
     length = field.shape[0] - 8
-    height = field.shape[1]
-    breadth = field.shape[2]
-    padded = jnp.pad(field, ((0, 0), (4, 4), (4, 4)))
-    summed = 3.0 * STENCIL[0] * padded[4 : 4 + length, 4 : 4 + height, 4 : 4 + breadth]
+    center = field[4 : 4 + length]
+    summed = 3.0 * STENCIL[0] * center
     for offset in range(1, 5):
         summed = summed + STENCIL[offset] * (
-            padded[4 + offset : 4 + offset + length, 4 : 4 + height, 4 : 4 + breadth]
-            + padded[4 - offset : 4 - offset + length, 4 : 4 + height, 4 : 4 + breadth]
-        )
-    for offset in range(1, 5):
-        summed = summed + STENCIL[offset] * (
-            padded[4 : 4 + length, 4 + offset : 4 + offset + height, 4 : 4 + breadth]
-            + padded[4 : 4 + length, 4 - offset : 4 - offset + height, 4 : 4 + breadth]
-        )
-    for offset in range(1, 5):
-        summed = summed + STENCIL[offset] * (
-            padded[4 : 4 + length, 4 : 4 + height, 4 + offset : 4 + offset + breadth]
-            + padded[4 : 4 + length, 4 : 4 + height, 4 - offset : 4 - offset + breadth]
-        )
+            field[4 + offset : 4 + offset + length] + field[4 - offset : 4 - offset + length]
+        )
+    for axis in (1, 2):
+        for offset in range(1, 5):
+            summed = summed + STENCIL[offset] * (
+                shifted(center, offset, axis) + shifted(center, -offset, axis)
+            )
     return summed
 
 

time: 261 us -> 283 us (1.084)
  local copies, waits for them, and re-layouts: 31.5 us -> 53 us
  waiting for transfers between devices: 76.3 us -> 87.4 us
  other arithmetic: 59.1 us -> 48.3 us
    slice x4 -> x64, local copies, waits for them, and re-layouts: 1.81 us -> 23.4 us  [shifted(): part = lax.slice_in_dim(field, offset, length, axis=axis)]
    ppermute x8, waiting for transfers between devices: 16 us -> 26.5 us  [padded_2(): before = lax.ppermute(last, axis, up)]
    concatenate x8 -> x0, other arithmetic: 6.09 us -> none  [padded_2(): array = jnp.concatenate([before, array, after], axis=dim)]
  transfers between devices with their start and end apart: 18 -> 18, of which waited for: 8 -> 12; matrix products, arithmetic and copies ran while one was open for 30% -> 35% of each run, Pallas kernels for 0% -> 0%
where the time goes in v8:
time: 283 us; the launch traced here: 282 us
  starting transfers between devices  90.6 us (32%)
  waiting for transfers between devices  87.4 us (31%)
  local copies, waits for them, and re-layouts  53 us (19%)
  other arithmetic  48.3 us (17%)
    ppermute x8, starting transfers between devices, padded_2(): before = lax.ppermute(last, axis, up)  56.7 us
    ppermute x8, waiting for transfers between devices, padded_2(): after = lax.ppermute(initial, axis, down)  54.7 us
    ppermute x8, waiting for transfers between devices, padded_2(): before = lax.ppermute(last, axis, up)  26.5 us
    slice x64, local copies, waits for them, and re-layouts, shifted(): part = lax.slice_in_dim(field, offset, length, axis=axis)  23.4 us
    ppermute x8, starting transfers between devices, padded_2(): after = lax.ppermute(initial, axis, down)  19.6 us
    unnamed x4, other arithmetic  14.8 us
    all_to_all x1, starting transfers between devices, body(): lax.all_to_all(outgoing, 'space', split_axis=0, concat_axis=0, tiled=True)  9 us
    mul x4, other arithmetic, body(): weighted = extend(courant * adjoints[moment])  9 us
  transfers between devices with their start and end apart: 18, of which 12 were waited for; matrix products, arithmetic and copies ran while one was open for 35% of the time, Pallas kernels for 0%

profile of v8, /device:TPU:100, one launch (start us, length us, event | category | flops | bytes accessed | tf_op | source)
XLA Modules:
  0.0 282.1 jit_solution(1032205199233950938)
XLA Ops:
  5.2 7.0 %collective-permute-start.1 = (f32[4,128,128]{2,1,0:T(8,128)}, f32[4,128,128]{2,1,0:T(8,128)}, u32[]{:S(2)}, u32[]{:S(2)}) collective-permute-start(f32[4,128,128]{2,1,0:T(8,128)} %get-tuple-element.72), channel_id=1, source_target_pairs={{0,1},{1,2},{2,3},{3,4},{4,5},{5,6},{6,7},{7,8},{8,9},{9,10},{10,1... | collective-permute-start | bytes 786440 | tf_op jit(solution)/shard_map/ppermute | solution.py:16
  13.9 3.5 %gather_fusion = f32[512,2,8,128]{3,2,1,0:T(8,128)} fusion(f32[129,2,8,128]{3,2,0,1:T(8,128)S(1)} %concatenate.123, s32[1024]{0:T(1024)S(1)} %pad_clamp_fusion.1), kind=kCustom, calls=%fused_computation | custom fusion | bytes 8390656 | tf_op jit(solution)/shard_map/jit(_take)/gather | solution.py:117
  17.4 9.0 %all-to-all-start = ((f32[16,32,2,8,128]{4,3,2,1,0:T(8,128)}), f32[16,32,2,8,128]{4,3,2,1,0:T(8,128)}, u32[]{:S(2)}, u32[]{:S(2)}) async-start(f32[16,32,2,8,128]{4,3,2,1,0:T(8,128)} %bitcast.97), calls=%async_computation | async-start | bytes 8388608 | tf_op jit(solution)/shard_map/all_to_all | solution.py:119
  34.3 2.8 select_reduce_fusion
  37.2 8.1 %scatter_custom_fusion = s32[128]{0:T(128)S(1)} fusion(s32[2048]{0:T(1024)S(1)} %bitcast.116, s32[2048]{0:T(1024)S(1)} %add_bitcast_fusion, s32[]{:T(128)} %constant.91.clone.1), kind=kCustom, calls=%fused_computation.411 | custom fusion | bytes 516 | tf_op jit(solution)/shard_map/scatter | solution.py:130
  45.6 14.6 %scatter_custom_fusion.2 = f32[524292]{0:T(1024)S(1)} fusion(s32[2048]{0:T(1024)S(1)} %bitcast.117, f32[2048]{0:T(1024)S(1)} %bitcast.118, f32[]{:T(128)} %constant.52.clone.1), kind=kCustom, calls=%fused_computation.59 | custom fusion | flops 2048 | bytes 2097172
  62.8 6.7 %fusion.256 = (f32[1,131072]{1,0:T(1,128)}, f32[1,131072]{1,0:T(1,128)}, f32[1,131072]{1,0:T(1,128)}, f32[1,131072]{1,0:T(1,128)}) fusion(f32[4,131073]{1,0:T(4,128)} %reshape.304), kind=kLoop, calls=%fused_computation.418 | loop fusion | bytes 4194304 | tf_op jit(solution)/shard_map/slice | solution.py:169
  74.0 4.0 %fusion.254 = (f32[8,128,128]{2,1,0:T(8,128)S(1)}, f32[8,128,128]{2,1,0:T(8,128)S(1)}) fusion(f32[8,128,128]{2,1,0:T(8,128)S(1)} %copy-done, f32[8,128,128]{2,1,0:T(8,128)S(1)} %bitcast.106, f32[8,128,124]{2,1,0:T(8,128)S(1)} %get-tuple-element.88, f32[8,128,124]{2,1,0:T(8,128)S(1)} %get-tuple-element.87, f32[8,128,125]{2,1,0:T(8,128)} %get-tuple-element.86, ...), kind=kLoop, calls=%fused_computation.417 | loop fusion | flops 6553600 | bytes 12419072 | tf_op jit(solution)/shard_map/mul | solution.py:164
  80.5 7.0 %collective-permute-start.3 = (f32[4,128,128]{2,1,0:T(8,128)S(1)}, f32[4,128,128]{2,1,0:T(8,128)S(1)}, u32[]{:S(2)}, u32[]{:S(2)}) collective-permute-start(f32[4,128,128]{2,1,0:T(8,128)S(1)} %get-tuple-element.54), channel_id=1, source_target_pairs={{0,1},{1,2},{2,3},{3,4},{4,5},{5,6},{6,7},{7,8},{8,9},{9,10},{10,1... | collective-permute-start | bytes 786440 | tf_op jit(solution)/shard_map/ppermute | solution.py:16
  88.7 35.8 %collective-permute-done.2 = f32[4,128,128]{2,1,0:T(8,128)S(1)} collective-permute-done((f32[4,128,128]{2,1,0:T(8,128)S(1)}, f32[4,128,128]{2,1,0:T(8,128)S(1)}, u32[]{:S(2)}, u32[]{:S(2)}) %collective-permute-start.2) | collective-permute-done | bytes 262176 | tf_op jit(solution)/shard_map/ppermute | solution.py:17
  126.4 5.0 %collective-permute-start.4 = (f32[4,128,128]{2,1,0:T(8,128)S(1)}, f32[4,128,128]{2,1,0:T(8,128)S(1)}, u32[]{:S(2)}, u32[]{:S(2)}) collective-permute-start(f32[4,128,128]{2,1,0:T(8,128)S(1)} %get-tuple-element.35), channel_id=1, source_target_pairs={{1,0},{2,1},{3,2},{4,3},{5,4},{6,5},{7,6},{8,7},{9,8},{10,9},{11,1... | collective-permute-start | bytes 786440 | tf_op jit(solution)/shard_map/ppermute | solution.py:17
  131.5 4.8 %collective-permute-start.5 = (f32[4,128,128]{2,1,0:T(8,128)S(1)}, f32[4,128,128]{2,1,0:T(8,128)S(1)}, u32[]{:S(2)}, u32[]{:S(2)}) collective-permute-start(f32[4,128,128]{2,1,0:T(8,128)S(1)} %get-tuple-element.36), channel_id=1, source_target_pairs={{0,1},{1,2},{2,3},{3,4},{4,5},{5,6},{6,7},{7,8},{8,9},{9,10},{10,1... | collective-permute-start | bytes 786440 | tf_op jit(solution)/shard_map/ppermute | solution.py:16
  137.4 3.6 %collective-permute-done.4 = f32[4,128,128]{2,1,0:T(8,128)S(1)} collective-permute-done((f32[4,128,128]{2,1,0:T(8,128)S(1)}, f32[4,128,128]{2,1,0:T(8,128)S(1)}, u32[]{:S(2)}, u32[]{:S(2)}) %collective-permute-start.4) | collective-permute-done | bytes 262176 | tf_op jit(solution)/shard_map/ppermute | solution.py:17
  141.0 5.1 %collective-permute-done.5 = f32[4,128,128]{2,1,0:T(8,128)S(1)} collective-permute-done((f32[4,128,128]{2,1,0:T(8,128)S(1)}, f32[4,128,128]{2,1,0:T(8,128)S(1)}, u32[]{:S(2)}, u32[]{:S(2)}) %collective-permute-start.5) | collective-permute-done | bytes 262176 | tf_op jit(solution)/shard_map/ppermute | solution.py:16
  150.7 7.5 %collective-permute-start.15 = (f32[4,128,128]{2,1,0:T(8,128)}, f32[4,128,128]{2,1,0:T(8,128)}, u32[]{:S(2)}, u32[]{:S(2)}) collective-permute-start(f32[4,128,128]{2,1,0:T(8,128)} %get-tuple-element.18), channel_id=1, source_target_pairs={{0,1},{1,2},{2,3},{3,4},{4,5},{5,6},{6,7},{7,8},{8,9},{9,10},{10,1... | collective-permute-start | bytes 786440 | tf_op jit(solution)/shard_map/ppermute | solution.py:16
  167.1 3.8 %gather_fusion.1 = f32[128,2,8,128]{3,2,1,0:T(8,128)} fusion(f32[512,2,8,128]{3,2,1,0:T(8,128)} %bitcast.17, s32[1024]{0:T(1024)S(1)} %pad_clamp_fusion), kind=kCustom, calls=%fused_computation.1 | custom fusion | bytes 2097664 | tf_op jit(solution)/shard_map/jit(_take)/gather | solution.py:132
  175.3 7.8 %collective-permute-start.7 = (f32[4,128,128]{2,1,0:T(8,128)S(1)}, f32[4,128,128]{2,1,0:T(8,128)S(1)}, u32[]{:S(2)}, u32[]{:S(2)}) collective-permute-start(f32[4,128,128]{2,1,0:T(8,128)S(1)} %bitcast.108), channel_id=1, source_target_pairs={{0,1},{1,2},{2,3},{3,4},{4,5},{5,6},{6,7},{7,8},{8,9},{9,10},{10,1... | collective-permute-start | bytes 786440 | tf_op jit(solution)/shard_map/ppermute | solution.py:16
  183.3 3.4 %collective-permute-done.6 = f32[4,128,128]{2,1,0:T(8,128)S(1)} collective-permute-done((f32[4,128,128]{2,1,0:T(8,128)S(1)}, f32[4,128,128]{2,1,0:T(8,128)S(1)}, u32[]{:S(2)}, u32[]{:S(2)}) %collective-permute-start.6) | collective-permute-done | bytes 262176 | tf_op jit(solution)/shard_map/ppermute | solution.py:17
  186.7 5.3 %collective-permute-done.7 = f32[4,128,128]{2,1,0:T(8,128)S(1)} collective-permute-done((f32[4,128,128]{2,1,0:T(8,128)S(1)}, f32[4,128,128]{2,1,0:T(8,128)S(1)}, u32[]{:S(2)}, u32[]{:S(2)}) %collective-permute-start.7) | collective-permute-done | bytes 262176 | tf_op jit(solution)/shard_map/ppermute | solution.py:16
  197.3 7.5 %collective-permute-start.9 = (f32[4,128,128]{2,1,0:T(8,128)S(1)}, f32[4,128,128]{2,1,0:T(8,128)S(1)}, u32[]{:S(2)}, u32[]{:S(2)}) collective-permute-start(f32[4,128,128]{2,1,0:T(8,128)S(1)} %get-tuple-element.142), channel_id=1, source_target_pairs={{0,1},{1,2},{2,3},{3,4},{4,5},{5,6},{6,7},{7,8},{8,9},{9,10},{10,1... | collective-permute-start | bytes 786440 | tf_op jit(solution)/shard_map/ppermute | solution.py:16
  205.1 4.0 %collective-permute-done.8 = f32[4,128,128]{2,1,0:T(8,128)S(1)} collective-permute-done((f32[4,128,128]{2,1,0:T(8,128)S(1)}, f32[4,128,128]{2,1,0:T(8,128)S(1)}, u32[]{:S(2)}, u32[]{:S(2)}) %collective-permute-start.8) | collective-permute-done | bytes 262176 | tf_op jit(solution)/shard_map/ppermute | solution.py:17
  209.0 5.3 %collective-permute-done.9 = f32[4,128,128]{2,1,0:T(8,128)S(1)} collective-permute-done((f32[4,128,128]{2,1,0:T(8,128)S(1)}, f32[4,128,128]{2,1,0:T(8,128)S(1)}, u32[]{:S(2)}, u32[]{:S(2)}) %collective-permute-start.9) | collective-permute-done | bytes 262176 | tf_op jit(solution)/shard_map/ppermute | solution.py:16
  219.8 7.5 %collective-permute-start.11 = (f32[4,128,128]{2,1,0:T(8,128)S(1)}, f32[4,128,128]{2,1,0:T(8,128)S(1)}, u32[]{:S(2)}, u32[]{:S(2)}) collective-permute-start(f32[4,128,128]{2,1,0:T(8,128)S(1)} %get-tuple-element.124), channel_id=1, source_target_pairs={{0,1},{1,2},{2,3},{3,4},{4,5},{5,6},{6,7},{7,8},{8,9},{9,10},{10,1... | collective-permute-start | bytes 786440 | tf_op jit(solution)/shard_map/ppermute | solution.py:16
  227.5 4.0 %collective-permute-done.10 = f32[4,128,128]{2,1,0:T(8,128)S(1)} collective-permute-done((f32[4,128,128]{2,1,0:T(8,128)S(1)}, f32[4,128,128]{2,1,0:T(8,128)S(1)}, u32[]{:S(2)}, u32[]{:S(2)}) %collective-permute-start.10) | collective-permute-done | bytes 262176 | tf_op jit(solution)/shard_map/ppermute | solution.py:17
  231.5 5.3 %collective-permute-done.11 = f32[4,128,128]{2,1,0:T(8,128)S(1)} collective-permute-done((f32[4,128,128]{2,1,0:T(8,128)S(1)}, f32[4,128,128]{2,1,0:T(8,128)S(1)}, u32[]{:S(2)}, u32[]{:S(2)}) %collective-permute-start.11) | collective-permute-done | bytes 262176 | tf_op jit(solution)/shard_map/ppermute | solution.py:16
  242.4 7.5 %collective-permute-start.13 = (f32[4,128,128]{2,1,0:T(8,128)S(1)}, f32[4,128,128]{2,1,0:T(8,128)S(1)}, u32[]{:S(2)}, u32[]{:S(2)}) collective-permute-start(f32[4,128,128]{2,1,0:T(8,128)S(1)} %get-tuple-element.106), channel_id=1, source_target_pairs={{0,1},{1,2},{2,3},{3,4},{4,5},{5,6},{6,7},{7,8},{8,9},{9,10},{10,1... | collective-permute-start | bytes 786440 | tf_op jit(solution)/shard_map/ppermute | solution.py:16
  250.1 4.0 %collective-permute-done.12 = f32[4,128,128]{2,1,0:T(8,128)S(1)} collective-permute-done((f32[4,128,128]{2,1,0:T(8,128)S(1)}, f32[4,128,128]{2,1,0:T(8,128)S(1)}, u32[]{:S(2)}, u32[]{:S(2)}) %collective-permute-start.12) | collective-permute-done | bytes 262176 | tf_op jit(solution)/shard_map/ppermute | solution.py:17
  254.1 5.3 %collective-permute-done.13 = f32[4,128,128]{2,1,0:T(8,128)S(1)} collective-permute-done((f32[4,128,128]{2,1,0:T(8,128)S(1)}, f32[4,128,128]{2,1,0:T(8,128)S(1)}, u32[]{:S(2)}, u32[]{:S(2)}) %collective-permute-start.13) | collective-permute-done | bytes 262176 | tf_op jit(solution)/shard_map/ppermute | solution.py:16
  259.4 3.0 %fusion.51 = f32[8,128,128]{2,1,0:T(8,128)S(1)} fusion(f32[8,128,128]{2,1,0:T(8,128)S(1)} %fusion.105, f32[8,128,128]{2,1,0:T(8,128)S(1)} %copy-done, f32[8,128,128]{2,1,0:T(8,128)S(1)} %fusion.78, f32[4,128,128]{2,1,0:T(8,128)S(1)} %collective-permute-done.13, f32[4,128,128]{2,1,0:T(8,128)S(1)} %collective-permute-done.12, ...), kind=kLoop, calls=%fused_computation.159 | loop fusion | flops 9437184 | bytes 14516776 | tf_op jit(solution)/shard_map/add | solution.py:173
  264.0 5.2 %all-to-all-start.1 = ((f32[16,9,8,128]{3,2,1,0:T(8,128)}), f32[16,9,8,128]{3,2,1,0:T(8,128)S(1)}, u32[]{:S(2)}, u32[]{:S(2)}) async-start(f32[16,9,8,128]{3,2,1,0:T(8,128)} %copy.30), calls=%async_computation.1 | async-start | bytes 1179648 | tf_op jit(solution)/shard_map/all_to_all | solution.py:184
  269.3 4.3 %fusion.240 = f32[1,8,128,128]{3,2,1,0:T(8,128)S(1)} fusion(f32[8,128,128]{2,1,0:T(8,128)} %bitcast.103, f32[8,128,124]{2,1,0:T(8,128)} %get-tuple-element.34, f32[8,128,124]{2,1,0:T(8,128)} %get-tuple-element.33, f32[8,128,125]{2,1,0:T(8,128)} %get-tuple-element.32, f32[8,128,125]{2,1,0:T(8,128)} %get-tuple-element.31, ...), kind=kLoop, calls=%fused_computation.370 | loop fusion | flops 6422528 | bytes 11370496 | tf_op jit(solution)/shard_map/stack | solution.py:187
  274.7 6.2 %all-to-all-done.1 = f32[16,9,8,128]{3,2,1,0:T(8,128)S(1)} async-done(((f32[16,9,8,128]{3,2,1,0:T(8,128)}), f32[16,9,8,128]{3,2,1,0:T(8,128)S(1)}, u32[]{:S(2)}, u32[]{:S(2)}) %all-to-all-start.1) | async-done | bytes 589856 | tf_op jit(solution)/shard_map/all_to_all | solution.py:184
  (169 shorter events, 65.6 us)
Async XLA Ops:
  0.6 11.7 %copy-start.11 = (s32[1,2048]{1,0:T(1,128)S(1)}, s32[1,2048]{1,0:T(1,128)}, u32[]{:S(2)}) copy-start(s32[1,2048]{1,0:T(1,128)} %param.11) | copy-start | bytes 24580
  0.6 13.2 %copy-start.10 = (f32[1,2,128,8,128]{4,3,2,1,0:T(8,128)S(1)}, f32[1,2,128,8,128]{4,3,2,1,0:T(8,128)}, u32[]{:S(2)}) copy-start(f32[1,2,128,8,128]{4,3,2,1,0:T(8,128)} %param.10) | copy-start | bytes 3145732
  2.8 71.1 %collective-permute-start = (f32[4,128,128]{2,1,0:T(8,128)}, f32[4,128,128]{2,1,0:T(8,128)S(1)}, u32[]{:S(2)}, u32[]{:S(2)}) collective-permute-start(f32[4,128,128]{2,1,0:T(8,128)} %get-tuple-element.71), channel_id=1, source_target_pairs={{1,0},{2,1},{3,2},{4,3},{5,4},{6,5},{7,6},{8,7},{9,8},{10,9},{11,1... | collective-permute-start | bytes 786440 | tf_op jit(solution)/shard_map/ppermute | solution.py:17
  5.2 68.7 %collective-permute-start.1 = (f32[4,128,128]{2,1,0:T(8,128)}, f32[4,128,128]{2,1,0:T(8,128)}, u32[]{:S(2)}, u32[]{:S(2)}) collective-permute-start(f32[4,128,128]{2,1,0:T(8,128)} %get-tuple-element.72), channel_id=1, source_target_pairs={{0,1},{1,2},{2,3},{3,4},{4,5},{5,6},{6,7},{7,8},{8,9},{9,10},{10,1... | collective-permute-start | bytes 786440 | tf_op jit(solution)/shard_map/ppermute | solution.py:16
  17.4 9.0 %copy-start.15 = (s32[1,512]{1,0:T(1,128)S(1)}, s32[1,512]{1,0:T(1,128)}, u32[]{:S(2)}) copy-start(s32[1,512]{1,0:T(1,128)} %param.15) | copy-start | bytes 6148
  17.4 149.7 %all-to-all-start = ((f32[16,32,2,8,128]{4,3,2,1,0:T(8,128)}), f32[16,32,2,8,128]{4,3,2,1,0:T(8,128)}, u32[]{:S(2)}, u32[]{:S(2)}) async-start(f32[16,32,2,8,128]{4,3,2,1,0:T(8,128)} %bitcast.97), calls=%async_computation | async-start | bytes 8388608 | tf_op jit(solution)/shard_map/all_to_all | solution.py:119
  31.8 13.6 %copy-start.17 = (s32[2]{0:T(128)S(1)}, s32[2]{0:T(128)}, u32[]{:S(2)}) copy-start(s32[2]{0:T(128)} %constant.371) | copy-start | bytes 28
  31.8 13.7 %copy-start.16 = (s32[2]{0:T(128)S(1)}, s32[2]{0:T(128)}, u32[]{:S(2)}) copy-start(s32[2]{0:T(128)} %constant.374) | copy-start | bytes 28
  31.8 13.8 %copy-start.13 = (f32[1,4,512]{2,1,0:T(4,128)S(1)}, f32[1,4,512]{2,1,0:T(4,128)}, u32[]{:S(2)}) copy-start(f32[1,4,512]{2,1,0:T(4,128)} %param.16) | copy-start | bytes 24580
  62.8 7.5 %copy-start.14 = (f32[1,4]{1,0:T(1,128)S(1)}, f32[1,4]{1,0:T(1,128)}, u32[]{:S(2)}) copy-start(f32[1,4]{1,0:T(1,128)} %param.13) | copy-start | bytes 52
  62.8 8.2 %copy-start.12 = (s32[1,128,16]{1,2,0:T(8,128)S(1)}, s32[1,128,16]{1,2,0:T(8,128)}, u32[]{:S(2)}) copy-start(s32[1,128,16]{1,2,0:T(8,128)} %param.17) | copy-start | bytes 24580
  69.6 4.4 %copy-start.6 = (f32[8,127,128]{2,1,0:T(8,128)S(1)}, f32[8,127,128]{2,1,0:T(8,128)}, u32[]{:S(2)}) copy-start(f32[8,127,128]{2,1,0:T(8,128)} %get-tuple-element.73) | copy-start | bytes 1560580
  78.1 46.5 %collective-permute-start.2 = (f32[4,128,128]{2,1,0:T(8,128)S(1)}, f32[4,128,128]{2,1,0:T(8,128)S(1)}, u32[]{:S(2)}, u32[]{:S(2)}) collective-permute-start(f32[4,128,128]{2,1,0:T(8,128)S(1)} %get-tuple-element.53), channel_id=1, source_target_pairs={{1,0},{2,1},{3,2},{4,3},{5,4},{6,5},{7,6},{8,7},{9,8},{10,9},{11,1... | collective-permute-start | bytes 786440 | tf_op jit(solution)/shard_map/ppermute | solution.py:17
  80.5 44.0 %collective-permute-start.3 = (f32[4,128,128]{2,1,0:T(8,128)S(1)}, f32[4,128,128]{2,1,0:T(8,128)S(1)}, u32[]{:S(2)}, u32[]{:S(2)}) collective-permute-start(f32[4,128,128]{2,1,0:T(8,128)S(1)} %get-tuple-element.54), channel_id=1, source_target_pairs={{0,1},{1,2},{2,3},{3,4},{4,5},{5,6},{6,7},{7,8},{8,9},{9,10},{10,1... | collective-permute-start | bytes 786440 | tf_op jit(solution)/shard_map/ppermute | solution.py:16
  88.3 36.3 %copy-start.8 = (f32[1,131072]{1,0:T(1,128)S(1)}, f32[1,131072]{1,0:T(1,128)}, u32[]{:S(2)}) copy-start(f32[1,131072]{1,0:T(1,128)} %get-tuple-element.11) | copy-start | bytes 1572868
  126.4 14.6 %collective-permute-start.4 = (f32[4,128,128]{2,1,0:T(8,128)S(1)}, f32[4,128,128]{2,1,0:T(8,128)S(1)}, u32[]{:S(2)}, u32[]{:S(2)}) collective-permute-start(f32[4,128,128]{2,1,0:T(8,128)S(1)} %get-tuple-element.35), channel_id=1, source_target_pairs={{1,0},{2,1},{3,2},{4,3},{5,4},{6,5},{7,6},{8,7},{9,8},{10,9},{11,1... | collective-permute-start | bytes 786440 | tf_op jit(solution)/shard_map/ppermute | solution.py:17
  131.5 14.7 %collective-permute-start.5 = (f32[4,128,128]{2,1,0:T(8,128)S(1)}, f32[4,128,128]{2,1,0:T(8,128)S(1)}, u32[]{:S(2)}, u32[]{:S(2)}) collective-permute-start(f32[4,128,128]{2,1,0:T(8,128)S(1)} %get-tuple-element.36), channel_id=1, source_target_pairs={{0,1},{1,2},{2,3},{3,4},{4,5},{5,6},{6,7},{7,8},{8,9},{9,10},{10,1... | collective-permute-start | bytes 786440 | tf_op jit(solution)/shard_map/ppermute | solution.py:16
  137.0 9.1 %copy-start.7 = (f32[1,131072]{1,0:T(1,128)S(1)}, f32[1,131072]{1,0:T(1,128)}, u32[]{:S(2)}) copy-start(f32[1,131072]{1,0:T(1,128)} %get-tuple-element.10) | copy-start | bytes 1572868
  148.8 120.5 %collective-permute-start.14 = (f32[4,128,128]{2,1,0:T(8,128)}, f32[4,128,128]{2,1,0:T(8,128)S(1)}, u32[]{:S(2)}, u32[]{:S(2)}) collective-permute-start(f32[4,128,128]{2,1,0:T(8,128)} %get-tuple-element.17), channel_id=1, source_target_pairs={{1,0},{2,1},{3,2},{4,3},{5,4},{6,5},{7,6},{8,7},{9,8},{10,9},{11,1... | collective-permute-start | bytes 786440 | tf_op jit(solution)/shard_map/ppermute | solution.py:17
  150.7 118.6 %collective-permute-start.15 = (f32[4,128,128]{2,1,0:T(8,128)}, f32[4,128,128]{2,1,0:T(8,128)}, u32[]{:S(2)}, u32[]{:S(2)}) collective-permute-start(f32[4,128,128]{2,1,0:T(8,128)} %get-tuple-element.18), channel_id=1, source_target_pairs={{0,1},{1,2},{2,3},{3,4},{4,5},{5,6},{6,7},{7,8},{8,9},{9,10},{10,1... | collective-permute-start | bytes 786440 | tf_op jit(solution)/shard_map/ppermute | solution.py:16
  173.4 13.3 %collective-permute-start.6 = (f32[4,128,128]{2,1,0:T(8,128)S(1)}, f32[4,128,128]{2,1,0:T(8,128)S(1)}, u32[]{:S(2)}, u32[]{:S(2)}) collective-permute-start(f32[4,128,128]{2,1,0:T(8,128)S(1)} %bitcast.109), channel_id=1, source_target_pairs={{1,0},{2,1},{3,2},{4,3},{5,4},{6,5},{7,6},{8,7},{9,8},{10,9},{11,1... | collective-permute-start | bytes 786440 | tf_op jit(solution)/shard_map/ppermute | solution.py:17
  175.3 16.7 %collective-permute-start.7 = (f32[4,128,128]{2,1,0:T(8,128)S(1)}, f32[4,128,128]{2,1,0:T(8,128)S(1)}, u32[]{:S(2)}, u32[]{:S(2)}) collective-permute-start(f32[4,128,128]{2,1,0:T(8,128)S(1)} %bitcast.108), channel_id=1, source_target_pairs={{0,1},{1,2},{2,3},{3,4},{4,5},{5,6},{6,7},{7,8},{8,9},{9,10},{10,1... | collective-permute-start | bytes 786440 | tf_op jit(solution)/shard_map/ppermute | solution.py:16
  195.4 13.7 %collective-permute-start.8 = (f32[4,128,128]{2,1,0:T(8,128)S(1)}, f32[4,128,128]{2,1,0:T(8,128)S(1)}, u32[]{:S(2)}, u32[]{:S(2)}) collective-permute-start(f32[4,128,128]{2,1,0:T(8,128)S(1)} %get-tuple-element.141), channel_id=1, source_target_pairs={{1,0},{2,1},{3,2},{4,3},{5,4},{6,5},{7,6},{8,7},{9,8},{10,9},{11,1... | collective-permute-start | bytes 786440 | tf_op jit(solution)/shard_map/ppermute | solution.py:17
  197.3 17.1 %collective-permute-start.9 = (f32[4,128,128]{2,1,0:T(8,128)S(1)}, f32[4,128,128]{2,1,0:T(8,128)S(1)}, u32[]{:S(2)}, u32[]{:S(2)}) collective-permute-start(f32[4,128,128]{2,1,0:T(8,128)S(1)} %get-tuple-element.142), channel_id=1, source_target_pairs={{0,1},{1,2},{2,3},{3,4},{4,5},{5,6},{6,7},{7,8},{8,9},{9,10},{10,1... | collective-permute-start | bytes 786440 | tf_op jit(solution)/shard_map/ppermute | solution.py:16
  217.8 13.7 %collective-permute-start.10 = (f32[4,128,128]{2,1,0:T(8,128)S(1)}, f32[4,128,128]{2,1,0:T(8,128)S(1)}, u32[]{:S(2)}, u32[]{:S(2)}) collective-permute-start(f32[4,128,128]{2,1,0:T(8,128)S(1)} %get-tuple-element.123), channel_id=1, source_target_pairs={{1,0},{2,1},{3,2},{4,3},{5,4},{6,5},{7,6},{8,7},{9,8},{10,9},{11,1... | collective-permute-start | bytes 786440 | tf_op jit(solution)/shard_map/ppermute | solution.py:17
  219.8 17.1 %collective-permute-start.11 = (f32[4,128,128]{2,1,0:T(8,128)S(1)}, f32[4,128,128]{2,1,0:T(8,128)S(1)}, u32[]{:S(2)}, u32[]{:S(2)}) collective-permute-start(f32[4,128,128]{2,1,0:T(8,128)S(1)} %get-tuple-element.124), channel_id=1, source_target_pairs={{0,1},{1,2},{2,3},{3,4},{4,5},{5,6},{6,7},{7,8},{8,9},{9,10},{10,1... | collective-permute-start | bytes 786440 | tf_op jit(solution)/shard_map/ppermute | solution.py:16
  240.2 19.2 %copy-start.2 = (f32[1,2,8,128,128]{4,3,2,1,0:T(8,128)S(1)}, f32[1,2,8,128,128]{4,3,2,1,0:T(8,128)}, u32[]{:S(2)}) copy-start(f32[1,2,8,128,128]{4,3,2,1,0:T(8,128)} %param.12) | copy-start | bytes 3145732
  240.3 13.8 %collective-permute-start.12 = (f32[4,128,128]{2,1,0:T(8,128)S(1)}, f32[4,128,128]{2,1,0:T(8,128)S(1)}, u32[]{:S(2)}, u32[]{:S(2)}) collective-permute-start(f32[4,128,128]{2,1,0:T(8,128)S(1)} %get-tuple-element.105), channel_id=1, source_target_pairs={{1,0},{2,1},{3,2},{4,3},{5,4},{6,5},{7,6},{8,7},{9,8},{10,9},{11,1... | collective-permute-start | bytes 786440 | tf_op jit(solution)/shard_map/ppermute | solution.py:17
  242.4 17.1 %collective-permute-start.13 = (f32[4,128,128]{2,1,0:T(8,128)S(1)}, f32[4,128,128]{2,1,0:T(8,128)S(1)}, u32[]{:S(2)}, u32[]{:S(2)}) collective-permute-start(f32[4,128,128]{2,1,0:T(8,128)S(1)} %get-tuple-element.106), channel_id=1, source_target_pairs={{0,1},{1,2},{2,3},{3,4},{4,5},{5,6},{6,7},{7,8},{8,9},{9,10},{10,1... | collective-permute-start | bytes 786440 | tf_op jit(solution)/shard_map/ppermute | solution.py:16
  262.5 6.9 %copy-start.4 = (f32[8,127,128]{2,1,0:T(8,128)S(1)}, f32[8,127,128]{2,1,0:T(8,128)}, u32[]{:S(2)}) copy-start(f32[8,127,128]{2,1,0:T(8,128)} %get-tuple-element.19) | copy-start | bytes 1560580
  262.5 6.9 %copy-start.5 = (f32[8,127,128]{2,1,0:T(8,128)S(1)}, f32[8,127,128]{2,1,0:T(8,128)}, u32[]{:S(2)}) copy-start(f32[8,127,128]{2,1,0:T(8,128)} %get-tuple-element.20) | copy-start | bytes 1560580
  264.0 16.8 %all-to-all-start.1 = ((f32[16,9,8,128]{3,2,1,0:T(8,128)}), f32[16,9,8,128]{3,2,1,0:T(8,128)S(1)}, u32[]{:S(2)}, u32[]{:S(2)}) async-start(f32[16,9,8,128]{3,2,1,0:T(8,128)} %copy.30), calls=%async_computation.1 | async-start | bytes 1179648 | tf_op jit(solution)/shard_map/all_to_all | solution.py:184
  (4 other events, 14.7 us)

commit v9 on v8

--- a/solution.py
+++ b/solution.py
@@ -161,7 +161,10 @@
         .add(traces, mode="drop")
     )
     for moment in range(horizon, 0, -1):
-        weighted = extend(courant * adjoints[moment])
+        scaled = courant * adjoints[moment]
+        if moment == 1:
+            fields[1], scaled = lax.optimization_barrier((fields[1], scaled))
+        weighted = extend(scaled)
         adjoints[moment - 1] = retreat(
             adjoints[moment + 1],
             adjoints[moment],

time: 283 us -> 288 us (1.018)
  waiting for transfers between devices: 87.4 us -> 93.4 us
    ppermute x8, waiting for transfers between devices: 54.7 us -> 64.1 us  [padded_2(): after = lax.ppermute(initial, axis, down)]
    slice x64, local copies, waits for them, and re-layouts: 23.4 us -> 18.6 us  [shifted(): part = lax.slice_in_dim(field, offset, length, axis=axis)]
    ppermute x8, starting transfers between devices: 56.7 us -> 53.5 us  [padded_2(): before = lax.ppermute(last, axis, up)]
    unnamed x38 -> x40, local copies, waits for them, and re-layouts: 0.08 us -> 3.21 us
  transfers between devices with their start and end apart: 18 -> 18, of which waited for: 12 -> 12; matrix products, arithmetic and copies ran while one was open for 35% -> 28% of each run, Pallas kernels for 0% -> 0%
where the time goes in v9:
time: 288 us; the launch traced here: 286 us
  waiting for transfers between devices  93.4 us (32%)
  starting transfers between devices  88.4 us (31%)
  local copies, waits for them, and re-layouts  52.2 us (18%)
  other arithmetic  49.7 us (17%)
    ppermute x8, waiting for transfers between devices, padded_2(): after = lax.ppermute(initial, axis, down)  64.1 us
    ppermute x8, starting transfers between devices, padded_2(): before = lax.ppermute(last, axis, up)  53.5 us
    ppermute x8, waiting for transfers between devices, padded_2(): before = lax.ppermute(last, axis, up)  24.8 us
    ppermute x8, starting transfers between devices, padded_2(): after = lax.ppermute(initial, axis, down)  20.6 us
    slice x64, local copies, waits for them, and re-layouts, shifted(): part = lax.slice_in_dim(field, offset, length, axis=axis)  18.6 us
    unnamed x4, other arithmetic  14.4 us
    all_to_all x1, starting transfers between devices, body(): lax.all_to_all(outgoing, 'space', split_axis=0, concat_axis=0, tiled=True)  9 us
    scatter x1, local copies, waits for them, and re-layouts, body(): where_from = jnp.zeros((per_device,), jnp.int32).at[jnp.where(owned, loca...  8.24 us
  transfers between devices with their start and end apart: 18, of which 12 were waited for; matrix products, arithmetic and copies ran while one was open for 28% of the time, Pallas kernels for 0%

profile of v9, /device:TPU:100, one launch (start us, length us, event | category | flops | bytes accessed | tf_op | source)
XLA Modules:
  0.0 286.5 jit_solution(5674835987564487723)
XLA Ops:
  5.3 7.0 %collective-permute-start.1 = (f32[4,128,128]{2,1,0:T(8,128)}, f32[4,128,128]{2,1,0:T(8,128)}, u32[]{:S(2)}, u32[]{:S(2)}) collective-permute-start(f32[4,128,128]{2,1,0:T(8,128)} %get-tuple-element.78), channel_id=1, source_target_pairs={{0,1},{1,2},{2,3},{3,4},{4,5},{5,6},{6,7},{7,8},{8,9},{9,10},{10,1... | collective-permute-start | bytes 786440 | tf_op jit(solution)/shard_map/ppermute | solution.py:16
  13.9 3.5 %gather_fusion = f32[512,2,8,128]{3,2,1,0:T(8,128)} fusion(f32[129,2,8,128]{3,2,0,1:T(8,128)S(1)} %concatenate.123, s32[1024]{0:T(1024)S(1)} %pad_clamp_fusion.1), kind=kCustom, calls=%fused_computation | custom fusion | bytes 8390656 | tf_op jit(solution)/shard_map/jit(_take)/gather | solution.py:117
  17.5 9.0 %all-to-all-start = ((f32[16,32,2,8,128]{4,3,2,1,0:T(8,128)}), f32[16,32,2,8,128]{4,3,2,1,0:T(8,128)}, u32[]{:S(2)}, u32[]{:S(2)}) async-start(f32[16,32,2,8,128]{4,3,2,1,0:T(8,128)} %bitcast.97), calls=%async_computation | async-start | bytes 8388608 | tf_op jit(solution)/shard_map/all_to_all | solution.py:119
  29.1 14.2 %scatter_custom_fusion.2 = f32[524292]{0:T(1024)S(1)} fusion(s32[2048]{0:T(1024)S(1)} %bitcast.117, f32[2048]{0:T(1024)S(1)} %bitcast.118, f32[]{:T(128)} %constant.52.clone.1), kind=kCustom, calls=%fused_computation.53 | custom fusion | flops 2048 | bytes 2097172
  46.0 6.5 %fusion.246 = (f32[1,131072]{1,0:T(1,128)}, f32[1,131072]{1,0:T(1,128)S(1)}, f32[1,131072]{1,0:T(1,128)S(1)}, f32[1,131072]{1,0:T(1,128)S(1)}) fusion(f32[4,131073]{1,0:T(4,128)} %reshape.304), kind=kLoop, calls=%fused_computation.402 | loop fusion | bytes 4194304 | tf_op jit(solution)/shard_map/slice | solution.py:172
  52.5 2.8 select_reduce_fusion
  55.4 8.2 %scatter_custom_fusion = s32[128]{0:T(128)S(1)} fusion(s32[2048]{0:T(1024)S(1)} %bitcast.116, s32[2048]{0:T(1024)S(1)} %add_bitcast_fusion, s32[]{:T(128)} %constant.91.clone.1), kind=kCustom, calls=%fused_computation.395 | custom fusion | bytes 516 | tf_op jit(solution)/shard_map/scatter | solution.py:130
  70.4 3.1 %fusion.244 = (f32[8,128,128]{2,1,0:T(8,128)S(1)}, f32[8,128,128]{2,1,0:T(8,128)S(1)}) fusion(f32[8,128,128]{2,1,0:T(8,128)S(1)} %copy-done, f32[8,128,128]{2,1,0:T(8,128)S(1)} %bitcast.105, f32[8,128,124]{2,1,0:T(8,128)S(1)} %get-tuple-element.94, f32[8,128,124]{2,1,0:T(8,128)S(1)} %get-tuple-element.93, f32[8,128,125]{2,1,0:T(8,128)S(1)} %get-tuple-element.92, ...), kind=kLoop, calls=%fused_computation.401 | loop fusion | flops 6553600 | bytes 12419072 | tf_op jit(solution)/shard_map/mul | solution.py:164
  76.1 6.9 %collective-permute-start.3 = (f32[4,128,128]{2,1,0:T(8,128)S(1)}, f32[4,128,128]{2,1,0:T(8,128)S(1)}, u32[]{:S(2)}, u32[]{:S(2)}) collective-permute-start(f32[4,128,128]{2,1,0:T(8,128)S(1)} %get-tuple-element.60), channel_id=1, source_target_pairs={{0,1},{1,2},{2,3},{3,4},{4,5},{5,6},{6,7},{7,8},{8,9},{9,10},{10,1... | collective-permute-start | bytes 786440 | tf_op jit(solution)/shard_map/ppermute | solution.py:16
  84.1 40.3 %collective-permute-done.2 = f32[4,128,128]{2,1,0:T(8,128)S(1)} collective-permute-done((f32[4,128,128]{2,1,0:T(8,128)S(1)}, f32[4,128,128]{2,1,0:T(8,128)S(1)}, u32[]{:S(2)}, u32[]{:S(2)}) %collective-permute-start.2) | collective-permute-done | bytes 262176 | tf_op jit(solution)/shard_map/ppermute | solution.py:17
  126.3 5.3 %collective-permute-start.4 = (f32[4,128,128]{2,1,0:T(8,128)S(1)}, f32[4,128,128]{2,1,0:T(8,128)S(1)}, u32[]{:S(2)}, u32[]{:S(2)}) collective-permute-start(f32[4,128,128]{2,1,0:T(8,128)S(1)} %get-tuple-element.41), channel_id=1, source_target_pairs={{1,0},{2,1},{3,2},{4,3},{5,4},{6,5},{7,6},{8,7},{9,8},{10,9},{11,1... | collective-permute-start | bytes 786440 | tf_op jit(solution)/shard_map/ppermute | solution.py:17
  131.6 4.5 %collective-permute-start.5 = (f32[4,128,128]{2,1,0:T(8,128)S(1)}, f32[4,128,128]{2,1,0:T(8,128)S(1)}, u32[]{:S(2)}, u32[]{:S(2)}) collective-permute-start(f32[4,128,128]{2,1,0:T(8,128)S(1)} %get-tuple-element.42), channel_id=1, source_target_pairs={{0,1},{1,2},{2,3},{3,4},{4,5},{5,6},{6,7},{7,8},{8,9},{9,10},{10,1... | collective-permute-start | bytes 786440 | tf_op jit(solution)/shard_map/ppermute | solution.py:16
  137.3 3.9 %collective-permute-done.4 = f32[4,128,128]{2,1,0:T(8,128)S(1)} collective-permute-done((f32[4,128,128]{2,1,0:T(8,128)S(1)}, f32[4,128,128]{2,1,0:T(8,128)S(1)}, u32[]{:S(2)}, u32[]{:S(2)}) %collective-permute-start.4) | collective-permute-done | bytes 262176 | tf_op jit(solution)/shard_map/ppermute | solution.py:17
  141.1 4.8 %collective-permute-done.5 = f32[4,128,128]{2,1,0:T(8,128)S(1)} collective-permute-done((f32[4,128,128]{2,1,0:T(8,128)S(1)}, f32[4,128,128]{2,1,0:T(8,128)S(1)}, u32[]{:S(2)}, u32[]{:S(2)}) %collective-permute-start.5) | collective-permute-done | bytes 262176 | tf_op jit(solution)/shard_map/ppermute | solution.py:16
  147.8 3.8 %gather_fusion.1 = f32[128,2,8,128]{3,2,1,0:T(8,128)} fusion(f32[512,2,8,128]{3,2,1,0:T(8,128)} %bitcast.17, s32[1024]{0:T(1024)S(1)} %pad_clamp_fusion), kind=kCustom, calls=%fused_computation.1 | custom fusion | bytes 2097664 | tf_op jit(solution)/shard_map/jit(_take)/gather | solution.py:132
  163.5 5.2 %collective-permute-start.15 = (f32[4,128,128]{2,1,0:T(8,128)S(1)}, f32[4,128,128]{2,1,0:T(8,128)S(1)}, u32[]{:S(2)}, u32[]{:S(2)}) collective-permute-start(f32[4,128,128]{2,1,0:T(8,128)S(1)} %get-tuple-element.38), channel_id=1, source_target_pairs={{0,1},{1,2},{2,3},{3,4},{4,5},{5,6},{6,7},{7,8},{8,9},{9,10},{10,1... | collective-permute-start | bytes 786440 | tf_op jit(solution)/shard_map/ppermute | solution.py:16
  173.3 7.1 %collective-permute-start.7 = (f32[4,128,128]{2,1,0:T(8,128)S(1)}, f32[4,128,128]{2,1,0:T(8,128)S(1)}, u32[]{:S(2)}, u32[]{:S(2)}) collective-permute-start(f32[4,128,128]{2,1,0:T(8,128)S(1)} %bitcast.108), channel_id=1, source_target_pairs={{0,1},{1,2},{2,3},{3,4},{4,5},{5,6},{6,7},{7,8},{8,9},{9,10},{10,1... | collective-permute-start | bytes 786440 | tf_op jit(solution)/shard_map/ppermute | solution.py:16
  180.6 7.9 %collective-permute-done.6 = f32[4,128,128]{2,1,0:T(8,128)S(1)} collective-permute-done((f32[4,128,128]{2,1,0:T(8,128)S(1)}, f32[4,128,128]{2,1,0:T(8,128)S(1)}, u32[]{:S(2)}, u32[]{:S(2)}) %collective-permute-start.6) | collective-permute-done | bytes 262176 | tf_op jit(solution)/shard_map/ppermute | solution.py:17
  188.5 4.0 %collective-permute-done.7 = f32[4,128,128]{2,1,0:T(8,128)S(1)} collective-permute-done((f32[4,128,128]{2,1,0:T(8,128)S(1)}, f32[4,128,128]{2,1,0:T(8,128)S(1)}, u32[]{:S(2)}, u32[]{:S(2)}) %collective-permute-start.7) | collective-permute-done | bytes 262176 | tf_op jit(solution)/shard_map/ppermute | solution.py:16
  199.4 7.7 %collective-permute-start.9 = (f32[4,128,128]{2,1,0:T(8,128)S(1)}, f32[4,128,128]{2,1,0:T(8,128)S(1)}, u32[]{:S(2)}, u32[]{:S(2)}) collective-permute-start(f32[4,128,128]{2,1,0:T(8,128)S(1)} %get-tuple-element.148), channel_id=1, source_target_pairs={{0,1},{1,2},{2,3},{3,4},{4,5},{5,6},{6,7},{7,8},{8,9},{9,10},{10,1... | collective-permute-start | bytes 786440 | tf_op jit(solution)/shard_map/ppermute | solution.py:16
  207.4 3.9 %collective-permute-done.8 = f32[4,128,128]{2,1,0:T(8,128)S(1)} collective-permute-done((f32[4,128,128]{2,1,0:T(8,128)S(1)}, f32[4,128,128]{2,1,0:T(8,128)S(1)}, u32[]{:S(2)}, u32[]{:S(2)}) %collective-permute-start.8) | collective-permute-done | bytes 262176 | tf_op jit(solution)/shard_map/ppermute | solution.py:17
  211.3 5.3 %collective-permute-done.9 = f32[4,128,128]{2,1,0:T(8,128)S(1)} collective-permute-done((f32[4,128,128]{2,1,0:T(8,128)S(1)}, f32[4,128,128]{2,1,0:T(8,128)S(1)}, u32[]{:S(2)}, u32[]{:S(2)}) %collective-permute-start.9) | collective-permute-done | bytes 262176 | tf_op jit(solution)/shard_map/ppermute | solution.py:16
  222.0 7.5 %collective-permute-start.11 = (f32[4,128,128]{2,1,0:T(8,128)S(1)}, f32[4,128,128]{2,1,0:T(8,128)S(1)}, u32[]{:S(2)}, u32[]{:S(2)}) collective-permute-start(f32[4,128,128]{2,1,0:T(8,128)S(1)} %get-tuple-element.130), channel_id=1, source_target_pairs={{0,1},{1,2},{2,3},{3,4},{4,5},{5,6},{6,7},{7,8},{8,9},{9,10},{10,1... | collective-permute-start | bytes 786440 | tf_op jit(solution)/shard_map/ppermute | solution.py:16
  229.8 4.0 %collective-permute-done.10 = f32[4,128,128]{2,1,0:T(8,128)S(1)} collective-permute-done((f32[4,128,128]{2,1,0:T(8,128)S(1)}, f32[4,128,128]{2,1,0:T(8,128)S(1)}, u32[]{:S(2)}, u32[]{:S(2)}) %collective-permute-start.10) | collective-permute-done | bytes 262176 | tf_op jit(solution)/shard_map/ppermute | solution.py:17
  233.8 5.3 %collective-permute-done.11 = f32[4,128,128]{2,1,0:T(8,128)S(1)} collective-permute-done((f32[4,128,128]{2,1,0:T(8,128)S(1)}, f32[4,128,128]{2,1,0:T(8,128)S(1)}, u32[]{:S(2)}, u32[]{:S(2)}) %collective-permute-start.11) | collective-permute-done | bytes 262176 | tf_op jit(solution)/shard_map/ppermute | solution.py:16
  244.8 7.5 %collective-permute-start.13 = (f32[4,128,128]{2,1,0:T(8,128)S(1)}, f32[4,128,128]{2,1,0:T(8,128)S(1)}, u32[]{:S(2)}, u32[]{:S(2)}) collective-permute-start(f32[4,128,128]{2,1,0:T(8,128)S(1)} %get-tuple-element.112), channel_id=1, source_target_pairs={{0,1},{1,2},{2,3},{3,4},{4,5},{5,6},{6,7},{7,8},{8,9},{9,10},{10,1... | collective-permute-start | bytes 786440 | tf_op jit(solution)/shard_map/ppermute | solution.py:16
  252.4 4.1 %collective-permute-done.12 = f32[4,128,128]{2,1,0:T(8,128)S(1)} collective-permute-done((f32[4,128,128]{2,1,0:T(8,128)S(1)}, f32[4,128,128]{2,1,0:T(8,128)S(1)}, u32[]{:S(2)}, u32[]{:S(2)}) %collective-permute-start.12) | collective-permute-done | bytes 262176 | tf_op jit(solution)/shard_map/ppermute | solution.py:17
  256.5 5.3 %collective-permute-done.13 = f32[4,128,128]{2,1,0:T(8,128)S(1)} collective-permute-done((f32[4,128,128]{2,1,0:T(8,128)S(1)}, f32[4,128,128]{2,1,0:T(8,128)S(1)}, u32[]{:S(2)}, u32[]{:S(2)}) %collective-permute-start.13) | collective-permute-done | bytes 262176 | tf_op jit(solution)/shard_map/ppermute | solution.py:16
  261.9 3.0 %fusion.25 = f32[8,128,128]{2,1,0:T(8,128)S(1)} fusion(f32[8,128,128]{2,1,0:T(8,128)S(1)} %fusion.79, f32[8,128,128]{2,1,0:T(8,128)S(1)} %copy-done, f32[8,128,128]{2,1,0:T(8,128)S(1)} %fusion.52, f32[4,128,128]{2,1,0:T(8,128)S(1)} %collective-permute-done.13, f32[4,128,128]{2,1,0:T(8,128)S(1)} %collective-permute-done.12, ...), kind=kLoop, calls=%fused_computation.121 | loop fusion | flops 9437184 | bytes 14516776 | tf_op jit(solution)/shard_map/add | solution.py:176
  266.5 5.3 %all-to-all-start.1 = ((f32[16,9,8,128]{3,2,1,0:T(8,128)}), f32[16,9,8,128]{3,2,1,0:T(8,128)}, u32[]{:S(2)}, u32[]{:S(2)}) async-start(f32[16,9,8,128]{3,2,1,0:T(8,128)} %copy.30), calls=%async_computation.1 | async-start | bytes 1179648 | tf_op jit(solution)/shard_map/all_to_all | solution.py:187
  272.7 5.1 %fusion.208 = f32[1,8,128,128]{3,2,1,0:T(8,128)S(1)} fusion(f32[8,128,128]{2,1,0:T(8,128)} %bitcast.106, f32[12,128,128]{2,1,0:T(8,128)} %get-tuple-element.40, f32[12,128,128]{2,1,0:T(8,128)S(1)} %constant_dynamic-update-slice_fusion, f32[8,128,124]{2,1,0:T(8,128)} %get-tuple-element.36, f32[8,128,124]{2,1,0:T(8,128)} %get-tuple-element.35, ...), kind=kLoop, calls=%fused_computation.305 | loop fusion | flops 5373952 | bytes 15040512 | tf_op jit(solution)/shard_map/stack | solution.py:190
  278.9 4.4 %all-to-all-done.1 = f32[16,9,8,128]{3,2,1,0:T(8,128)} async-done(((f32[16,9,8,128]{3,2,1,0:T(8,128)}), f32[16,9,8,128]{3,2,1,0:T(8,128)}, u32[]{:S(2)}, u32[]{:S(2)}) %all-to-all-start.1) | async-done | bytes 589856 | tf_op jit(solution)/shard_map/all_to_all | solution.py:187
  (172 shorter events, 67.5 us)
Async XLA Ops:
  0.6 11.7 %copy-start.11 = (s32[1,2048]{1,0:T(1,128)S(1)}, s32[1,2048]{1,0:T(1,128)}, u32[]{:S(2)}) copy-start(s32[1,2048]{1,0:T(1,128)} %param.11) | copy-start | bytes 24580
  0.6 13.2 %copy-start.10 = (f32[1,2,128,8,128]{4,3,2,1,0:T(8,128)S(1)}, f32[1,2,128,8,128]{4,3,2,1,0:T(8,128)}, u32[]{:S(2)}) copy-start(f32[1,2,128,8,128]{4,3,2,1,0:T(8,128)} %param.10) | copy-start | bytes 3145732
  2.9 66.0 %collective-permute-start = (f32[4,128,128]{2,1,0:T(8,128)}, f32[4,128,128]{2,1,0:T(8,128)}, u32[]{:S(2)}, u32[]{:S(2)}) collective-permute-start(f32[4,128,128]{2,1,0:T(8,128)} %get-tuple-element.77), channel_id=1, source_target_pairs={{1,0},{2,1},{3,2},{4,3},{5,4},{6,5},{7,6},{8,7},{9,8},{10,9},{11,1... | collective-permute-start | bytes 786440 | tf_op jit(solution)/shard_map/ppermute | solution.py:17
  5.3 63.6 %collective-permute-start.1 = (f32[4,128,128]{2,1,0:T(8,128)}, f32[4,128,128]{2,1,0:T(8,128)}, u32[]{:S(2)}, u32[]{:S(2)}) collective-permute-start(f32[4,128,128]{2,1,0:T(8,128)} %get-tuple-element.78), channel_id=1, source_target_pairs={{0,1},{1,2},{2,3},{3,4},{4,5},{5,6},{6,7},{7,8},{8,9},{9,10},{10,1... | collective-permute-start | bytes 786440 | tf_op jit(solution)/shard_map/ppermute | solution.py:16
  17.5 9.0 %copy-start.15 = (s32[1,512]{1,0:T(1,128)S(1)}, s32[1,512]{1,0:T(1,128)}, u32[]{:S(2)}) copy-start(s32[1,512]{1,0:T(1,128)} %param.15) | copy-start | bytes 6148
  17.5 130.3 %all-to-all-start = ((f32[16,32,2,8,128]{4,3,2,1,0:T(8,128)}), f32[16,32,2,8,128]{4,3,2,1,0:T(8,128)}, u32[]{:S(2)}, u32[]{:S(2)}) async-start(f32[16,32,2,8,128]{4,3,2,1,0:T(8,128)} %bitcast.97), calls=%async_computation | async-start | bytes 8388608 | tf_op jit(solution)/shard_map/all_to_all | solution.py:119
  26.5 2.4 copy-start.17
  26.5 2.5 copy-start.16
  26.5 2.6 copy-start.13
  46.0 17.7 %copy-start.14 = (f32[1,4]{1,0:T(1,128)S(1)}, f32[1,4]{1,0:T(1,128)}, u32[]{:S(2)}) copy-start(f32[1,4]{1,0:T(1,128)} %param.13) | copy-start | bytes 52
  46.0 18.4 %copy-start.12 = (s32[1,128,16]{1,2,0:T(8,128)S(1)}, s32[1,128,16]{1,2,0:T(8,128)}, u32[]{:S(2)}) copy-start(s32[1,128,16]{1,2,0:T(8,128)} %param.17) | copy-start | bytes 24580
  68.4 1.8 copy-start.6
  68.4 2.0 copy-start.7
  73.5 51.0 %collective-permute-start.2 = (f32[4,128,128]{2,1,0:T(8,128)S(1)}, f32[4,128,128]{2,1,0:T(8,128)S(1)}, u32[]{:S(2)}, u32[]{:S(2)}) collective-permute-start(f32[4,128,128]{2,1,0:T(8,128)S(1)} %get-tuple-element.59), channel_id=1, source_target_pairs={{1,0},{2,1},{3,2},{4,3},{5,4},{6,5},{7,6},{8,7},{9,8},{10,9},{11,1... | collective-permute-start | bytes 786440 | tf_op jit(solution)/shard_map/ppermute | solution.py:17
  76.1 48.4 %collective-permute-start.3 = (f32[4,128,128]{2,1,0:T(8,128)S(1)}, f32[4,128,128]{2,1,0:T(8,128)S(1)}, u32[]{:S(2)}, u32[]{:S(2)}) collective-permute-start(f32[4,128,128]{2,1,0:T(8,128)S(1)} %get-tuple-element.60), channel_id=1, source_target_pairs={{0,1},{1,2},{2,3},{3,4},{4,5},{5,6},{6,7},{7,8},{8,9},{9,10},{10,1... | collective-permute-start | bytes 786440 | tf_op jit(solution)/shard_map/ppermute | solution.py:16
  126.3 14.8 %collective-permute-start.4 = (f32[4,128,128]{2,1,0:T(8,128)S(1)}, f32[4,128,128]{2,1,0:T(8,128)S(1)}, u32[]{:S(2)}, u32[]{:S(2)}) collective-permute-start(f32[4,128,128]{2,1,0:T(8,128)S(1)} %get-tuple-element.41), channel_id=1, source_target_pairs={{1,0},{2,1},{3,2},{4,3},{5,4},{6,5},{7,6},{8,7},{9,8},{10,9},{11,1... | collective-permute-start | bytes 786440 | tf_op jit(solution)/shard_map/ppermute | solution.py:17
  131.6 14.3 %collective-permute-start.5 = (f32[4,128,128]{2,1,0:T(8,128)S(1)}, f32[4,128,128]{2,1,0:T(8,128)S(1)}, u32[]{:S(2)}, u32[]{:S(2)}) collective-permute-start(f32[4,128,128]{2,1,0:T(8,128)S(1)} %get-tuple-element.42), channel_id=1, source_target_pairs={{0,1},{1,2},{2,3},{3,4},{4,5},{5,6},{6,7},{7,8},{8,9},{9,10},{10,1... | collective-permute-start | bytes 786440 | tf_op jit(solution)/shard_map/ppermute | solution.py:16
  163.5 32.3 %collective-permute-start.15 = (f32[4,128,128]{2,1,0:T(8,128)S(1)}, f32[4,128,128]{2,1,0:T(8,128)S(1)}, u32[]{:S(2)}, u32[]{:S(2)}) collective-permute-start(f32[4,128,128]{2,1,0:T(8,128)S(1)} %get-tuple-element.38), channel_id=1, source_target_pairs={{0,1},{1,2},{2,3},{3,4},{4,5},{5,6},{6,7},{7,8},{8,9},{9,10},{10,1... | collective-permute-start | bytes 786440 | tf_op jit(solution)/shard_map/ppermute | solution.py:16
  168.7 103.0 %collective-permute-start.14 = (f32[4,128,128]{2,1,0:T(8,128)}, f32[4,128,128]{2,1,0:T(8,128)}, u32[]{:S(2)}, u32[]{:S(2)}) collective-permute-start(f32[4,128,128]{2,1,0:T(8,128)} %get-tuple-element.37), channel_id=1, source_target_pairs={{1,0},{2,1},{3,2},{4,3},{5,4},{6,5},{7,6},{8,7},{9,8},{10,9},{11,1... | collective-permute-start | bytes 786440 | tf_op jit(solution)/shard_map/ppermute | solution.py:17
  170.9 17.6 %collective-permute-start.6 = (f32[4,128,128]{2,1,0:T(8,128)S(1)}, f32[4,128,128]{2,1,0:T(8,128)S(1)}, u32[]{:S(2)}, u32[]{:S(2)}) collective-permute-start(f32[4,128,128]{2,1,0:T(8,128)S(1)} %bitcast.109), channel_id=1, source_target_pairs={{1,0},{2,1},{3,2},{4,3},{5,4},{6,5},{7,6},{8,7},{9,8},{10,9},{11,1... | collective-permute-start | bytes 786440 | tf_op jit(solution)/shard_map/ppermute | solution.py:17
  173.3 19.2 %collective-permute-start.7 = (f32[4,128,128]{2,1,0:T(8,128)S(1)}, f32[4,128,128]{2,1,0:T(8,128)S(1)}, u32[]{:S(2)}, u32[]{:S(2)}) collective-permute-start(f32[4,128,128]{2,1,0:T(8,128)S(1)} %bitcast.108), channel_id=1, source_target_pairs={{0,1},{1,2},{2,3},{3,4},{4,5},{5,6},{6,7},{7,8},{8,9},{9,10},{10,1... | collective-permute-start | bytes 786440 | tf_op jit(solution)/shard_map/ppermute | solution.py:16
  197.5 13.8 %collective-permute-start.8 = (f32[4,128,128]{2,1,0:T(8,128)S(1)}, f32[4,128,128]{2,1,0:T(8,128)S(1)}, u32[]{:S(2)}, u32[]{:S(2)}) collective-permute-start(f32[4,128,128]{2,1,0:T(8,128)S(1)} %get-tuple-element.147), channel_id=1, source_target_pairs={{1,0},{2,1},{3,2},{4,3},{5,4},{6,5},{7,6},{8,7},{9,8},{10,9},{11,1... | collective-permute-start | bytes 786440 | tf_op jit(solution)/shard_map/ppermute | solution.py:17
  199.4 17.2 %collective-permute-start.9 = (f32[4,128,128]{2,1,0:T(8,128)S(1)}, f32[4,128,128]{2,1,0:T(8,128)S(1)}, u32[]{:S(2)}, u32[]{:S(2)}) collective-permute-start(f32[4,128,128]{2,1,0:T(8,128)S(1)} %get-tuple-element.148), channel_id=1, source_target_pairs={{0,1},{1,2},{2,3},{3,4},{4,5},{5,6},{6,7},{7,8},{8,9},{9,10},{10,1... | collective-permute-start | bytes 786440 | tf_op jit(solution)/shard_map/ppermute | solution.py:16
  220.1 13.7 %collective-permute-start.10 = (f32[4,128,128]{2,1,0:T(8,128)S(1)}, f32[4,128,128]{2,1,0:T(8,128)S(1)}, u32[]{:S(2)}, u32[]{:S(2)}) collective-permute-start(f32[4,128,128]{2,1,0:T(8,128)S(1)} %get-tuple-element.129), channel_id=1, source_target_pairs={{1,0},{2,1},{3,2},{4,3},{5,4},{6,5},{7,6},{8,7},{9,8},{10,9},{11,1... | collective-permute-start | bytes 786440 | tf_op jit(solution)/shard_map/ppermute | solution.py:17
  222.0 17.1 %collective-permute-start.11 = (f32[4,128,128]{2,1,0:T(8,128)S(1)}, f32[4,128,128]{2,1,0:T(8,128)S(1)}, u32[]{:S(2)}, u32[]{:S(2)}) collective-permute-start(f32[4,128,128]{2,1,0:T(8,128)S(1)} %get-tuple-element.130), channel_id=1, source_target_pairs={{0,1},{1,2},{2,3},{3,4},{4,5},{5,6},{6,7},{7,8},{8,9},{9,10},{10,1... | collective-permute-start | bytes 786440 | tf_op jit(solution)/shard_map/ppermute | solution.py:16
  242.7 19.2 %copy-start.2 = (f32[1,2,8,128,128]{4,3,2,1,0:T(8,128)S(1)}, f32[1,2,8,128,128]{4,3,2,1,0:T(8,128)}, u32[]{:S(2)}) copy-start(f32[1,2,8,128,128]{4,3,2,1,0:T(8,128)} %param.12) | copy-start | bytes 3145732
  242.7 13.8 %collective-permute-start.12 = (f32[4,128,128]{2,1,0:T(8,128)S(1)}, f32[4,128,128]{2,1,0:T(8,128)S(1)}, u32[]{:S(2)}, u32[]{:S(2)}) collective-permute-start(f32[4,128,128]{2,1,0:T(8,128)S(1)} %get-tuple-element.111), channel_id=1, source_target_pairs={{1,0},{2,1},{3,2},{4,3},{5,4},{6,5},{7,6},{8,7},{9,8},{10,9},{11,1... | collective-permute-start | bytes 786440 | tf_op jit(solution)/shard_map/ppermute | solution.py:17
  244.8 17.1 %collective-permute-start.13 = (f32[4,128,128]{2,1,0:T(8,128)S(1)}, f32[4,128,128]{2,1,0:T(8,128)S(1)}, u32[]{:S(2)}, u32[]{:S(2)}) collective-permute-start(f32[4,128,128]{2,1,0:T(8,128)S(1)} %get-tuple-element.112), channel_id=1, source_target_pairs={{0,1},{1,2},{2,3},{3,4},{4,5},{5,6},{6,7},{7,8},{8,9},{9,10},{10,1... | collective-permute-start | bytes 786440 | tf_op jit(solution)/shard_map/ppermute | solution.py:16
  261.9 3.0 %copy-start.3 = (f32[128,1024]{1,0:T(8,128)S(1)}, f32[128,1024]{1,0:T(8,128)}, u32[]{:S(2)}) copy-start(f32[128,1024]{1,0:T(8,128)} %convert_reduce_fusion) | copy-start | bytes 1572868
  265.5 7.2 %copy-start.8 = (f32[8,127,128]{2,1,0:T(8,128)S(1)}, f32[8,127,128]{2,1,0:T(8,128)}, u32[]{:S(2)}) copy-start(f32[8,127,128]{2,1,0:T(8,128)} %get-tuple-element.21) | copy-start | bytes 1560580
  265.6 7.2 %copy-start.9 = (f32[8,127,128]{2,1,0:T(8,128)S(1)}, f32[8,127,128]{2,1,0:T(8,128)}, u32[]{:S(2)}) copy-start(f32[8,127,128]{2,1,0:T(8,128)} %get-tuple-element.22) | copy-start | bytes 1560580
  266.5 16.9 %all-to-all-start.1 = ((f32[16,9,8,128]{3,2,1,0:T(8,128)}), f32[16,9,8,128]{3,2,1,0:T(8,128)}, u32[]{:S(2)}, u32[]{:S(2)}) async-start(f32[16,9,8,128]{3,2,1,0:T(8,128)} %copy.30), calls=%async_computation.1 | async-start | bytes 1179648 | tf_op jit(solution)/shard_map/all_to_all | solution.py:187
  (4 other events, 5.6 us)

commit v10 on v4

--- a/solution.py
+++ b/solution.py
@@ -112,6 +112,33 @@
     by_block = jnp.concatenate([by_block, jnp.zeros_like(by_block[:1])], axis=0)
     outgoing = jnp.take(by_block, source_of, axis=0, mode="clip")
     outgoing = outgoing.reshape(devices, capacity, 2, block_rows, breadth)
+    wavelet_row = wavelet[0]
+    receivers = receiver_cell[0]
+    traces = residual[0]
+    horizon = wavelet_row.shape[0]
+    adjoints = [None] * (horizon + 2)
+    adjoints[horizon + 1] = adjoint_state[0, 0]
+    adjoints[horizon] = adjoint_state[0, 1]
+    cells = length * height * breadth
+    local_cells = receivers - first_row * height * breadth
+    inside = (local_cells >= 0) & (local_cells < cells)
+    steps = lax.broadcasted_iota(jnp.int32, traces.shape, 0)
+    spots = jnp.where(inside[None, :], local_cells[None, :], cells)
+    injections = (
+        jnp.zeros((horizon, cells + 1), jnp.float32)
+        .at[steps, jnp.broadcast_to(spots, traces.shape)]
+        .add(traces, mode="drop")
+    )
+    for moment in range(horizon, 0, -1):
+        weighted = extend(courant * adjoints[moment])
+        if moment == horizon - 1:
+            outgoing, weighted = lax.optimization_barrier((outgoing, weighted))
+        adjoints[moment - 1] = retreat(
+            adjoints[moment + 1],
+            adjoints[moment],
+            weighted,
+            injections[moment - 1, :cells].reshape(length, height, breadth),
+        )
     incoming = lax.all_to_all(outgoing, "space", split_axis=0, concat_axis=0, tiled=True)
     incoming = incoming.reshape(devices * capacity, 2, block_rows, breadth)
     matches = (peers[:, None] == lanes[None, :]).astype(jnp.int32)
@@ -127,14 +154,7 @@
     )
     placed = jnp.transpose(jnp.take(incoming, where_from, axis=0), (1, 0, 2, 3))
     levels = placed.reshape(2, length, height, breadth)
-    wavelet_row = wavelet[0]
-    receivers = receiver_cell[0]
-    traces = residual[0]
-    horizon = wavelet_row.shape[0]
     fields = [levels[0], levels[1]]
-    adjoints = [None] * (horizon + 2)
-    adjoints[horizon + 1] = adjoint_state[0, 0]
-    adjoints[horizon] = adjoint_state[0, 1]
     for moment in range(1, horizon + 1):
         fields.append(
             advance(
@@ -145,24 +165,6 @@
                 source_cell,
                 first_row,
             )
-        )
-    cells = length * height * breadth
-    local_cells = receivers - first_row * height * breadth
-    inside = (local_cells >= 0) & (local_cells < cells)
-    steps = lax.broadcasted_iota(jnp.int32, traces.shape, 0)
-    spots = jnp.where(inside[None, :], local_cells[None, :], cells)
-    injections = (
-        jnp.zeros((horizon, cells + 1), jnp.float32)
-        .at[steps, jnp.broadcast_to(spots, traces.shape)]
-        .add(traces, mode="drop")
-    )
-    for moment in range(horizon, 0, -1):
-        weighted = extend(courant * adjoints[moment])
-        adjoints[moment - 1] = retreat(
-            adjoints[moment + 1],
-            adjoints[moment],
-            weighted,
-            injections[moment - 1, :cells].reshape(length, height, breadth),
         )
     partial_value = jnp.zeros((length, height, breadth), jnp.float32)
     for moment in range(1, horizon + 1):

time: 261 us -> 285 us (1.092)
  waiting for transfers between devices: 76.3 us -> 102 us
    all_to_all x1, waiting for transfers between devices: 0.01 us -> 66.6 us  [body(): lax.all_to_all(outgoing, 'space', split_axis=0, concat_axis=0, tiled=True)]
    ppermute x8, waiting for transfers between devices: 53.3 us -> 12.1 us  [padded_2(): after = lax.ppermute(initial, axis, down)]
    ppermute x8, starting transfers between devices: 54.7 us -> 49.7 us  [padded_2(): before = lax.ppermute(last, axis, up)]
  transfers between devices with their start and end apart: 18 -> 18, of which waited for: 8 -> 9; matrix products, arithmetic and copies ran while one was open for 30% -> 25% of each run, Pallas kernels for 0% -> 0%
where the time goes in v10:
time: 285 us; the launch traced here: 284 us
  waiting for transfers between devices  102 us (36%)
  starting transfers between devices  88.9 us (31%)
  other arithmetic  58.4 us (20%)
  local copies, waits for them, and re-layouts  31.9 us (11%)
    all_to_all x1, waiting for transfers between devices, body(): lax.all_to_all(outgoing, 'space', split_axis=0, concat_axis=0, tiled=True)  66.6 us
    ppermute x8, starting transfers between devices, padded_2(): before = lax.ppermute(last, axis, up)  49.7 us
    ppermute x8, starting transfers between devices, padded_2(): after = lax.ppermute(initial, axis, down)  24 us
    ppermute x8, waiting for transfers between devices, padded_2(): before = lax.ppermute(last, axis, up)  16.7 us
    unnamed x4, other arithmetic  14.5 us
    ppermute x8, waiting for transfers between devices, padded_2(): after = lax.ppermute(initial, axis, down)  12.1 us
    mul x4, other arithmetic, body(): weighted = extend(courant * adjoints[moment])  10.3 us
    add x3, other arithmetic, inject_dense(): return field + jnp.where(cells == local_cell, values[0], 0.0)  8.87 us
  transfers between devices with their start and end apart: 18, of which 9 were waited for; matrix products, arithmetic and copies ran while one was open for 25% of the time, Pallas kernels for 0%

profile of v10, /device:TPU:100, one launch (start us, length us, event | category | flops | bytes accessed | tf_op | source)
XLA Modules:
  0.0 284.4 jit_solution(5601699219072605939)
XLA Ops:
  5.2 7.0 %collective-permute-start.1 = (f32[4,128,128]{2,1,0:T(8,128)}, f32[4,128,128]{2,1,0:T(8,128)S(1)}, u32[]{:S(2)}, u32[]{:S(2)}) collective-permute-start(f32[4,128,128]{2,1,0:T(8,128)} %get-tuple-element.33), channel_id=1, source_target_pairs={{0,1},{1,2},{2,3},{3,4},{4,5},{5,6},{6,7},{7,8},{8,9},{9,10},{10,1... | collective-permute-start | bytes 786440 | tf_op jit(solution)/shard_map/ppermute | solution.py:16
  12.5 14.3 %scatter_custom_fusion.2 = f32[524292]{0:T(1024)S(1)} fusion(s32[2048]{0:T(1024)S(1)} %bitcast.110, f32[2048]{0:T(1024)S(1)} %bitcast.111, f32[]{:T(128)} %constant.52.clone.1), kind=kCustom, calls=%fused_computation.90 | custom fusion | flops 2048 | bytes 2097172
  29.5 6.8 %fusion.313 = (f32[1,131072]{1,0:T(1,128)}, f32[1,131072]{1,0:T(1,128)}, f32[1,131072]{1,0:T(1,128)}, f32[1,131072]{1,0:T(1,128)}) fusion(f32[4,131073]{1,0:T(4,128)} %reshape.304), kind=kLoop, calls=%fused_computation.552 | loop fusion | bytes 4194304 | tf_op jit(solution)/shard_map/slice | solution.py:140
  39.0 3.3 %fusion.311 = (f32[8,128,128]{2,1,0:T(8,128)S(1)}, f32[8,128,128]{2,1,0:T(8,128)S(1)}) fusion(f32[8,128,128]{2,1,0:T(8,128)S(1)} %copy-done, f32[8,128,128]{2,1,0:T(8,128)S(1)} %bitcast.99, f32[16,136,136]{2,1,0:T(8,128)S(1)} %select_maximum_fusion.12, f32[8,128,128]{2,1,0:T(8,128)S(1)} %bitcast_multiply_fusion, f32[4,128,128]{2,1,0:T(8,128)} %copy-done.16, ...), kind=kLoop, calls=%fused_computation.551 | loop fusion | flops 6553600 | bytes 12582912 | tf_op jit(solution)/shard_map/mul | solution.py:133
  43.2 3.1 %collective-permute-start.2 = (f32[4,128,128]{2,1,0:T(8,128)S(1)}, f32[4,128,128]{2,1,0:T(8,128)S(1)}, u32[]{:S(2)}, u32[]{:S(2)}) collective-permute-start(f32[4,128,128]{2,1,0:T(8,128)S(1)} %get-tuple-element.31), channel_id=1, source_target_pairs={{0,1},{1,2},{2,3},{3,4},{4,5},{5,6},{6,7},{7,8},{8,9},{9,10},{10,1... | collective-permute-start | bytes 786440 | tf_op jit(solution)/shard_map/ppermute | solution.py:16
  46.2 4.3 %collective-permute-start.3 = (f32[4,128,128]{2,1,0:T(8,128)S(1)}, f32[4,128,128]{2,1,0:T(8,128)}, u32[]{:S(2)}, u32[]{:S(2)}) collective-permute-start(f32[4,128,128]{2,1,0:T(8,128)S(1)} %get-tuple-element.32), channel_id=1, source_target_pairs={{1,0},{2,1},{3,2},{4,3},{5,4},{6,5},{7,6},{8,7},{9,8},{10,9},{11,1... | collective-permute-start | bytes 786440 | tf_op jit(solution)/shard_map/ppermute | solution.py:17
  51.6 3.5 %gather_fusion = f32[512,2,8,128]{3,2,1,0:T(8,128)} fusion(f32[129,2,8,128]{3,2,0,1:T(8,128)S(1)} %concatenate.124, s32[1024]{0:T(1024)S(1)} %pad_clamp_fusion.1), kind=kCustom, calls=%fused_computation | custom fusion | bytes 8390656 | tf_op jit(solution)/shard_map/jit(_take)/gather | solution.py:113
  55.0 4.7 %collective-permute-done.2 = f32[4,128,128]{2,1,0:T(8,128)S(1)} collective-permute-done((f32[4,128,128]{2,1,0:T(8,128)S(1)}, f32[4,128,128]{2,1,0:T(8,128)S(1)}, u32[]{:S(2)}, u32[]{:S(2)}) %collective-permute-start.2) | collective-permute-done | bytes 262176 | tf_op jit(solution)/shard_map/ppermute | solution.py:16
  60.8 8.7 %all-to-all-start = ((f32[16,32,2,8,128]{4,3,2,1,0:T(8,128)}), f32[16,32,2,8,128]{4,3,2,1,0:T(8,128)}, u32[]{:S(2)}, u32[]{:S(2)}) async-start(f32[16,32,2,8,128]{4,3,2,1,0:T(8,128)} %bitcast.86), calls=%async_computation | async-start | bytes 8388608 | tf_op jit(solution)/shard_map/all_to_all | solution.py:142
  73.3 8.0 %scatter_custom_fusion.1 = s32[128]{0:T(128)S(1)} fusion(s32[2048]{0:T(1024)S(1)} %bitcast.109, s32[2048]{0:T(1024)S(1)} %add_bitcast_fusion, s32[]{:T(128)} %constant.91.clone.1), kind=kCustom, calls=%fused_computation.545 | custom fusion | bytes 516 | tf_op jit(solution)/shard_map/scatter | solution.py:153
  90.5 7.0 %collective-permute-start.5 = (f32[4,128,128]{2,1,0:T(8,128)}, f32[4,128,128]{2,1,0:T(8,128)}, u32[]{:S(2)}, u32[]{:S(2)}) collective-permute-start(f32[4,128,128]{2,1,0:T(8,128)} %get-tuple-element.23), channel_id=1, source_target_pairs={{0,1},{1,2},{2,3},{3,4},{4,5},{5,6},{6,7},{7,8},{8,9},{9,10},{10,1... | collective-permute-start | bytes 786440 | tf_op jit(solution)/shard_map/ppermute | solution.py:16
  97.5 66.6 %all-to-all-done = f32[16,32,2,8,128]{4,3,2,1,0:T(8,128)} async-done(((f32[16,32,2,8,128]{4,3,2,1,0:T(8,128)}), f32[16,32,2,8,128]{4,3,2,1,0:T(8,128)}, u32[]{:S(2)}, u32[]{:S(2)}) %all-to-all-start) | async-done | bytes 4194336 | tf_op jit(solution)/shard_map/all_to_all | solution.py:142
  164.1 3.8 %gather_fusion.1 = f32[128,2,8,128]{3,2,1,0:T(8,128)} fusion(f32[512,2,8,128]{3,2,1,0:T(8,128)} %bitcast.17, s32[1024]{0:T(1024)S(1)} %pad_clamp_fusion), kind=kCustom, calls=%fused_computation.1 | custom fusion | bytes 2097664 | tf_op jit(solution)/shard_map/jit(_take)/gather | solution.py:155
  169.3 4.9 %collective-permute-start.6 = (f32[4,128,128]{2,1,0:T(8,128)S(1)}, f32[4,128,128]{2,1,0:T(8,128)S(1)}, u32[]{:S(2)}, u32[]{:S(2)}) collective-permute-start(f32[4,128,128]{2,1,0:T(8,128)S(1)} %bitcast.102), channel_id=1, source_target_pairs={{1,0},{2,1},{3,2},{4,3},{5,4},{6,5},{7,6},{8,7},{9,8},{10,9},{11,1... | collective-permute-start | bytes 786440 | tf_op jit(solution)/shard_map/ppermute | solution.py:17
  174.2 4.6 %collective-permute-start.7 = (f32[4,128,128]{2,1,0:T(8,128)S(1)}, f32[4,128,128]{2,1,0:T(8,128)S(1)}, u32[]{:S(2)}, u32[]{:S(2)}) collective-permute-start(f32[4,128,128]{2,1,0:T(8,128)S(1)} %bitcast.101), channel_id=1, source_target_pairs={{0,1},{1,2},{2,3},{3,4},{4,5},{5,6},{6,7},{7,8},{8,9},{9,10},{10,1... | collective-permute-start | bytes 786440 | tf_op jit(solution)/shard_map/ppermute | solution.py:16
  178.9 6.3 %collective-permute-done.6 = f32[4,128,128]{2,1,0:T(8,128)S(1)} collective-permute-done((f32[4,128,128]{2,1,0:T(8,128)S(1)}, f32[4,128,128]{2,1,0:T(8,128)S(1)}, u32[]{:S(2)}, u32[]{:S(2)}) %collective-permute-start.6) | collective-permute-done | bytes 262176 | tf_op jit(solution)/shard_map/ppermute | solution.py:17
  187.5 2.9 %fusion.135 = f32[8,128,128]{2,1,0:T(8,128)S(1)} fusion(f32[8,128,128]{2,1,0:T(8,128)S(1)} %copy-done, f32[8,128,128]{2,1,0:T(8,128)S(1)} %bitcast.88, f32[4,128,128]{2,1,0:T(8,128)S(1)} %collective-permute-done.7, f32[4,128,128]{2,1,0:T(8,128)S(1)} %collective-permute-done.6, f32[16,136,136]{2,1,0:T(8,128)S(1)} %select_maximum_fusion.8, ...), kind=kLoop, calls=%fused_computation.266 | loop fusion | flops 7077888 | bytes 11010600 | tf_op jit(solution)/shard_map/add | solution.py:63
  190.4 4.2 %collective-permute-start.8 = (f32[4,128,128]{2,1,0:T(8,128)S(1)}, f32[4,128,128]{2,1,0:T(8,128)S(1)}, u32[]{:S(2)}, u32[]{:S(2)}) collective-permute-start(f32[4,128,128]{2,1,0:T(8,128)S(1)} %get-tuple-element.29), channel_id=1, source_target_pairs={{1,0},{2,1},{3,2},{4,3},{5,4},{6,5},{7,6},{8,7},{9,8},{10,9},{11,1... | collective-permute-start | bytes 786440 | tf_op jit(solution)/shard_map/ppermute | solution.py:17
  194.7 5.2 %collective-permute-start.9 = (f32[4,128,128]{2,1,0:T(8,128)S(1)}, f32[4,128,128]{2,1,0:T(8,128)S(1)}, u32[]{:S(2)}, u32[]{:S(2)}) collective-permute-start(f32[4,128,128]{2,1,0:T(8,128)S(1)} %get-tuple-element.30), channel_id=1, source_target_pairs={{0,1},{1,2},{2,3},{3,4},{4,5},{5,6},{6,7},{7,8},{8,9},{9,10},{10,1... | collective-permute-start | bytes 786440 | tf_op jit(solution)/shard_map/ppermute | solution.py:16
  201.5 3.3 %collective-permute-done.8 = f32[4,128,128]{2,1,0:T(8,128)S(1)} collective-permute-done((f32[4,128,128]{2,1,0:T(8,128)S(1)}, f32[4,128,128]{2,1,0:T(8,128)S(1)}, u32[]{:S(2)}, u32[]{:S(2)}) %collective-permute-start.8) | collective-permute-done | bytes 262176 | tf_op jit(solution)/shard_map/ppermute | solution.py:17
  204.8 5.0 %collective-permute-done.9 = f32[4,128,128]{2,1,0:T(8,128)S(1)} collective-permute-done((f32[4,128,128]{2,1,0:T(8,128)S(1)}, f32[4,128,128]{2,1,0:T(8,128)S(1)}, u32[]{:S(2)}, u32[]{:S(2)}) %collective-permute-start.9) | collective-permute-done | bytes 262176 | tf_op jit(solution)/shard_map/ppermute | solution.py:16
  210.4 3.0 %fusion.108 = f32[8,128,128]{2,1,0:T(8,128)S(1)} fusion(f32[8,128,128]{2,1,0:T(8,128)S(1)} %copy-done, f32[8,128,128]{2,1,0:T(8,128)S(1)} %fusion.135, f32[4,128,128]{2,1,0:T(8,128)S(1)} %collective-permute-done.9, f32[4,128,128]{2,1,0:T(8,128)S(1)} %collective-permute-done.8, f32[16,136,136]{2,1,0:T(8,128)S(1)} %select_maximum_fusion.6, ...), kind=kLoop, calls=%fused_computation.239 | loop fusion | flops 7077888 | bytes 11010600 | tf_op jit(solution)/shard_map/add | solution.py:63
  215.4 7.8 %collective-permute-start.11 = (f32[4,128,128]{2,1,0:T(8,128)S(1)}, f32[4,128,128]{2,1,0:T(8,128)S(1)}, u32[]{:S(2)}, u32[]{:S(2)}) collective-permute-start(f32[4,128,128]{2,1,0:T(8,128)S(1)} %get-tuple-element.28), channel_id=1, source_target_pairs={{0,1},{1,2},{2,3},{3,4},{4,5},{5,6},{6,7},{7,8},{8,9},{9,10},{10,1... | collective-permute-start | bytes 786440 | tf_op jit(solution)/shard_map/ppermute | solution.py:16
  223.2 3.3 %fusion.307 = (f32[8,128,128]{2,1,0:T(8,128)S(1)}, f32[8,128,128]{2,1,0:T(8,128)S(1)}) fusion(f32[8,128,128]{2,1,0:T(8,128)S(1)} %copy-done, f32[8,128,128]{2,1,0:T(8,128)S(1)} %bitcast.97, f32[16,136,136]{2,1,0:T(8,128)S(1)} %select_maximum_fusion.10, f32[8,128,128]{2,1,0:T(8,128)S(1)} %get-tuple-element.9, f32[4,128,128]{2,1,0:T(8,128)} %collective-permute-done.5, ...), kind=kLoop, calls=%fused_computation.549 | loop fusion | flops 6553600 | bytes 12582912 | tf_op jit(solution)/shard_map/mul | solution.py:133
  228.5 7.5 %collective-permute-start.15 = (f32[4,128,128]{2,1,0:T(8,128)S(1)}, f32[4,128,128]{2,1,0:T(8,128)S(1)}, u32[]{:S(2)}, u32[]{:S(2)}) collective-permute-start(f32[4,128,128]{2,1,0:T(8,128)S(1)} %get-tuple-element.21), channel_id=1, source_target_pairs={{0,1},{1,2},{2,3},{3,4},{4,5},{5,6},{6,7},{7,8},{8,9},{9,10},{10,1... | collective-permute-start | bytes 786440 | tf_op jit(solution)/shard_map/ppermute | solution.py:16
  236.8 3.0 %fusion.81 = f32[8,128,128]{2,1,0:T(8,128)S(1)} fusion(f32[8,128,128]{2,1,0:T(8,128)S(1)} %copy-done, f32[8,128,128]{2,1,0:T(8,128)S(1)} %fusion.108, f32[4,128,128]{2,1,0:T(8,128)S(1)} %collective-permute-done.11, f32[4,128,128]{2,1,0:T(8,128)S(1)} %collective-permute-done.10, f32[16,136,136]{2,1,0:T(8,128)S(1)} %select_maximum_fusion.4, ...), kind=kLoop, calls=%fused_computation.212 | loop fusion | flops 7077888 | bytes 11010600 | tf_op jit(solution)/shard_map/add | solution.py:63
  241.7 7.5 %collective-permute-start.13 = (f32[4,128,128]{2,1,0:T(8,128)S(1)}, f32[4,128,128]{2,1,0:T(8,128)S(1)}, u32[]{:S(2)}, u32[]{:S(2)}) collective-permute-start(f32[4,128,128]{2,1,0:T(8,128)S(1)} %get-tuple-element.26), channel_id=1, source_target_pairs={{0,1},{1,2},{2,3},{3,4},{4,5},{5,6},{6,7},{7,8},{8,9},{9,10},{10,1... | collective-permute-start | bytes 786440 | tf_op jit(solution)/shard_map/ppermute | solution.py:16
  252.5 5.3 %collective-permute-done.13 = f32[4,128,128]{2,1,0:T(8,128)S(1)} collective-permute-done((f32[4,128,128]{2,1,0:T(8,128)S(1)}, f32[4,128,128]{2,1,0:T(8,128)S(1)}, u32[]{:S(2)}, u32[]{:S(2)}) %collective-permute-start.13) | collective-permute-done | bytes 262176 | tf_op jit(solution)/shard_map/ppermute | solution.py:16
  258.6 3.0 %fusion.54 = f32[8,128,128]{2,1,0:T(8,128)S(1)} fusion(f32[8,128,128]{2,1,0:T(8,128)S(1)} %fusion.108, f32[8,128,128]{2,1,0:T(8,128)S(1)} %copy-done, f32[8,128,128]{2,1,0:T(8,128)S(1)} %fusion.81, f32[4,128,128]{2,1,0:T(8,128)S(1)} %collective-permute-done.13, f32[4,128,128]{2,1,0:T(8,128)S(1)} %collective-permute-done.12, ...), kind=kLoop, calls=%fused_computation.185 | loop fusion | flops 9437184 | bytes 14680616 | tf_op jit(solution)/shard_map/add | solution.py:171
  263.2 6.5 %all-to-all-start.1 = ((f32[16,9,8,128]{3,2,1,0:T(8,128)}), f32[16,9,8,128]{3,2,1,0:T(8,128)}, u32[]{:S(2)}, u32[]{:S(2)}) async-start(f32[16,9,8,128]{3,2,1,0:T(8,128)} %copy.30), calls=%async_computation.1 | async-start | bytes 1179648 | tf_op jit(solution)/shard_map/all_to_all | solution.py:182
  269.7 3.5 %fusion.297 = f32[1,8,128,128]{3,2,1,0:T(8,128)S(1)} fusion(f32[8,128,128]{2,1,0:T(8,128)} %bitcast.96, f32[16,136,136]{2,1,0:T(8,128)S(1)} %select_maximum_fusion, f32[8,128,128]{2,1,0:T(8,128)S(1)} %copy-done.5, f32[4,128,128]{2,1,0:T(8,128)} %copy-done.15, f32[4,128,128]{2,1,0:T(8,128)S(1)} %collective-permute-done.14, f32[8,128,128]{2,1,0:T(8,128)S(1)} %copy-done.3, ...), kind=kLoop, calls=%fused_computation.504 | loop fusion | flops 6422528 | bytes 11534336 | tf_op jit(solution)/shard_map/stack | solution.py:185
  274.3 7.0 %all-to-all-done.1 = f32[16,9,8,128]{3,2,1,0:T(8,128)} async-done(((f32[16,9,8,128]{3,2,1,0:T(8,128)}), f32[16,9,8,128]{3,2,1,0:T(8,128)}, u32[]{:S(2)}, u32[]{:S(2)}) %all-to-all-start.1) | async-done | bytes 589856 | tf_op jit(solution)/shard_map/all_to_all | solution.py:182
  (125 shorter events, 47.3 us)
Async XLA Ops:
  0.6 11.7 %copy-start.23 = (s32[2]{0:T(128)S(1)}, s32[2]{0:T(128)}, u32[]{:S(2)}) copy-start(s32[2]{0:T(128)} %constant.131) | copy-start | bytes 28
  0.6 11.8 %copy-start.22 = (s32[2]{0:T(128)S(1)}, s32[2]{0:T(128)}, u32[]{:S(2)}) copy-start(s32[2]{0:T(128)} %constant.134) | copy-start | bytes 28
  0.7 11.6 %copy-start.21 = (s32[1,512]{1,0:T(1,128)S(1)}, s32[1,512]{1,0:T(1,128)}, u32[]{:S(2)}) copy-start(s32[1,512]{1,0:T(1,128)} %param.15) | copy-start | bytes 6148
  0.7 11.9 %copy-start.19 = (f32[1,4,512]{2,1,0:T(4,128)S(1)}, f32[1,4,512]{2,1,0:T(4,128)}, u32[]{:S(2)}) copy-start(f32[1,4,512]{2,1,0:T(4,128)} %param.16) | copy-start | bytes 24580
  2.8 35.4 %collective-permute-start = (f32[4,128,128]{2,1,0:T(8,128)}, f32[4,128,128]{2,1,0:T(8,128)S(1)}, u32[]{:S(2)}, u32[]{:S(2)}) collective-permute-start(f32[4,128,128]{2,1,0:T(8,128)} %get-tuple-element.34), channel_id=1, source_target_pairs={{1,0},{2,1},{3,2},{4,3},{5,4},{6,5},{7,6},{8,7},{9,8},{10,9},{11,1... | collective-permute-start | bytes 786440 | tf_op jit(solution)/shard_map/ppermute | solution.py:17
  5.2 33.0 %collective-permute-start.1 = (f32[4,128,128]{2,1,0:T(8,128)}, f32[4,128,128]{2,1,0:T(8,128)S(1)}, u32[]{:S(2)}, u32[]{:S(2)}) collective-permute-start(f32[4,128,128]{2,1,0:T(8,128)} %get-tuple-element.33), channel_id=1, source_target_pairs={{0,1},{1,2},{2,3},{3,4},{4,5},{5,6},{6,7},{7,8},{8,9},{9,10},{10,1... | collective-permute-start | bytes 786440 | tf_op jit(solution)/shard_map/ppermute | solution.py:16
  43.2 16.5 %collective-permute-start.2 = (f32[4,128,128]{2,1,0:T(8,128)S(1)}, f32[4,128,128]{2,1,0:T(8,128)S(1)}, u32[]{:S(2)}, u32[]{:S(2)}) collective-permute-start(f32[4,128,128]{2,1,0:T(8,128)S(1)} %get-tuple-element.31), channel_id=1, source_target_pairs={{0,1},{1,2},{2,3},{3,4},{4,5},{5,6},{6,7},{7,8},{8,9},{9,10},{10,1... | collective-permute-start | bytes 786440 | tf_op jit(solution)/shard_map/ppermute | solution.py:16
  46.2 13.5 %collective-permute-start.3 = (f32[4,128,128]{2,1,0:T(8,128)S(1)}, f32[4,128,128]{2,1,0:T(8,128)}, u32[]{:S(2)}, u32[]{:S(2)}) collective-permute-start(f32[4,128,128]{2,1,0:T(8,128)S(1)} %get-tuple-element.32), channel_id=1, source_target_pairs={{1,0},{2,1},{3,2},{4,3},{5,4},{6,5},{7,6},{8,7},{9,8},{10,9},{11,1... | collective-permute-start | bytes 786440 | tf_op jit(solution)/shard_map/ppermute | solution.py:17
  51.5 8.2 %copy-start.11 = (f32[8,128,128]{2,1,0:T(8,128)S(1)}, f32[8,128,128]{2,1,0:T(8,128)}, u32[]{:S(2)}) copy-start(f32[8,128,128]{2,1,0:T(8,128)} %copy-done.10) | copy-start | bytes 1572868
  60.7 12.4 %copy-start.18 = (s32[1,128,16]{1,2,0:T(8,128)S(1)}, s32[1,128,16]{1,2,0:T(8,128)}, u32[]{:S(2)}) copy-start(s32[1,128,16]{1,2,0:T(8,128)} %param.17) | copy-start | bytes 24580
  60.7 20.7 %copy-start.20 = (f32[1,4]{1,0:T(1,128)S(1)}, f32[1,4]{1,0:T(1,128)}, u32[]{:S(2)}) copy-start(f32[1,4]{1,0:T(1,128)} %param.13) | copy-start | bytes 52
  60.8 103.3 %all-to-all-start = ((f32[16,32,2,8,128]{4,3,2,1,0:T(8,128)}), f32[16,32,2,8,128]{4,3,2,1,0:T(8,128)}, u32[]{:S(2)}, u32[]{:S(2)}) async-start(f32[16,32,2,8,128]{4,3,2,1,0:T(8,128)} %bitcast.86), calls=%async_computation | async-start | bytes 8388608 | tf_op jit(solution)/shard_map/all_to_all | solution.py:142
  87.1 136.0 %copy-start.1 = (f32[8,128,128]{2,1,0:T(8,128)}, f32[8,128,128]{2,1,0:T(8,128)S(1)}, u32[]{:S(2)}) copy-start(f32[8,128,128]{2,1,0:T(8,128)S(1)} %get-tuple-element.10) | copy-start | bytes 1572868
  88.0 111.8 %collective-permute-start.4 = (f32[4,128,128]{2,1,0:T(8,128)}, f32[4,128,128]{2,1,0:T(8,128)S(1)}, u32[]{:S(2)}, u32[]{:S(2)}) collective-permute-start(f32[4,128,128]{2,1,0:T(8,128)} %get-tuple-element.24), channel_id=1, source_target_pairs={{1,0},{2,1},{3,2},{4,3},{5,4},{6,5},{7,6},{8,7},{9,8},{10,9},{11,1... | collective-permute-start | bytes 786440 | tf_op jit(solution)/shard_map/ppermute | solution.py:17
  90.5 109.4 %collective-permute-start.5 = (f32[4,128,128]{2,1,0:T(8,128)}, f32[4,128,128]{2,1,0:T(8,128)}, u32[]{:S(2)}, u32[]{:S(2)}) collective-permute-start(f32[4,128,128]{2,1,0:T(8,128)} %get-tuple-element.23), channel_id=1, source_target_pairs={{0,1},{1,2},{2,3},{3,4},{4,5},{5,6},{6,7},{7,8},{8,9},{9,10},{10,1... | collective-permute-start | bytes 786440 | tf_op jit(solution)/shard_map/ppermute | solution.py:16
  169.3 15.8 %collective-permute-start.6 = (f32[4,128,128]{2,1,0:T(8,128)S(1)}, f32[4,128,128]{2,1,0:T(8,128)S(1)}, u32[]{:S(2)}, u32[]{:S(2)}) collective-permute-start(f32[4,128,128]{2,1,0:T(8,128)S(1)} %bitcast.102), channel_id=1, source_target_pairs={{1,0},{2,1},{3,2},{4,3},{5,4},{6,5},{7,6},{8,7},{9,8},{10,9},{11,1... | collective-permute-start | bytes 786440 | tf_op jit(solution)/shard_map/ppermute | solution.py:17
  174.2 12.6 %collective-permute-start.7 = (f32[4,128,128]{2,1,0:T(8,128)S(1)}, f32[4,128,128]{2,1,0:T(8,128)S(1)}, u32[]{:S(2)}, u32[]{:S(2)}) collective-permute-start(f32[4,128,128]{2,1,0:T(8,128)S(1)} %bitcast.101), channel_id=1, source_target_pairs={{0,1},{1,2},{2,3},{3,4},{4,5},{5,6},{6,7},{7,8},{8,9},{9,10},{10,1... | collective-permute-start | bytes 786440 | tf_op jit(solution)/shard_map/ppermute | solution.py:16
  190.4 14.4 %collective-permute-start.8 = (f32[4,128,128]{2,1,0:T(8,128)S(1)}, f32[4,128,128]{2,1,0:T(8,128)S(1)}, u32[]{:S(2)}, u32[]{:S(2)}) collective-permute-start(f32[4,128,128]{2,1,0:T(8,128)S(1)} %get-tuple-element.29), channel_id=1, source_target_pairs={{1,0},{2,1},{3,2},{4,3},{5,4},{6,5},{7,6},{8,7},{9,8},{10,9},{11,1... | collective-permute-start | bytes 786440 | tf_op jit(solution)/shard_map/ppermute | solution.py:17
  194.7 15.1 %collective-permute-start.9 = (f32[4,128,128]{2,1,0:T(8,128)S(1)}, f32[4,128,128]{2,1,0:T(8,128)S(1)}, u32[]{:S(2)}, u32[]{:S(2)}) collective-permute-start(f32[4,128,128]{2,1,0:T(8,128)S(1)} %get-tuple-element.30), channel_id=1, source_target_pairs={{0,1},{1,2},{2,3},{3,4},{4,5},{5,6},{6,7},{7,8},{8,9},{9,10},{10,1... | collective-permute-start | bytes 786440 | tf_op jit(solution)/shard_map/ppermute | solution.py:16
  210.4 12.8 %copy-start.13 = (f32[1,131072]{1,0:T(1,128)S(1)}, f32[1,131072]{1,0:T(1,128)}, u32[]{:S(2)}) copy-start(f32[1,131072]{1,0:T(1,128)} %get-tuple-element.14) | copy-start | bytes 1572868
  213.5 22.6 %collective-permute-start.10 = (f32[4,128,128]{2,1,0:T(8,128)S(1)}, f32[4,128,128]{2,1,0:T(8,128)S(1)}, u32[]{:S(2)}, u32[]{:S(2)}) collective-permute-start(f32[4,128,128]{2,1,0:T(8,128)S(1)} %get-tuple-element.27), channel_id=1, source_target_pairs={{1,0},{2,1},{3,2},{4,3},{5,4},{6,5},{7,6},{8,7},{9,8},{10,9},{11,1... | collective-permute-start | bytes 786440 | tf_op jit(solution)/shard_map/ppermute | solution.py:17
  215.4 20.7 %collective-permute-start.11 = (f32[4,128,128]{2,1,0:T(8,128)S(1)}, f32[4,128,128]{2,1,0:T(8,128)S(1)}, u32[]{:S(2)}, u32[]{:S(2)}) collective-permute-start(f32[4,128,128]{2,1,0:T(8,128)S(1)} %get-tuple-element.28), channel_id=1, source_target_pairs={{0,1},{1,2},{2,3},{3,4},{4,5},{5,6},{6,7},{7,8},{8,9},{9,10},{10,1... | collective-permute-start | bytes 786440 | tf_op jit(solution)/shard_map/ppermute | solution.py:16
  226.5 22.8 %copy-start.4 = (f32[8,128,128]{2,1,0:T(8,128)}, f32[8,128,128]{2,1,0:T(8,128)S(1)}, u32[]{:S(2)}) copy-start(f32[8,128,128]{2,1,0:T(8,128)S(1)} %get-tuple-element.7) | copy-start | bytes 1572868
  226.6 32.0 %copy-start.6 = (f32[8,128,128]{2,1,0:T(8,128)}, f32[8,128,128]{2,1,0:T(8,128)S(1)}, u32[]{:S(2)}) copy-start(f32[8,128,128]{2,1,0:T(8,128)S(1)} %get-tuple-element.8) | copy-start | bytes 1572868
  226.6 22.7 %collective-permute-start.14 = (f32[4,128,128]{2,1,0:T(8,128)S(1)}, f32[4,128,128]{2,1,0:T(8,128)S(1)}, u32[]{:S(2)}, u32[]{:S(2)}) collective-permute-start(f32[4,128,128]{2,1,0:T(8,128)S(1)} %get-tuple-element.22), channel_id=1, source_target_pairs={{1,0},{2,1},{3,2},{4,3},{5,4},{6,5},{7,6},{8,7},{9,8},{10,9},{11,1... | collective-permute-start | bytes 786440 | tf_op jit(solution)/shard_map/ppermute | solution.py:17
  228.5 20.8 %collective-permute-start.15 = (f32[4,128,128]{2,1,0:T(8,128)S(1)}, f32[4,128,128]{2,1,0:T(8,128)S(1)}, u32[]{:S(2)}, u32[]{:S(2)}) collective-permute-start(f32[4,128,128]{2,1,0:T(8,128)S(1)} %get-tuple-element.21), channel_id=1, source_target_pairs={{0,1},{1,2},{2,3},{3,4},{4,5},{5,6},{6,7},{7,8},{8,9},{9,10},{10,1... | collective-permute-start | bytes 786440 | tf_op jit(solution)/shard_map/ppermute | solution.py:16
  239.8 12.7 %collective-permute-start.12 = (f32[4,128,128]{2,1,0:T(8,128)S(1)}, f32[4,128,128]{2,1,0:T(8,128)S(1)}, u32[]{:S(2)}, u32[]{:S(2)}) collective-permute-start(f32[4,128,128]{2,1,0:T(8,128)S(1)} %get-tuple-element.25), channel_id=1, source_target_pairs={{1,0},{2,1},{3,2},{4,3},{5,4},{6,5},{7,6},{8,7},{9,8},{10,9},{11,1... | collective-permute-start | bytes 786440 | tf_op jit(solution)/shard_map/ppermute | solution.py:17
  241.7 16.1 %collective-permute-start.13 = (f32[4,128,128]{2,1,0:T(8,128)S(1)}, f32[4,128,128]{2,1,0:T(8,128)S(1)}, u32[]{:S(2)}, u32[]{:S(2)}) collective-permute-start(f32[4,128,128]{2,1,0:T(8,128)S(1)} %get-tuple-element.26), channel_id=1, source_target_pairs={{0,1},{1,2},{2,3},{3,4},{4,5},{5,6},{6,7},{7,8},{8,9},{9,10},{10,1... | collective-permute-start | bytes 786440 | tf_op jit(solution)/shard_map/ppermute | solution.py:16
  249.3 9.2 %copy-start.15 = (f32[4,128,128]{2,1,0:T(8,128)}, f32[4,128,128]{2,1,0:T(8,128)S(1)}, u32[]{:S(2)}) copy-start(f32[4,128,128]{2,1,0:T(8,128)S(1)} %collective-permute-done.15) | copy-start | bytes 786436
  250.0 8.6 %copy-start.2 = (f32[8,128,128]{2,1,0:T(8,128)S(1)}, f32[8,128,128]{2,1,0:T(8,128)}, u32[]{:S(2)}) copy-start(f32[8,128,128]{2,1,0:T(8,128)} %copy-done.1) | copy-start | bytes 1572868
  250.0 8.6 %copy-start.9 = (f32[1,2,8,128,128]{4,3,2,1,0:T(8,128)S(1)}, f32[1,2,8,128,128]{4,3,2,1,0:T(8,128)}, u32[]{:S(2)}) copy-start(f32[1,2,8,128,128]{4,3,2,1,0:T(8,128)} %param.12) | copy-start | bytes 3145732
  263.2 18.1 %all-to-all-start.1 = ((f32[16,9,8,128]{3,2,1,0:T(8,128)}), f32[16,9,8,128]{3,2,1,0:T(8,128)}, u32[]{:S(2)}, u32[]{:S(2)}) async-start(f32[16,9,8,128]{3,2,1,0:T(8,128)} %copy.30), calls=%async_computation.1 | async-start | bytes 1179648 | tf_op jit(solution)/shard_map/all_to_all | solution.py:182
  (10 other events, 38.2 us)

commit v11 on v4

--- a/solution.py
+++ b/solution.py
@@ -135,7 +135,7 @@
     adjoints = [None] * (horizon + 2)
     adjoints[horizon + 1] = adjoint_state[0, 0]
     adjoints[horizon] = adjoint_state[0, 1]
-    for moment in range(1, horizon + 1):
+    for moment in range(1, horizon):
         fields.append(
             advance(
                 fields[-2],
@@ -146,6 +146,9 @@
                 first_row,
             )
         )
+    last_curvature = inject_dense(
+        courant * laplace(extend(fields[-1])), source_cell, wavelet_row[horizon - 1 :], first_row
+    )
     cells = length * height * breadth
     local_cells = receivers - first_row * height * breadth
     inside = (local_cells >= 0) & (local_cells < cells)
@@ -165,10 +168,11 @@
             injections[moment - 1, :cells].reshape(length, height, breadth),
         )
     partial_value = jnp.zeros((length, height, breadth), jnp.float32)
-    for moment in range(1, horizon + 1):
+    for moment in range(1, horizon):
         partial_value = partial_value + adjoints[moment] * (
             fields[moment + 1] - 2.0 * fields[moment] + fields[moment - 1]
         )
+    partial_value = partial_value + adjoints[horizon] * last_curvature
     slab_rows = partial_value.reshape(length * height, breadth)
     row_ids = lax.broadcasted_iota(jnp.int32, (1, 1, length * height), 2)
     counts = jnp.sum((check_rows[0][:, :, None] == row_ids).astype(jnp.float32), axis=1)

time: 261 us -> 261 us (level)
  no operation moved by 1% of the time
where the time goes in v11:
time: 261 us; the launch traced here: 260 us
  starting transfers between devices  90.1 us (35%)
  waiting for transfers between devices  75.9 us (29%)
  other arithmetic  59.5 us (23%)
  local copies, waits for them, and re-layouts  31.5 us (12%)
    ppermute x8, starting transfers between devices, padded_2(): before = lax.ppermute(last, axis, up)  55.1 us
    ppermute x8, waiting for transfers between devices, padded_2(): after = lax.ppermute(initial, axis, down)  52.9 us
    ppermute x8, starting transfers between devices, padded_2(): after = lax.ppermute(initial, axis, down)  20.7 us
    ppermute x8, waiting for transfers between devices, padded_2(): before = lax.ppermute(last, axis, up)  16 us
    unnamed x4, other arithmetic  14.8 us
    mul x4, other arithmetic, body(): weighted = extend(courant * adjoints[moment])  11.5 us
    all_to_all x1, starting transfers between devices, body(): lax.all_to_all(outgoing, 'space', split_axis=0, concat_axis=0, tiled=True)  9.02 us
    add x3, other arithmetic, inject_dense(): return field + jnp.where(cells == local_cell, values[0], 0.0)  8.8 us
  transfers between devices with their start and end apart: 18, of which 8 were waited for; matrix products, arithmetic and copies ran while one was open for 30% of the time, Pallas kernels for 0%

profile of v11, /device:TPU:100, one launch (start us, length us, event | category | flops | bytes accessed | tf_op | source)
XLA Modules:
  0.0 259.8 jit_solution(4632206319296646872)
XLA Ops:
  5.2 7.0 %collective-permute-start.1 = (f32[4,128,128]{2,1,0:T(8,128)}, f32[4,128,128]{2,1,0:T(8,128)S(1)}, u32[]{:S(2)}, u32[]{:S(2)}) collective-permute-start(f32[4,128,128]{2,1,0:T(8,128)} %get-tuple-element.23), channel_id=1, source_target_pairs={{0,1},{1,2},{2,3},{3,4},{4,5},{5,6},{6,7},{7,8},{8,9},{9,10},{10,1... | collective-permute-start | bytes 786440 | tf_op jit(solution)/shard_map/ppermute | solution.py:16
  15.0 3.5 %gather_fusion = f32[512,2,8,128]{3,2,1,0:T(8,128)} fusion(f32[129,2,8,128]{3,2,0,1:T(8,128)S(1)} %concatenate.142, s32[1024]{0:T(1024)S(1)} %pad_clamp_fusion.1), kind=kCustom, calls=%fused_computation | custom fusion | bytes 8390656 | tf_op jit(solution)/shard_map/jit(_take)/gather | solution.py:113
  18.6 9.0 %all-to-all-start = ((f32[16,32,2,8,128]{4,3,2,1,0:T(8,128)}), f32[16,32,2,8,128]{4,3,2,1,0:T(8,128)}, u32[]{:S(2)}, u32[]{:S(2)}) async-start(f32[16,32,2,8,128]{4,3,2,1,0:T(8,128)} %bitcast.86), calls=%async_computation | async-start | bytes 8388608 | tf_op jit(solution)/shard_map/all_to_all | solution.py:115
  27.9 14.6 %scatter_custom_fusion.2 = f32[524292]{0:T(1024)S(1)} fusion(s32[2048]{0:T(1024)S(1)} %bitcast.109, f32[2048]{0:T(1024)S(1)} %bitcast.111, f32[]{:T(128)} %constant.52.clone.1), kind=kCustom, calls=%fused_computation.82 | custom fusion | flops 2048 | bytes 2097172
  45.2 7.1 %fusion.320 = (f32[1,131072]{1,0:T(1,128)}, f32[1,131072]{1,0:T(1,128)}, f32[1,131072]{1,0:T(1,128)}, f32[1,131072]{1,0:T(1,128)}) fusion(f32[4,131073]{1,0:T(4,128)} %reshape.304), kind=kLoop, calls=%fused_computation.566 | loop fusion | bytes 4194304 | tf_op jit(solution)/shard_map/slice | solution.py:168
  52.3 2.8 %select_reduce_fusion = s32[16,128]{0,1:T(8,128)S(1)} fusion(s32[16,128]{0,1:T(8,128)S(1)} %copy.27), kind=kOutput, calls=%fused_computation.86 | output fusion | flops 4388864 | bytes 16384 | tf_op jit(solution)/shard_map/jit(cumsum)/reduce_window_sum | solution.py:119
  55.3 8.2 %scatter_custom_fusion = s32[128]{0:T(128)S(1)} fusion(s32[2048]{0:T(1024)S(1)} %bitcast.110, s32[2048]{0:T(1024)S(1)} %add_bitcast_fusion, s32[]{:T(128)} %constant.91.clone.1), kind=kCustom, calls=%fused_computation.559 | custom fusion | bytes 516 | tf_op jit(solution)/shard_map/scatter | solution.py:126
  67.7 3.4 %fusion.318 = (f32[8,128,128]{2,1,0:T(8,128)S(1)}, f32[8,128,128]{2,1,0:T(8,128)S(1)}) fusion(f32[8,128,128]{2,1,0:T(8,128)S(1)} %copy-done, f32[8,128,128]{2,1,0:T(8,128)S(1)} %bitcast.99, f32[16,136,136]{2,1,0:T(8,128)S(1)} %select_maximum_fusion.14, f32[8,128,128]{2,1,0:T(8,128)S(1)} %bitcast_multiply_fusion, f32[4,128,128]{2,1,0:T(8,128)} %copy-done.14, ...), kind=kLoop, calls=%fused_computation.565 | loop fusion | flops 6553600 | bytes 12582912 | tf_op jit(solution)/shard_map/mul | solution.py:163
  73.7 7.0 %collective-permute-start.3 = (f32[4,128,128]{2,1,0:T(8,128)S(1)}, f32[4,128,128]{2,1,0:T(8,128)S(1)}, u32[]{:S(2)}, u32[]{:S(2)}) collective-permute-start(f32[4,128,128]{2,1,0:T(8,128)S(1)} %get-tuple-element.21), channel_id=1, source_target_pairs={{0,1},{1,2},{2,3},{3,4},{4,5},{5,6},{6,7},{7,8},{8,9},{9,10},{10,1... | collective-permute-start | bytes 786440 | tf_op jit(solution)/shard_map/ppermute | solution.py:16
  81.4 44.3 %collective-permute-done.2 = f32[4,128,128]{2,1,0:T(8,128)S(1)} collective-permute-done((f32[4,128,128]{2,1,0:T(8,128)S(1)}, f32[4,128,128]{2,1,0:T(8,128)S(1)}, u32[]{:S(2)}, u32[]{:S(2)}) %collective-permute-start.2) | collective-permute-done | bytes 262176 | tf_op jit(solution)/shard_map/ppermute | solution.py:17
  126.4 3.4 %fusion.316 = (f32[8,128,128]{2,1,0:T(8,128)S(1)}, f32[8,128,128]{2,1,0:T(8,128)S(1)}) fusion(f32[8,128,128]{2,1,0:T(8,128)S(1)} %copy-done, f32[8,128,128]{2,1,0:T(8,128)S(1)} %bitcast.98, f32[16,136,136]{2,1,0:T(8,128)S(1)} %select_maximum_fusion.12, f32[8,128,128]{2,1,0:T(8,128)S(1)} %get-tuple-element.7, f32[4,128,128]{2,1,0:T(8,128)} %copy-done.16, ...), kind=kLoop, calls=%fused_computation.564 | loop fusion | flops 6553600 | bytes 12582912 | tf_op jit(solution)/shard_map/mul | solution.py:163
  130.8 5.2 %collective-permute-start.4 = (f32[4,128,128]{2,1,0:T(8,128)}, f32[4,128,128]{2,1,0:T(8,128)S(1)}, u32[]{:S(2)}, u32[]{:S(2)}) collective-permute-start(f32[4,128,128]{2,1,0:T(8,128)} %get-tuple-element.20), channel_id=1, source_target_pairs={{1,0},{2,1},{3,2},{4,3},{5,4},{6,5},{7,6},{8,7},{9,8},{10,9},{11,1... | collective-permute-start | bytes 786440 | tf_op jit(solution)/shard_map/ppermute | solution.py:17
  135.9 4.4 %collective-permute-start.5 = (f32[4,128,128]{2,1,0:T(8,128)}, f32[4,128,128]{2,1,0:T(8,128)}, u32[]{:S(2)}, u32[]{:S(2)}) collective-permute-start(f32[4,128,128]{2,1,0:T(8,128)} %get-tuple-element.19), channel_id=1, source_target_pairs={{0,1},{1,2},{2,3},{3,4},{4,5},{5,6},{6,7},{7,8},{8,9},{9,10},{10,1... | collective-permute-start | bytes 786440 | tf_op jit(solution)/shard_map/ppermute | solution.py:16
  140.3 3.8 %gather_fusion.1 = f32[128,2,8,128]{3,2,1,0:T(8,128)} fusion(f32[512,2,8,128]{3,2,1,0:T(8,128)} %bitcast.17, s32[1024]{0:T(1024)S(1)} %pad_clamp_fusion), kind=kCustom, calls=%fused_computation.1 | custom fusion | bytes 2097664 | tf_op jit(solution)/shard_map/jit(_take)/gather | solution.py:128
  145.6 3.0 %collective-permute-start.6 = (f32[4,128,128]{2,1,0:T(8,128)S(1)}, f32[4,128,128]{2,1,0:T(8,128)S(1)}, u32[]{:S(2)}, u32[]{:S(2)}) collective-permute-start(f32[4,128,128]{2,1,0:T(8,128)S(1)} %bitcast.102), channel_id=1, source_target_pairs={{1,0},{2,1},{3,2},{4,3},{5,4},{6,5},{7,6},{8,7},{9,8},{10,9},{11,1... | collective-permute-start | bytes 786440 | tf_op jit(solution)/shard_map/ppermute | solution.py:17
  148.6 6.5 %collective-permute-start.7 = (f32[4,128,128]{2,1,0:T(8,128)S(1)}, f32[4,128,128]{2,1,0:T(8,128)S(1)}, u32[]{:S(2)}, u32[]{:S(2)}) collective-permute-start(f32[4,128,128]{2,1,0:T(8,128)S(1)} %bitcast.101), channel_id=1, source_target_pairs={{0,1},{1,2},{2,3},{3,4},{4,5},{5,6},{6,7},{7,8},{8,9},{9,10},{10,1... | collective-permute-start | bytes 786440 | tf_op jit(solution)/shard_map/ppermute | solution.py:16
  155.2 3.7 %collective-permute-done.6 = f32[4,128,128]{2,1,0:T(8,128)S(1)} collective-permute-done((f32[4,128,128]{2,1,0:T(8,128)S(1)}, f32[4,128,128]{2,1,0:T(8,128)S(1)}, u32[]{:S(2)}, u32[]{:S(2)}) %collective-permute-start.6) | collective-permute-done | bytes 262176 | tf_op jit(solution)/shard_map/ppermute | solution.py:17
  158.9 5.3 %collective-permute-done.7 = f32[4,128,128]{2,1,0:T(8,128)S(1)} collective-permute-done((f32[4,128,128]{2,1,0:T(8,128)S(1)}, f32[4,128,128]{2,1,0:T(8,128)S(1)}, u32[]{:S(2)}, u32[]{:S(2)}) %collective-permute-start.7) | collective-permute-done | bytes 262176 | tf_op jit(solution)/shard_map/ppermute | solution.py:16
  164.9 2.9 %fusion.132 = f32[8,128,128]{2,1,0:T(8,128)S(1)} fusion(f32[8,128,128]{2,1,0:T(8,128)S(1)} %copy-done, f32[8,128,128]{2,1,0:T(8,128)S(1)} %bitcast.88, f32[4,128,128]{2,1,0:T(8,128)S(1)} %collective-permute-done.7, f32[4,128,128]{2,1,0:T(8,128)S(1)} %collective-permute-done.6, f32[16,136,136]{2,1,0:T(8,128)S(1)} %select_maximum_fusion.8, ...), kind=kLoop, calls=%fused_computation.260 | loop fusion | flops 7077888 | bytes 11010600 | tf_op jit(solution)/shard_map/add | solution.py:63
  169.7 7.5 %collective-permute-start.9 = (f32[4,128,128]{2,1,0:T(8,128)S(1)}, f32[4,128,128]{2,1,0:T(8,128)S(1)}, u32[]{:S(2)}, u32[]{:S(2)}) collective-permute-start(f32[4,128,128]{2,1,0:T(8,128)S(1)} %get-tuple-element.30), channel_id=1, source_target_pairs={{0,1},{1,2},{2,3},{3,4},{4,5},{5,6},{6,7},{7,8},{8,9},{9,10},{10,1... | collective-permute-start | bytes 786440 | tf_op jit(solution)/shard_map/ppermute | solution.py:16
  181.4 5.3 %collective-permute-done.9 = f32[4,128,128]{2,1,0:T(8,128)S(1)} collective-permute-done((f32[4,128,128]{2,1,0:T(8,128)S(1)}, f32[4,128,128]{2,1,0:T(8,128)S(1)}, u32[]{:S(2)}, u32[]{:S(2)}) %collective-permute-start.9) | collective-permute-done | bytes 262176 | tf_op jit(solution)/shard_map/ppermute | solution.py:16
  187.4 3.0 %fusion.105 = f32[8,128,128]{2,1,0:T(8,128)S(1)} fusion(f32[8,128,128]{2,1,0:T(8,128)S(1)} %copy-done, f32[8,128,128]{2,1,0:T(8,128)S(1)} %fusion.132, f32[4,128,128]{2,1,0:T(8,128)S(1)} %collective-permute-done.9, f32[4,128,128]{2,1,0:T(8,128)S(1)} %collective-permute-done.8, f32[16,136,136]{2,1,0:T(8,128)S(1)} %select_maximum_fusion.6, ...), kind=kLoop, calls=%fused_computation.233 | loop fusion | flops 7077888 | bytes 11010600 | tf_op jit(solution)/shard_map/add | solution.py:63
  192.4 7.5 %collective-permute-start.11 = (f32[4,128,128]{2,1,0:T(8,128)S(1)}, f32[4,128,128]{2,1,0:T(8,128)S(1)}, u32[]{:S(2)}, u32[]{:S(2)}) collective-permute-start(f32[4,128,128]{2,1,0:T(8,128)S(1)} %get-tuple-element.28), channel_id=1, source_target_pairs={{0,1},{1,2},{2,3},{3,4},{4,5},{5,6},{6,7},{7,8},{8,9},{9,10},{10,1... | collective-permute-start | bytes 786440 | tf_op jit(solution)/shard_map/ppermute | solution.py:16
  200.0 3.4 %fusion.314 = (f32[8,128,128]{2,1,0:T(8,128)S(1)}, f32[8,128,128]{2,1,0:T(8,128)S(1)}) fusion(f32[8,128,128]{2,1,0:T(8,128)S(1)} %copy-done, f32[8,128,128]{2,1,0:T(8,128)S(1)} %bitcast.97, f32[16,136,136]{2,1,0:T(8,128)S(1)} %select_maximum_fusion.10, f32[8,128,128]{2,1,0:T(8,128)S(1)} %get-tuple-element.5, f32[4,128,128]{2,1,0:T(8,128)} %collective-permute-done.5, ...), kind=kLoop, calls=%fused_computation.563 | loop fusion | flops 6553600 | bytes 12582912 | tf_op jit(solution)/shard_map/mul | solution.py:163
  205.4 7.5 %collective-permute-start.15 = (f32[4,128,128]{2,1,0:T(8,128)S(1)}, f32[4,128,128]{2,1,0:T(8,128)S(1)}, u32[]{:S(2)}, u32[]{:S(2)}) collective-permute-start(f32[4,128,128]{2,1,0:T(8,128)S(1)} %get-tuple-element.17), channel_id=1, source_target_pairs={{0,1},{1,2},{2,3},{3,4},{4,5},{5,6},{6,7},{7,8},{8,9},{9,10},{10,1... | collective-permute-start | bytes 786440 | tf_op jit(solution)/shard_map/ppermute | solution.py:16
  213.6 2.9 %fusion.78 = f32[8,128,128]{2,1,0:T(8,128)S(1)} fusion(f32[8,128,128]{2,1,0:T(8,128)S(1)} %copy-done, f32[8,128,128]{2,1,0:T(8,128)S(1)} %fusion.105, f32[4,128,128]{2,1,0:T(8,128)S(1)} %collective-permute-done.11, f32[4,128,128]{2,1,0:T(8,128)S(1)} %collective-permute-done.10, f32[16,136,136]{2,1,0:T(8,128)S(1)} %select_maximum_fusion.4, ...), kind=kLoop, calls=%fused_computation.206 | loop fusion | flops 7077888 | bytes 11010600 | tf_op jit(solution)/shard_map/add | solution.py:63
  218.5 7.5 %collective-permute-start.13 = (f32[4,128,128]{2,1,0:T(8,128)S(1)}, f32[4,128,128]{2,1,0:T(8,128)S(1)}, u32[]{:S(2)}, u32[]{:S(2)}) collective-permute-start(f32[4,128,128]{2,1,0:T(8,128)S(1)} %get-tuple-element.26), channel_id=1, source_target_pairs={{0,1},{1,2},{2,3},{3,4},{4,5},{5,6},{6,7},{7,8},{8,9},{9,10},{10,1... | collective-permute-start | bytes 786440 | tf_op jit(solution)/shard_map/ppermute | solution.py:16
  229.1 5.3 %collective-permute-done.13 = f32[4,128,128]{2,1,0:T(8,128)S(1)} collective-permute-done((f32[4,128,128]{2,1,0:T(8,128)S(1)}, f32[4,128,128]{2,1,0:T(8,128)S(1)}, u32[]{:S(2)}, u32[]{:S(2)}) %collective-permute-start.13) | collective-permute-done | bytes 262176 | tf_op jit(solution)/shard_map/ppermute | solution.py:16
  235.2 3.0 %fusion.51 = f32[8,128,128]{2,1,0:T(8,128)S(1)} fusion(f32[8,128,128]{2,1,0:T(8,128)S(1)} %copy-done, f32[8,128,128]{2,1,0:T(8,128)S(1)} %fusion.78, f32[4,128,128]{2,1,0:T(8,128)S(1)} %collective-permute-done.13, f32[4,128,128]{2,1,0:T(8,128)S(1)} %collective-permute-done.12, f32[16,136,136]{2,1,0:T(8,128)S(1)} %select_maximum_fusion.2, ...), kind=kLoop, calls=%fused_computation.179 | loop fusion | flops 8781824 | bytes 14680616 | tf_op jit(solution)/shard_map/add | solution.py:175
  239.8 5.3 %all-to-all-start.1 = ((f32[16,9,8,128]{3,2,1,0:T(8,128)}), f32[16,9,8,128]{3,2,1,0:T(8,128)}, u32[]{:S(2)}, u32[]{:S(2)}) async-start(f32[16,9,8,128]{3,2,1,0:T(8,128)} %copy.30), calls=%async_computation.1 | async-start | bytes 1179648 | tf_op jit(solution)/shard_map/all_to_all | solution.py:184
  245.1 3.5 %fusion.304 = f32[1,8,128,128]{3,2,1,0:T(8,128)S(1)} fusion(f32[8,128,128]{2,1,0:T(8,128)} %bitcast.96, f32[16,136,136]{2,1,0:T(8,128)S(1)} %select_maximum_fusion, f32[8,128,128]{2,1,0:T(8,128)S(1)} %copy-done.5, f32[4,128,128]{2,1,0:T(8,128)} %copy-done.15, f32[4,128,128]{2,1,0:T(8,128)S(1)} %collective-permute-done.14, f32[8,128,128]{2,1,0:T(8,128)S(1)} %copy-done.3, ...), kind=kLoop, calls=%fused_computation.518 | loop fusion | flops 6422528 | bytes 11534336 | tf_op jit(solution)/shard_map/stack | solution.py:187
  249.7 7.0 %all-to-all-done.1 = f32[16,9,8,128]{3,2,1,0:T(8,128)} async-done(((f32[16,9,8,128]{3,2,1,0:T(8,128)}), f32[16,9,8,128]{3,2,1,0:T(8,128)}, u32[]{:S(2)}, u32[]{:S(2)}) %all-to-all-start.1) | async-done | bytes 589856 | tf_op jit(solution)/shard_map/all_to_all | solution.py:184
  (125 shorter events, 43.7 us)
Async XLA Ops:
  0.6 11.6 %copy-start.17 = (s32[1,2048]{1,0:T(1,128)S(1)}, s32[1,2048]{1,0:T(1,128)}, u32[]{:S(2)}) copy-start(s32[1,2048]{1,0:T(1,128)} %param.11) | copy-start | bytes 24580
  2.8 64.3 %collective-permute-start = (f32[4,128,128]{2,1,0:T(8,128)}, f32[4,128,128]{2,1,0:T(8,128)S(1)}, u32[]{:S(2)}, u32[]{:S(2)}) collective-permute-start(f32[4,128,128]{2,1,0:T(8,128)} %get-tuple-element.24), channel_id=1, source_target_pairs={{1,0},{2,1},{3,2},{4,3},{5,4},{6,5},{7,6},{8,7},{9,8},{10,9},{11,1... | collective-permute-start | bytes 786440 | tf_op jit(solution)/shard_map/ppermute | solution.py:17
  5.2 61.9 %collective-permute-start.1 = (f32[4,128,128]{2,1,0:T(8,128)}, f32[4,128,128]{2,1,0:T(8,128)S(1)}, u32[]{:S(2)}, u32[]{:S(2)}) collective-permute-start(f32[4,128,128]{2,1,0:T(8,128)} %get-tuple-element.23), channel_id=1, source_target_pairs={{0,1},{1,2},{2,3},{3,4},{4,5},{5,6},{6,7},{7,8},{8,9},{9,10},{10,1... | collective-permute-start | bytes 786440 | tf_op jit(solution)/shard_map/ppermute | solution.py:16
  18.5 9.0 %copy-start.21 = (s32[1,512]{1,0:T(1,128)S(1)}, s32[1,512]{1,0:T(1,128)}, u32[]{:S(2)}) copy-start(s32[1,512]{1,0:T(1,128)} %param.15) | copy-start | bytes 6148
  18.5 9.1 %copy-start.23 = (s32[2]{0:T(128)S(1)}, s32[2]{0:T(128)}, u32[]{:S(2)}) copy-start(s32[2]{0:T(128)} %constant.131) | copy-start | bytes 28
  18.5 9.2 %copy-start.22 = (s32[2]{0:T(128)S(1)}, s32[2]{0:T(128)}, u32[]{:S(2)}) copy-start(s32[2]{0:T(128)} %constant.134) | copy-start | bytes 28
  18.5 9.3 %copy-start.19 = (f32[1,4,512]{2,1,0:T(4,128)S(1)}, f32[1,4,512]{2,1,0:T(4,128)}, u32[]{:S(2)}) copy-start(f32[1,4,512]{2,1,0:T(4,128)} %param.16) | copy-start | bytes 24580
  18.6 121.8 %all-to-all-start = ((f32[16,32,2,8,128]{4,3,2,1,0:T(8,128)}), f32[16,32,2,8,128]{4,3,2,1,0:T(8,128)}, u32[]{:S(2)}, u32[]{:S(2)}) async-start(f32[16,32,2,8,128]{4,3,2,1,0:T(8,128)} %bitcast.86), calls=%async_computation | async-start | bytes 8388608 | tf_op jit(solution)/shard_map/all_to_all | solution.py:115
  45.2 18.4 %copy-start.20 = (f32[1,4]{1,0:T(1,128)S(1)}, f32[1,4]{1,0:T(1,128)}, u32[]{:S(2)}) copy-start(f32[1,4]{1,0:T(1,128)} %param.13) | copy-start | bytes 52
  45.2 19.1 %copy-start.18 = (s32[1,128,16]{1,2,0:T(8,128)S(1)}, s32[1,128,16]{1,2,0:T(8,128)}, u32[]{:S(2)}) copy-start(s32[1,128,16]{1,2,0:T(8,128)} %param.17) | copy-start | bytes 24580
  52.2 15.5 %copy-start = (f32[8,128,128]{2,1,0:T(8,128)S(1)}, f32[8,128,128]{2,1,0:T(8,128)}, u32[]{:S(2)}) copy-start(f32[8,128,128]{2,1,0:T(8,128)} %param.9) | copy-start | bytes 1572868
  52.2 15.5 %copy-start.8 = (f32[1,2,8,128,128]{4,3,2,1,0:T(8,128)S(1)}, f32[1,2,8,128,128]{4,3,2,1,0:T(8,128)}, u32[]{:S(2)}) copy-start(f32[1,2,8,128,128]{4,3,2,1,0:T(8,128)} %param.12) | copy-start | bytes 3145732
  71.1 55.3 %copy-start.12 = (f32[1,131072]{1,0:T(1,128)S(1)}, f32[1,131072]{1,0:T(1,128)}, u32[]{:S(2)}) copy-start(f32[1,131072]{1,0:T(1,128)} %get-tuple-element.11) | copy-start | bytes 1572868
  71.2 54.5 %collective-permute-start.2 = (f32[4,128,128]{2,1,0:T(8,128)S(1)}, f32[4,128,128]{2,1,0:T(8,128)S(1)}, u32[]{:S(2)}, u32[]{:S(2)}) collective-permute-start(f32[4,128,128]{2,1,0:T(8,128)S(1)} %get-tuple-element.22), channel_id=1, source_target_pairs={{1,0},{2,1},{3,2},{4,3},{5,4},{6,5},{7,6},{8,7},{9,8},{10,9},{11,1... | collective-permute-start | bytes 786440 | tf_op jit(solution)/shard_map/ppermute | solution.py:17
  73.7 52.0 %collective-permute-start.3 = (f32[4,128,128]{2,1,0:T(8,128)S(1)}, f32[4,128,128]{2,1,0:T(8,128)S(1)}, u32[]{:S(2)}, u32[]{:S(2)}) collective-permute-start(f32[4,128,128]{2,1,0:T(8,128)S(1)} %get-tuple-element.21), channel_id=1, source_target_pairs={{0,1},{1,2},{2,3},{3,4},{4,5},{5,6},{6,7},{7,8},{8,9},{9,10},{10,1... | collective-permute-start | bytes 786440 | tf_op jit(solution)/shard_map/ppermute | solution.py:16
  129.9 70.1 %copy-start.1 = (f32[8,128,128]{2,1,0:T(8,128)}, f32[8,128,128]{2,1,0:T(8,128)S(1)}, u32[]{:S(2)}) copy-start(f32[8,128,128]{2,1,0:T(8,128)S(1)} %get-tuple-element.6) | copy-start | bytes 1572868
  130.8 46.5 %collective-permute-start.4 = (f32[4,128,128]{2,1,0:T(8,128)}, f32[4,128,128]{2,1,0:T(8,128)S(1)}, u32[]{:S(2)}, u32[]{:S(2)}) collective-permute-start(f32[4,128,128]{2,1,0:T(8,128)} %get-tuple-element.20), channel_id=1, source_target_pairs={{1,0},{2,1},{3,2},{4,3},{5,4},{6,5},{7,6},{8,7},{9,8},{10,9},{11,1... | collective-permute-start | bytes 786440 | tf_op jit(solution)/shard_map/ppermute | solution.py:17
  135.9 41.3 %collective-permute-start.5 = (f32[4,128,128]{2,1,0:T(8,128)}, f32[4,128,128]{2,1,0:T(8,128)}, u32[]{:S(2)}, u32[]{:S(2)}) collective-permute-start(f32[4,128,128]{2,1,0:T(8,128)} %get-tuple-element.19), channel_id=1, source_target_pairs={{0,1},{1,2},{2,3},{3,4},{4,5},{5,6},{6,7},{7,8},{8,9},{9,10},{10,1... | collective-permute-start | bytes 786440 | tf_op jit(solution)/shard_map/ppermute | solution.py:16
  145.6 13.3 %collective-permute-start.6 = (f32[4,128,128]{2,1,0:T(8,128)S(1)}, f32[4,128,128]{2,1,0:T(8,128)S(1)}, u32[]{:S(2)}, u32[]{:S(2)}) collective-permute-start(f32[4,128,128]{2,1,0:T(8,128)S(1)} %bitcast.102), channel_id=1, source_target_pairs={{1,0},{2,1},{3,2},{4,3},{5,4},{6,5},{7,6},{8,7},{9,8},{10,9},{11,1... | collective-permute-start | bytes 786440 | tf_op jit(solution)/shard_map/ppermute | solution.py:17
  148.6 15.6 %collective-permute-start.7 = (f32[4,128,128]{2,1,0:T(8,128)S(1)}, f32[4,128,128]{2,1,0:T(8,128)S(1)}, u32[]{:S(2)}, u32[]{:S(2)}) collective-permute-start(f32[4,128,128]{2,1,0:T(8,128)S(1)} %bitcast.101), channel_id=1, source_target_pairs={{0,1},{1,2},{2,3},{3,4},{4,5},{5,6},{6,7},{7,8},{8,9},{9,10},{10,1... | collective-permute-start | bytes 786440 | tf_op jit(solution)/shard_map/ppermute | solution.py:16
  167.8 13.7 %collective-permute-start.8 = (f32[4,128,128]{2,1,0:T(8,128)S(1)}, f32[4,128,128]{2,1,0:T(8,128)S(1)}, u32[]{:S(2)}, u32[]{:S(2)}) collective-permute-start(f32[4,128,128]{2,1,0:T(8,128)S(1)} %get-tuple-element.29), channel_id=1, source_target_pairs={{1,0},{2,1},{3,2},{4,3},{5,4},{6,5},{7,6},{8,7},{9,8},{10,9},{11,1... | collective-permute-start | bytes 786440 | tf_op jit(solution)/shard_map/ppermute | solution.py:17
  169.7 17.1 %collective-permute-start.9 = (f32[4,128,128]{2,1,0:T(8,128)S(1)}, f32[4,128,128]{2,1,0:T(8,128)S(1)}, u32[]{:S(2)}, u32[]{:S(2)}) collective-permute-start(f32[4,128,128]{2,1,0:T(8,128)S(1)} %get-tuple-element.30), channel_id=1, source_target_pairs={{0,1},{1,2},{2,3},{3,4},{4,5},{5,6},{6,7},{7,8},{8,9},{9,10},{10,1... | collective-permute-start | bytes 786440 | tf_op jit(solution)/shard_map/ppermute | solution.py:16
  187.4 12.6 %copy-start.11 = (f32[1,131072]{1,0:T(1,128)S(1)}, f32[1,131072]{1,0:T(1,128)}, u32[]{:S(2)}) copy-start(f32[1,131072]{1,0:T(1,128)} %get-tuple-element.10) | copy-start | bytes 1572868
  190.5 22.5 %collective-permute-start.10 = (f32[4,128,128]{2,1,0:T(8,128)S(1)}, f32[4,128,128]{2,1,0:T(8,128)S(1)}, u32[]{:S(2)}, u32[]{:S(2)}) collective-permute-start(f32[4,128,128]{2,1,0:T(8,128)S(1)} %get-tuple-element.27), channel_id=1, source_target_pairs={{1,0},{2,1},{3,2},{4,3},{5,4},{6,5},{7,6},{8,7},{9,8},{10,9},{11,1... | collective-permute-start | bytes 786440 | tf_op jit(solution)/shard_map/ppermute | solution.py:17
  192.4 20.6 %collective-permute-start.11 = (f32[4,128,128]{2,1,0:T(8,128)S(1)}, f32[4,128,128]{2,1,0:T(8,128)S(1)}, u32[]{:S(2)}, u32[]{:S(2)}) collective-permute-start(f32[4,128,128]{2,1,0:T(8,128)S(1)} %get-tuple-element.28), channel_id=1, source_target_pairs={{0,1},{1,2},{2,3},{3,4},{4,5},{5,6},{6,7},{7,8},{8,9},{9,10},{10,1... | collective-permute-start | bytes 786440 | tf_op jit(solution)/shard_map/ppermute | solution.py:16
  203.4 22.7 %copy-start.4 = (f32[8,128,128]{2,1,0:T(8,128)}, f32[8,128,128]{2,1,0:T(8,128)S(1)}, u32[]{:S(2)}) copy-start(f32[8,128,128]{2,1,0:T(8,128)S(1)} %get-tuple-element.3) | copy-start | bytes 1572868
  203.4 31.7 %copy-start.6 = (f32[8,128,128]{2,1,0:T(8,128)}, f32[8,128,128]{2,1,0:T(8,128)S(1)}, u32[]{:S(2)}) copy-start(f32[8,128,128]{2,1,0:T(8,128)S(1)} %get-tuple-element.4) | copy-start | bytes 1572868
  203.5 22.6 %collective-permute-start.14 = (f32[4,128,128]{2,1,0:T(8,128)S(1)}, f32[4,128,128]{2,1,0:T(8,128)S(1)}, u32[]{:S(2)}, u32[]{:S(2)}) collective-permute-start(f32[4,128,128]{2,1,0:T(8,128)S(1)} %get-tuple-element.18), channel_id=1, source_target_pairs={{1,0},{2,1},{3,2},{4,3},{5,4},{6,5},{7,6},{8,7},{9,8},{10,9},{11,1... | collective-permute-start | bytes 786440 | tf_op jit(solution)/shard_map/ppermute | solution.py:17
  205.4 20.7 %collective-permute-start.15 = (f32[4,128,128]{2,1,0:T(8,128)S(1)}, f32[4,128,128]{2,1,0:T(8,128)S(1)}, u32[]{:S(2)}, u32[]{:S(2)}) collective-permute-start(f32[4,128,128]{2,1,0:T(8,128)S(1)} %get-tuple-element.17), channel_id=1, source_target_pairs={{0,1},{1,2},{2,3},{3,4},{4,5},{5,6},{6,7},{7,8},{8,9},{9,10},{10,1... | collective-permute-start | bytes 786440 | tf_op jit(solution)/shard_map/ppermute | solution.py:16
  216.6 12.5 %collective-permute-start.12 = (f32[4,128,128]{2,1,0:T(8,128)S(1)}, f32[4,128,128]{2,1,0:T(8,128)S(1)}, u32[]{:S(2)}, u32[]{:S(2)}) collective-permute-start(f32[4,128,128]{2,1,0:T(8,128)S(1)} %get-tuple-element.25), channel_id=1, source_target_pairs={{1,0},{2,1},{3,2},{4,3},{5,4},{6,5},{7,6},{8,7},{9,8},{10,9},{11,1... | collective-permute-start | bytes 786440 | tf_op jit(solution)/shard_map/ppermute | solution.py:17
  218.5 15.9 %collective-permute-start.13 = (f32[4,128,128]{2,1,0:T(8,128)S(1)}, f32[4,128,128]{2,1,0:T(8,128)S(1)}, u32[]{:S(2)}, u32[]{:S(2)}) collective-permute-start(f32[4,128,128]{2,1,0:T(8,128)S(1)} %get-tuple-element.26), channel_id=1, source_target_pairs={{0,1},{1,2},{2,3},{3,4},{4,5},{5,6},{6,7},{7,8},{8,9},{9,10},{10,1... | collective-permute-start | bytes 786440 | tf_op jit(solution)/shard_map/ppermute | solution.py:16
  239.8 16.9 %all-to-all-start.1 = ((f32[16,9,8,128]{3,2,1,0:T(8,128)}), f32[16,9,8,128]{3,2,1,0:T(8,128)}, u32[]{:S(2)}, u32[]{:S(2)}) async-start(f32[16,9,8,128]{3,2,1,0:T(8,128)} %copy.30), calls=%async_computation.1 | async-start | bytes 1179648 | tf_op jit(solution)/shard_map/all_to_all | solution.py:184
  (10 other events, 50.9 us)

commit v12 on v4

--- a/solution.py
+++ b/solution.py
@@ -178,8 +178,9 @@
     pieces = stacked.reshape(length + 1, shot_devices, height // shot_devices, breadth)
     pieces = jnp.transpose(pieces, (1, 0, 2, 3))
     gathered = lax.all_to_all(pieces, "shot", split_axis=0, concat_axis=0, tiled=True)
-    grad_share = jnp.sum(gathered[:, :length], axis=0)
-    check_share = jnp.sum(gathered[:, length], axis=0)
+    shares = jnp.sum(gathered, axis=0)
+    grad_share = shares[:length]
+    check_share = shares[length]
     adjoint_carry = jnp.stack([adjoints[1], adjoints[0]])[None]
     return (grad_share, adjoint_carry, check_share[None])
 

time: 261 us -> 260 us (level)
  no operation moved by 1% of the time
where the time goes in v12:
time: 260 us; the launch traced here: 259 us
  starting transfers between devices  90.1 us (35%)
  waiting for transfers between devices  76.1 us (29%)
  other arithmetic  57.1 us (22%)
  local copies, waits for them, and re-layouts  32.8 us (13%)
    ppermute x8, starting transfers between devices, padded_2(): before = lax.ppermute(last, axis, up)  54.8 us
    ppermute x8, waiting for transfers between devices, padded_2(): after = lax.ppermute(initial, axis, down)  53.1 us
    ppermute x8, starting transfers between devices, padded_2(): after = lax.ppermute(initial, axis, down)  21 us
    ppermute x8, waiting for transfers between devices, padded_2(): before = lax.ppermute(last, axis, up)  16 us
    unnamed x4, other arithmetic  14.5 us
    mul x4, other arithmetic, body(): weighted = extend(courant * adjoints[moment])  11.4 us
    all_to_all x1, starting transfers between devices, body(): lax.all_to_all(outgoing, 'space', split_axis=0, concat_axis=0, tiled=True)  9.02 us
    add x3, other arithmetic, inject_dense(): return field + jnp.where(cells == local_cell, values[0], 0.0)  8.8 us
  transfers between devices with their start and end apart: 18, of which 8 were waited for; matrix products, arithmetic and copies ran while one was open for 30% of the time, Pallas kernels for 0%

profile of v12, /device:TPU:100, one launch (start us, length us, event | category | flops | bytes accessed | tf_op | source)
XLA Modules:
  0.0 258.9 jit_solution(8281477606322890097)
XLA Ops:
  5.2 7.0 %collective-permute-start.1 = (f32[4,128,128]{2,1,0:T(8,128)}, f32[4,128,128]{2,1,0:T(8,128)S(1)}, u32[]{:S(2)}, u32[]{:S(2)}) collective-permute-start(f32[4,128,128]{2,1,0:T(8,128)} %get-tuple-element.23), channel_id=1, source_target_pairs={{0,1},{1,2},{2,3},{3,4},{4,5},{5,6},{6,7},{7,8},{8,9},{9,10},{10,1... | collective-permute-start | bytes 786440 | tf_op jit(solution)/shard_map/ppermute | solution.py:16
  15.0 3.5 %gather_fusion = f32[512,2,8,128]{3,2,1,0:T(8,128)} fusion(f32[129,2,8,128]{3,2,0,1:T(8,128)S(1)} %concatenate.142, s32[1024]{0:T(1024)S(1)} %pad_clamp_fusion.1), kind=kCustom, calls=%fused_computation | custom fusion | bytes 8390656 | tf_op jit(solution)/shard_map/jit(_take)/gather | solution.py:113
  18.6 9.0 %all-to-all-start = ((f32[16,32,2,8,128]{4,3,2,1,0:T(8,128)}), f32[16,32,2,8,128]{4,3,2,1,0:T(8,128)}, u32[]{:S(2)}, u32[]{:S(2)}) async-start(f32[16,32,2,8,128]{4,3,2,1,0:T(8,128)} %bitcast.85), calls=%async_computation | async-start | bytes 8388608 | tf_op jit(solution)/shard_map/all_to_all | solution.py:115
  27.9 14.3 %scatter_custom_fusion.2 = f32[524292]{0:T(1024)S(1)} fusion(s32[2048]{0:T(1024)S(1)} %bitcast.109, f32[2048]{0:T(1024)S(1)} %bitcast.110, f32[]{:T(128)} %constant.52.clone.1), kind=kCustom, calls=%fused_computation.82 | custom fusion | flops 2048 | bytes 2097172
  44.9 7.1 %fusion.323 = (f32[1,131072]{1,0:T(1,128)}, f32[1,131072]{1,0:T(1,128)}, f32[1,131072]{1,0:T(1,128)}, f32[1,131072]{1,0:T(1,128)}) fusion(f32[4,131073]{1,0:T(4,128)} %reshape.304), kind=kLoop, calls=%fused_computation.567 | loop fusion | bytes 4194304 | tf_op jit(solution)/shard_map/slice | solution.py:165
  52.1 2.8 %select_reduce_fusion = s32[16,128]{0,1:T(8,128)S(1)} fusion(s32[16,128]{0,1:T(8,128)S(1)} %copy.27), kind=kOutput, calls=%fused_computation.86 | output fusion | flops 4388864 | bytes 16384 | tf_op jit(solution)/shard_map/jit(cumsum)/reduce_window_sum | solution.py:119
  55.1 8.2 %scatter_custom_fusion = s32[128]{0:T(128)S(1)} fusion(s32[2048]{0:T(1024)S(1)} %bitcast.108, s32[2048]{0:T(1024)S(1)} %add_bitcast_fusion, s32[]{:T(128)} %constant.91.clone.1), kind=kCustom, calls=%fused_computation.560 | custom fusion | bytes 516 | tf_op jit(solution)/shard_map/scatter | solution.py:126
  67.5 3.4 %fusion.321 = (f32[8,128,128]{2,1,0:T(8,128)S(1)}, f32[8,128,128]{2,1,0:T(8,128)S(1)}) fusion(f32[8,128,128]{2,1,0:T(8,128)S(1)} %copy-done, f32[8,128,128]{2,1,0:T(8,128)S(1)} %bitcast.98, f32[16,136,136]{2,1,0:T(8,128)S(1)} %select_maximum_fusion.14, f32[8,128,128]{2,1,0:T(8,128)S(1)} %bitcast_multiply_fusion, f32[4,128,128]{2,1,0:T(8,128)} %copy-done.14, ...), kind=kLoop, calls=%fused_computation.566 | loop fusion | flops 6553600 | bytes 12582912 | tf_op jit(solution)/shard_map/mul | solution.py:160
  73.7 6.9 %collective-permute-start.3 = (f32[4,128,128]{2,1,0:T(8,128)S(1)}, f32[4,128,128]{2,1,0:T(8,128)S(1)}, u32[]{:S(2)}, u32[]{:S(2)}) collective-permute-start(f32[4,128,128]{2,1,0:T(8,128)S(1)} %get-tuple-element.21), channel_id=1, source_target_pairs={{0,1},{1,2},{2,3},{3,4},{4,5},{5,6},{6,7},{7,8},{8,9},{9,10},{10,1... | collective-permute-start | bytes 786440 | tf_op jit(solution)/shard_map/ppermute | solution.py:16
  81.3 44.5 %collective-permute-done.2 = f32[4,128,128]{2,1,0:T(8,128)S(1)} collective-permute-done((f32[4,128,128]{2,1,0:T(8,128)S(1)}, f32[4,128,128]{2,1,0:T(8,128)S(1)}, u32[]{:S(2)}, u32[]{:S(2)}) %collective-permute-start.2) | collective-permute-done | bytes 262176 | tf_op jit(solution)/shard_map/ppermute | solution.py:17
  126.4 3.4 %fusion.319 = (f32[8,128,128]{2,1,0:T(8,128)S(1)}, f32[8,128,128]{2,1,0:T(8,128)S(1)}) fusion(f32[8,128,128]{2,1,0:T(8,128)S(1)} %copy-done, f32[8,128,128]{2,1,0:T(8,128)S(1)} %bitcast.97, f32[16,136,136]{2,1,0:T(8,128)S(1)} %select_maximum_fusion.12, f32[8,128,128]{2,1,0:T(8,128)S(1)} %get-tuple-element.7, f32[4,128,128]{2,1,0:T(8,128)} %copy-done.16, ...), kind=kLoop, calls=%fused_computation.565 | loop fusion | flops 6553600 | bytes 12582912 | tf_op jit(solution)/shard_map/mul | solution.py:160
  130.8 5.2 %collective-permute-start.4 = (f32[4,128,128]{2,1,0:T(8,128)}, f32[4,128,128]{2,1,0:T(8,128)S(1)}, u32[]{:S(2)}, u32[]{:S(2)}) collective-permute-start(f32[4,128,128]{2,1,0:T(8,128)} %get-tuple-element.20), channel_id=1, source_target_pairs={{1,0},{2,1},{3,2},{4,3},{5,4},{6,5},{7,6},{8,7},{9,8},{10,9},{11,1... | collective-permute-start | bytes 786440 | tf_op jit(solution)/shard_map/ppermute | solution.py:17
  136.0 4.3 %collective-permute-start.5 = (f32[4,128,128]{2,1,0:T(8,128)}, f32[4,128,128]{2,1,0:T(8,128)}, u32[]{:S(2)}, u32[]{:S(2)}) collective-permute-start(f32[4,128,128]{2,1,0:T(8,128)} %get-tuple-element.19), channel_id=1, source_target_pairs={{0,1},{1,2},{2,3},{3,4},{4,5},{5,6},{6,7},{7,8},{8,9},{9,10},{10,1... | collective-permute-start | bytes 786440 | tf_op jit(solution)/shard_map/ppermute | solution.py:16
  140.3 3.8 %gather_fusion.1 = f32[128,2,8,128]{3,2,1,0:T(8,128)} fusion(f32[512,2,8,128]{3,2,1,0:T(8,128)} %bitcast.17, s32[1024]{0:T(1024)S(1)} %pad_clamp_fusion), kind=kCustom, calls=%fused_computation.1 | custom fusion | bytes 2097664 | tf_op jit(solution)/shard_map/jit(_take)/gather | solution.py:128
  145.6 3.0 %collective-permute-start.6 = (f32[4,128,128]{2,1,0:T(8,128)S(1)}, f32[4,128,128]{2,1,0:T(8,128)S(1)}, u32[]{:S(2)}, u32[]{:S(2)}) collective-permute-start(f32[4,128,128]{2,1,0:T(8,128)S(1)} %bitcast.101), channel_id=1, source_target_pairs={{1,0},{2,1},{3,2},{4,3},{5,4},{6,5},{7,6},{8,7},{9,8},{10,9},{11,1... | collective-permute-start | bytes 786440 | tf_op jit(solution)/shard_map/ppermute | solution.py:17
  148.6 6.4 %collective-permute-start.7 = (f32[4,128,128]{2,1,0:T(8,128)S(1)}, f32[4,128,128]{2,1,0:T(8,128)S(1)}, u32[]{:S(2)}, u32[]{:S(2)}) collective-permute-start(f32[4,128,128]{2,1,0:T(8,128)S(1)} %bitcast.100), channel_id=1, source_target_pairs={{0,1},{1,2},{2,3},{3,4},{4,5},{5,6},{6,7},{7,8},{8,9},{9,10},{10,1... | collective-permute-start | bytes 786440 | tf_op jit(solution)/shard_map/ppermute | solution.py:16
  155.1 3.7 %collective-permute-done.6 = f32[4,128,128]{2,1,0:T(8,128)S(1)} collective-permute-done((f32[4,128,128]{2,1,0:T(8,128)S(1)}, f32[4,128,128]{2,1,0:T(8,128)S(1)}, u32[]{:S(2)}, u32[]{:S(2)}) %collective-permute-start.6) | collective-permute-done | bytes 262176 | tf_op jit(solution)/shard_map/ppermute | solution.py:17
  158.8 5.3 %collective-permute-done.7 = f32[4,128,128]{2,1,0:T(8,128)S(1)} collective-permute-done((f32[4,128,128]{2,1,0:T(8,128)S(1)}, f32[4,128,128]{2,1,0:T(8,128)S(1)}, u32[]{:S(2)}, u32[]{:S(2)}) %collective-permute-start.7) | collective-permute-done | bytes 262176 | tf_op jit(solution)/shard_map/ppermute | solution.py:16
  164.8 2.9 %fusion.135 = f32[8,128,128]{2,1,0:T(8,128)S(1)} fusion(f32[8,128,128]{2,1,0:T(8,128)S(1)} %copy-done, f32[8,128,128]{2,1,0:T(8,128)S(1)} %bitcast.87, f32[4,128,128]{2,1,0:T(8,128)S(1)} %collective-permute-done.7, f32[4,128,128]{2,1,0:T(8,128)S(1)} %collective-permute-done.6, f32[16,136,136]{2,1,0:T(8,128)S(1)} %select_maximum_fusion.8, ...), kind=kLoop, calls=%fused_computation.263 | loop fusion | flops 7077888 | bytes 11010600 | tf_op jit(solution)/shard_map/add | solution.py:63
  169.7 7.5 %collective-permute-start.9 = (f32[4,128,128]{2,1,0:T(8,128)S(1)}, f32[4,128,128]{2,1,0:T(8,128)S(1)}, u32[]{:S(2)}, u32[]{:S(2)}) collective-permute-start(f32[4,128,128]{2,1,0:T(8,128)S(1)} %get-tuple-element.30), channel_id=1, source_target_pairs={{0,1},{1,2},{2,3},{3,4},{4,5},{5,6},{6,7},{7,8},{8,9},{9,10},{10,1... | collective-permute-start | bytes 786440 | tf_op jit(solution)/shard_map/ppermute | solution.py:16
  181.5 5.3 %collective-permute-done.9 = f32[4,128,128]{2,1,0:T(8,128)S(1)} collective-permute-done((f32[4,128,128]{2,1,0:T(8,128)S(1)}, f32[4,128,128]{2,1,0:T(8,128)S(1)}, u32[]{:S(2)}, u32[]{:S(2)}) %collective-permute-start.9) | collective-permute-done | bytes 262176 | tf_op jit(solution)/shard_map/ppermute | solution.py:16
  187.5 3.0 %fusion.108 = f32[8,128,128]{2,1,0:T(8,128)S(1)} fusion(f32[8,128,128]{2,1,0:T(8,128)S(1)} %copy-done, f32[8,128,128]{2,1,0:T(8,128)S(1)} %fusion.135, f32[4,128,128]{2,1,0:T(8,128)S(1)} %collective-permute-done.9, f32[4,128,128]{2,1,0:T(8,128)S(1)} %collective-permute-done.8, f32[16,136,136]{2,1,0:T(8,128)S(1)} %select_maximum_fusion.6, ...), kind=kLoop, calls=%fused_computation.236 | loop fusion | flops 7077888 | bytes 11010600 | tf_op jit(solution)/shard_map/add | solution.py:63
  192.4 7.5 %collective-permute-start.11 = (f32[4,128,128]{2,1,0:T(8,128)S(1)}, f32[4,128,128]{2,1,0:T(8,128)S(1)}, u32[]{:S(2)}, u32[]{:S(2)}) collective-permute-start(f32[4,128,128]{2,1,0:T(8,128)S(1)} %get-tuple-element.28), channel_id=1, source_target_pairs={{0,1},{1,2},{2,3},{3,4},{4,5},{5,6},{6,7},{7,8},{8,9},{9,10},{10,1... | collective-permute-start | bytes 786440 | tf_op jit(solution)/shard_map/ppermute | solution.py:16
  200.0 3.3 %fusion.317 = (f32[8,128,128]{2,1,0:T(8,128)S(1)}, f32[8,128,128]{2,1,0:T(8,128)S(1)}) fusion(f32[8,128,128]{2,1,0:T(8,128)S(1)} %copy-done, f32[8,128,128]{2,1,0:T(8,128)S(1)} %bitcast.96, f32[16,136,136]{2,1,0:T(8,128)S(1)} %select_maximum_fusion.10, f32[8,128,128]{2,1,0:T(8,128)S(1)} %get-tuple-element.5, f32[4,128,128]{2,1,0:T(8,128)} %collective-permute-done.5, ...), kind=kLoop, calls=%fused_computation.564 | loop fusion | flops 6553600 | bytes 12582912 | tf_op jit(solution)/shard_map/mul | solution.py:160
  205.4 7.5 %collective-permute-start.15 = (f32[4,128,128]{2,1,0:T(8,128)S(1)}, f32[4,128,128]{2,1,0:T(8,128)S(1)}, u32[]{:S(2)}, u32[]{:S(2)}) collective-permute-start(f32[4,128,128]{2,1,0:T(8,128)S(1)} %get-tuple-element.17), channel_id=1, source_target_pairs={{0,1},{1,2},{2,3},{3,4},{4,5},{5,6},{6,7},{7,8},{8,9},{9,10},{10,1... | collective-permute-start | bytes 786440 | tf_op jit(solution)/shard_map/ppermute | solution.py:16
  213.6 2.9 %fusion.81 = f32[8,128,128]{2,1,0:T(8,128)S(1)} fusion(f32[8,128,128]{2,1,0:T(8,128)S(1)} %copy-done, f32[8,128,128]{2,1,0:T(8,128)S(1)} %fusion.108, f32[4,128,128]{2,1,0:T(8,128)S(1)} %collective-permute-done.11, f32[4,128,128]{2,1,0:T(8,128)S(1)} %collective-permute-done.10, f32[16,136,136]{2,1,0:T(8,128)S(1)} %select_maximum_fusion.4, ...), kind=kLoop, calls=%fused_computation.209 | loop fusion | flops 7077888 | bytes 11010600 | tf_op jit(solution)/shard_map/add | solution.py:63
  218.4 7.5 %collective-permute-start.13 = (f32[4,128,128]{2,1,0:T(8,128)S(1)}, f32[4,128,128]{2,1,0:T(8,128)S(1)}, u32[]{:S(2)}, u32[]{:S(2)}) collective-permute-start(f32[4,128,128]{2,1,0:T(8,128)S(1)} %get-tuple-element.26), channel_id=1, source_target_pairs={{0,1},{1,2},{2,3},{3,4},{4,5},{5,6},{6,7},{7,8},{8,9},{9,10},{10,1... | collective-permute-start | bytes 786440 | tf_op jit(solution)/shard_map/ppermute | solution.py:16
  229.0 5.3 %collective-permute-done.13 = f32[4,128,128]{2,1,0:T(8,128)S(1)} collective-permute-done((f32[4,128,128]{2,1,0:T(8,128)S(1)}, f32[4,128,128]{2,1,0:T(8,128)S(1)}, u32[]{:S(2)}, u32[]{:S(2)}) %collective-permute-start.13) | collective-permute-done | bytes 262176 | tf_op jit(solution)/shard_map/ppermute | solution.py:16
  235.0 3.0 %fusion.54 = f32[8,128,128]{2,1,0:T(8,128)S(1)} fusion(f32[8,128,128]{2,1,0:T(8,128)S(1)} %fusion.108, f32[8,128,128]{2,1,0:T(8,128)S(1)} %copy-done, f32[8,128,128]{2,1,0:T(8,128)S(1)} %fusion.81, f32[4,128,128]{2,1,0:T(8,128)S(1)} %collective-permute-done.13, f32[4,128,128]{2,1,0:T(8,128)S(1)} %collective-permute-done.12, ...), kind=kLoop, calls=%fused_computation.182 | loop fusion | flops 9437184 | bytes 14680616 | tf_op jit(solution)/shard_map/add | solution.py:169
  239.6 5.3 %all-to-all-start.1 = ((f32[16,9,8,128]{3,2,1,0:T(8,128)}), f32[16,9,8,128]{3,2,1,0:T(8,128)}, u32[]{:S(2)}, u32[]{:S(2)}) async-start(f32[16,9,8,128]{3,2,1,0:T(8,128)} %copy.30), calls=%async_computation.1 | async-start | bytes 1179648 | tf_op jit(solution)/shard_map/all_to_all | solution.py:180
  244.9 3.5 %fusion.307 = f32[1,8,128,128]{3,2,1,0:T(8,128)S(1)} fusion(f32[8,128,128]{2,1,0:T(8,128)} %bitcast.95, f32[16,136,136]{2,1,0:T(8,128)S(1)} %select_maximum_fusion, f32[8,128,128]{2,1,0:T(8,128)S(1)} %copy-done.5, f32[4,128,128]{2,1,0:T(8,128)} %copy-done.15, f32[4,128,128]{2,1,0:T(8,128)S(1)} %collective-permute-done.14, f32[8,128,128]{2,1,0:T(8,128)S(1)} %copy-done.3, ...), kind=kLoop, calls=%fused_computation.520 | loop fusion | flops 6422528 | bytes 11534336 | tf_op jit(solution)/shard_map/stack | solution.py:184
  249.5 7.0 %all-to-all-done.1 = f32[16,9,8,128]{3,2,1,0:T(8,128)} async-done(((f32[16,9,8,128]{3,2,1,0:T(8,128)}), f32[16,9,8,128]{3,2,1,0:T(8,128)}, u32[]{:S(2)}, u32[]{:S(2)}) %all-to-all-start.1) | async-done | bytes 589856 | tf_op jit(solution)/shard_map/all_to_all | solution.py:180
  (126 shorter events, 43.1 us)
Async XLA Ops:
  0.6 11.6 %copy-start.17 = (s32[1,2048]{1,0:T(1,128)S(1)}, s32[1,2048]{1,0:T(1,128)}, u32[]{:S(2)}) copy-start(s32[1,2048]{1,0:T(1,128)} %param.11) | copy-start | bytes 24580
  2.8 64.1 %collective-permute-start = (f32[4,128,128]{2,1,0:T(8,128)}, f32[4,128,128]{2,1,0:T(8,128)S(1)}, u32[]{:S(2)}, u32[]{:S(2)}) collective-permute-start(f32[4,128,128]{2,1,0:T(8,128)} %get-tuple-element.24), channel_id=1, source_target_pairs={{1,0},{2,1},{3,2},{4,3},{5,4},{6,5},{7,6},{8,7},{9,8},{10,9},{11,1... | collective-permute-start | bytes 786440 | tf_op jit(solution)/shard_map/ppermute | solution.py:17
  5.2 61.7 %collective-permute-start.1 = (f32[4,128,128]{2,1,0:T(8,128)}, f32[4,128,128]{2,1,0:T(8,128)S(1)}, u32[]{:S(2)}, u32[]{:S(2)}) collective-permute-start(f32[4,128,128]{2,1,0:T(8,128)} %get-tuple-element.23), channel_id=1, source_target_pairs={{0,1},{1,2},{2,3},{3,4},{4,5},{5,6},{6,7},{7,8},{8,9},{9,10},{10,1... | collective-permute-start | bytes 786440 | tf_op jit(solution)/shard_map/ppermute | solution.py:16
  18.6 9.0 %copy-start.21 = (s32[1,512]{1,0:T(1,128)S(1)}, s32[1,512]{1,0:T(1,128)}, u32[]{:S(2)}) copy-start(s32[1,512]{1,0:T(1,128)} %param.15) | copy-start | bytes 6148
  18.6 9.1 %copy-start.23 = (s32[2]{0:T(128)S(1)}, s32[2]{0:T(128)}, u32[]{:S(2)}) copy-start(s32[2]{0:T(128)} %constant.131) | copy-start | bytes 28
  18.6 9.2 %copy-start.22 = (s32[2]{0:T(128)S(1)}, s32[2]{0:T(128)}, u32[]{:S(2)}) copy-start(s32[2]{0:T(128)} %constant.134) | copy-start | bytes 28
  18.6 9.3 %copy-start.19 = (f32[1,4,512]{2,1,0:T(4,128)S(1)}, f32[1,4,512]{2,1,0:T(4,128)}, u32[]{:S(2)}) copy-start(f32[1,4,512]{2,1,0:T(4,128)} %param.16) | copy-start | bytes 24580
  18.6 121.7 %all-to-all-start = ((f32[16,32,2,8,128]{4,3,2,1,0:T(8,128)}), f32[16,32,2,8,128]{4,3,2,1,0:T(8,128)}, u32[]{:S(2)}, u32[]{:S(2)}) async-start(f32[16,32,2,8,128]{4,3,2,1,0:T(8,128)} %bitcast.85), calls=%async_computation | async-start | bytes 8388608 | tf_op jit(solution)/shard_map/all_to_all | solution.py:115
  44.9 18.5 %copy-start.20 = (f32[1,4]{1,0:T(1,128)S(1)}, f32[1,4]{1,0:T(1,128)}, u32[]{:S(2)}) copy-start(f32[1,4]{1,0:T(1,128)} %param.13) | copy-start | bytes 52
  44.9 19.1 %copy-start.18 = (s32[1,128,16]{1,2,0:T(8,128)S(1)}, s32[1,128,16]{1,2,0:T(8,128)}, u32[]{:S(2)}) copy-start(s32[1,128,16]{1,2,0:T(8,128)} %param.17) | copy-start | bytes 24580
  52.0 15.5 %copy-start = (f32[8,128,128]{2,1,0:T(8,128)S(1)}, f32[8,128,128]{2,1,0:T(8,128)}, u32[]{:S(2)}) copy-start(f32[8,128,128]{2,1,0:T(8,128)} %param.9) | copy-start | bytes 1572868
  52.0 15.5 %copy-start.8 = (f32[1,2,8,128,128]{4,3,2,1,0:T(8,128)S(1)}, f32[1,2,8,128,128]{4,3,2,1,0:T(8,128)}, u32[]{:S(2)}) copy-start(f32[1,2,8,128,128]{4,3,2,1,0:T(8,128)} %param.12) | copy-start | bytes 3145732
  70.9 55.5 %copy-start.12 = (f32[1,131072]{1,0:T(1,128)S(1)}, f32[1,131072]{1,0:T(1,128)}, u32[]{:S(2)}) copy-start(f32[1,131072]{1,0:T(1,128)} %get-tuple-element.11) | copy-start | bytes 1572868
  71.0 54.7 %collective-permute-start.2 = (f32[4,128,128]{2,1,0:T(8,128)S(1)}, f32[4,128,128]{2,1,0:T(8,128)S(1)}, u32[]{:S(2)}, u32[]{:S(2)}) collective-permute-start(f32[4,128,128]{2,1,0:T(8,128)S(1)} %get-tuple-element.22), channel_id=1, source_target_pairs={{1,0},{2,1},{3,2},{4,3},{5,4},{6,5},{7,6},{8,7},{9,8},{10,9},{11,1... | collective-permute-start | bytes 786440 | tf_op jit(solution)/shard_map/ppermute | solution.py:17
  73.7 52.0 %collective-permute-start.3 = (f32[4,128,128]{2,1,0:T(8,128)S(1)}, f32[4,128,128]{2,1,0:T(8,128)S(1)}, u32[]{:S(2)}, u32[]{:S(2)}) collective-permute-start(f32[4,128,128]{2,1,0:T(8,128)S(1)} %get-tuple-element.21), channel_id=1, source_target_pairs={{0,1},{1,2},{2,3},{3,4},{4,5},{5,6},{6,7},{7,8},{8,9},{9,10},{10,1... | collective-permute-start | bytes 786440 | tf_op jit(solution)/shard_map/ppermute | solution.py:16
  129.9 70.1 %copy-start.1 = (f32[8,128,128]{2,1,0:T(8,128)}, f32[8,128,128]{2,1,0:T(8,128)S(1)}, u32[]{:S(2)}) copy-start(f32[8,128,128]{2,1,0:T(8,128)S(1)} %get-tuple-element.6) | copy-start | bytes 1572868
  130.8 46.5 %collective-permute-start.4 = (f32[4,128,128]{2,1,0:T(8,128)}, f32[4,128,128]{2,1,0:T(8,128)S(1)}, u32[]{:S(2)}, u32[]{:S(2)}) collective-permute-start(f32[4,128,128]{2,1,0:T(8,128)} %get-tuple-element.20), channel_id=1, source_target_pairs={{1,0},{2,1},{3,2},{4,3},{5,4},{6,5},{7,6},{8,7},{9,8},{10,9},{11,1... | collective-permute-start | bytes 786440 | tf_op jit(solution)/shard_map/ppermute | solution.py:17
  136.0 41.3 %collective-permute-start.5 = (f32[4,128,128]{2,1,0:T(8,128)}, f32[4,128,128]{2,1,0:T(8,128)}, u32[]{:S(2)}, u32[]{:S(2)}) collective-permute-start(f32[4,128,128]{2,1,0:T(8,128)} %get-tuple-element.19), channel_id=1, source_target_pairs={{0,1},{1,2},{2,3},{3,4},{4,5},{5,6},{6,7},{7,8},{8,9},{9,10},{10,1... | collective-permute-start | bytes 786440 | tf_op jit(solution)/shard_map/ppermute | solution.py:16
  145.6 13.3 %collective-permute-start.6 = (f32[4,128,128]{2,1,0:T(8,128)S(1)}, f32[4,128,128]{2,1,0:T(8,128)S(1)}, u32[]{:S(2)}, u32[]{:S(2)}) collective-permute-start(f32[4,128,128]{2,1,0:T(8,128)S(1)} %bitcast.101), channel_id=1, source_target_pairs={{1,0},{2,1},{3,2},{4,3},{5,4},{6,5},{7,6},{8,7},{9,8},{10,9},{11,1... | collective-permute-start | bytes 786440 | tf_op jit(solution)/shard_map/ppermute | solution.py:17
  148.6 15.6 %collective-permute-start.7 = (f32[4,128,128]{2,1,0:T(8,128)S(1)}, f32[4,128,128]{2,1,0:T(8,128)S(1)}, u32[]{:S(2)}, u32[]{:S(2)}) collective-permute-start(f32[4,128,128]{2,1,0:T(8,128)S(1)} %bitcast.100), channel_id=1, source_target_pairs={{0,1},{1,2},{2,3},{3,4},{4,5},{5,6},{6,7},{7,8},{8,9},{9,10},{10,1... | collective-permute-start | bytes 786440 | tf_op jit(solution)/shard_map/ppermute | solution.py:16
  167.8 13.7 %collective-permute-start.8 = (f32[4,128,128]{2,1,0:T(8,128)S(1)}, f32[4,128,128]{2,1,0:T(8,128)S(1)}, u32[]{:S(2)}, u32[]{:S(2)}) collective-permute-start(f32[4,128,128]{2,1,0:T(8,128)S(1)} %get-tuple-element.29), channel_id=1, source_target_pairs={{1,0},{2,1},{3,2},{4,3},{5,4},{6,5},{7,6},{8,7},{9,8},{10,9},{11,1... | collective-permute-start | bytes 786440 | tf_op jit(solution)/shard_map/ppermute | solution.py:17
  169.7 17.1 %collective-permute-start.9 = (f32[4,128,128]{2,1,0:T(8,128)S(1)}, f32[4,128,128]{2,1,0:T(8,128)S(1)}, u32[]{:S(2)}, u32[]{:S(2)}) collective-permute-start(f32[4,128,128]{2,1,0:T(8,128)S(1)} %get-tuple-element.30), channel_id=1, source_target_pairs={{0,1},{1,2},{2,3},{3,4},{4,5},{5,6},{6,7},{7,8},{8,9},{9,10},{10,1... | collective-permute-start | bytes 786440 | tf_op jit(solution)/shard_map/ppermute | solution.py:16
  187.4 12.6 %copy-start.11 = (f32[1,131072]{1,0:T(1,128)S(1)}, f32[1,131072]{1,0:T(1,128)}, u32[]{:S(2)}) copy-start(f32[1,131072]{1,0:T(1,128)} %get-tuple-element.10) | copy-start | bytes 1572868
  190.5 22.4 %collective-permute-start.10 = (f32[4,128,128]{2,1,0:T(8,128)S(1)}, f32[4,128,128]{2,1,0:T(8,128)S(1)}, u32[]{:S(2)}, u32[]{:S(2)}) collective-permute-start(f32[4,128,128]{2,1,0:T(8,128)S(1)} %get-tuple-element.27), channel_id=1, source_target_pairs={{1,0},{2,1},{3,2},{4,3},{5,4},{6,5},{7,6},{8,7},{9,8},{10,9},{11,1... | collective-permute-start | bytes 786440 | tf_op jit(solution)/shard_map/ppermute | solution.py:17
  192.4 20.5 %collective-permute-start.11 = (f32[4,128,128]{2,1,0:T(8,128)S(1)}, f32[4,128,128]{2,1,0:T(8,128)S(1)}, u32[]{:S(2)}, u32[]{:S(2)}) collective-permute-start(f32[4,128,128]{2,1,0:T(8,128)S(1)} %get-tuple-element.28), channel_id=1, source_target_pairs={{0,1},{1,2},{2,3},{3,4},{4,5},{5,6},{6,7},{7,8},{8,9},{9,10},{10,1... | collective-permute-start | bytes 786440 | tf_op jit(solution)/shard_map/ppermute | solution.py:16
  203.4 22.6 %copy-start.4 = (f32[8,128,128]{2,1,0:T(8,128)}, f32[8,128,128]{2,1,0:T(8,128)S(1)}, u32[]{:S(2)}) copy-start(f32[8,128,128]{2,1,0:T(8,128)S(1)} %get-tuple-element.3) | copy-start | bytes 1572868
  203.4 31.6 %copy-start.6 = (f32[8,128,128]{2,1,0:T(8,128)}, f32[8,128,128]{2,1,0:T(8,128)S(1)}, u32[]{:S(2)}) copy-start(f32[8,128,128]{2,1,0:T(8,128)S(1)} %get-tuple-element.4) | copy-start | bytes 1572868
  203.4 22.5 %collective-permute-start.14 = (f32[4,128,128]{2,1,0:T(8,128)S(1)}, f32[4,128,128]{2,1,0:T(8,128)S(1)}, u32[]{:S(2)}, u32[]{:S(2)}) collective-permute-start(f32[4,128,128]{2,1,0:T(8,128)S(1)} %get-tuple-element.18), channel_id=1, source_target_pairs={{1,0},{2,1},{3,2},{4,3},{5,4},{6,5},{7,6},{8,7},{9,8},{10,9},{11,1... | collective-permute-start | bytes 786440 | tf_op jit(solution)/shard_map/ppermute | solution.py:17
  205.4 20.6 %collective-permute-start.15 = (f32[4,128,128]{2,1,0:T(8,128)S(1)}, f32[4,128,128]{2,1,0:T(8,128)S(1)}, u32[]{:S(2)}, u32[]{:S(2)}) collective-permute-start(f32[4,128,128]{2,1,0:T(8,128)S(1)} %get-tuple-element.17), channel_id=1, source_target_pairs={{0,1},{1,2},{2,3},{3,4},{4,5},{5,6},{6,7},{7,8},{8,9},{9,10},{10,1... | collective-permute-start | bytes 786440 | tf_op jit(solution)/shard_map/ppermute | solution.py:16
  216.5 12.5 %collective-permute-start.12 = (f32[4,128,128]{2,1,0:T(8,128)S(1)}, f32[4,128,128]{2,1,0:T(8,128)S(1)}, u32[]{:S(2)}, u32[]{:S(2)}) collective-permute-start(f32[4,128,128]{2,1,0:T(8,128)S(1)} %get-tuple-element.25), channel_id=1, source_target_pairs={{1,0},{2,1},{3,2},{4,3},{5,4},{6,5},{7,6},{8,7},{9,8},{10,9},{11,1... | collective-permute-start | bytes 786440 | tf_op jit(solution)/shard_map/ppermute | solution.py:17
  218.4 15.9 %collective-permute-start.13 = (f32[4,128,128]{2,1,0:T(8,128)S(1)}, f32[4,128,128]{2,1,0:T(8,128)S(1)}, u32[]{:S(2)}, u32[]{:S(2)}) collective-permute-start(f32[4,128,128]{2,1,0:T(8,128)S(1)} %get-tuple-element.26), channel_id=1, source_target_pairs={{0,1},{1,2},{2,3},{3,4},{4,5},{5,6},{6,7},{7,8},{8,9},{9,10},{10,1... | collective-permute-start | bytes 786440 | tf_op jit(solution)/shard_map/ppermute | solution.py:16
  239.6 16.9 %all-to-all-start.1 = ((f32[16,9,8,128]{3,2,1,0:T(8,128)}), f32[16,9,8,128]{3,2,1,0:T(8,128)}, u32[]{:S(2)}, u32[]{:S(2)}) async-start(f32[16,9,8,128]{3,2,1,0:T(8,128)} %copy.30), calls=%async_computation.1 | async-start | bytes 1179648 | tf_op jit(solution)/shard_map/all_to_all | solution.py:180
  (10 other events, 50.9 us)

commit v13 on v12

--- a/solution.py
+++ b/solution.py
@@ -125,7 +125,7 @@
         .at[jnp.where(owned, local_block, per_device).reshape(-1)]
         .set(sender_grid.reshape(-1), mode="drop")
     )
-    placed = jnp.transpose(jnp.take(incoming, where_from, axis=0), (1, 0, 2, 3))
+    placed = jnp.transpose(jnp.take(incoming, where_from, axis=0, mode="clip"), (1, 0, 2, 3))
     levels = placed.reshape(2, length, height, breadth)
     wavelet_row = wavelet[0]
     receivers = receiver_cell[0]

time: 260 us -> 258 us (level)
  transfers between devices with their start and end apart: 18 -> 18, of which waited for: 8 -> 8; matrix products, arithmetic and copies ran while one was open for 30% -> 29% of each run, Pallas kernels for 0% -> 0%
where the time goes in v13:
time: 258 us; the launch traced here: 257 us
  starting transfers between devices  90.4 us (35%)
  waiting for transfers between devices  75.9 us (29%)
  other arithmetic  55.9 us (22%)
  local copies, waits for them, and re-layouts  31.8 us (12%)
    ppermute x8, starting transfers between devices, padded_2(): before = lax.ppermute(last, axis, up)  55.5 us
    ppermute x8, waiting for transfers between devices, padded_2(): after = lax.ppermute(initial, axis, down)  53.2 us
    ppermute x8, starting transfers between devices, padded_2(): after = lax.ppermute(initial, axis, down)  20.6 us
    ppermute x8, waiting for transfers between devices, padded_2(): before = lax.ppermute(last, axis, up)  15.7 us
    unnamed x4, other arithmetic  14.7 us
    mul x4, other arithmetic, body(): weighted = extend(courant * adjoints[moment])  11.4 us
    all_to_all x1, starting transfers between devices, body(): lax.all_to_all(outgoing, 'space', split_axis=0, concat_axis=0, tiled=True)  9.02 us
    add x3, other arithmetic, inject_dense(): return field + jnp.where(cells == local_cell, values[0], 0.0)  8.8 us
  transfers between devices with their start and end apart: 18, of which 8 were waited for; matrix products, arithmetic and copies ran while one was open for 29% of the time, Pallas kernels for 0%

profile of v13, /device:TPU:100, one launch (start us, length us, event | category | flops | bytes accessed | tf_op | source)
XLA Modules:
  0.0 256.7 jit_solution(2256448113229304884)
XLA Ops:
  5.2 7.0 %collective-permute-start.1 = (f32[4,128,128]{2,1,0:T(8,128)}, f32[4,128,128]{2,1,0:T(8,128)S(1)}, u32[]{:S(2)}, u32[]{:S(2)}) collective-permute-start(f32[4,128,128]{2,1,0:T(8,128)} %get-tuple-element.23), channel_id=1, source_target_pairs={{0,1},{1,2},{2,3},{3,4},{4,5},{5,6},{6,7},{7,8},{8,9},{9,10},{10,1... | collective-permute-start | bytes 786440 | tf_op jit(solution)/shard_map/ppermute | solution.py:16
  15.0 3.5 %gather_fusion = f32[512,2,8,128]{3,2,1,0:T(8,128)} fusion(f32[129,2,8,128]{3,2,0,1:T(8,128)S(1)} %concatenate.142, s32[1024]{0:T(1024)S(1)} %pad_clamp_fusion.1), kind=kCustom, calls=%fused_computation | custom fusion | bytes 8390656 | tf_op jit(solution)/shard_map/jit(_take)/gather | solution.py:113
  18.6 9.0 %all-to-all-start = ((f32[16,32,2,8,128]{4,3,2,1,0:T(8,128)}), f32[16,32,2,8,128]{4,3,2,1,0:T(8,128)}, u32[]{:S(2)}, u32[]{:S(2)}) async-start(f32[16,32,2,8,128]{4,3,2,1,0:T(8,128)} %bitcast.84), calls=%async_computation | async-start | bytes 8388608 | tf_op jit(solution)/shard_map/all_to_all | solution.py:115
  27.9 14.5 %scatter_custom_fusion.2 = f32[524292]{0:T(1024)S(1)} fusion(s32[2048]{0:T(1024)S(1)} %bitcast.110, f32[2048]{0:T(1024)S(1)} %bitcast.111, f32[]{:T(128)} %constant.43.clone.1), kind=kCustom, calls=%fused_computation.82 | custom fusion | flops 2048 | bytes 2097172
  45.1 7.1 %fusion.323 = (f32[1,131072]{1,0:T(1,128)}, f32[1,131072]{1,0:T(1,128)}, f32[1,131072]{1,0:T(1,128)}, f32[1,131072]{1,0:T(1,128)}) fusion(f32[4,131073]{1,0:T(4,128)} %reshape.299), kind=kLoop, calls=%fused_computation.564 | loop fusion | bytes 4194304 | tf_op jit(solution)/shard_map/slice | solution.py:165
  52.3 2.8 %select_reduce_fusion = s32[16,128]{0,1:T(8,128)S(1)} fusion(s32[16,128]{0,1:T(8,128)S(1)} %copy.27), kind=kOutput, calls=%fused_computation.85 | output fusion | flops 4388864 | bytes 16384 | tf_op jit(solution)/shard_map/jit(cumsum)/reduce_window_sum | solution.py:119
  55.3 8.2 %scatter_custom_fusion.1 = s32[128]{0:T(128)S(1)} fusion(s32[2048]{0:T(1024)S(1)} %bitcast.109, s32[2048]{0:T(1024)S(1)} %add_bitcast_fusion, s32[]{:T(128)} %constant.79.clone.1), kind=kCustom, calls=%fused_computation.557 | custom fusion | bytes 516 | tf_op jit(solution)/shard_map/scatter | solution.py:126
  64.9 3.4 %fusion.321 = (f32[8,128,128]{2,1,0:T(8,128)S(1)}, f32[8,128,128]{2,1,0:T(8,128)S(1)}) fusion(f32[8,128,128]{2,1,0:T(8,128)S(1)} %copy-done, f32[8,128,128]{2,1,0:T(8,128)S(1)} %bitcast.99, f32[16,136,136]{2,1,0:T(8,128)S(1)} %select_maximum_fusion.14, f32[8,128,128]{2,1,0:T(8,128)S(1)} %bitcast_multiply_fusion, f32[4,128,128]{2,1,0:T(8,128)} %copy-done.14, ...), kind=kLoop, calls=%fused_computation.563 | loop fusion | flops 6553600 | bytes 12582912 | tf_op jit(solution)/shard_map/mul | solution.py:160
  70.8 7.1 %collective-permute-start.3 = (f32[4,128,128]{2,1,0:T(8,128)S(1)}, f32[4,128,128]{2,1,0:T(8,128)S(1)}, u32[]{:S(2)}, u32[]{:S(2)}) collective-permute-start(f32[4,128,128]{2,1,0:T(8,128)S(1)} %get-tuple-element.21), channel_id=1, source_target_pairs={{0,1},{1,2},{2,3},{3,4},{4,5},{5,6},{6,7},{7,8},{8,9},{9,10},{10,1... | collective-permute-start | bytes 786440 | tf_op jit(solution)/shard_map/ppermute | solution.py:16
  81.4 44.3 %collective-permute-done.2 = f32[4,128,128]{2,1,0:T(8,128)S(1)} collective-permute-done((f32[4,128,128]{2,1,0:T(8,128)S(1)}, f32[4,128,128]{2,1,0:T(8,128)S(1)}, u32[]{:S(2)}, u32[]{:S(2)}) %collective-permute-start.2) | collective-permute-done | bytes 262176 | tf_op jit(solution)/shard_map/ppermute | solution.py:17
  126.4 3.4 %fusion.319 = (f32[8,128,128]{2,1,0:T(8,128)S(1)}, f32[8,128,128]{2,1,0:T(8,128)S(1)}) fusion(f32[8,128,128]{2,1,0:T(8,128)S(1)} %copy-done, f32[8,128,128]{2,1,0:T(8,128)S(1)} %bitcast.98, f32[16,136,136]{2,1,0:T(8,128)S(1)} %select_maximum_fusion.12, f32[8,128,128]{2,1,0:T(8,128)S(1)} %get-tuple-element.7, f32[4,128,128]{2,1,0:T(8,128)} %copy-done.16, ...), kind=kLoop, calls=%fused_computation.562 | loop fusion | flops 6553600 | bytes 12582912 | tf_op jit(solution)/shard_map/mul | solution.py:160
  130.8 5.1 %collective-permute-start.4 = (f32[4,128,128]{2,1,0:T(8,128)}, f32[4,128,128]{2,1,0:T(8,128)S(1)}, u32[]{:S(2)}, u32[]{:S(2)}) collective-permute-start(f32[4,128,128]{2,1,0:T(8,128)} %get-tuple-element.20), channel_id=1, source_target_pairs={{1,0},{2,1},{3,2},{4,3},{5,4},{6,5},{7,6},{8,7},{9,8},{10,9},{11,1... | collective-permute-start | bytes 786440 | tf_op jit(solution)/shard_map/ppermute | solution.py:17
  135.9 4.4 %collective-permute-start.5 = (f32[4,128,128]{2,1,0:T(8,128)}, f32[4,128,128]{2,1,0:T(8,128)}, u32[]{:S(2)}, u32[]{:S(2)}) collective-permute-start(f32[4,128,128]{2,1,0:T(8,128)} %get-tuple-element.19), channel_id=1, source_target_pairs={{0,1},{1,2},{2,3},{3,4},{4,5},{5,6},{6,7},{7,8},{8,9},{9,10},{10,1... | collective-permute-start | bytes 786440 | tf_op jit(solution)/shard_map/ppermute | solution.py:16
  140.4 2.8 %gather_fusion.1 = f32[128,2,8,128]{3,2,1,0:T(8,128)S(1)} fusion(f32[512,2,8,128]{3,2,1,0:T(8,128)} %bitcast.14, s32[1024]{0:T(1024)S(1)} %pad_clamp_fusion), kind=kCustom, calls=%fused_computation.1 | custom fusion | bytes 2097664 | tf_op jit(solution)/shard_map/jit(_take)/gather | solution.py:128
  143.3 2.9 %collective-permute-start.6 = (f32[4,128,128]{2,1,0:T(8,128)S(1)}, f32[4,128,128]{2,1,0:T(8,128)S(1)}, u32[]{:S(2)}, u32[]{:S(2)}) collective-permute-start(f32[4,128,128]{2,1,0:T(8,128)S(1)} %bitcast.102), channel_id=1, source_target_pairs={{1,0},{2,1},{3,2},{4,3},{5,4},{6,5},{7,6},{8,7},{9,8},{10,9},{11,1... | collective-permute-start | bytes 786440 | tf_op jit(solution)/shard_map/ppermute | solution.py:17
  146.2 6.5 %collective-permute-start.7 = (f32[4,128,128]{2,1,0:T(8,128)S(1)}, f32[4,128,128]{2,1,0:T(8,128)S(1)}, u32[]{:S(2)}, u32[]{:S(2)}) collective-permute-start(f32[4,128,128]{2,1,0:T(8,128)S(1)} %bitcast.101), channel_id=1, source_target_pairs={{0,1},{1,2},{2,3},{3,4},{4,5},{5,6},{6,7},{7,8},{8,9},{9,10},{10,1... | collective-permute-start | bytes 786440 | tf_op jit(solution)/shard_map/ppermute | solution.py:16
  152.8 4.1 %collective-permute-done.6 = f32[4,128,128]{2,1,0:T(8,128)S(1)} collective-permute-done((f32[4,128,128]{2,1,0:T(8,128)S(1)}, f32[4,128,128]{2,1,0:T(8,128)S(1)}, u32[]{:S(2)}, u32[]{:S(2)}) %collective-permute-start.6) | collective-permute-done | bytes 262176 | tf_op jit(solution)/shard_map/ppermute | solution.py:17
  156.9 5.0 %collective-permute-done.7 = f32[4,128,128]{2,1,0:T(8,128)S(1)} collective-permute-done((f32[4,128,128]{2,1,0:T(8,128)S(1)}, f32[4,128,128]{2,1,0:T(8,128)S(1)}, u32[]{:S(2)}, u32[]{:S(2)}) %collective-permute-start.7) | collective-permute-done | bytes 262176 | tf_op jit(solution)/shard_map/ppermute | solution.py:16
  162.5 2.9 %fusion.135 = f32[8,128,128]{2,1,0:T(8,128)S(1)} fusion(f32[8,128,128]{2,1,0:T(8,128)S(1)} %copy-done, f32[8,128,128]{2,1,0:T(8,128)S(1)} %bitcast.86, f32[4,128,128]{2,1,0:T(8,128)S(1)} %collective-permute-done.7, f32[4,128,128]{2,1,0:T(8,128)S(1)} %collective-permute-done.6, f32[16,136,136]{2,1,0:T(8,128)S(1)} %select_maximum_fusion.8, ...), kind=kLoop, calls=%fused_computation.262 | loop fusion | flops 7077888 | bytes 11010600 | tf_op jit(solution)/shard_map/add | solution.py:63
  167.4 7.5 %collective-permute-start.9 = (f32[4,128,128]{2,1,0:T(8,128)S(1)}, f32[4,128,128]{2,1,0:T(8,128)S(1)}, u32[]{:S(2)}, u32[]{:S(2)}) collective-permute-start(f32[4,128,128]{2,1,0:T(8,128)S(1)} %get-tuple-element.30), channel_id=1, source_target_pairs={{0,1},{1,2},{2,3},{3,4},{4,5},{5,6},{6,7},{7,8},{8,9},{9,10},{10,1... | collective-permute-start | bytes 786440 | tf_op jit(solution)/shard_map/ppermute | solution.py:16
  179.1 5.3 %collective-permute-done.9 = f32[4,128,128]{2,1,0:T(8,128)S(1)} collective-permute-done((f32[4,128,128]{2,1,0:T(8,128)S(1)}, f32[4,128,128]{2,1,0:T(8,128)S(1)}, u32[]{:S(2)}, u32[]{:S(2)}) %collective-permute-start.9) | collective-permute-done | bytes 262176 | tf_op jit(solution)/shard_map/ppermute | solution.py:16
  185.1 3.0 %fusion.108 = f32[8,128,128]{2,1,0:T(8,128)S(1)} fusion(f32[8,128,128]{2,1,0:T(8,128)S(1)} %copy-done, f32[8,128,128]{2,1,0:T(8,128)S(1)} %fusion.135, f32[4,128,128]{2,1,0:T(8,128)S(1)} %collective-permute-done.9, f32[4,128,128]{2,1,0:T(8,128)S(1)} %collective-permute-done.8, f32[16,136,136]{2,1,0:T(8,128)S(1)} %select_maximum_fusion.6, ...), kind=kLoop, calls=%fused_computation.235 | loop fusion | flops 7077888 | bytes 11010600 | tf_op jit(solution)/shard_map/add | solution.py:63
  190.1 7.5 %collective-permute-start.11 = (f32[4,128,128]{2,1,0:T(8,128)S(1)}, f32[4,128,128]{2,1,0:T(8,128)S(1)}, u32[]{:S(2)}, u32[]{:S(2)}) collective-permute-start(f32[4,128,128]{2,1,0:T(8,128)S(1)} %get-tuple-element.28), channel_id=1, source_target_pairs={{0,1},{1,2},{2,3},{3,4},{4,5},{5,6},{6,7},{7,8},{8,9},{9,10},{10,1... | collective-permute-start | bytes 786440 | tf_op jit(solution)/shard_map/ppermute | solution.py:16
  197.7 3.3 %fusion.317 = (f32[8,128,128]{2,1,0:T(8,128)S(1)}, f32[8,128,128]{2,1,0:T(8,128)S(1)}) fusion(f32[8,128,128]{2,1,0:T(8,128)S(1)} %copy-done, f32[8,128,128]{2,1,0:T(8,128)S(1)} %bitcast.97, f32[16,136,136]{2,1,0:T(8,128)S(1)} %select_maximum_fusion.10, f32[8,128,128]{2,1,0:T(8,128)S(1)} %get-tuple-element.5, f32[4,128,128]{2,1,0:T(8,128)} %collective-permute-done.5, ...), kind=kLoop, calls=%fused_computation.561 | loop fusion | flops 6553600 | bytes 12582912 | tf_op jit(solution)/shard_map/mul | solution.py:160
  203.0 7.8 %collective-permute-start.15 = (f32[4,128,128]{2,1,0:T(8,128)S(1)}, f32[4,128,128]{2,1,0:T(8,128)S(1)}, u32[]{:S(2)}, u32[]{:S(2)}) collective-permute-start(f32[4,128,128]{2,1,0:T(8,128)S(1)} %get-tuple-element.17), channel_id=1, source_target_pairs={{0,1},{1,2},{2,3},{3,4},{4,5},{5,6},{6,7},{7,8},{8,9},{9,10},{10,1... | collective-permute-start | bytes 786440 | tf_op jit(solution)/shard_map/ppermute | solution.py:16
  211.5 2.9 %fusion.81 = f32[8,128,128]{2,1,0:T(8,128)S(1)} fusion(f32[8,128,128]{2,1,0:T(8,128)S(1)} %copy-done, f32[8,128,128]{2,1,0:T(8,128)S(1)} %fusion.108, f32[4,128,128]{2,1,0:T(8,128)S(1)} %collective-permute-done.11, f32[4,128,128]{2,1,0:T(8,128)S(1)} %collective-permute-done.10, f32[16,136,136]{2,1,0:T(8,128)S(1)} %select_maximum_fusion.4, ...), kind=kLoop, calls=%fused_computation.208 | loop fusion | flops 7077888 | bytes 11010600 | tf_op jit(solution)/shard_map/add | solution.py:63
  216.3 7.5 %collective-permute-start.13 = (f32[4,128,128]{2,1,0:T(8,128)S(1)}, f32[4,128,128]{2,1,0:T(8,128)S(1)}, u32[]{:S(2)}, u32[]{:S(2)}) collective-permute-start(f32[4,128,128]{2,1,0:T(8,128)S(1)} %get-tuple-element.26), channel_id=1, source_target_pairs={{0,1},{1,2},{2,3},{3,4},{4,5},{5,6},{6,7},{7,8},{8,9},{9,10},{10,1... | collective-permute-start | bytes 786440 | tf_op jit(solution)/shard_map/ppermute | solution.py:16
  226.9 5.3 %collective-permute-done.13 = f32[4,128,128]{2,1,0:T(8,128)S(1)} collective-permute-done((f32[4,128,128]{2,1,0:T(8,128)S(1)}, f32[4,128,128]{2,1,0:T(8,128)S(1)}, u32[]{:S(2)}, u32[]{:S(2)}) %collective-permute-start.13) | collective-permute-done | bytes 262176 | tf_op jit(solution)/shard_map/ppermute | solution.py:16
  232.9 3.0 %fusion.54 = f32[8,128,128]{2,1,0:T(8,128)S(1)} fusion(f32[8,128,128]{2,1,0:T(8,128)S(1)} %fusion.108, f32[8,128,128]{2,1,0:T(8,128)S(1)} %copy-done, f32[8,128,128]{2,1,0:T(8,128)S(1)} %fusion.81, f32[4,128,128]{2,1,0:T(8,128)S(1)} %collective-permute-done.13, f32[4,128,128]{2,1,0:T(8,128)S(1)} %collective-permute-done.12, ...), kind=kLoop, calls=%fused_computation.181 | loop fusion | flops 9437184 | bytes 14680616 | tf_op jit(solution)/shard_map/add | solution.py:169
  237.5 5.3 %all-to-all-start.1 = ((f32[16,9,8,128]{3,2,1,0:T(8,128)}), f32[16,9,8,128]{3,2,1,0:T(8,128)}, u32[]{:S(2)}, u32[]{:S(2)}) async-start(f32[16,9,8,128]{3,2,1,0:T(8,128)} %copy.30), calls=%async_computation.1 | async-start | bytes 1179648 | tf_op jit(solution)/shard_map/all_to_all | solution.py:180
  242.8 3.5 %fusion.307 = f32[1,8,128,128]{3,2,1,0:T(8,128)S(1)} fusion(f32[8,128,128]{2,1,0:T(8,128)} %bitcast.96, f32[16,136,136]{2,1,0:T(8,128)S(1)} %select_maximum_fusion, f32[8,128,128]{2,1,0:T(8,128)S(1)} %copy-done.5, f32[4,128,128]{2,1,0:T(8,128)} %copy-done.15, f32[4,128,128]{2,1,0:T(8,128)S(1)} %collective-permute-done.14, f32[8,128,128]{2,1,0:T(8,128)S(1)} %copy-done.3, ...), kind=kLoop, calls=%fused_computation.519 | loop fusion | flops 6422528 | bytes 11534336 | tf_op jit(solution)/shard_map/stack | solution.py:184
  247.4 7.0 %all-to-all-done.1 = f32[16,9,8,128]{3,2,1,0:T(8,128)} async-done(((f32[16,9,8,128]{3,2,1,0:T(8,128)}), f32[16,9,8,128]{3,2,1,0:T(8,128)}, u32[]{:S(2)}, u32[]{:S(2)}) %all-to-all-start.1) | async-done | bytes 589856 | tf_op jit(solution)/shard_map/all_to_all | solution.py:180
  (123 shorter events, 41.4 us)
Async XLA Ops:
  0.6 11.6 %copy-start.17 = (s32[1,2048]{1,0:T(1,128)S(1)}, s32[1,2048]{1,0:T(1,128)}, u32[]{:S(2)}) copy-start(s32[1,2048]{1,0:T(1,128)} %param.11) | copy-start | bytes 24580
  2.8 61.4 %collective-permute-start = (f32[4,128,128]{2,1,0:T(8,128)}, f32[4,128,128]{2,1,0:T(8,128)S(1)}, u32[]{:S(2)}, u32[]{:S(2)}) collective-permute-start(f32[4,128,128]{2,1,0:T(8,128)} %get-tuple-element.24), channel_id=1, source_target_pairs={{1,0},{2,1},{3,2},{4,3},{5,4},{6,5},{7,6},{8,7},{9,8},{10,9},{11,1... | collective-permute-start | bytes 786440 | tf_op jit(solution)/shard_map/ppermute | solution.py:17
  5.2 59.0 %collective-permute-start.1 = (f32[4,128,128]{2,1,0:T(8,128)}, f32[4,128,128]{2,1,0:T(8,128)S(1)}, u32[]{:S(2)}, u32[]{:S(2)}) collective-permute-start(f32[4,128,128]{2,1,0:T(8,128)} %get-tuple-element.23), channel_id=1, source_target_pairs={{0,1},{1,2},{2,3},{3,4},{4,5},{5,6},{6,7},{7,8},{8,9},{9,10},{10,1... | collective-permute-start | bytes 786440 | tf_op jit(solution)/shard_map/ppermute | solution.py:16
  18.6 9.0 %copy-start.21 = (s32[1,512]{1,0:T(1,128)S(1)}, s32[1,512]{1,0:T(1,128)}, u32[]{:S(2)}) copy-start(s32[1,512]{1,0:T(1,128)} %param.15) | copy-start | bytes 6148
  18.6 9.1 %copy-start.23 = (s32[2]{0:T(128)S(1)}, s32[2]{0:T(128)}, u32[]{:S(2)}) copy-start(s32[2]{0:T(128)} %constant.117) | copy-start | bytes 28
  18.6 9.2 %copy-start.22 = (s32[2]{0:T(128)S(1)}, s32[2]{0:T(128)}, u32[]{:S(2)}) copy-start(s32[2]{0:T(128)} %constant.120) | copy-start | bytes 28
  18.6 9.3 %copy-start.19 = (f32[1,4,512]{2,1,0:T(4,128)S(1)}, f32[1,4,512]{2,1,0:T(4,128)}, u32[]{:S(2)}) copy-start(f32[1,4,512]{2,1,0:T(4,128)} %param.16) | copy-start | bytes 24580
  18.6 121.8 %all-to-all-start = ((f32[16,32,2,8,128]{4,3,2,1,0:T(8,128)}), f32[16,32,2,8,128]{4,3,2,1,0:T(8,128)}, u32[]{:S(2)}, u32[]{:S(2)}) async-start(f32[16,32,2,8,128]{4,3,2,1,0:T(8,128)} %bitcast.84), calls=%async_computation | async-start | bytes 8388608 | tf_op jit(solution)/shard_map/all_to_all | solution.py:115
  45.1 18.5 %copy-start.20 = (f32[1,4]{1,0:T(1,128)S(1)}, f32[1,4]{1,0:T(1,128)}, u32[]{:S(2)}) copy-start(f32[1,4]{1,0:T(1,128)} %param.13) | copy-start | bytes 52
  52.2 12.7 %copy-start = (f32[8,128,128]{2,1,0:T(8,128)S(1)}, f32[8,128,128]{2,1,0:T(8,128)}, u32[]{:S(2)}) copy-start(f32[8,128,128]{2,1,0:T(8,128)} %param.9) | copy-start | bytes 1572868
  52.2 12.7 %copy-start.8 = (f32[1,2,8,128,128]{4,3,2,1,0:T(8,128)S(1)}, f32[1,2,8,128,128]{4,3,2,1,0:T(8,128)}, u32[]{:S(2)}) copy-start(f32[1,2,8,128,128]{4,3,2,1,0:T(8,128)} %param.12) | copy-start | bytes 3145732
  64.9 13.7 %copy-start.18 = (s32[1,128,16]{1,2,0:T(8,128)S(1)}, s32[1,128,16]{1,2,0:T(8,128)}, u32[]{:S(2)}) copy-start(s32[1,128,16]{1,2,0:T(8,128)} %param.17) | copy-start | bytes 24580
  68.4 58.1 %copy-start.12 = (f32[1,131072]{1,0:T(1,128)S(1)}, f32[1,131072]{1,0:T(1,128)}, u32[]{:S(2)}) copy-start(f32[1,131072]{1,0:T(1,128)} %get-tuple-element.11) | copy-start | bytes 1572868
  68.4 57.3 %collective-permute-start.2 = (f32[4,128,128]{2,1,0:T(8,128)S(1)}, f32[4,128,128]{2,1,0:T(8,128)S(1)}, u32[]{:S(2)}, u32[]{:S(2)}) collective-permute-start(f32[4,128,128]{2,1,0:T(8,128)S(1)} %get-tuple-element.22), channel_id=1, source_target_pairs={{1,0},{2,1},{3,2},{4,3},{5,4},{6,5},{7,6},{8,7},{9,8},{10,9},{11,1... | collective-permute-start | bytes 786440 | tf_op jit(solution)/shard_map/ppermute | solution.py:17
  70.8 54.9 %collective-permute-start.3 = (f32[4,128,128]{2,1,0:T(8,128)S(1)}, f32[4,128,128]{2,1,0:T(8,128)S(1)}, u32[]{:S(2)}, u32[]{:S(2)}) collective-permute-start(f32[4,128,128]{2,1,0:T(8,128)S(1)} %get-tuple-element.21), channel_id=1, source_target_pairs={{0,1},{1,2},{2,3},{3,4},{4,5},{5,6},{6,7},{7,8},{8,9},{9,10},{10,1... | collective-permute-start | bytes 786440 | tf_op jit(solution)/shard_map/ppermute | solution.py:16
  129.9 67.8 %copy-start.1 = (f32[8,128,128]{2,1,0:T(8,128)}, f32[8,128,128]{2,1,0:T(8,128)S(1)}, u32[]{:S(2)}) copy-start(f32[8,128,128]{2,1,0:T(8,128)S(1)} %get-tuple-element.6) | copy-start | bytes 1572868
  130.8 44.2 %collective-permute-start.4 = (f32[4,128,128]{2,1,0:T(8,128)}, f32[4,128,128]{2,1,0:T(8,128)S(1)}, u32[]{:S(2)}, u32[]{:S(2)}) collective-permute-start(f32[4,128,128]{2,1,0:T(8,128)} %get-tuple-element.20), channel_id=1, source_target_pairs={{1,0},{2,1},{3,2},{4,3},{5,4},{6,5},{7,6},{8,7},{9,8},{10,9},{11,1... | collective-permute-start | bytes 786440 | tf_op jit(solution)/shard_map/ppermute | solution.py:17
  135.9 39.1 %collective-permute-start.5 = (f32[4,128,128]{2,1,0:T(8,128)}, f32[4,128,128]{2,1,0:T(8,128)}, u32[]{:S(2)}, u32[]{:S(2)}) collective-permute-start(f32[4,128,128]{2,1,0:T(8,128)} %get-tuple-element.19), channel_id=1, source_target_pairs={{0,1},{1,2},{2,3},{3,4},{4,5},{5,6},{6,7},{7,8},{8,9},{9,10},{10,1... | collective-permute-start | bytes 786440 | tf_op jit(solution)/shard_map/ppermute | solution.py:16
  143.3 13.6 %collective-permute-start.6 = (f32[4,128,128]{2,1,0:T(8,128)S(1)}, f32[4,128,128]{2,1,0:T(8,128)S(1)}, u32[]{:S(2)}, u32[]{:S(2)}) collective-permute-start(f32[4,128,128]{2,1,0:T(8,128)S(1)} %bitcast.102), channel_id=1, source_target_pairs={{1,0},{2,1},{3,2},{4,3},{5,4},{6,5},{7,6},{8,7},{9,8},{10,9},{11,1... | collective-permute-start | bytes 786440 | tf_op jit(solution)/shard_map/ppermute | solution.py:17
  146.2 15.7 %collective-permute-start.7 = (f32[4,128,128]{2,1,0:T(8,128)S(1)}, f32[4,128,128]{2,1,0:T(8,128)S(1)}, u32[]{:S(2)}, u32[]{:S(2)}) collective-permute-start(f32[4,128,128]{2,1,0:T(8,128)S(1)} %bitcast.101), channel_id=1, source_target_pairs={{0,1},{1,2},{2,3},{3,4},{4,5},{5,6},{6,7},{7,8},{8,9},{9,10},{10,1... | collective-permute-start | bytes 786440 | tf_op jit(solution)/shard_map/ppermute | solution.py:16
  165.5 13.7 %collective-permute-start.8 = (f32[4,128,128]{2,1,0:T(8,128)S(1)}, f32[4,128,128]{2,1,0:T(8,128)S(1)}, u32[]{:S(2)}, u32[]{:S(2)}) collective-permute-start(f32[4,128,128]{2,1,0:T(8,128)S(1)} %get-tuple-element.29), channel_id=1, source_target_pairs={{1,0},{2,1},{3,2},{4,3},{5,4},{6,5},{7,6},{8,7},{9,8},{10,9},{11,1... | collective-permute-start | bytes 786440 | tf_op jit(solution)/shard_map/ppermute | solution.py:17
  167.4 17.1 %collective-permute-start.9 = (f32[4,128,128]{2,1,0:T(8,128)S(1)}, f32[4,128,128]{2,1,0:T(8,128)S(1)}, u32[]{:S(2)}, u32[]{:S(2)}) collective-permute-start(f32[4,128,128]{2,1,0:T(8,128)S(1)} %get-tuple-element.30), channel_id=1, source_target_pairs={{0,1},{1,2},{2,3},{3,4},{4,5},{5,6},{6,7},{7,8},{8,9},{9,10},{10,1... | collective-permute-start | bytes 786440 | tf_op jit(solution)/shard_map/ppermute | solution.py:16
  185.1 12.6 %copy-start.11 = (f32[1,131072]{1,0:T(1,128)S(1)}, f32[1,131072]{1,0:T(1,128)}, u32[]{:S(2)}) copy-start(f32[1,131072]{1,0:T(1,128)} %get-tuple-element.10) | copy-start | bytes 1572868
  188.2 22.6 %collective-permute-start.10 = (f32[4,128,128]{2,1,0:T(8,128)S(1)}, f32[4,128,128]{2,1,0:T(8,128)S(1)}, u32[]{:S(2)}, u32[]{:S(2)}) collective-permute-start(f32[4,128,128]{2,1,0:T(8,128)S(1)} %get-tuple-element.27), channel_id=1, source_target_pairs={{1,0},{2,1},{3,2},{4,3},{5,4},{6,5},{7,6},{8,7},{9,8},{10,9},{11,1... | collective-permute-start | bytes 786440 | tf_op jit(solution)/shard_map/ppermute | solution.py:17
  190.1 20.7 %collective-permute-start.11 = (f32[4,128,128]{2,1,0:T(8,128)S(1)}, f32[4,128,128]{2,1,0:T(8,128)S(1)}, u32[]{:S(2)}, u32[]{:S(2)}) collective-permute-start(f32[4,128,128]{2,1,0:T(8,128)S(1)} %get-tuple-element.28), channel_id=1, source_target_pairs={{0,1},{1,2},{2,3},{3,4},{4,5},{5,6},{6,7},{7,8},{8,9},{9,10},{10,1... | collective-permute-start | bytes 786440 | tf_op jit(solution)/shard_map/ppermute | solution.py:16
  201.0 22.8 %copy-start.4 = (f32[8,128,128]{2,1,0:T(8,128)}, f32[8,128,128]{2,1,0:T(8,128)S(1)}, u32[]{:S(2)}) copy-start(f32[8,128,128]{2,1,0:T(8,128)S(1)} %get-tuple-element.3) | copy-start | bytes 1572868
  201.1 31.9 %copy-start.6 = (f32[8,128,128]{2,1,0:T(8,128)}, f32[8,128,128]{2,1,0:T(8,128)S(1)}, u32[]{:S(2)}) copy-start(f32[8,128,128]{2,1,0:T(8,128)S(1)} %get-tuple-element.4) | copy-start | bytes 1572868
  201.1 22.7 %collective-permute-start.14 = (f32[4,128,128]{2,1,0:T(8,128)S(1)}, f32[4,128,128]{2,1,0:T(8,128)S(1)}, u32[]{:S(2)}, u32[]{:S(2)}) collective-permute-start(f32[4,128,128]{2,1,0:T(8,128)S(1)} %get-tuple-element.18), channel_id=1, source_target_pairs={{1,0},{2,1},{3,2},{4,3},{5,4},{6,5},{7,6},{8,7},{9,8},{10,9},{11,1... | collective-permute-start | bytes 786440 | tf_op jit(solution)/shard_map/ppermute | solution.py:17
  203.0 20.8 %collective-permute-start.15 = (f32[4,128,128]{2,1,0:T(8,128)S(1)}, f32[4,128,128]{2,1,0:T(8,128)S(1)}, u32[]{:S(2)}, u32[]{:S(2)}) collective-permute-start(f32[4,128,128]{2,1,0:T(8,128)S(1)} %get-tuple-element.17), channel_id=1, source_target_pairs={{0,1},{1,2},{2,3},{3,4},{4,5},{5,6},{6,7},{7,8},{8,9},{9,10},{10,1... | collective-permute-start | bytes 786440 | tf_op jit(solution)/shard_map/ppermute | solution.py:16
  214.4 12.5 %collective-permute-start.12 = (f32[4,128,128]{2,1,0:T(8,128)S(1)}, f32[4,128,128]{2,1,0:T(8,128)S(1)}, u32[]{:S(2)}, u32[]{:S(2)}) collective-permute-start(f32[4,128,128]{2,1,0:T(8,128)S(1)} %get-tuple-element.25), channel_id=1, source_target_pairs={{1,0},{2,1},{3,2},{4,3},{5,4},{6,5},{7,6},{8,7},{9,8},{10,9},{11,1... | collective-permute-start | bytes 786440 | tf_op jit(solution)/shard_map/ppermute | solution.py:17
  216.3 15.9 %collective-permute-start.13 = (f32[4,128,128]{2,1,0:T(8,128)S(1)}, f32[4,128,128]{2,1,0:T(8,128)S(1)}, u32[]{:S(2)}, u32[]{:S(2)}) collective-permute-start(f32[4,128,128]{2,1,0:T(8,128)S(1)} %get-tuple-element.26), channel_id=1, source_target_pairs={{0,1},{1,2},{2,3},{3,4},{4,5},{5,6},{6,7},{7,8},{8,9},{9,10},{10,1... | collective-permute-start | bytes 786440 | tf_op jit(solution)/shard_map/ppermute | solution.py:16
  237.5 16.9 %all-to-all-start.1 = ((f32[16,9,8,128]{3,2,1,0:T(8,128)}), f32[16,9,8,128]{3,2,1,0:T(8,128)}, u32[]{:S(2)}, u32[]{:S(2)}) async-start(f32[16,9,8,128]{3,2,1,0:T(8,128)} %copy.30), calls=%async_computation.1 | async-start | bytes 1179648 | tf_op jit(solution)/shard_map/all_to_all | solution.py:180
  (10 other events, 48.9 us)
